TPU v7x, 512 devices: a whole 4x8x8 slice. The times are simulated.
512 devices in a mesh: sub: 8 (over x, core), seq: 8 (over y), exp: 8 (over z).
Axes of the slice: x: 4, y: 8, z: 8, core: 2. Of those that a mesh axis runs over, the one named last changes fastest.
Arguments:
- node_features: bfloat16 [64, 1536, 1024], P(('sub', 'exp'), 'seq'), parts along dimension 0, may hold values from -24 to 24
- block_mask: int32 [64, 12, 12], P(('sub', 'exp')), parts along dimension 0, may hold values from 0 to 1, as said below
- w_qkv: bfloat16 [1024, 3072], P('exp', 'seq'), may hold values from -4 to 4
- w_out: bfloat16 [1024, 1024], P('seq', 'exp'), may hold values from -0.1875 to 0.1875
- norm_gain: float32 [1024], replicated, may hold values from 0.5 to 1.5
- routes: int32 [64, 1536, 2], P(('sub', 'exp'), 'seq'), parts along dimension 0, may hold values from 0 to 63, all different within a row; in each aligned block of 192 rows (0 to 191, 192 to 383, ..., all dimensions but the last counted through in order) at most 12 rows name the same one
- gates: float32 [64, 1536, 2], P(('sub', 'exp'), 'seq'), parts along dimension 0, may hold values from 0.1 to 1
- w_gate_up: bfloat16 [64, 1024, 1024], P(('seq', 'exp')), may hold values from -0.1875 to 0.1875
- w_down: bfloat16 [64, 512, 1024], P(('seq', 'exp')), may hold values from -0.25 to 0.25
Outputs:
- layer_out: bfloat16 [64, 1536, 1024], P(('sub', 'exp'), 'seq'), parts along dimension 0
There are 8 independent parts, one for each index of `sub`. A program takes and returns all parts, laid end to end along the dimension named above; an argument that names none is the same for every part. Nothing has to cross between parts.
Inputs may be any that keep to these rules, and one draw needn't show every extreme that they name: In each aligned block of 192 rows (one device's nodes, subgraphs then nodes in order) no expert is named by more than 12 of the rows' routes, a bound that some block reaches; the 2 experts of a node differ. `block_mask`: the diagonal blocks are 1.
All inputs are finite; a program needn't handle non-finite values.
Results may differ from a plain program's by a relative error of at most 0.0065.
The roundings to bfloat16 on the way count: a program that leaves them out, or rounds other values in their place, can miss the bound.
Values may be sent and summed in bfloat16 or wider, within the bound.
No kernel may reach another device: no remote copies, remote signals or barrier semaphores. Data moves between devices by JAX's collectives and lax.ppermute only.
A program may use at most 64 MiB of HBM per device.

v0:
```python
import math

import jax
import jax.numpy as jnp
from jax import lax
from jax.sharding import PartitionSpec as P

HEAD_DIM = 64
TOP = 2
BLOCK = 128


def per_device(
    node_features, block_mask, w_qkv, w_out, norm_gain, routes, gates, w_gate_up, w_down
):
    feats = node_features[0]
    node_dev, width = feats.shape
    seq_count = lax.axis_size("seq")
    exp_count = lax.axis_size("exp")
    experts = seq_count * exp_count * w_gate_up.shape[0]
    head_cols = w_qkv.shape[1]
    qkv_all, out_all = (
        lax.all_gather(w_qkv[None], ("seq", "exp"), axis=0, tiled=True),
        lax.all_gather(w_out[None], ("seq", "exp"), axis=0, tiled=True),
    )
    qkv_tiles = qkv_all.reshape(seq_count, exp_count, w_qkv.shape[0], head_cols)
    local_proj = jnp.einsum(
        "nek,sekc->nsc",
        feats.reshape(node_dev, exp_count, w_qkv.shape[0]),
        qkv_tiles,
        preferred_element_type=jnp.float32,
    )
    local_proj = local_proj.astype(jnp.bfloat16).reshape(node_dev, seq_count * head_cols)
    projected = lax.all_to_all(local_proj, "seq", split_axis=1, concat_axis=0, tiled=True)
    nodes = projected.shape[0]
    heads_here = head_cols // (3 * HEAD_DIM)
    split = projected.reshape(nodes, heads_here, 3, HEAD_DIM)
    query = split[:, :, 0]
    keys = split[:, :, 1]
    values = split[:, :, 2]
    col_mask = jnp.repeat(block_mask[0], BLOCK, axis=1) > 0
    span = math.gcd(nodes, 512)
    scale = 1.0 / math.sqrt(HEAD_DIM)

    def attend(index):
        start = index * span
        rows_query = lax.dynamic_slice_in_dim(query, start, span, 0)
        rows_mask = lax.dynamic_slice_in_dim(col_mask, start // BLOCK, span // BLOCK, 0)
        allowed = jnp.repeat(rows_mask, BLOCK, axis=0)
        scores = (
            jnp.einsum("qhd,khd->hqk", rows_query, keys, preferred_element_type=jnp.float32) * scale
        )
        scores = jnp.where(allowed[None], scores, -1e30)
        top = jnp.max(scores, axis=-1, keepdims=True)
        weights = jnp.exp(scores - top)
        probs = (weights / jnp.sum(weights, axis=-1, keepdims=True)).astype(jnp.bfloat16)
        return jnp.einsum("hqk,khd->qhd", probs, values, preferred_element_type=jnp.float32).astype(
            jnp.bfloat16
        )

    blocks = lax.map(attend, jnp.arange(nodes // span, dtype=jnp.int32))
    attended = blocks.reshape(nodes, heads_here * HEAD_DIM)
    node_attended = lax.all_to_all(attended, "seq", split_axis=0, concat_axis=1, tiled=True)
    out_tiles = out_all.reshape(seq_count, exp_count, w_out.shape[0], w_out.shape[1])
    attn_out = jnp.einsum(
        "nsk,sekc->nec",
        node_attended.reshape(node_dev, seq_count, w_out.shape[0]),
        out_tiles,
        preferred_element_type=jnp.float32,
    )
    mixed = feats.astype(jnp.float32) + attn_out.reshape(node_dev, width)
    mean_square = jnp.mean(mixed * mixed, axis=-1, keepdims=True)
    normed = (mixed * lax.rsqrt(mean_square + 1e-06) * norm_gain).astype(jnp.bfloat16)
    capacity = 2 * TOP * node_dev // experts
    pair_routes = routes[0].reshape(node_dev * TOP)
    onehot = (pair_routes[:, None] == jnp.arange(experts, dtype=jnp.int32)).astype(jnp.int32)
    earlier = jnp.cumsum(onehot, axis=0, dtype=jnp.int32) - onehot
    slots = jnp.sum(earlier * onehot, axis=1, dtype=jnp.int32)
    position = pair_routes * capacity + slots
    outgoing = (
        jnp.zeros((experts * capacity, width), jnp.bfloat16)
        .at[position]
        .set(jnp.repeat(normed, TOP, axis=0))
    )
    outgoing = outgoing.reshape(experts, capacity, width)
    hidden_units = w_down.shape[1]
    received = lax.all_to_all(outgoing, ("seq", "exp"), split_axis=0, concat_axis=0, tiled=True)
    sources, items, columns = received.shape
    flat_rows = received.reshape(sources * items, columns)
    both = jnp.dot(flat_rows, w_gate_up[0], preferred_element_type=jnp.float32)
    hidden = (jax.nn.silu(both[:, :hidden_units]) * both[:, hidden_units:]).astype(jnp.bfloat16)
    result = jnp.dot(hidden, w_down[0], preferred_element_type=jnp.float32).astype(jnp.bfloat16)
    processed = result.reshape(sources, items, columns)
    returned = lax.all_to_all(
        processed, ("seq", "exp"), split_axis=0, concat_axis=0, tiled=True
    ).reshape(experts * capacity, width)
    picked = returned[position].astype(jnp.float32).reshape(node_dev, TOP, width)
    expert_sum = jnp.sum(picked * gates[0][:, :, None], axis=1)
    return (mixed + expert_sum).astype(jnp.bfloat16)[None]


def solution(mesh):
    in_specs = (
        P(("sub", "exp"), "seq", None),
        P(("sub", "exp"), None, None),
        P("exp", "seq"),
        P("seq", "exp"),
        P(),
        P(("sub", "exp"), "seq", None),
        P(("sub", "exp"), "seq", None),
        P(("seq", "exp"), None, None),
        P(("seq", "exp"), None, None),
    )
    out_specs = P(("sub", "exp"), "seq", None)
    return jax.shard_map(
        per_device, mesh=mesh, in_specs=in_specs, out_specs=out_specs, check_vma=False
    )
```

profile of v0, /device:TPU:24, one launch (start us, length us, event | category | flops | bytes accessed | tf_op | source)
XLA Modules:
  0.0 382.8 jit_solution(14159090257780799350)
XLA Ops:
  8.3 97.1 %all-gather.5.cloned.1.call-done = bf16[8192,384]{1,0:T(8,128)(2,1)} async-done(((bf16[128,384]{1,0:T(8,128)(2,1)}), bf16[8192,384]{1,0:T(8,128)(2,1)}) %all-gather.5.cloned.1.call-update) | async-done | bytes 6291472 | tf_op jit(solution)/shard_map/all_gather | solution.py:23
  105.4 5.2 %bitcast_convert_fusion = bf16[192,8,384]{2,0,1:T(8,128)(2,1)} fusion(bf16[8,8,128,384]{3,2,1,0:T(8,128)(2,1)} %bitcast.99, bf16[192,8,128]{2,1,0:T(8,128)(2,1)S(1)} %bitcast.103), kind=kOutput, calls=%fused_computation.28 | convolution fusion | flops 1208549376 | bytes 7864320 | tf_op jit(solution)/shard_map/nek,sekc->nsc/dot_general | solution.py:27
  110.7 6.1 %all-to-all-start = ((bf16[192,8,384]{2,0,1:T(8,128)(2,1)}), bf16[192,8,384]{2,0,1:T(8,128)(2,1)S(1)}, u32[]{:S(2)}, u32[]{:S(2)}) async-start(bf16[192,8,384]{2,0,1:T(8,128)(2,1)} %bitcast_convert_fusion), calls=%async_computation | async-start | bytes 2359296 | tf_op jit(solution)/shard_map/all_to_all | solution.py:34
  118.1 26.0 %all-to-all-done = bf16[192,8,384]{2,0,1:T(8,128)(2,1)S(1)} async-done(((bf16[192,8,384]{2,0,1:T(8,128)(2,1)}), bf16[192,8,384]{2,0,1:T(8,128)(2,1)S(1)}, u32[]{:S(2)}, u32[]{:S(2)}) %all-to-all-start) | async-done | bytes 1179680 | tf_op jit(solution)/shard_map/all_to_all | solution.py:34
  144.1 2.0 copy.18
  146.1 2.9 reshape.112
  150.1 28.0 %while.12 = (s32[]{:T(128)}, bf16[3,512,2,64]{1,3,2,0:T(8,128)(2,1)}, s32[3]{0:T(128)S(1)}, pred[12,1536]{1,0:T(8,128)(4,1)S(1)}, bf16[1536,2,64]{0,2,1:T(8,128)...) while((s32[]{:T(128)}, ...), condition=%wide.region_3.4_spmd, body=%wide.region_0.3_spmd.sunk | while | flops 618205184 | bytes 5532574 | solution.py:61
  151.5 3.5 fusion.73
  155.0 4.4 %fusion.74 = bf16[3,512,2,64]{1,3,2,0:T(8,128)(2,1)} fusion(bf16[3,512,2,64]{1,3,2,0:T(8,128)(2,1)} %get-tuple-element.174, s32[]{:T(128)} %get-tuple-element.173, bf16[1536,2,64]{0,2,1:T(8,128)(2,1)S(1)} %copy-done.3, f32[2,512]{1,0:T(2,128)S(1)} %fusion.73, pred[512,1536]{1,0:T(8,128)(4,1)S(1)} %bitcast.97, ...), kind=kOutput, calls=%fused_computation.13.clone.1 | convolution fusion | flops 410585600 | bytes 1839620 | tf_op jit(solution)/shard_map/while/body/eval_jaxpr/hqk,khd->qhd/dot_general | solution.py:57
  160.9 3.5 fusion.73
  164.4 4.4 %fusion.74 = bf16[3,512,2,64]{1,3,2,0:T(8,128)(2,1)} fusion(bf16[3,512,2,64]{1,3,2,0:T(8,128)(2,1)} %get-tuple-element.174, s32[]{:T(128)} %get-tuple-element.173, bf16[1536,2,64]{0,2,1:T(8,128)(2,1)S(1)} %copy-done.3, f32[2,512]{1,0:T(2,128)S(1)} %fusion.73, pred[512,1536]{1,0:T(8,128)(4,1)S(1)} %bitcast.97, ...), kind=kOutput, calls=%fused_computation.13.clone.1 | convolution fusion | flops 410585600 | bytes 1839620 | tf_op jit(solution)/shard_map/while/body/eval_jaxpr/hqk,khd->qhd/dot_general | solution.py:57
  170.2 3.5 fusion.73
  173.7 4.4 %fusion.74 = bf16[3,512,2,64]{1,3,2,0:T(8,128)(2,1)} fusion(bf16[3,512,2,64]{1,3,2,0:T(8,128)(2,1)} %get-tuple-element.174, s32[]{:T(128)} %get-tuple-element.173, bf16[1536,2,64]{0,2,1:T(8,128)(2,1)S(1)} %copy-done.3, f32[2,512]{1,0:T(2,128)S(1)} %fusion.73, pred[512,1536]{1,0:T(8,128)(4,1)S(1)} %bitcast.97, ...), kind=kOutput, calls=%fused_computation.13.clone.1 | convolution fusion | flops 410585600 | bytes 1839620 | tf_op jit(solution)/shard_map/while/body/eval_jaxpr/hqk,khd->qhd/dot_general | solution.py:57
  178.1 2.2 copy.28
  181.4 8.0 %all-to-all-start.1 = ((bf16[8,192,128]{2,1,0:T(8,128)(2,1)}), bf16[8,192,128]{2,1,0:T(8,128)(2,1)S(1)}, u32[]{:S(2)}, u32[]{:S(2)}) async-start(bf16[8,192,128]{2,1,0:T(8,128)(2,1)} %reshape.145), calls=%async_computation.1 | async-start | bytes 786432 | tf_op jit(solution)/shard_map/all_to_all | solution.py:63
  191.0 16.6 %all-gather.7.cloned.1.call-done = bf16[8192,128]{1,0:T(8,128)(2,1)} async-done(((bf16[128,128]{1,0:T(8,128)(2,1)}), bf16[8192,128]{1,0:T(8,128)(2,1)}) %all-gather.7.cloned.1.call-update) | async-done | bytes 2097168 | tf_op jit(solution)/shard_map/all_gather | solution.py:24
  207.6 4.0 %copy.21 = bf16[8,8,128,128]{2,3,1,0:T(8,128)(2,1)} copy(bf16[8,8,128,128]{3,2,1,0:T(8,128)(2,1)} %bitcast.101) | data formatting | bytes 4194304 | tf_op jit(solution)/shard_map/reshape | solution.py:64
  212.3 2.7 multiply_reduce_fusion.1
  216.5 3.0 reshape.134
  219.4 4.0 %scatter_custom_fusion = bf16[768,1024]{1,0:T(8,128)(2,1)} fusion(s32[384]{0:T(512)S(1)} %fusion.50, bf16[384,1024]{1,0:T(8,128)(2,1)} %reshape.134, bf16[]{:T(256)} %constant.96.clone.1), kind=kCustom, calls=%fused_computation.42 | custom fusion | bytes 1573376 | tf_op jit(solution)/shard_map/scatter | solution.py:83
  223.4 3.6 reshape.116
  227.0 59.8 %all_to_all.39 = bf16[64,12,1024]{2,1,0:T(8,128)(2,1)} all-to-all(bf16[64,12,1024]{2,1,0:T(8,128)(2,1)} %reshape.116), channel_id=1, replica_groups=mesh['sub'=8,'seq'=8,'exp'=8] {'seq','exp'}, dimensions={0} | all-to-all | bytes 3145728 | tf_op jit(solution)/shard_map/all_to_all | solution.py:87
  286.8 3.6 reshape.117
  290.4 3.3 fusion.33
  293.7 2.2 convolution_convert_fusion
  295.9 3.6 reshape.118
  299.5 7.7 %all-to-all-start.3 = ((bf16[64,12,1024]{2,1,0:T(8,128)(2,1)}), bf16[64,12,1024]{2,1,0:T(8,128)(2,1)}, u32[]{:S(2)}, u32[]{:S(2)}) async-start(bf16[64,12,1024]{2,1,0:T(8,128)(2,1)} %reshape.118), calls=%async_computation.3 | async-start | bytes 4194304 | tf_op jit(solution)/shard_map/all_to_all | solution.py:94
  307.3 52.9 %all-to-all-done.3 = bf16[64,12,1024]{2,1,0:T(8,128)(2,1)} async-done(((bf16[64,12,1024]{2,1,0:T(8,128)(2,1)}), bf16[64,12,1024]{2,1,0:T(8,128)(2,1)}, u32[]{:S(2)}, u32[]{:S(2)}) %all-to-all-start.3) | async-done | bytes 1572896 | tf_op jit(solution)/shard_map/all_to_all | solution.py:94
  360.2 3.6 reshape.119
  363.8 5.0 %gather_fusion = bf16[384,1024]{1,0:T(8,128)(2,1)} fusion(bf16[768,1024]{1,0:T(8,128)(2,1)} %reshape.119, s32[1024]{0:T(1024)S(1)} %pad_clamp_fusion), kind=kCustom, calls=%fused_computation | custom fusion | bytes 1574400 | tf_op jit(solution)/shard_map/gather | solution.py:97
  368.7 3.0 reshape.121
  371.7 3.4 multiply_reduce_fusion
  (64 shorter events, 12.4 us)
Async XLA Ops:
  6.5 283.9 %copy-start = (bf16[1,1024,1024]{2,1,0:T(8,128)(2,1)S(1)}, bf16[1,1024,1024]{2,1,0:T(8,128)(2,1)}, u32[]{:S(2)}) copy-start(bf16[1,1024,1024]{2,1,0:T(8,128)(2,1)} %param.18) | copy-start | bytes 6291460
  6.5 98.9 %all-gather.5.cloned.1.call-start = ((), (), s32[]{:S(2)}) async-start(), calls=%async_computation.4 | async-start | bytes 6389760 | tf_op jit(solution)/shard_map/all_gather | solution.py:23
  110.7 6.8 %copy-start.4 = (s32[1,192,2]{1,2,0:T(2,128)S(1)}, s32[1,192,2]{1,2,0:T(2,128)}, u32[]{:S(2)}) copy-start(s32[1,192,2]{1,2,0:T(2,128)} %param.16) | copy-start | bytes 4612
  110.7 7.2 %copy-start.5 = (s32[1,12,12]{2,0,1:T(1,128)S(1)}, s32[1,12,12]{2,0,1:T(1,128)}, u32[]{:S(2)}) copy-start(s32[1,12,12]{2,0,1:T(1,128)} %param.12) | copy-start | bytes 1732
  110.7 33.4 %all-to-all-start = ((bf16[192,8,384]{2,0,1:T(8,128)(2,1)}), bf16[192,8,384]{2,0,1:T(8,128)(2,1)S(1)}, u32[]{:S(2)}, u32[]{:S(2)}) async-start(bf16[192,8,384]{2,0,1:T(8,128)(2,1)} %bitcast_convert_fusion), calls=%async_computation | async-start | bytes 2359296 | tf_op jit(solution)/shard_map/all_to_all | solution.py:34
  116.7 90.9 %all-gather.7.cloned.1.call-start = ((), (), s32[]{:S(2)}) async-start(), calls=%async_computation.5 | async-start | bytes 2129920 | tf_op jit(solution)/shard_map/all_gather | solution.py:24
  151.5 3.5 copy-start.3
  160.9 3.5 copy-start.3
  170.2 3.5 copy-start.3
  181.4 30.2 %all-to-all-start.1 = ((bf16[8,192,128]{2,1,0:T(8,128)(2,1)}), bf16[8,192,128]{2,1,0:T(8,128)(2,1)S(1)}, u32[]{:S(2)}, u32[]{:S(2)}) async-start(bf16[8,192,128]{2,1,0:T(8,128)(2,1)} %reshape.145), calls=%async_computation.1 | async-start | bytes 786432 | tf_op jit(solution)/shard_map/all_to_all | solution.py:63
  207.6 4.7 %copy-start.1 = (bf16[1,192,1024]{2,1,0:T(8,128)(2,1)S(1)}, bf16[1,192,1024]{2,1,0:T(8,128)(2,1)}, u32[]{:S(2)}) copy-start(bf16[1,192,1024]{2,1,0:T(8,128)(2,1)} %param.11) | copy-start | bytes 1179652
  211.6 3.4 copy-start.6
  211.6 0.7 copy-start.2
  290.4 3.3 copy-start.8
  299.5 7.7 %copy-start.7 = (f32[1,192,2]{1,2,0:T(2,128)S(1)}, f32[1,192,2]{1,2,0:T(2,128)}, u32[]{:S(2)}) copy-start(f32[1,192,2]{1,2,0:T(2,128)} %param.17) | copy-start | bytes 4612
  299.5 60.7 %all-to-all-start.3 = ((bf16[64,12,1024]{2,1,0:T(8,128)(2,1)}), bf16[64,12,1024]{2,1,0:T(8,128)(2,1)}, u32[]{:S(2)}, u32[]{:S(2)}) async-start(bf16[64,12,1024]{2,1,0:T(8,128)(2,1)} %reshape.118), calls=%async_computation.3 | async-start | bytes 4194304 | tf_op jit(solution)/shard_map/all_to_all | solution.py:94
Sparse Core Ops, SparseCore 0:
  10.4 94.9 all-gather.4
  120.6 86.9 all-gather.6
where the time goes:
time: 384 us; the launch traced here: 383 us
  waiting for transfers between devices  194 us (51%)
  blocking collectives  59.8 us (16%)
  local copies, waits for them, and re-layouts  49.3 us (13%)
  matrix products  37 us (10%)
  starting transfers between devices  21.8 us (6%)
  between operations  13.6 us (4%)
  other arithmetic  5.53 us (1%)
    all_gather x1, waiting for transfers between devices, per_device(): lax.all_gather(w_qkv[None], ('seq', 'exp'), axis=0, tiled=True)  97.1 us
    all_to_all x1, blocking collectives, per_device(): lax.all_to_all(outgoing, ('seq', 'exp'), split_axis=0, concat_axis=0, til...  59.8 us
    all_to_all x1, waiting for transfers between devices, per_device(): lax.all_to_all(processed, ('seq', 'exp'), split_axis=0, concat_axis=0, ti...  52.9 us
    all_to_all x1, waiting for transfers between devices, per_device(): lax.all_to_all(local_proj, 'seq', split_axis=1, concat_axis=0, tiled=True)  26 us
    all_gather x1, waiting for transfers between devices, per_device(): lax.all_gather(w_out[None], ('seq', 'exp'), axis=0, tiled=True)  16.6 us
    dot_general x3, matrix products, attend(): jnp.einsum('hqk,khd->qhd', probs, values, preferred_element_type=jnp.floa...  13.2 us
    sub x3, matrix products, attend(): weights = jnp.exp(scores - top)  10.4 us
    all_to_all x1, starting transfers between devices, per_device(): lax.all_to_all(attended, 'seq', split_axis=0, concat_axis=1, tiled=True)  8.03 us
  transfers between devices with their start and end apart: 5, of which 4 were waited for; matrix products, arithmetic and copies ran while one was open for 11% of the time, Pallas kernels for 0%

commit v1 on v0

--- a/solution.py
+++ b/solution.py
@@ -19,19 +19,27 @@
     exp_count = lax.axis_size("exp")
     experts = seq_count * exp_count * w_gate_up.shape[0]
     head_cols = w_qkv.shape[1]
-    qkv_all, out_all = (
-        lax.all_gather(w_qkv[None], ("seq", "exp"), axis=0, tiled=True),
-        lax.all_gather(w_out[None], ("seq", "exp"), axis=0, tiled=True),
+    cols_slice = lax.all_gather(w_qkv, "exp", axis=0, tiled=True)
+    out_rows = lax.all_gather(w_out[None], "exp", axis=0, tiled=True)
+    out_all = lax.all_gather(out_rows[None], "seq", axis=0, tiled=True)
+    me = lax.axis_index("seq")
+    right = [(i, (i + 1) % seq_count) for i in range(seq_count)]
+    left = [(i, (i - 1) % seq_count) for i in range(seq_count)]
+    relative = [None] * seq_count
+    relative[0] = feats
+    moving_r, moving_l = feats, feats
+    for step in range(1, seq_count // 2 + 1):
+        moving_r = lax.ppermute(moving_r, "seq", right)
+        relative[(seq_count - step) % seq_count] = moving_r
+        if step < seq_count - step:
+            moving_l = lax.ppermute(moving_l, "seq", left)
+            relative[step] = moving_l
+    stacked = jnp.stack(relative)
+    order = (jnp.arange(seq_count, dtype=jnp.int32) - me) % seq_count
+    gathered = jnp.take(stacked, order, axis=0).reshape(seq_count * node_dev, width)
+    projected = jnp.dot(gathered, cols_slice, preferred_element_type=jnp.float32).astype(
+        jnp.bfloat16
     )
-    qkv_tiles = qkv_all.reshape(seq_count, exp_count, w_qkv.shape[0], head_cols)
-    local_proj = jnp.einsum(
-        "nek,sekc->nsc",
-        feats.reshape(node_dev, exp_count, w_qkv.shape[0]),
-        qkv_tiles,
-        preferred_element_type=jnp.float32,
-    )
-    local_proj = local_proj.astype(jnp.bfloat16).reshape(node_dev, seq_count * head_cols)
-    projected = lax.all_to_all(local_proj, "seq", split_axis=1, concat_axis=0, tiled=True)
     nodes = projected.shape[0]
     heads_here = head_cols // (3 * HEAD_DIM)
     split = projected.reshape(nodes, heads_here, 3, HEAD_DIM)
@@ -61,7 +69,7 @@
     blocks = lax.map(attend, jnp.arange(nodes // span, dtype=jnp.int32))
     attended = blocks.reshape(nodes, heads_here * HEAD_DIM)
     node_attended = lax.all_to_all(attended, "seq", split_axis=0, concat_axis=1, tiled=True)
-    out_tiles = out_all.reshape(seq_count, exp_count, w_out.shape[0], w_out.shape[1])
+    out_tiles = out_all
     attn_out = jnp.einsum(
         "nsk,sekc->nec",
         node_attended.reshape(node_dev, seq_count, w_out.shape[0]),

time: 384 us -> 346 us (0.901)
  waiting for transfers between devices: 194 us -> 71.1 us
  blocking collectives: 59.8 us -> 112 us
  starting transfers between devices: 21.8 us -> 43.8 us
  local copies, waits for them, and re-layouts: 49.3 us -> 59.7 us
  matrix products: 37 us -> 33.1 us
    all_gather x2 -> x1, waiting for transfers between devices: 114 us -> 0.02 us  [per_device(): out_all = lax.all_gather(out_rows[None], 'seq', axis=0, tiled=True)]
    all_gather x0 -> x2, blocking collectives: none -> 59.8 us  [the longest x1 33.4 us: per_device(): out_rows = lax.all_gather(w_out[None], 'exp', axis=0, tiled=True)]
    all_to_all x1 -> x0, waiting for transfers between devices: 26 us -> none  [per_device(): lax.all_to_all(local_proj, 'seq', split_axis=1, concat_axis=0, tiled=True)]
    ppermute x0 -> x7, starting transfers between devices: none -> 25.1 us  [the longest x4 18.2 us: per_device(): moving_r = lax.ppermute(moving_r, 'seq', right)]
    ppermute x0 -> x7, waiting for transfers between devices: none -> 16.4 us  [the longest x4 16.4 us: per_device(): moving_r = lax.ppermute(moving_r, 'seq', right)]
    unnamed x21 -> x25, local copies, waits for them, and re-layouts: 1.98 us -> 12 us
    all_to_all x1, blocking collectives: 59.8 us -> 51.8 us  [per_device(): lax.all_to_all(outgoing, ('seq', 'exp'), split_axis=0, concat_axis=0, til...]
    reshape x2 -> x0, local copies, waits for them, and re-layouts: 6.87 us -> none  [the longest x1 3.98 us: per_device(): out_all.reshape(seq_count, exp_count, w_out.shape[0], w_out.shape[1])]
  transfers between devices with their start and end apart: 5 -> 10, of which waited for: 4 -> 5; matrix products, arithmetic and copies ran while one was open for 11% -> 17% of each run, Pallas kernels for 0% -> 0%
where the time goes in v1:
time: 346 us; the launch traced here: 344 us
  blocking collectives  112 us (32%)
  waiting for transfers between devices  71.1 us (21%)
  local copies, waits for them, and re-layouts  59.7 us (17%)
  starting transfers between devices  43.8 us (13%)
  matrix products  33.1 us (10%)
  between operations  13.7 us (4%)
  other arithmetic  8.59 us (2%)
    all_to_all x1, blocking collectives, per_device(): lax.all_to_all(outgoing, ('seq', 'exp'), split_axis=0, concat_axis=0, til...  51.8 us
    all_to_all x1, waiting for transfers between devices, per_device(): lax.all_to_all(processed, ('seq', 'exp'), split_axis=0, concat_axis=0, ti...  51.8 us
    all_gather x1, blocking collectives, per_device(): out_rows = lax.all_gather(w_out[None], 'exp', axis=0, tiled=True)  33.4 us
    all_gather x1, blocking collectives, per_device(): cols_slice = lax.all_gather(w_qkv, 'exp', axis=0, tiled=True)  26.4 us
    ppermute x4, starting transfers between devices, per_device(): moving_r = lax.ppermute(moving_r, 'seq', right)  18.2 us
    ppermute x4, waiting for transfers between devices, per_device(): moving_r = lax.ppermute(moving_r, 'seq', right)  16.4 us
    dot_general x3, matrix products, attend(): jnp.einsum('hqk,khd->qhd', probs, values, preferred_element_type=jnp.floa...  13.2 us
    unnamed x25, local copies, waits for them, and re-layouts  12 us
  transfers between devices with their start and end apart: 10, of which 5 were waited for; matrix products, arithmetic and copies ran while one was open for 17% of the time, Pallas kernels for 0%

profile of v1, /device:TPU:24, one launch (start us, length us, event | category | flops | bytes accessed | tf_op | source)
XLA Modules:
  0.0 343.6 jit_solution(16411049561203123971)
XLA Ops:
  9.0 4.7 %collective-permute-start.3 = (bf16[192,1024]{1,0:T(8,128)(2,1)}, bf16[192,1024]{1,0:T(8,128)(2,1)S(1)}, u32[]{:S(2)}, u32[]{:S(2)}) collective-permute-start(bf16[192,1024]{1,0:T(8,128)(2,1)} %bitcast.114), channel_id=1, source_target_pairs={{0,8},{8,16},{16,24},{24,32},{32,40},{40,48},{48,56},{56,0},{1,9},... | collective-permute-start | bytes 1179656 | tf_op jit(solution)/shard_map/ppermute | solution.py:32
  13.7 33.4 %all-gather = bf16[1024,128]{1,0:T(8,128)(2,1)} all-gather(bf16[128,128]{1,0:T(8,128)(2,1)} %param.14), channel_id=2, replica_groups=mesh['sub'=8,'seq'=8,'exp'=8] {'exp'}, dimensions={0}, use_global_device_ids=true | all-gather | bytes 294912 | tf_op jit(solution)/shard_map/all_gather | solution.py:23
  47.1 26.4 %all_gather.9 = bf16[1024,384]{1,0:T(8,128)(2,1)S(1)} all-gather(bf16[128,384]{1,0:T(8,128)(2,1)} %param.13), channel_id=1, replica_groups=mesh['sub'=8,'seq'=8,'exp'=8] {'exp'}, dimensions={0}, use_global_device_ids=true | all-gather | bytes 884736 | tf_op jit(solution)/shard_map/all_gather | solution.py:22
  73.5 3.3 collective-permute-start.4
  80.1 10.9 %collective-permute-done.4 = bf16[192,1024]{1,0:T(8,128)(2,1)} collective-permute-done((bf16[192,1024]{1,0:T(8,128)(2,1)S(1)}, bf16[192,1024]{1,0:T(8,128)(2,1)}, u32[]{:S(2)}, u32[]{:S(2)}) %collective-permute-start.4) | collective-permute-done | bytes 393248 | tf_op jit(solution)/shard_map/ppermute | solution.py:32
  91.1 4.7 %collective-permute-start.5 = (bf16[192,1024]{1,0:T(8,128)(2,1)}, bf16[192,1024]{1,0:T(8,128)(2,1)}, u32[]{:S(2)}, u32[]{:S(2)}) collective-permute-start(bf16[192,1024]{1,0:T(8,128)(2,1)} %collective-permute-done.4), channel_id=1, source_target_pairs={{0,8},{8,16},{16,24},{24,32},{32,40},{40,48},{48,56},{56,0},{1,9},... | collective-permute-start | bytes 1179656 | tf_op jit(solution)/shard_map/ppermute | solution.py:32
  105.0 5.5 %collective-permute-start.6 = (bf16[192,1024]{1,0:T(8,128)(2,1)}, bf16[192,1024]{1,0:T(8,128)(2,1)S(1)}, u32[]{:S(2)}, u32[]{:S(2)}) collective-permute-start(bf16[192,1024]{1,0:T(8,128)(2,1)} %collective-permute-done.5), channel_id=1, source_target_pairs={{0,8},{8,16},{16,24},{24,32},{32,40},{40,48},{48,56},{56,0},{1,9},... | collective-permute-start | bytes 1179656 | tf_op jit(solution)/shard_map/ppermute | solution.py:32
  113.1 3.0 collective-permute-done.6
  121.2 4.3 %gather_fusion = bf16[8,192,1024]{2,1,0:T(8,128)(2,1)} fusion(bf16[8,192,1024]{2,1,0:T(8,128)(2,1)} %bitcast_dynamic-update-slice_fusion, s32[1024]{0:T(1024)S(1)} %pad_clamp_fusion.1), kind=kCustom, calls=%fused_computation | custom fusion | bytes 6291488 | tf_op jit(solution)/shard_map/jit(_take)/gather | solution.py:39
  130.3 28.2 %while.12 = (s32[]{:T(128)}, bf16[3,512,2,64]{1,3,2,0:T(8,128)(2,1)}, s32[3]{0:T(128)S(1)}, pred[12,1536]{1,0:T(8,128)(4,1)S(1)}, bf16[1536,2,64]{0,2,1:T(8,128)...) while((s32[]{:T(128)}, ...), condition=%wide.region_3.4_spmd, body=%wide.region_0.3_spmd.sunk | while | flops 618205184 | bytes 3959682 | solution.py:69
  131.9 3.4 fusion.75
  135.3 4.4 %fusion.76 = bf16[3,512,2,64]{1,3,2,0:T(8,128)(2,1)} fusion(bf16[3,512,2,64]{1,3,2,0:T(8,128)(2,1)} %get-tuple-element.174, s32[]{:T(128)} %get-tuple-element.173, bf16[1536,2,64]{0,2,1:T(8,128)(2,1)S(1)} %get-tuple-element.194, f32[2,512]{1,0:T(2,128)S(1)} %fusion.75, pred[512,1536]{1,0:T(8,128)(4,1)S(1)} %bitcast.110, ...), kind=kOutput, calls=%fused_computation.14.clone.1 | convolution fusion | flops 410585600 | bytes 1839620 | tf_op jit(solution)/shard_map/while/body/eval_jaxpr/hqk,khd->qhd/dot_general | solution.py:65
  141.3 3.4 fusion.75
  144.7 4.4 %fusion.76 = bf16[3,512,2,64]{1,3,2,0:T(8,128)(2,1)} fusion(bf16[3,512,2,64]{1,3,2,0:T(8,128)(2,1)} %get-tuple-element.174, s32[]{:T(128)} %get-tuple-element.173, bf16[1536,2,64]{0,2,1:T(8,128)(2,1)S(1)} %get-tuple-element.194, f32[2,512]{1,0:T(2,128)S(1)} %fusion.75, pred[512,1536]{1,0:T(8,128)(4,1)S(1)} %bitcast.110, ...), kind=kOutput, calls=%fused_computation.14.clone.1 | convolution fusion | flops 410585600 | bytes 1839620 | tf_op jit(solution)/shard_map/while/body/eval_jaxpr/hqk,khd->qhd/dot_general | solution.py:65
  150.7 3.4 %fusion.75 = f32[2,512]{1,0:T(2,128)S(1)} fusion(pred[512,1536]{1,0:T(8,128)(4,1)S(1)} %bitcast.109, bf16[1536,2,64]{0,2,1:T(8,128)(2,1)} %get-tuple-element.193, bf16[1536,2,64]{0,2,1:T(8,128)(2,1)} %get-tuple-element.192, s32[]{:T(128)S(6)} %select_n.121), kind=kOutput, calls=%fused_computation.89.clone.1 | convolution fusion | flops 207619584 | bytes 1314820 | tf_op jit(solution)/shard_map/while/body/eval_jaxpr/sub | solution.py:63
  154.1 4.4 %fusion.76 = bf16[3,512,2,64]{1,3,2,0:T(8,128)(2,1)} fusion(bf16[3,512,2,64]{1,3,2,0:T(8,128)(2,1)} %get-tuple-element.174, s32[]{:T(128)} %get-tuple-element.173, bf16[1536,2,64]{0,2,1:T(8,128)(2,1)S(1)} %get-tuple-element.194, f32[2,512]{1,0:T(2,128)S(1)} %fusion.75, pred[512,1536]{1,0:T(8,128)(4,1)S(1)} %bitcast.110, ...), kind=kOutput, calls=%fused_computation.14.clone.1 | convolution fusion | flops 410585600 | bytes 1839620 | tf_op jit(solution)/shard_map/while/body/eval_jaxpr/hqk,khd->qhd/dot_general | solution.py:65
  161.8 8.2 %all-to-all-start = ((bf16[8,192,128]{2,1,0:T(8,128)(2,1)}), bf16[8,192,128]{2,1,0:T(8,128)(2,1)S(1)}, u32[]{:S(2)}, u32[]{:S(2)}) async-start(bf16[8,192,128]{2,1,0:T(8,128)(2,1)} %reshape.189), calls=%async_computation | async-start | bytes 786432 | tf_op jit(solution)/shard_map/all_to_all | solution.py:71
  171.7 3.9 %copy.32 = bf16[8,8,128,128]{2,3,1,0:T(8,128)(2,1)} copy(bf16[8,8,128,128]{3,2,1,0:T(8,128)(2,1)} %bitcast.112) | data formatting | bytes 4194304 | tf_op jit(solution)/shard_map/all_gather | solution.py:24
  175.7 2.9 all-to-all-done
  183.4 3.0 reshape.182
  186.4 4.0 %scatter_custom_fusion = bf16[768,1024]{1,0:T(8,128)(2,1)} fusion(s32[384]{0:T(512)S(1)} %fusion.48, bf16[384,1024]{1,0:T(8,128)(2,1)} %reshape.182, bf16[]{:T(256)} %constant.125.clone.1), kind=kCustom, calls=%fused_computation.44 | custom fusion | bytes 1573376 | tf_op jit(solution)/shard_map/scatter | solution.py:91
  190.4 3.6 %reshape.157 = bf16[64,12,1024]{2,1,0:T(8,128)(2,1)} reshape(bf16[768,1024]{1,0:T(8,128)(2,1)} %scatter_custom_fusion) | data formatting | bytes 3145728 | tf_op jit(solution)/shard_map/reshape | solution.py:93
  194.0 51.8 %all_to_all.26 = bf16[64,12,1024]{2,1,0:T(8,128)(2,1)} all-to-all(bf16[64,12,1024]{2,1,0:T(8,128)(2,1)} %reshape.157), channel_id=1, replica_groups=mesh['sub'=8,'seq'=8,'exp'=8] {'seq','exp'}, dimensions={0} | all-to-all | bytes 3145728 | tf_op jit(solution)/shard_map/all_to_all | solution.py:95
  245.8 3.6 %reshape.158 = bf16[768,1024]{1,0:T(8,128)(2,1)} reshape(bf16[64,12,1024]{2,1,0:T(8,128)(2,1)} %all_to_all.26) | data formatting | bytes 3145728 | tf_op jit(solution)/shard_map/reshape | solution.py:97
  249.4 3.3 fusion.33
  254.9 3.6 %reshape.159 = bf16[64,12,1024]{2,1,0:T(8,128)(2,1)} reshape(bf16[768,1024]{1,0:T(8,128)(2,1)} %convolution_convert_fusion.1) | data formatting | bytes 3145728 | tf_op jit(solution)/shard_map/reshape | solution.py:101
  258.5 10.5 %all-to-all-start.2 = ((bf16[64,12,1024]{2,1,0:T(8,128)(2,1)}), bf16[64,12,1024]{2,1,0:T(8,128)(2,1)}, u32[]{:S(2)}, u32[]{:S(2)}) async-start(bf16[64,12,1024]{2,1,0:T(8,128)(2,1)} %reshape.159), calls=%async_computation.2 | async-start | bytes 4194304 | tf_op jit(solution)/shard_map/all_to_all | solution.py:102
  269.2 51.8 %all-to-all-done.2 = bf16[64,12,1024]{2,1,0:T(8,128)(2,1)} async-done(((bf16[64,12,1024]{2,1,0:T(8,128)(2,1)}), bf16[64,12,1024]{2,1,0:T(8,128)(2,1)}, u32[]{:S(2)}, u32[]{:S(2)}) %all-to-all-start.2) | async-done | bytes 1572896 | tf_op jit(solution)/shard_map/all_to_all | solution.py:102
  320.9 3.6 %reshape.160 = bf16[768,1024]{1,0:T(8,128)(2,1)} reshape(bf16[64,12,1024]{2,1,0:T(8,128)(2,1)} %all-to-all-done.2) | data formatting | bytes 3145728 | tf_op jit(solution)/shard_map/reshape | solution.py:104
  324.5 5.0 %gather_fusion.1 = bf16[384,1024]{1,0:T(8,128)(2,1)} fusion(bf16[768,1024]{1,0:T(8,128)(2,1)} %reshape.160, s32[1024]{0:T(1024)S(1)} %pad_clamp_fusion), kind=kCustom, calls=%fused_computation.1 | custom fusion | bytes 1574400 | tf_op jit(solution)/shard_map/gather | solution.py:105
  329.5 3.0 reshape.161
  332.5 3.4 %multiply_reduce_fusion = f32[192,1024]{1,0:T(8,128)S(1)} fusion(f32[192,2,1024]{2,1,0:T(2,128)} %reshape.161, f32[192,2]{1,0:T(8,128)S(1)} %copy.37), kind=kLoop, calls=%fused_computation.36 | loop fusion | flops 589824 | bytes 2360832 | tf_op jit(solution)/shard_map/reduce_sum | solution.py:106
  (79 shorter events, 42.9 us)
Async XLA Ops:
  6.5 242.9 %copy-start = (bf16[1,1024,1024]{2,1,0:T(8,128)(2,1)S(1)}, bf16[1,1024,1024]{2,1,0:T(8,128)(2,1)}, u32[]{:S(2)}) copy-start(bf16[1,1024,1024]{2,1,0:T(8,128)(2,1)} %param.18) | copy-start | bytes 6291460
  6.5 165.2 %all-gather.4.cloned.1.call-start = ((), (), s32[]{:S(2)}) async-start(), calls=%async_computation.3 | async-start | bytes 2359296 | tf_op jit(solution)/shard_map/all_gather | solution.py:24
  6.5 71.1 %collective-permute-start = (bf16[192,1024]{1,0:T(8,128)(2,1)}, bf16[192,1024]{1,0:T(8,128)(2,1)}, u32[]{:S(2)}, u32[]{:S(2)}) collective-permute-start(bf16[192,1024]{1,0:T(8,128)(2,1)} %bitcast.113), channel_id=1, source_target_pairs={{0,56},{8,0},{16,8},{24,16},{32,24},{40,32},{48,40},{56,48},{1,57}... | collective-permute-start | bytes 1179656 | tf_op jit(solution)/shard_map/ppermute | solution.py:35
  9.0 64.5 %collective-permute-start.3 = (bf16[192,1024]{1,0:T(8,128)(2,1)}, bf16[192,1024]{1,0:T(8,128)(2,1)S(1)}, u32[]{:S(2)}, u32[]{:S(2)}) collective-permute-start(bf16[192,1024]{1,0:T(8,128)(2,1)} %bitcast.114), channel_id=1, source_target_pairs={{0,8},{8,16},{16,24},{24,32},{32,40},{40,48},{48,56},{56,0},{1,9},... | collective-permute-start | bytes 1179656 | tf_op jit(solution)/shard_map/ppermute | solution.py:32
  73.5 17.5 %collective-permute-start.4 = (bf16[192,1024]{1,0:T(8,128)(2,1)S(1)}, bf16[192,1024]{1,0:T(8,128)(2,1)}, u32[]{:S(2)}, u32[]{:S(2)}) collective-permute-start(bf16[192,1024]{1,0:T(8,128)(2,1)S(1)} %collective-permute-done.3), channel_id=1, source_target_pairs={{0,8},{8,16},{16,24},{24,32},{32,40},{40,48},{48,56},{56,0},{1,9},... | collective-permute-start | bytes 1179656 | tf_op jit(solution)/shard_map/ppermute | solution.py:32
  77.6 21.4 %collective-permute-start.1 = (bf16[192,1024]{1,0:T(8,128)(2,1)}, bf16[192,1024]{1,0:T(8,128)(2,1)}, u32[]{:S(2)}, u32[]{:S(2)}) collective-permute-start(bf16[192,1024]{1,0:T(8,128)(2,1)} %collective-permute-done), channel_id=1, source_target_pairs={{0,56},{8,0},{16,8},{24,16},{32,24},{40,32},{48,40},{56,48},{1,57}... | collective-permute-start | bytes 1179656 | tf_op jit(solution)/shard_map/ppermute | solution.py:35
  91.1 14.0 %collective-permute-start.5 = (bf16[192,1024]{1,0:T(8,128)(2,1)}, bf16[192,1024]{1,0:T(8,128)(2,1)}, u32[]{:S(2)}, u32[]{:S(2)}) collective-permute-start(bf16[192,1024]{1,0:T(8,128)(2,1)} %collective-permute-done.4), channel_id=1, source_target_pairs={{0,8},{8,16},{16,24},{24,32},{32,40},{40,48},{48,56},{56,0},{1,9},... | collective-permute-start | bytes 1179656 | tf_op jit(solution)/shard_map/ppermute | solution.py:32
  99.0 13.3 %collective-permute-start.2 = (bf16[192,1024]{1,0:T(8,128)(2,1)}, bf16[192,1024]{1,0:T(8,128)(2,1)S(1)}, u32[]{:S(2)}, u32[]{:S(2)}) collective-permute-start(bf16[192,1024]{1,0:T(8,128)(2,1)} %collective-permute-done.1), channel_id=1, source_target_pairs={{0,56},{8,0},{16,8},{24,16},{32,24},{40,32},{48,40},{56,48},{1,57}... | collective-permute-start | bytes 1179656 | tf_op jit(solution)/shard_map/ppermute | solution.py:35
  105.0 11.1 %collective-permute-start.6 = (bf16[192,1024]{1,0:T(8,128)(2,1)}, bf16[192,1024]{1,0:T(8,128)(2,1)S(1)}, u32[]{:S(2)}, u32[]{:S(2)}) collective-permute-start(bf16[192,1024]{1,0:T(8,128)(2,1)} %collective-permute-done.5), channel_id=1, source_target_pairs={{0,8},{8,16},{16,24},{24,32},{32,40},{40,48},{48,56},{56,0},{1,9},... | collective-permute-start | bytes 1179656 | tf_op jit(solution)/shard_map/ppermute | solution.py:32
  158.5 12.7 %copy-start.3 = (s32[1,192,2]{1,2,0:T(2,128)S(1)}, s32[1,192,2]{1,2,0:T(2,128)}, u32[]{:S(2)}) copy-start(s32[1,192,2]{1,2,0:T(2,128)} %param.16) | copy-start | bytes 4612
  161.8 17.5 %copy-start.1 = (bf16[1,192,1024]{2,1,0:T(8,128)(2,1)S(1)}, bf16[1,192,1024]{2,1,0:T(8,128)(2,1)}, u32[]{:S(2)}) copy-start(bf16[1,192,1024]{2,1,0:T(8,128)(2,1)} %param.11) | copy-start | bytes 1179652
  161.8 16.7 %all-to-all-start = ((bf16[8,192,128]{2,1,0:T(8,128)(2,1)}), bf16[8,192,128]{2,1,0:T(8,128)(2,1)S(1)}, u32[]{:S(2)}, u32[]{:S(2)}) async-start(bf16[8,192,128]{2,1,0:T(8,128)(2,1)} %reshape.189), calls=%async_computation | async-start | bytes 786432 | tf_op jit(solution)/shard_map/all_to_all | solution.py:71
  171.7 10.3 %copy-start.4 = (f32[1024]{0:T(1024)S(1)}, f32[1024]{0:T(1024)}, u32[]{:S(2)}) copy-start(f32[1024]{0:T(1024)} %param.15) | copy-start | bytes 12292
  178.6 0.7 copy-start.2
  249.4 3.3 copy-start.6
  254.9 14.1 %copy-start.5 = (f32[1,192,2]{1,2,0:T(2,128)S(1)}, f32[1,192,2]{1,2,0:T(2,128)}, u32[]{:S(2)}) copy-start(f32[1,192,2]{1,2,0:T(2,128)} %param.17) | copy-start | bytes 4612
  258.5 62.4 %all-to-all-start.2 = ((bf16[64,12,1024]{2,1,0:T(8,128)(2,1)}), bf16[64,12,1024]{2,1,0:T(8,128)(2,1)}, u32[]{:S(2)}, u32[]{:S(2)}) async-start(bf16[64,12,1024]{2,1,0:T(8,128)(2,1)} %reshape.159), calls=%async_computation.2 | async-start | bytes 4194304 | tf_op jit(solution)/shard_map/all_to_all | solution.py:102
Sparse Core Ops, SparseCore 0:
  47.2 43.0 all-gather.3

commit v2 on v0

--- a/solution.py
+++ b/solution.py
@@ -10,6 +10,27 @@
 BLOCK = 128
 
 
+def ring_gather(piece, axis, count):
+    right = [(i, (i + 1) % count) for i in range(count)]
+    left = [(i, (i - 1) % count) for i in range(count)]
+    relative = [None] * count
+    relative[0] = piece
+    moving_r, moving_l = piece, piece
+    for step in range(1, count // 2 + 1):
+        moving_r = lax.ppermute(moving_r, axis, right)
+        relative[(count - step) % count] = moving_r
+        if step < count - step:
+            moving_l = lax.ppermute(moving_l, axis, left)
+            relative[step] = moving_l
+    return relative
+
+
+def in_order(relative, axis, count):
+    me = lax.axis_index(axis)
+    order = (jnp.arange(count, dtype=jnp.int32) - me) % count
+    return jnp.take(jnp.stack(relative), order, axis=0)
+
+
 def per_device(
     node_features, block_mask, w_qkv, w_out, norm_gain, routes, gates, w_gate_up, w_down
 ):
@@ -19,19 +40,15 @@
     exp_count = lax.axis_size("exp")
     experts = seq_count * exp_count * w_gate_up.shape[0]
     head_cols = w_qkv.shape[1]
-    qkv_all, out_all = (
-        lax.all_gather(w_qkv[None], ("seq", "exp"), axis=0, tiled=True),
-        lax.all_gather(w_out[None], ("seq", "exp"), axis=0, tiled=True),
-    )
-    qkv_tiles = qkv_all.reshape(seq_count, exp_count, w_qkv.shape[0], head_cols)
-    local_proj = jnp.einsum(
-        "nek,sekc->nsc",
-        feats.reshape(node_dev, exp_count, w_qkv.shape[0]),
-        qkv_tiles,
-        preferred_element_type=jnp.float32,
-    )
-    local_proj = local_proj.astype(jnp.bfloat16).reshape(node_dev, seq_count * head_cols)
-    projected = lax.all_to_all(local_proj, "seq", split_axis=1, concat_axis=0, tiled=True)
+    out_all = lax.all_gather(w_out[None], ("seq", "exp"), axis=0, tiled=True)
+    cols_slice = in_order(ring_gather(w_qkv, "exp", exp_count), "exp", exp_count)
+    cols_slice = cols_slice.reshape(exp_count * w_qkv.shape[0], head_cols)
+    chunks = ring_gather(feats, "seq", seq_count)
+    projected_rel = [
+        jnp.dot(chunk, cols_slice, preferred_element_type=jnp.float32).astype(jnp.bfloat16)
+        for chunk in chunks
+    ]
+    projected = in_order(projected_rel, "seq", seq_count).reshape(seq_count * node_dev, head_cols)
     nodes = projected.shape[0]
     heads_here = head_cols // (3 * HEAD_DIM)
     split = projected.reshape(nodes, heads_here, 3, HEAD_DIM)
@@ -76,26 +93,22 @@
     onehot = (pair_routes[:, None] == jnp.arange(experts, dtype=jnp.int32)).astype(jnp.int32)
     earlier = jnp.cumsum(onehot, axis=0, dtype=jnp.int32) - onehot
     slots = jnp.sum(earlier * onehot, axis=1, dtype=jnp.int32)
-    position = pair_routes * capacity + slots
-    outgoing = (
-        jnp.zeros((experts * capacity, width), jnp.bfloat16)
-        .at[position]
-        .set(jnp.repeat(normed, TOP, axis=0))
-    )
-    outgoing = outgoing.reshape(experts, capacity, width)
+    position = (pair_routes * capacity + slots).reshape(node_dev, TOP)
+    places = jnp.arange(experts * capacity, dtype=jnp.int32).reshape(experts, capacity)
+    select = (places[:, :, None, None] == position[None, None]).astype(jnp.bfloat16)
+    outgoing = jnp.einsum(
+        "ecn,nd->ecd", jnp.sum(select, axis=3), normed, preferred_element_type=jnp.float32
+    ).astype(jnp.bfloat16)
     hidden_units = w_down.shape[1]
     received = lax.all_to_all(outgoing, ("seq", "exp"), split_axis=0, concat_axis=0, tiled=True)
-    sources, items, columns = received.shape
-    flat_rows = received.reshape(sources * items, columns)
-    both = jnp.dot(flat_rows, w_gate_up[0], preferred_element_type=jnp.float32)
-    hidden = (jax.nn.silu(both[:, :hidden_units]) * both[:, hidden_units:]).astype(jnp.bfloat16)
-    result = jnp.dot(hidden, w_down[0], preferred_element_type=jnp.float32).astype(jnp.bfloat16)
-    processed = result.reshape(sources, items, columns)
-    returned = lax.all_to_all(
-        processed, ("seq", "exp"), split_axis=0, concat_axis=0, tiled=True
-    ).reshape(experts * capacity, width)
-    picked = returned[position].astype(jnp.float32).reshape(node_dev, TOP, width)
-    expert_sum = jnp.sum(picked * gates[0][:, :, None], axis=1)
+    both = jnp.einsum("eck,kf->ecf", received, w_gate_up[0], preferred_element_type=jnp.float32)
+    hidden = (jax.nn.silu(both[..., :hidden_units]) * both[..., hidden_units:]).astype(jnp.bfloat16)
+    processed = jnp.einsum(
+        "ecf,fd->ecd", hidden, w_down[0], preferred_element_type=jnp.float32
+    ).astype(jnp.bfloat16)
+    returned = lax.all_to_all(processed, ("seq", "exp"), split_axis=0, concat_axis=0, tiled=True)
+    picked = jnp.einsum("ecnk,ecd->knd", select, returned, preferred_element_type=jnp.float32)
+    expert_sum = picked[0] * gates[0][:, 0, None] + picked[1] * gates[0][:, 1, None]
     return (mixed + expert_sum).astype(jnp.bfloat16)[None]
 
 

time: 384 us -> 296 us (0.77)
  waiting for transfers between devices: 194 us -> 79.1 us
  starting transfers between devices: 21.8 us -> 71 us
  local copies, waits for them, and re-layouts: 49.3 us -> 31.4 us
  blocking collectives: 59.8 us -> 49.8 us
  matrix products: 37 us -> 44.2 us
    all_gather x2 -> x1, waiting for transfers between devices: 114 us -> 0.02 us  [per_device(): out_all = lax.all_gather(w_out[None], ('seq', 'exp'), axis=0, tiled=True)]
    ppermute x0 -> x14, starting transfers between devices: none -> 52.7 us  [the longest x6 27.9 us: ring_gather(): moving_l = lax.ppermute(moving_l, axis, left)]
    all_to_all x1 -> x0, waiting for transfers between devices: 26 us -> none  [per_device(): lax.all_to_all(local_proj, 'seq', split_axis=1, concat_axis=0, tiled=True)]
    ppermute x0 -> x14, waiting for transfers between devices: none -> 24.2 us  [the longest x8 23.5 us: ring_gather(): moving_r = lax.ppermute(moving_r, axis, right)]
    reshape x6 -> x0, local copies, waits for them, and re-layouts: 20.3 us -> none  [the longest x1 3.64 us: per_device(): flat_rows = received.reshape(sources * items, columns)]
    all_to_all x1, blocking collectives: 59.8 us -> 49.8 us  [per_device(): lax.all_to_all(outgoing, ('seq', 'exp'), split_axis=0, concat_axis=0, til...]
    dot_general x3 -> x12, matrix products: 10.7 us -> 17.9 us  [the longest x8 10.2 us: per_device(): jnp.dot(chunk, cols_slice, preferred_element_type=jnp.float32)]
    all_to_all x1 -> x0, starting transfers between devices: 6.05 us -> none  [per_device(): lax.all_to_all(local_proj, 'seq', split_axis=1, concat_axis=0, tiled=True)]
  transfers between devices with their start and end apart: 5 -> 17, of which waited for: 4 -> 8; matrix products, arithmetic and copies ran while one was open for 11% -> 22% of each run, Pallas kernels for 0% -> 0%
where the time goes in v2:
time: 296 us; the launch traced here: 295 us
  waiting for transfers between devices  79.1 us (27%)
  starting transfers between devices  71 us (24%)
  blocking collectives  49.8 us (17%)
  matrix products  44.2 us (15%)
  local copies, waits for them, and re-layouts  31.4 us (11%)
  between operations  13.8 us (5%)
  other arithmetic  3.57 us (1%)
    all_to_all x1, waiting for transfers between devices, per_device(): lax.all_to_all(processed, ('seq', 'exp'), split_axis=0, concat_axis=0, ti...  51.2 us
    all_to_all x1, blocking collectives, per_device(): lax.all_to_all(outgoing, ('seq', 'exp'), split_axis=0, concat_axis=0, til...  49.8 us
    ppermute x6, starting transfers between devices, ring_gather(): moving_l = lax.ppermute(moving_l, axis, left)  27.9 us
    ppermute x8, starting transfers between devices, ring_gather(): moving_r = lax.ppermute(moving_r, axis, right)  24.8 us
    ppermute x8, waiting for transfers between devices, ring_gather(): moving_r = lax.ppermute(moving_r, axis, right)  23.5 us
    dot_general x3, matrix products, attend(): jnp.einsum('hqk,khd->qhd', probs, values, preferred_element_type=jnp.floa...  13.2 us
    sub x3, matrix products, attend(): weights = jnp.exp(scores - top)  10.4 us
    dot_general x8, matrix products, per_device(): jnp.dot(chunk, cols_slice, preferred_element_type=jnp.float32)  10.2 us
  transfers between devices with their start and end apart: 17, of which 8 were waited for; matrix products, arithmetic and copies ran while one was open for 22% of the time, Pallas kernels for 0%

profile of v2, /device:TPU:24, one launch (start us, length us, event | category | flops | bytes accessed | tf_op | source)
XLA Modules:
  0.0 294.9 jit_solution(17561156418879392415)
XLA Ops:
  6.5 11.1 %collective-permute-start = (bf16[128,384]{1,0:T(8,128)(2,1)}, bf16[128,384]{1,0:T(8,128)(2,1)S(1)}, u32[]{:S(2)}, u32[]{:S(2)}) collective-permute-start(bf16[128,384]{1,0:T(8,128)(2,1)} %param.13), channel_id=1, source_target_pairs={{0,7},{1,0},{2,1},{3,2},{4,3},{5,4},{6,5},{7,6},{8,15},{9,8},{10,9... | collective-permute-start | bytes 294920 | tf_op jit(solution)/shard_map/ppermute | solution.py:23
  19.5 2.4 collective-permute-start.7
  21.9 4.7 %collective-permute-start.10 = (bf16[192,1024]{1,0:T(8,128)(2,1)}, bf16[192,1024]{1,0:T(8,128)(2,1)}, u32[]{:S(2)}, u32[]{:S(2)}) collective-permute-start(bf16[192,1024]{1,0:T(8,128)(2,1)} %bitcast.218), channel_id=1, source_target_pairs={{0,8},{8,16},{16,24},{24,32},{32,40},{40,48},{48,56},{56,0},{1,9},... | collective-permute-start | bytes 1179656 | tf_op jit(solution)/shard_map/ppermute | solution.py:20
  31.4 5.1 %collective-permute-start.1 = (bf16[128,384]{1,0:T(8,128)(2,1)S(1)}, bf16[128,384]{1,0:T(8,128)(2,1)S(1)}, u32[]{:S(2)}, u32[]{:S(2)}) collective-permute-start(bf16[128,384]{1,0:T(8,128)(2,1)S(1)} %collective-permute-done), channel_id=1, source_target_pairs={{0,7},{1,0},{2,1},{3,2},{4,3},{5,4},{6,5},{7,6},{8,15},{9,8},{10,9... | collective-permute-start | bytes 294920 | tf_op jit(solution)/shard_map/ppermute | solution.py:23
  39.1 5.1 %collective-permute-start.2 = (bf16[128,384]{1,0:T(8,128)(2,1)S(1)}, bf16[128,384]{1,0:T(8,128)(2,1)S(1)}, u32[]{:S(2)}, u32[]{:S(2)}) collective-permute-start(bf16[128,384]{1,0:T(8,128)(2,1)S(1)} %collective-permute-done.1), channel_id=1, source_target_pairs={{0,7},{1,0},{2,1},{3,2},{4,3},{5,4},{6,5},{7,6},{8,15},{9,8},{10,9... | collective-permute-start | bytes 294920 | tf_op jit(solution)/shard_map/ppermute | solution.py:23
  46.9 5.2 %collective-permute-done.5 = bf16[128,384]{1,0:T(8,128)(2,1)S(1)} collective-permute-done((bf16[128,384]{1,0:T(8,128)(2,1)S(1)}, bf16[128,384]{1,0:T(8,128)(2,1)S(1)}, u32[]{:S(2)}, u32[]{:S(2)}) %collective-permute-start.5) | collective-permute-done | bytes 98336 | tf_op jit(solution)/shard_map/ppermute | solution.py:20
  54.6 5.3 %collective-permute-done.6 = bf16[128,384]{1,0:T(8,128)(2,1)S(1)} collective-permute-done((bf16[128,384]{1,0:T(8,128)(2,1)S(1)}, bf16[128,384]{1,0:T(8,128)(2,1)S(1)}, u32[]{:S(2)}, u32[]{:S(2)}) %collective-permute-start.6) | collective-permute-done | bytes 98336 | tf_op jit(solution)/shard_map/ppermute | solution.py:20
  64.3 3.6 %collective-permute-start.11 = (bf16[192,1024]{1,0:T(8,128)(2,1)}, bf16[192,1024]{1,0:T(8,128)(2,1)S(1)}, u32[]{:S(2)}, u32[]{:S(2)}) collective-permute-start(bf16[192,1024]{1,0:T(8,128)(2,1)} %collective-permute-done.10), channel_id=1, source_target_pairs={{0,8},{8,16},{16,24},{24,32},{32,40},{40,48},{48,56},{56,0},{1,9},... | collective-permute-start | bytes 1179656 | tf_op jit(solution)/shard_map/ppermute | solution.py:20
  68.2 2.4 collective-permute-start.8
  70.7 4.2 %collective-permute-done.11 = bf16[192,1024]{1,0:T(8,128)(2,1)S(1)} collective-permute-done((bf16[192,1024]{1,0:T(8,128)(2,1)}, bf16[192,1024]{1,0:T(8,128)(2,1)S(1)}, u32[]{:S(2)}, u32[]{:S(2)}) %collective-permute-start.11) | collective-permute-done | bytes 393248 | tf_op jit(solution)/shard_map/ppermute | solution.py:20
  75.0 4.1 %collective-permute-start.12 = (bf16[192,1024]{1,0:T(8,128)(2,1)S(1)}, bf16[192,1024]{1,0:T(8,128)(2,1)S(1)}, u32[]{:S(2)}, u32[]{:S(2)}) collective-permute-start(bf16[192,1024]{1,0:T(8,128)(2,1)S(1)} %collective-permute-done.11), channel_id=1, source_target_pairs={{0,8},{8,16},{16,24},{24,32},{32,40},{40,48},{48,56},{56,0},{1,9},... | collective-permute-start | bytes 1179656 | tf_op jit(solution)/shard_map/ppermute | solution.py:20
  84.0 3.5 %collective-permute-done.12 = bf16[192,1024]{1,0:T(8,128)(2,1)S(1)} collective-permute-done((bf16[192,1024]{1,0:T(8,128)(2,1)S(1)}, bf16[192,1024]{1,0:T(8,128)(2,1)S(1)}, u32[]{:S(2)}, u32[]{:S(2)}) %collective-permute-start.12) | collective-permute-done | bytes 393248 | tf_op jit(solution)/shard_map/ppermute | solution.py:20
  87.6 4.8 %collective-permute-start.13 = (bf16[192,1024]{1,0:T(8,128)(2,1)S(1)}, bf16[192,1024]{1,0:T(8,128)(2,1)S(1)}, u32[]{:S(2)}, u32[]{:S(2)}) collective-permute-start(bf16[192,1024]{1,0:T(8,128)(2,1)S(1)} %collective-permute-done.12), channel_id=1, source_target_pairs={{0,8},{8,16},{16,24},{24,32},{32,40},{40,48},{48,56},{56,0},{1,9},... | collective-permute-start | bytes 1179656 | tf_op jit(solution)/shard_map/ppermute | solution.py:20
  95.1 5.2 %collective-permute-done.13 = bf16[192,1024]{1,0:T(8,128)(2,1)S(1)} collective-permute-done((bf16[192,1024]{1,0:T(8,128)(2,1)S(1)}, bf16[192,1024]{1,0:T(8,128)(2,1)S(1)}, u32[]{:S(2)}, u32[]{:S(2)}) %collective-permute-start.13) | collective-permute-done | bytes 393248 | tf_op jit(solution)/shard_map/ppermute | solution.py:20
  109.6 2.9 gather.15
  113.6 28.2 %while.12 = (s32[]{:T(128)}, bf16[3,512,2,64]{1,3,2,0:T(8,128)(2,1)}, s32[3]{0:T(128)S(1)}, pred[12,1536]{1,0:T(8,128)(4,1)S(1)}, bf16[1536,2,64]{0,2,1:T(8,128)...) while((s32[]{:T(128)}, ...), condition=%wide.region_3.4_spmd, body=%wide.region_0.3_spmd.sunk | while | flops 618205184 | bytes 5532574 | solution.py:78
  115.2 3.5 %fusion.128 = f32[2,512]{1,0:T(2,128)S(1)} fusion(pred[512,1536]{1,0:T(8,128)(4,1)S(1)} %bitcast.212, bf16[1536,2,64]{0,2,1:T(8,128)(2,1)} %get-tuple-element.195, bf16[1536,2,64]{0,2,1:T(8,128)(2,1)} %get-tuple-element.194, s32[]{:T(128)S(6)} %select_n.177), kind=kOutput, calls=%fused_computation.143.clone.1 | convolution fusion | flops 207619584 | bytes 1314820 | tf_op jit(solution)/shard_map/while/body/eval_jaxpr/sub | solution.py:72
  118.7 4.4 %fusion.129 = bf16[3,512,2,64]{1,3,2,0:T(8,128)(2,1)} fusion(bf16[3,512,2,64]{1,3,2,0:T(8,128)(2,1)} %get-tuple-element.176, s32[]{:T(128)} %get-tuple-element.175, bf16[1536,2,64]{0,2,1:T(8,128)(2,1)S(1)} %copy-done.3, f32[2,512]{1,0:T(2,128)S(1)} %fusion.128, pred[512,1536]{1,0:T(8,128)(4,1)S(1)} %bitcast.213, ...), kind=kOutput, calls=%fused_computation.13.clone.1 | convolution fusion | flops 410585600 | bytes 1839620 | tf_op jit(solution)/shard_map/while/body/eval_jaxpr/hqk,khd->qhd/dot_general | solution.py:74
  124.6 3.5 %fusion.128 = f32[2,512]{1,0:T(2,128)S(1)} fusion(pred[512,1536]{1,0:T(8,128)(4,1)S(1)} %bitcast.212, bf16[1536,2,64]{0,2,1:T(8,128)(2,1)} %get-tuple-element.195, bf16[1536,2,64]{0,2,1:T(8,128)(2,1)} %get-tuple-element.194, s32[]{:T(128)S(6)} %select_n.177), kind=kOutput, calls=%fused_computation.143.clone.1 | convolution fusion | flops 207619584 | bytes 1314820 | tf_op jit(solution)/shard_map/while/body/eval_jaxpr/sub | solution.py:72
  128.1 4.4 %fusion.129 = bf16[3,512,2,64]{1,3,2,0:T(8,128)(2,1)} fusion(bf16[3,512,2,64]{1,3,2,0:T(8,128)(2,1)} %get-tuple-element.176, s32[]{:T(128)} %get-tuple-element.175, bf16[1536,2,64]{0,2,1:T(8,128)(2,1)S(1)} %copy-done.3, f32[2,512]{1,0:T(2,128)S(1)} %fusion.128, pred[512,1536]{1,0:T(8,128)(4,1)S(1)} %bitcast.213, ...), kind=kOutput, calls=%fused_computation.13.clone.1 | convolution fusion | flops 410585600 | bytes 1839620 | tf_op jit(solution)/shard_map/while/body/eval_jaxpr/hqk,khd->qhd/dot_general | solution.py:74
  134.0 3.5 %fusion.128 = f32[2,512]{1,0:T(2,128)S(1)} fusion(pred[512,1536]{1,0:T(8,128)(4,1)S(1)} %bitcast.212, bf16[1536,2,64]{0,2,1:T(8,128)(2,1)} %get-tuple-element.195, bf16[1536,2,64]{0,2,1:T(8,128)(2,1)} %get-tuple-element.194, s32[]{:T(128)S(6)} %select_n.177), kind=kOutput, calls=%fused_computation.143.clone.1 | convolution fusion | flops 207619584 | bytes 1314820 | tf_op jit(solution)/shard_map/while/body/eval_jaxpr/sub | solution.py:72
  137.5 4.4 %fusion.129 = bf16[3,512,2,64]{1,3,2,0:T(8,128)(2,1)} fusion(bf16[3,512,2,64]{1,3,2,0:T(8,128)(2,1)} %get-tuple-element.176, s32[]{:T(128)} %get-tuple-element.175, bf16[1536,2,64]{0,2,1:T(8,128)(2,1)S(1)} %copy-done.3, f32[2,512]{1,0:T(2,128)S(1)} %fusion.128, pred[512,1536]{1,0:T(8,128)(4,1)S(1)} %bitcast.213, ...), kind=kOutput, calls=%fused_computation.13.clone.1 | convolution fusion | flops 410585600 | bytes 1839620 | tf_op jit(solution)/shard_map/while/body/eval_jaxpr/hqk,khd->qhd/dot_general | solution.py:74
  145.1 8.2 %all-to-all-start = ((bf16[8,192,128]{2,1,0:T(8,128)(2,1)}), bf16[8,192,128]{2,1,0:T(8,128)(2,1)S(1)}, u32[]{:S(2)}, u32[]{:S(2)}) async-start(bf16[8,192,128]{2,1,0:T(8,128)(2,1)} %reshape.240), calls=%async_computation | async-start | bytes 786432 | tf_op jit(solution)/shard_map/all_to_all | solution.py:80
  154.2 3.9 %copy.25 = bf16[8,8,128,128]{2,3,1,0:T(8,128)(2,1)} copy(bf16[8,8,128,128]{3,2,1,0:T(8,128)(2,1)} %bitcast.216) | data formatting | bytes 4194304 | tf_op jit(solution)/shard_map/reshape | solution.py:81
  158.2 3.6 %all-to-all-done = bf16[8,192,128]{2,1,0:T(8,128)(2,1)S(1)} async-done(((bf16[8,192,128]{2,1,0:T(8,128)(2,1)}), bf16[8,192,128]{2,1,0:T(8,128)(2,1)S(1)}, u32[]{:S(2)}, u32[]{:S(2)}) %all-to-all-start) | async-done | bytes 393248 | tf_op jit(solution)/shard_map/all_to_all | solution.py:80
  162.6 2.7 multiply_reduce_fusion
  166.8 49.8 %all_to_all.26 = bf16[64,12,1024]{2,1,0:T(8,128)(2,1)S(1)} all-to-all(bf16[64,12,1024]{2,1,0:T(8,128)(2,1)S(1)} %copy.31), channel_id=1, replica_groups=mesh['sub'=8,'seq'=8,'exp'=8] {'seq','exp'}, dimensions={0} | all-to-all | bytes 3145728 | tf_op jit(solution)/shard_map/all_to_all | solution.py:103
  216.6 2.2 fusion.33
  219.8 2.2 copy.33
  222.0 10.1 %all-to-all-start.2 = ((bf16[64,12,1024]{2,1,0:T(8,128)(2,1)}), bf16[64,12,1024]{2,1,0:T(8,128)(2,1)}, u32[]{:S(2)}, u32[]{:S(2)}) async-start(bf16[64,12,1024]{2,1,0:T(8,128)(2,1)} %copy.33), calls=%async_computation.2 | async-start | bytes 4194304 | tf_op jit(solution)/shard_map/all_to_all | solution.py:109
  232.1 51.2 %all-to-all-done.2 = bf16[64,12,1024]{2,1,0:T(8,128)(2,1)} async-done(((bf16[64,12,1024]{2,1,0:T(8,128)(2,1)}), bf16[64,12,1024]{2,1,0:T(8,128)(2,1)}, u32[]{:S(2)}, u32[]{:S(2)}) %all-to-all-start.2) | async-done | bytes 1572896 | tf_op jit(solution)/shard_map/all_to_all | solution.py:109
  283.3 3.8 %fusion.41 = f32[2,192,1024]{2,1,0:T(8,128)S(1)} fusion(bf16[64,12,1024]{2,1,0:T(8,128)(2,1)} %all-to-all-done.2, s32[192,2]{0,1:T(2,128)S(1)} %copy.30, s32[64,12]{0,1:T(8,128)S(1)} %multiply_add_fusion), kind=kOutput, calls=%fused_computation.40 | convolution fusion | flops 604274688 | bytes 3150336 | tf_op jit(solution)/shard_map/ecnk,ecd->knd/dot_general | solution.py:110
  (104 shorter events, 48.2 us)
Async XLA Ops:
  6.5 210.0 %copy-start = (bf16[1,1024,1024]{2,1,0:T(8,128)(2,1)S(1)}, bf16[1,1024,1024]{2,1,0:T(8,128)(2,1)}, u32[]{:S(2)}) copy-start(bf16[1,1024,1024]{2,1,0:T(8,128)(2,1)} %param.18) | copy-start | bytes 6291460
  6.5 147.7 %all-gather.3.cloned.1.call-start = ((), (), s32[]{:S(2)}) async-start(), calls=%async_computation.3 | async-start | bytes 2129920 | tf_op jit(solution)/shard_map/all_gather | solution.py:43
  6.5 24.9 %collective-permute-start = (bf16[128,384]{1,0:T(8,128)(2,1)}, bf16[128,384]{1,0:T(8,128)(2,1)S(1)}, u32[]{:S(2)}, u32[]{:S(2)}) collective-permute-start(bf16[128,384]{1,0:T(8,128)(2,1)} %param.13), channel_id=1, source_target_pairs={{0,7},{1,0},{2,1},{3,2},{4,3},{5,4},{6,5},{7,6},{8,15},{9,8},{10,9... | collective-permute-start | bytes 294920 | tf_op jit(solution)/shard_map/ppermute | solution.py:23
  17.6 18.9 %collective-permute-start.3 = (bf16[128,384]{1,0:T(8,128)(2,1)}, bf16[128,384]{1,0:T(8,128)(2,1)S(1)}, u32[]{:S(2)}, u32[]{:S(2)}) collective-permute-start(bf16[128,384]{1,0:T(8,128)(2,1)} %param.13), channel_id=1, source_target_pairs={{0,1},{1,2},{2,3},{3,4},{4,5},{5,6},{6,7},{7,0},{8,9},{9,10},{10,1... | collective-permute-start | bytes 294920 | tf_op jit(solution)/shard_map/ppermute | solution.py:20
  19.5 48.6 %collective-permute-start.7 = (bf16[192,1024]{1,0:T(8,128)(2,1)}, bf16[192,1024]{1,0:T(8,128)(2,1)}, u32[]{:S(2)}, u32[]{:S(2)}) collective-permute-start(bf16[192,1024]{1,0:T(8,128)(2,1)} %bitcast.217), channel_id=1, source_target_pairs={{0,56},{8,0},{16,8},{24,16},{32,24},{40,32},{48,40},{56,48},{1,57}... | collective-permute-start | bytes 1179656 | tf_op jit(solution)/shard_map/ppermute | solution.py:23
  21.9 42.4 %collective-permute-start.10 = (bf16[192,1024]{1,0:T(8,128)(2,1)}, bf16[192,1024]{1,0:T(8,128)(2,1)}, u32[]{:S(2)}, u32[]{:S(2)}) collective-permute-start(bf16[192,1024]{1,0:T(8,128)(2,1)} %bitcast.218), channel_id=1, source_target_pairs={{0,8},{8,16},{16,24},{24,32},{32,40},{40,48},{48,56},{56,0},{1,9},... | collective-permute-start | bytes 1179656 | tf_op jit(solution)/shard_map/ppermute | solution.py:20
  31.4 7.7 %collective-permute-start.1 = (bf16[128,384]{1,0:T(8,128)(2,1)S(1)}, bf16[128,384]{1,0:T(8,128)(2,1)S(1)}, u32[]{:S(2)}, u32[]{:S(2)}) collective-permute-start(bf16[128,384]{1,0:T(8,128)(2,1)S(1)} %collective-permute-done), channel_id=1, source_target_pairs={{0,7},{1,0},{2,1},{3,2},{4,3},{5,4},{6,5},{7,6},{8,15},{9,8},{10,9... | collective-permute-start | bytes 294920 | tf_op jit(solution)/shard_map/ppermute | solution.py:23
  36.6 7.7 %collective-permute-start.4 = (bf16[128,384]{1,0:T(8,128)(2,1)S(1)}, bf16[128,384]{1,0:T(8,128)(2,1)S(1)}, u32[]{:S(2)}, u32[]{:S(2)}) collective-permute-start(bf16[128,384]{1,0:T(8,128)(2,1)S(1)} %collective-permute-done.3), channel_id=1, source_target_pairs={{0,1},{1,2},{2,3},{3,4},{4,5},{5,6},{6,7},{7,0},{8,9},{9,10},{10,1... | collective-permute-start | bytes 294920 | tf_op jit(solution)/shard_map/ppermute | solution.py:20
  39.1 14.8 %collective-permute-start.2 = (bf16[128,384]{1,0:T(8,128)(2,1)S(1)}, bf16[128,384]{1,0:T(8,128)(2,1)S(1)}, u32[]{:S(2)}, u32[]{:S(2)}) collective-permute-start(bf16[128,384]{1,0:T(8,128)(2,1)S(1)} %collective-permute-done.1), channel_id=1, source_target_pairs={{0,7},{1,0},{2,1},{3,2},{4,3},{5,4},{6,5},{7,6},{8,15},{9,8},{10,9... | collective-permute-start | bytes 294920 | tf_op jit(solution)/shard_map/ppermute | solution.py:23
  44.3 7.8 %collective-permute-start.5 = (bf16[128,384]{1,0:T(8,128)(2,1)S(1)}, bf16[128,384]{1,0:T(8,128)(2,1)S(1)}, u32[]{:S(2)}, u32[]{:S(2)}) collective-permute-start(bf16[128,384]{1,0:T(8,128)(2,1)S(1)} %collective-permute-done.4), channel_id=1, source_target_pairs={{0,1},{1,2},{2,3},{3,4},{4,5},{5,6},{6,7},{7,0},{8,9},{9,10},{10,1... | collective-permute-start | bytes 294920 | tf_op jit(solution)/shard_map/ppermute | solution.py:20
  52.1 7.8 %collective-permute-start.6 = (bf16[128,384]{1,0:T(8,128)(2,1)S(1)}, bf16[128,384]{1,0:T(8,128)(2,1)S(1)}, u32[]{:S(2)}, u32[]{:S(2)}) collective-permute-start(bf16[128,384]{1,0:T(8,128)(2,1)S(1)} %collective-permute-done.5), channel_id=1, source_target_pairs={{0,1},{1,2},{2,3},{3,4},{4,5},{5,6},{6,7},{7,0},{8,9},{9,10},{10,1... | collective-permute-start | bytes 294920 | tf_op jit(solution)/shard_map/ppermute | solution.py:20
  64.3 14.7 %copy-start.2 = (bf16[1,192,1024]{2,1,0:T(8,128)(2,1)S(1)}, bf16[1,192,1024]{2,1,0:T(8,128)(2,1)}, u32[]{:S(2)}) copy-start(bf16[1,192,1024]{2,1,0:T(8,128)(2,1)} %param.11) | copy-start | bytes 1179652
  64.3 10.6 %collective-permute-start.11 = (bf16[192,1024]{1,0:T(8,128)(2,1)}, bf16[192,1024]{1,0:T(8,128)(2,1)S(1)}, u32[]{:S(2)}, u32[]{:S(2)}) collective-permute-start(bf16[192,1024]{1,0:T(8,128)(2,1)} %collective-permute-done.10), channel_id=1, source_target_pairs={{0,8},{8,16},{16,24},{24,32},{32,40},{40,48},{48,56},{56,0},{1,9},... | collective-permute-start | bytes 1179656 | tf_op jit(solution)/shard_map/ppermute | solution.py:20
  68.2 11.9 %collective-permute-start.8 = (bf16[192,1024]{1,0:T(8,128)(2,1)}, bf16[192,1024]{1,0:T(8,128)(2,1)S(1)}, u32[]{:S(2)}, u32[]{:S(2)}) collective-permute-start(bf16[192,1024]{1,0:T(8,128)(2,1)} %collective-permute-done.7), channel_id=1, source_target_pairs={{0,56},{8,0},{16,8},{24,16},{32,24},{40,32},{48,40},{56,48},{1,57}... | collective-permute-start | bytes 1179656 | tf_op jit(solution)/shard_map/ppermute | solution.py:23
  75.0 12.6 %collective-permute-start.12 = (bf16[192,1024]{1,0:T(8,128)(2,1)S(1)}, bf16[192,1024]{1,0:T(8,128)(2,1)S(1)}, u32[]{:S(2)}, u32[]{:S(2)}) collective-permute-start(bf16[192,1024]{1,0:T(8,128)(2,1)S(1)} %collective-permute-done.11), channel_id=1, source_target_pairs={{0,8},{8,16},{16,24},{24,32},{32,40},{40,48},{48,56},{56,0},{1,9},... | collective-permute-start | bytes 1179656 | tf_op jit(solution)/shard_map/ppermute | solution.py:20
  80.1 14.0 %collective-permute-start.9 = (bf16[192,1024]{1,0:T(8,128)(2,1)S(1)}, bf16[192,1024]{1,0:T(8,128)(2,1)S(1)}, u32[]{:S(2)}, u32[]{:S(2)}) collective-permute-start(bf16[192,1024]{1,0:T(8,128)(2,1)S(1)} %collective-permute-done.8), channel_id=1, source_target_pairs={{0,56},{8,0},{16,8},{24,16},{32,24},{40,32},{48,40},{56,48},{1,57}... | collective-permute-start | bytes 1179656 | tf_op jit(solution)/shard_map/ppermute | solution.py:23
  87.6 12.8 %collective-permute-start.13 = (bf16[192,1024]{1,0:T(8,128)(2,1)S(1)}, bf16[192,1024]{1,0:T(8,128)(2,1)S(1)}, u32[]{:S(2)}, u32[]{:S(2)}) collective-permute-start(bf16[192,1024]{1,0:T(8,128)(2,1)S(1)} %collective-permute-done.12), channel_id=1, source_target_pairs={{0,8},{8,16},{16,24},{24,32},{32,40},{40,48},{48,56},{56,0},{1,9},... | collective-permute-start | bytes 1179656 | tf_op jit(solution)/shard_map/ppermute | solution.py:20
  115.2 3.5 %copy-start.3 = (bf16[1536,2,64]{0,2,1:T(8,128)(2,1)S(1)}, bf16[1536,2,64]{0,2,1:T(8,128)(2,1)}, u32[]{:S(2)}) copy-start(bf16[1536,2,64]{0,2,1:T(8,128)(2,1)} %get-tuple-element.196) | copy-start | bytes 1179652 | tf_op jit(solution)/shard_map/while
  124.6 3.5 %copy-start.3 = (bf16[1536,2,64]{0,2,1:T(8,128)(2,1)S(1)}, bf16[1536,2,64]{0,2,1:T(8,128)(2,1)}, u32[]{:S(2)}) copy-start(bf16[1536,2,64]{0,2,1:T(8,128)(2,1)} %get-tuple-element.196) | copy-start | bytes 1179652 | tf_op jit(solution)/shard_map/while
  134.0 3.5 %copy-start.3 = (bf16[1536,2,64]{0,2,1:T(8,128)(2,1)S(1)}, bf16[1536,2,64]{0,2,1:T(8,128)(2,1)}, u32[]{:S(2)}) copy-start(bf16[1536,2,64]{0,2,1:T(8,128)(2,1)} %get-tuple-element.196) | copy-start | bytes 1179652 | tf_op jit(solution)/shard_map/while
  145.1 16.7 %all-to-all-start = ((bf16[8,192,128]{2,1,0:T(8,128)(2,1)}), bf16[8,192,128]{2,1,0:T(8,128)(2,1)S(1)}, u32[]{:S(2)}, u32[]{:S(2)}) async-start(bf16[8,192,128]{2,1,0:T(8,128)(2,1)} %reshape.240), calls=%async_computation | async-start | bytes 786432 | tf_op jit(solution)/shard_map/all_to_all | solution.py:80
  161.8 0.7 copy-start.1
  162.6 2.7 copy-start.4
  216.6 2.2 copy-start.6
  222.0 10.1 %copy-start.5 = (f32[1,192,2]{1,2,0:T(2,128)S(1)}, f32[1,192,2]{1,2,0:T(2,128)}, u32[]{:S(2)}) copy-start(f32[1,192,2]{1,2,0:T(2,128)} %param.17) | copy-start | bytes 4612
  222.0 61.3 %all-to-all-start.2 = ((bf16[64,12,1024]{2,1,0:T(8,128)(2,1)}), bf16[64,12,1024]{2,1,0:T(8,128)(2,1)}, u32[]{:S(2)}, u32[]{:S(2)}) async-start(bf16[64,12,1024]{2,1,0:T(8,128)(2,1)} %copy.33), calls=%async_computation.2 | async-start | bytes 4194304 | tf_op jit(solution)/shard_map/all_to_all | solution.py:109
Sparse Core Ops, SparseCore 0:
  26.8 81.4 all-gather.2

commit v3 on v2

--- a/solution.py
+++ b/solution.py
@@ -10,19 +10,27 @@
 BLOCK = 128
 
 
-def ring_gather(piece, axis, count):
-    right = [(i, (i + 1) % count) for i in range(count)]
-    left = [(i, (i - 1) % count) for i in range(count)]
-    relative = [None] * count
-    relative[0] = piece
-    moving_r, moving_l = piece, piece
-    for step in range(1, count // 2 + 1):
-        moving_r = lax.ppermute(moving_r, axis, right)
-        relative[(count - step) % count] = moving_r
-        if step < count - step:
-            moving_l = lax.ppermute(moving_l, axis, left)
-            relative[step] = moving_l
-    return relative
+def ring_gather(pieces, axes, counts):
+    relatives = [[piece] + [None] * (count - 1) for piece, count in zip(pieces, counts)]
+    moving = [[piece, piece] for piece in pieces]
+    for step in range(1, max(counts) // 2 + 1):
+        for which, (axis, count) in enumerate(zip(axes, counts)):
+            if step > count // 2:
+                continue
+            right = [(i, (i + 1) % count) for i in range(count)]
+            left = [(i, (i - 1) % count) for i in range(count)]
+            moving[which][0] = lax.ppermute(moving[which][0], axis, right)
+            relatives[which][(count - step) % count] = moving[which][0]
+            if step < count - step:
+                moving[which][1] = lax.ppermute(moving[which][1], axis, left)
+                relatives[which][step] = moving[which][1]
+        moving = lax.optimization_barrier(moving)
+        for which, count in enumerate(counts):
+            if step <= count // 2:
+                relatives[which][(count - step) % count] = moving[which][0]
+                if step < count - step:
+                    relatives[which][step] = moving[which][1]
+    return relatives
 
 
 def in_order(relative, axis, count):
@@ -41,9 +49,9 @@
     experts = seq_count * exp_count * w_gate_up.shape[0]
     head_cols = w_qkv.shape[1]
     out_all = lax.all_gather(w_out[None], ("seq", "exp"), axis=0, tiled=True)
-    cols_slice = in_order(ring_gather(w_qkv, "exp", exp_count), "exp", exp_count)
+    col_pieces, chunks = ring_gather((w_qkv, feats), ("exp", "seq"), (exp_count, seq_count))
+    cols_slice = in_order(col_pieces, "exp", exp_count)
     cols_slice = cols_slice.reshape(exp_count * w_qkv.shape[0], head_cols)
-    chunks = ring_gather(feats, "seq", seq_count)
     projected_rel = [
         jnp.dot(chunk, cols_slice, preferred_element_type=jnp.float32).astype(jnp.bfloat16)
         for chunk in chunks

time: 296 us -> 287 us (0.970)
  the two profiles are of different devices: /device:TPU:24 before, /device:TPU:30 now
where the time goes in v3:
time: 287 us; the launch traced here: 286 us
  starting transfers between devices  71.5 us (25%)
  waiting for transfers between devices  66.6 us (23%)
  blocking collectives  52.9 us (18%)
  matrix products  43.1 us (15%)
  local copies, waits for them, and re-layouts  31.9 us (11%)
  between operations  13.9 us (5%)
  other arithmetic  3.57 us (1%)
    all_to_all x1, waiting for transfers between devices, per_device(): lax.all_to_all(processed, ('seq', 'exp'), split_axis=0, concat_axis=0, ti...  53 us
    all_to_all x1, blocking collectives, per_device(): lax.all_to_all(outgoing, ('seq', 'exp'), split_axis=0, concat_axis=0, til...  52.9 us
    ppermute x8, starting transfers between devices, ring_gather(): moving[which][0] = lax.ppermute(moving[which][0], axis, right)  33.3 us
    ppermute x6, starting transfers between devices, ring_gather(): moving[which][1] = lax.ppermute(moving[which][1], axis, left)  24.3 us
    dot_general x3, matrix products, attend(): jnp.einsum('hqk,khd->qhd', probs, values, preferred_element_type=jnp.floa...  13.2 us
    sub x3, matrix products, attend(): weights = jnp.exp(scores - top)  10.4 us
    dot_general x8, matrix products, per_device(): jnp.dot(chunk, cols_slice, preferred_element_type=jnp.float32)  9.11 us
    gather x4, local copies, waits for them, and re-layouts, in_order(): return jnp.take(jnp.stack(relative), order, axis=0)  8.92 us
  transfers between devices with their start and end apart: 17, of which 8 were waited for; matrix products, arithmetic and copies ran while one was open for 21% of the time, Pallas kernels for 0%

profile of v3, /device:TPU:30, one launch (start us, length us, event | category | flops | bytes accessed | tf_op | source)
XLA Modules:
  0.0 285.6 jit_solution(2361354468106866882)
XLA Ops:
  6.5 4.8 %collective-permute-start.2 = (bf16[192,1024]{1,0:T(8,128)(2,1)}, bf16[192,1024]{1,0:T(8,128)(2,1)}, u32[]{:S(2)}, u32[]{:S(2)}) collective-permute-start(bf16[192,1024]{1,0:T(8,128)(2,1)} %bitcast.203), channel_id=1, source_target_pairs={{0,8},{8,16},{16,24},{24,32},{32,40},{40,48},{48,56},{56,0},{1,9},... | collective-permute-start | bytes 1179656 | tf_op jit(solution)/shard_map/ppermute | solution.py:22
  13.3 4.3 %collective-permute-start = (bf16[128,384]{1,0:T(8,128)(2,1)}, bf16[128,384]{1,0:T(8,128)(2,1)S(1)}, u32[]{:S(2)}, u32[]{:S(2)}) collective-permute-start(bf16[128,384]{1,0:T(8,128)(2,1)} %param.13), channel_id=1, source_target_pairs={{0,1},{1,2},{2,3},{3,4},{4,5},{5,6},{6,7},{7,0},{8,9},{9,10},{10,1... | collective-permute-start | bytes 294920 | tf_op jit(solution)/shard_map/ppermute | solution.py:22
  17.6 8.6 %collective-permute-start.1 = (bf16[128,384]{1,0:T(8,128)(2,1)}, bf16[128,384]{1,0:T(8,128)(2,1)S(1)}, u32[]{:S(2)}, u32[]{:S(2)}) collective-permute-start(bf16[128,384]{1,0:T(8,128)(2,1)} %param.13), channel_id=1, source_target_pairs={{0,7},{1,0},{2,1},{3,2},{4,3},{5,4},{6,5},{7,6},{8,15},{9,8},{10,9... | collective-permute-start | bytes 294920 | tf_op jit(solution)/shard_map/ppermute | solution.py:25
  28.7 5.1 %collective-permute-start.6 = (bf16[192,1024]{1,0:T(8,128)(2,1)}, bf16[192,1024]{1,0:T(8,128)(2,1)}, u32[]{:S(2)}, u32[]{:S(2)}) collective-permute-start(bf16[192,1024]{1,0:T(8,128)(2,1)} %collective-permute-done.2), channel_id=1, source_target_pairs={{0,8},{8,16},{16,24},{24,32},{32,40},{40,48},{48,56},{56,0},{1,9},... | collective-permute-start | bytes 1179656 | tf_op jit(solution)/shard_map/ppermute | solution.py:22
  38.6 6.4 %collective-permute-start.5 = (bf16[128,384]{1,0:T(8,128)(2,1)S(1)}, bf16[128,384]{1,0:T(8,128)(2,1)S(1)}, u32[]{:S(2)}, u32[]{:S(2)}) collective-permute-start(bf16[128,384]{1,0:T(8,128)(2,1)S(1)} %collective-permute-done.1), channel_id=1, source_target_pairs={{0,7},{1,0},{2,1},{3,2},{4,3},{5,4},{6,5},{7,6},{8,15},{9,8},{10,9... | collective-permute-start | bytes 294920 | tf_op jit(solution)/shard_map/ppermute | solution.py:25
  47.9 4.1 %collective-permute-start.10 = (bf16[192,1024]{1,0:T(8,128)(2,1)}, bf16[192,1024]{1,0:T(8,128)(2,1)}, u32[]{:S(2)}, u32[]{:S(2)}) collective-permute-start(bf16[192,1024]{1,0:T(8,128)(2,1)} %collective-permute-done.6), channel_id=1, source_target_pairs={{0,8},{8,16},{16,24},{24,32},{32,40},{40,48},{48,56},{56,0},{1,9},... | collective-permute-start | bytes 1179656 | tf_op jit(solution)/shard_map/ppermute | solution.py:22
  55.4 4.0 %collective-permute-start.8 = (bf16[128,384]{1,0:T(8,128)(2,1)S(1)}, bf16[128,384]{1,0:T(8,128)(2,1)S(1)}, u32[]{:S(2)}, u32[]{:S(2)}) collective-permute-start(bf16[128,384]{1,0:T(8,128)(2,1)S(1)} %collective-permute-done.4), channel_id=1, source_target_pairs={{0,1},{1,2},{2,3},{3,4},{4,5},{5,6},{6,7},{7,0},{8,9},{9,10},{10,1... | collective-permute-start | bytes 294920 | tf_op jit(solution)/shard_map/ppermute | solution.py:22
  59.4 3.5 %collective-permute-start.9 = (bf16[128,384]{1,0:T(8,128)(2,1)}, bf16[128,384]{1,0:T(8,128)(2,1)S(1)}, u32[]{:S(2)}, u32[]{:S(2)}) collective-permute-start(bf16[128,384]{1,0:T(8,128)(2,1)} %copy-done.10), channel_id=1, source_target_pairs={{0,7},{1,0},{2,1},{3,2},{4,3},{5,4},{6,5},{7,6},{8,15},{9,8},{10,9... | collective-permute-start | bytes 294920 | tf_op jit(solution)/shard_map/ppermute | solution.py:25
  63.6 2.5 collective-permute-done.9
  66.1 5.2 %collective-permute-start.13 = (bf16[192,1024]{1,0:T(8,128)(2,1)}, bf16[192,1024]{1,0:T(8,128)(2,1)S(1)}, u32[]{:S(2)}, u32[]{:S(2)}) collective-permute-start(bf16[192,1024]{1,0:T(8,128)(2,1)} %collective-permute-done.10), channel_id=1, source_target_pairs={{0,8},{8,16},{16,24},{24,32},{32,40},{40,48},{48,56},{56,0},{1,9},... | collective-permute-start | bytes 1179656 | tf_op jit(solution)/shard_map/ppermute | solution.py:22
  72.2 3.9 %collective-permute-start.12 = (bf16[128,384]{1,0:T(8,128)(2,1)S(1)}, bf16[128,384]{1,0:T(8,128)(2,1)S(1)}, u32[]{:S(2)}, u32[]{:S(2)}) collective-permute-start(bf16[128,384]{1,0:T(8,128)(2,1)S(1)} %collective-permute-done.8), channel_id=1, source_target_pairs={{0,1},{1,2},{2,3},{3,4},{4,5},{5,6},{6,7},{7,0},{8,9},{9,10},{10,1... | collective-permute-start | bytes 294920 | tf_op jit(solution)/shard_map/ppermute | solution.py:22
  76.2 3.8 %collective-permute-done.12 = bf16[128,384]{1,0:T(8,128)(2,1)S(1)} collective-permute-done((bf16[128,384]{1,0:T(8,128)(2,1)S(1)}, bf16[128,384]{1,0:T(8,128)(2,1)S(1)}, u32[]{:S(2)}, u32[]{:S(2)}) %collective-permute-start.12) | collective-permute-done | bytes 98336 | tf_op jit(solution)/shard_map/ppermute | solution.py:22
  95.4 2.1 gather_fusion.1
  99.5 2.9 %gather.15 = bf16[1536,2,3,64]{0,3,2,1:T(8,128)(2,1)S(1)} reshape(bf16[8,192,384]{1,0,2:T(8,128)(2,1)} %copy.22) | data formatting | bytes 2359296 | tf_op jit(solution)/shard_map/jit(_take)/gather | solution.py:39
  103.6 28.4 %while.12 = (s32[]{:T(128)}, bf16[3,512,2,64]{1,3,2,0:T(8,128)(2,1)}, s32[3]{0:T(128)S(1)}, pred[12,1536]{1,0:T(8,128)(4,1)S(1)}, bf16[1536,2,64]{0,2,1:T(8,128)...) while((s32[]{:T(128)}, ...), condition=%wide.region_3.4_spmd, body=%wide.region_0.3_spmd.sunk | while | flops 618205184 | bytes 5532574 | solution.py:86
  105.2 3.5 %fusion.128 = f32[2,512]{1,0:T(2,128)S(1)} fusion(pred[512,1536]{1,0:T(8,128)(4,1)S(1)} %bitcast.198, bf16[1536,2,64]{0,2,1:T(8,128)(2,1)} %get-tuple-element.225, bf16[1536,2,64]{0,2,1:T(8,128)(2,1)} %get-tuple-element.224, s32[]{:T(128)S(6)} %select_n.177), kind=kOutput, calls=%fused_computation.143.clone.1 | convolution fusion | flops 207619584 | bytes 1314820 | tf_op jit(solution)/shard_map/while/body/eval_jaxpr/sub | solution.py:80
  108.7 4.4 %fusion.129 = bf16[3,512,2,64]{1,3,2,0:T(8,128)(2,1)} fusion(bf16[3,512,2,64]{1,3,2,0:T(8,128)(2,1)} %get-tuple-element.206, s32[]{:T(128)} %get-tuple-element.205, bf16[1536,2,64]{0,2,1:T(8,128)(2,1)S(1)} %copy-done.5, f32[2,512]{1,0:T(2,128)S(1)} %fusion.128, pred[512,1536]{1,0:T(8,128)(4,1)S(1)} %bitcast.199, ...), kind=kOutput, calls=%fused_computation.13.clone.1 | convolution fusion | flops 410585600 | bytes 1839620 | tf_op jit(solution)/shard_map/while/body/eval_jaxpr/hqk,khd->qhd/dot_general | solution.py:82
  114.7 3.5 %fusion.128 = f32[2,512]{1,0:T(2,128)S(1)} fusion(pred[512,1536]{1,0:T(8,128)(4,1)S(1)} %bitcast.198, bf16[1536,2,64]{0,2,1:T(8,128)(2,1)} %get-tuple-element.225, bf16[1536,2,64]{0,2,1:T(8,128)(2,1)} %get-tuple-element.224, s32[]{:T(128)S(6)} %select_n.177), kind=kOutput, calls=%fused_computation.143.clone.1 | convolution fusion | flops 207619584 | bytes 1314820 | tf_op jit(solution)/shard_map/while/body/eval_jaxpr/sub | solution.py:80
  118.1 4.4 %fusion.129 = bf16[3,512,2,64]{1,3,2,0:T(8,128)(2,1)} fusion(bf16[3,512,2,64]{1,3,2,0:T(8,128)(2,1)} %get-tuple-element.206, s32[]{:T(128)} %get-tuple-element.205, bf16[1536,2,64]{0,2,1:T(8,128)(2,1)S(1)} %copy-done.5, f32[2,512]{1,0:T(2,128)S(1)} %fusion.128, pred[512,1536]{1,0:T(8,128)(4,1)S(1)} %bitcast.199, ...), kind=kOutput, calls=%fused_computation.13.clone.1 | convolution fusion | flops 410585600 | bytes 1839620 | tf_op jit(solution)/shard_map/while/body/eval_jaxpr/hqk,khd->qhd/dot_general | solution.py:82
  124.1 3.5 %fusion.128 = f32[2,512]{1,0:T(2,128)S(1)} fusion(pred[512,1536]{1,0:T(8,128)(4,1)S(1)} %bitcast.198, bf16[1536,2,64]{0,2,1:T(8,128)(2,1)} %get-tuple-element.225, bf16[1536,2,64]{0,2,1:T(8,128)(2,1)} %get-tuple-element.224, s32[]{:T(128)S(6)} %select_n.177), kind=kOutput, calls=%fused_computation.143.clone.1 | convolution fusion | flops 207619584 | bytes 1314820 | tf_op jit(solution)/shard_map/while/body/eval_jaxpr/sub | solution.py:80
  127.6 4.4 %fusion.129 = bf16[3,512,2,64]{1,3,2,0:T(8,128)(2,1)} fusion(bf16[3,512,2,64]{1,3,2,0:T(8,128)(2,1)} %get-tuple-element.206, s32[]{:T(128)} %get-tuple-element.205, bf16[1536,2,64]{0,2,1:T(8,128)(2,1)S(1)} %copy-done.5, f32[2,512]{1,0:T(2,128)S(1)} %fusion.128, pred[512,1536]{1,0:T(8,128)(4,1)S(1)} %bitcast.199, ...), kind=kOutput, calls=%fused_computation.13.clone.1 | convolution fusion | flops 410585600 | bytes 1839620 | tf_op jit(solution)/shard_map/while/body/eval_jaxpr/hqk,khd->qhd/dot_general | solution.py:82
  132.0 2.2 copy.36
  135.3 5.1 %all-to-all-start = ((bf16[8,192,128]{2,1,0:T(8,128)(2,1)}), bf16[8,192,128]{2,1,0:T(8,128)(2,1)S(1)}, u32[]{:S(2)}, u32[]{:S(2)}) async-start(bf16[8,192,128]{2,1,0:T(8,128)(2,1)} %reshape.240), calls=%async_computation | async-start | bytes 786432 | tf_op jit(solution)/shard_map/all_to_all | solution.py:88
  141.3 3.9 %copy.25 = bf16[8,8,128,128]{2,3,1,0:T(8,128)(2,1)} copy(bf16[8,8,128,128]{3,2,1,0:T(8,128)(2,1)} %bitcast.202) | data formatting | bytes 4194304 | tf_op jit(solution)/shard_map/reshape | solution.py:89
  145.2 3.7 %all-to-all-done = bf16[8,192,128]{2,1,0:T(8,128)(2,1)S(1)} async-done(((bf16[8,192,128]{2,1,0:T(8,128)(2,1)}), bf16[8,192,128]{2,1,0:T(8,128)(2,1)S(1)}, u32[]{:S(2)}, u32[]{:S(2)}) %all-to-all-start) | async-done | bytes 393248 | tf_op jit(solution)/shard_map/all_to_all | solution.py:88
  149.6 2.7 multiply_reduce_fusion
  153.9 52.9 %all_to_all.26 = bf16[64,12,1024]{2,1,0:T(8,128)(2,1)S(1)} all-to-all(bf16[64,12,1024]{2,1,0:T(8,128)(2,1)S(1)} %copy.31), channel_id=1, replica_groups=mesh['sub'=8,'seq'=8,'exp'=8] {'seq','exp'}, dimensions={0} | all-to-all | bytes 3145728 | tf_op jit(solution)/shard_map/all_to_all | solution.py:111
  206.8 2.2 fusion.33
  210.0 2.2 copy.33
  212.2 8.8 %all-to-all-start.2 = ((bf16[64,12,1024]{2,1,0:T(8,128)(2,1)}), bf16[64,12,1024]{2,1,0:T(8,128)(2,1)}, u32[]{:S(2)}, u32[]{:S(2)}) async-start(bf16[64,12,1024]{2,1,0:T(8,128)(2,1)} %copy.33), calls=%async_computation.2 | async-start | bytes 4194304 | tf_op jit(solution)/shard_map/all_to_all | solution.py:117
  221.0 53.0 %all-to-all-done.2 = bf16[64,12,1024]{2,1,0:T(8,128)(2,1)} async-done(((bf16[64,12,1024]{2,1,0:T(8,128)(2,1)}), bf16[64,12,1024]{2,1,0:T(8,128)(2,1)}, u32[]{:S(2)}, u32[]{:S(2)}) %all-to-all-start.2) | async-done | bytes 1572896 | tf_op jit(solution)/shard_map/all_to_all | solution.py:117
  274.0 3.8 %fusion.41 = f32[2,192,1024]{2,1,0:T(8,128)S(1)} fusion(bf16[64,12,1024]{2,1,0:T(8,128)(2,1)} %all-to-all-done.2, s32[192,2]{0,1:T(2,128)S(1)} %copy.30, s32[64,12]{0,1:T(8,128)S(1)} %multiply_add_fusion), kind=kOutput, calls=%fused_computation.40 | convolution fusion | flops 604274688 | bytes 3150336 | tf_op jit(solution)/shard_map/ecnk,ecd->knd/dot_general | solution.py:118
  (117 shorter events, 44.3 us)
Async XLA Ops:
  6.5 200.3 %copy-start = (bf16[1,1024,1024]{2,1,0:T(8,128)(2,1)S(1)}, bf16[1,1024,1024]{2,1,0:T(8,128)(2,1)}, u32[]{:S(2)}) copy-start(bf16[1,1024,1024]{2,1,0:T(8,128)(2,1)} %param.18) | copy-start | bytes 6291460
  6.5 134.8 %all-gather.3.cloned.1.call-start = ((), (), s32[]{:S(2)}) async-start(), calls=%async_computation.3 | async-start | bytes 2129920 | tf_op jit(solution)/shard_map/all_gather | solution.py:51
  6.5 22.2 %collective-permute-start.2 = (bf16[192,1024]{1,0:T(8,128)(2,1)}, bf16[192,1024]{1,0:T(8,128)(2,1)}, u32[]{:S(2)}, u32[]{:S(2)}) collective-permute-start(bf16[192,1024]{1,0:T(8,128)(2,1)} %bitcast.203), channel_id=1, source_target_pairs={{0,8},{8,16},{16,24},{24,32},{32,40},{40,48},{48,56},{56,0},{1,9},... | collective-permute-start | bytes 1179656 | tf_op jit(solution)/shard_map/ppermute | solution.py:22
  11.4 17.3 %collective-permute-start.3 = (bf16[192,1024]{1,0:T(8,128)(2,1)}, bf16[192,1024]{1,0:T(8,128)(2,1)}, u32[]{:S(2)}, u32[]{:S(2)}) collective-permute-start(bf16[192,1024]{1,0:T(8,128)(2,1)} %bitcast.204), channel_id=1, source_target_pairs={{0,56},{8,0},{16,8},{24,16},{32,24},{40,32},{48,40},{56,48},{1,57}... | collective-permute-start | bytes 1179656 | tf_op jit(solution)/shard_map/ppermute | solution.py:25
  13.3 14.7 %collective-permute-start = (bf16[128,384]{1,0:T(8,128)(2,1)}, bf16[128,384]{1,0:T(8,128)(2,1)S(1)}, u32[]{:S(2)}, u32[]{:S(2)}) collective-permute-start(bf16[128,384]{1,0:T(8,128)(2,1)} %param.13), channel_id=1, source_target_pairs={{0,1},{1,2},{2,3},{3,4},{4,5},{5,6},{6,7},{7,0},{8,9},{9,10},{10,1... | collective-permute-start | bytes 294920 | tf_op jit(solution)/shard_map/ppermute | solution.py:22
  17.6 11.1 %collective-permute-start.1 = (bf16[128,384]{1,0:T(8,128)(2,1)}, bf16[128,384]{1,0:T(8,128)(2,1)S(1)}, u32[]{:S(2)}, u32[]{:S(2)}) collective-permute-start(bf16[128,384]{1,0:T(8,128)(2,1)} %param.13), channel_id=1, source_target_pairs={{0,7},{1,0},{2,1},{3,2},{4,3},{5,4},{6,5},{7,6},{8,15},{9,8},{10,9... | collective-permute-start | bytes 294920 | tf_op jit(solution)/shard_map/ppermute | solution.py:25
  28.0 26.3 %copy-start.8 = (bf16[128,384]{1,0:T(8,128)(2,1)}, bf16[128,384]{1,0:T(8,128)(2,1)S(1)}, u32[]{:S(2)}) copy-start(bf16[128,384]{1,0:T(8,128)(2,1)S(1)} %collective-permute-done) | copy-start | bytes 294916
  28.7 19.2 %collective-permute-start.6 = (bf16[192,1024]{1,0:T(8,128)(2,1)}, bf16[192,1024]{1,0:T(8,128)(2,1)}, u32[]{:S(2)}, u32[]{:S(2)}) collective-permute-start(bf16[192,1024]{1,0:T(8,128)(2,1)} %collective-permute-done.2), channel_id=1, source_target_pairs={{0,8},{8,16},{16,24},{24,32},{32,40},{40,48},{48,56},{56,0},{1,9},... | collective-permute-start | bytes 1179656 | tf_op jit(solution)/shard_map/ppermute | solution.py:22
  33.8 14.1 %collective-permute-start.7 = (bf16[192,1024]{1,0:T(8,128)(2,1)}, bf16[192,1024]{1,0:T(8,128)(2,1)}, u32[]{:S(2)}, u32[]{:S(2)}) collective-permute-start(bf16[192,1024]{1,0:T(8,128)(2,1)} %collective-permute-done.3), channel_id=1, source_target_pairs={{0,56},{8,0},{16,8},{24,16},{32,24},{40,32},{48,40},{56,48},{1,57}... | collective-permute-start | bytes 1179656 | tf_op jit(solution)/shard_map/ppermute | solution.py:25
  36.7 9.0 %collective-permute-start.4 = (bf16[128,384]{1,0:T(8,128)(2,1)S(1)}, bf16[128,384]{1,0:T(8,128)(2,1)S(1)}, u32[]{:S(2)}, u32[]{:S(2)}) collective-permute-start(bf16[128,384]{1,0:T(8,128)(2,1)S(1)} %collective-permute-done), channel_id=1, source_target_pairs={{0,1},{1,2},{2,3},{3,4},{4,5},{5,6},{6,7},{7,0},{8,9},{9,10},{10,1... | collective-permute-start | bytes 294920 | tf_op jit(solution)/shard_map/ppermute | solution.py:22
  38.6 8.6 %collective-permute-start.5 = (bf16[128,384]{1,0:T(8,128)(2,1)S(1)}, bf16[128,384]{1,0:T(8,128)(2,1)S(1)}, u32[]{:S(2)}, u32[]{:S(2)}) collective-permute-start(bf16[128,384]{1,0:T(8,128)(2,1)S(1)} %collective-permute-done.1), channel_id=1, source_target_pairs={{0,7},{1,0},{2,1},{3,2},{4,3},{5,4},{6,5},{7,6},{8,15},{9,8},{10,9... | collective-permute-start | bytes 294920 | tf_op jit(solution)/shard_map/ppermute | solution.py:25
  45.7 20.4 %copy-start.9 = (bf16[128,384]{1,0:T(8,128)(2,1)}, bf16[128,384]{1,0:T(8,128)(2,1)S(1)}, u32[]{:S(2)}) copy-start(bf16[128,384]{1,0:T(8,128)(2,1)S(1)} %collective-permute-done.4) | copy-start | bytes 294916
  47.9 18.3 %collective-permute-start.10 = (bf16[192,1024]{1,0:T(8,128)(2,1)}, bf16[192,1024]{1,0:T(8,128)(2,1)}, u32[]{:S(2)}, u32[]{:S(2)}) collective-permute-start(bf16[192,1024]{1,0:T(8,128)(2,1)} %collective-permute-done.6), channel_id=1, source_target_pairs={{0,8},{8,16},{16,24},{24,32},{32,40},{40,48},{48,56},{56,0},{1,9},... | collective-permute-start | bytes 1179656 | tf_op jit(solution)/shard_map/ppermute | solution.py:22
  52.0 14.1 %collective-permute-start.11 = (bf16[192,1024]{1,0:T(8,128)(2,1)}, bf16[192,1024]{1,0:T(8,128)(2,1)}, u32[]{:S(2)}, u32[]{:S(2)}) collective-permute-start(bf16[192,1024]{1,0:T(8,128)(2,1)} %collective-permute-done.7), channel_id=1, source_target_pairs={{0,56},{8,0},{16,8},{24,16},{32,24},{40,32},{48,40},{56,48},{1,57}... | collective-permute-start | bytes 1179656 | tf_op jit(solution)/shard_map/ppermute | solution.py:25
  55.4 8.3 %collective-permute-start.8 = (bf16[128,384]{1,0:T(8,128)(2,1)S(1)}, bf16[128,384]{1,0:T(8,128)(2,1)S(1)}, u32[]{:S(2)}, u32[]{:S(2)}) collective-permute-start(bf16[128,384]{1,0:T(8,128)(2,1)S(1)} %collective-permute-done.4), channel_id=1, source_target_pairs={{0,1},{1,2},{2,3},{3,4},{4,5},{5,6},{6,7},{7,0},{8,9},{9,10},{10,1... | collective-permute-start | bytes 294920 | tf_op jit(solution)/shard_map/ppermute | solution.py:22
  59.4 6.8 %collective-permute-start.9 = (bf16[128,384]{1,0:T(8,128)(2,1)}, bf16[128,384]{1,0:T(8,128)(2,1)S(1)}, u32[]{:S(2)}, u32[]{:S(2)}) collective-permute-start(bf16[128,384]{1,0:T(8,128)(2,1)} %copy-done.10), channel_id=1, source_target_pairs={{0,7},{1,0},{2,1},{3,2},{4,3},{5,4},{6,5},{7,6},{8,15},{9,8},{10,9... | collective-permute-start | bytes 294920 | tf_op jit(solution)/shard_map/ppermute | solution.py:25
  66.1 13.8 %collective-permute-start.13 = (bf16[192,1024]{1,0:T(8,128)(2,1)}, bf16[192,1024]{1,0:T(8,128)(2,1)S(1)}, u32[]{:S(2)}, u32[]{:S(2)}) collective-permute-start(bf16[192,1024]{1,0:T(8,128)(2,1)} %collective-permute-done.10), channel_id=1, source_target_pairs={{0,8},{8,16},{16,24},{24,32},{32,40},{40,48},{48,56},{56,0},{1,9},... | collective-permute-start | bytes 1179656 | tf_op jit(solution)/shard_map/ppermute | solution.py:22
  72.2 7.7 %collective-permute-start.12 = (bf16[128,384]{1,0:T(8,128)(2,1)S(1)}, bf16[128,384]{1,0:T(8,128)(2,1)S(1)}, u32[]{:S(2)}, u32[]{:S(2)}) collective-permute-start(bf16[128,384]{1,0:T(8,128)(2,1)S(1)} %collective-permute-done.8), channel_id=1, source_target_pairs={{0,1},{1,2},{2,3},{3,4},{4,5},{5,6},{6,7},{7,0},{8,9},{9,10},{10,1... | collective-permute-start | bytes 294920 | tf_op jit(solution)/shard_map/ppermute | solution.py:22
  80.0 2.0 copy-start.6
  82.0 0.9 copy-start.4
  82.9 2.1 copy-start.2
  86.9 2.8 copy-start.7
  94.4 1.0 copy-start.3
  105.2 3.5 %copy-start.5 = (bf16[1536,2,64]{0,2,1:T(8,128)(2,1)S(1)}, bf16[1536,2,64]{0,2,1:T(8,128)(2,1)}, u32[]{:S(2)}) copy-start(bf16[1536,2,64]{0,2,1:T(8,128)(2,1)} %get-tuple-element.226) | copy-start | bytes 1179652 | tf_op jit(solution)/shard_map/while
  114.6 3.5 %copy-start.5 = (bf16[1536,2,64]{0,2,1:T(8,128)(2,1)S(1)}, bf16[1536,2,64]{0,2,1:T(8,128)(2,1)}, u32[]{:S(2)}) copy-start(bf16[1536,2,64]{0,2,1:T(8,128)(2,1)} %get-tuple-element.226) | copy-start | bytes 1179652 | tf_op jit(solution)/shard_map/while
  124.1 3.5 %copy-start.5 = (bf16[1536,2,64]{0,2,1:T(8,128)(2,1)S(1)}, bf16[1536,2,64]{0,2,1:T(8,128)(2,1)}, u32[]{:S(2)}) copy-start(bf16[1536,2,64]{0,2,1:T(8,128)(2,1)} %get-tuple-element.226) | copy-start | bytes 1179652 | tf_op jit(solution)/shard_map/while
  135.3 13.6 %all-to-all-start = ((bf16[8,192,128]{2,1,0:T(8,128)(2,1)}), bf16[8,192,128]{2,1,0:T(8,128)(2,1)S(1)}, u32[]{:S(2)}, u32[]{:S(2)}) async-start(bf16[8,192,128]{2,1,0:T(8,128)(2,1)} %reshape.240), calls=%async_computation | async-start | bytes 786432 | tf_op jit(solution)/shard_map/all_to_all | solution.py:88
  148.9 0.7 copy-start.1
  149.6 2.7 copy-start.11
  206.8 2.2 copy-start.13
  212.2 8.8 %copy-start.12 = (f32[1,192,2]{1,2,0:T(2,128)S(1)}, f32[1,192,2]{1,2,0:T(2,128)}, u32[]{:S(2)}) copy-start(f32[1,192,2]{1,2,0:T(2,128)} %param.17) | copy-start | bytes 4612
  212.2 61.8 %all-to-all-start.2 = ((bf16[64,12,1024]{2,1,0:T(8,128)(2,1)}), bf16[64,12,1024]{2,1,0:T(8,128)(2,1)}, u32[]{:S(2)}, u32[]{:S(2)}) async-start(bf16[64,12,1024]{2,1,0:T(8,128)(2,1)} %copy.33), calls=%async_computation.2 | async-start | bytes 4194304 | tf_op jit(solution)/shard_map/all_to_all | solution.py:117
  (1 other events, 0.6 us)
Sparse Core Ops, SparseCore 0:
  26.3 82.4 all-gather.2

commit v4 on v3

--- a/solution.py
+++ b/solution.py
@@ -52,18 +52,22 @@
     col_pieces, chunks = ring_gather((w_qkv, feats), ("exp", "seq"), (exp_count, seq_count))
     cols_slice = in_order(col_pieces, "exp", exp_count)
     cols_slice = cols_slice.reshape(exp_count * w_qkv.shape[0], head_cols)
-    projected_rel = [
-        jnp.dot(chunk, cols_slice, preferred_element_type=jnp.float32).astype(jnp.bfloat16)
-        for chunk in chunks
-    ]
-    projected = in_order(projected_rel, "seq", seq_count).reshape(seq_count * node_dev, head_cols)
+    gathered = jnp.stack(chunks).reshape(seq_count * node_dev, width)
+    projected = jnp.dot(gathered, cols_slice, preferred_element_type=jnp.float32).astype(
+        jnp.bfloat16
+    )
     nodes = projected.shape[0]
     heads_here = head_cols // (3 * HEAD_DIM)
-    split = projected.reshape(nodes, heads_here, 3, HEAD_DIM)
-    query = split[:, :, 0]
-    keys = split[:, :, 1]
-    values = split[:, :, 2]
+    split = projected.reshape(seq_count, node_dev, heads_here, 3, HEAD_DIM)
+    me = lax.axis_index("seq")
+    to_node = (jnp.arange(seq_count, dtype=jnp.int32) - me) % seq_count
+    to_ring = (jnp.arange(seq_count, dtype=jnp.int32) + me) % seq_count
+    query = jnp.take(split[:, :, :, 0], to_node, axis=0).reshape(nodes, heads_here, HEAD_DIM)
+    keys = split[:, :, :, 1].reshape(nodes, heads_here, HEAD_DIM)
+    values = split[:, :, :, 2].reshape(nodes, heads_here, HEAD_DIM)
     col_mask = jnp.repeat(block_mask[0], BLOCK, axis=1) > 0
+    col_mask = jnp.take(col_mask.reshape(-1, seq_count, node_dev), to_ring, axis=1)
+    col_mask = col_mask.reshape(-1, nodes)
     span = math.gcd(nodes, 512)
     scale = 1.0 / math.sqrt(HEAD_DIM)
 

time: 287 us -> 287 us (level)
  the two profiles are of different devices: /device:TPU:30 before, /device:TPU:24 now
where the time goes in v4:
time: 287 us; the launch traced here: 285 us
  starting transfers between devices  69.7 us (24%)
  waiting for transfers between devices  62.6 us (22%)
  blocking collectives  53.6 us (19%)
  local copies, waits for them, and re-layouts  40.3 us (14%)
  matrix products  38.7 us (13%)
  between operations  13.9 us (5%)
  other arithmetic  4.05 us (1%)
    all_to_all x1, blocking collectives, per_device(): lax.all_to_all(outgoing, ('seq', 'exp'), split_axis=0, concat_axis=0, til...  53.6 us
    all_to_all x1, waiting for transfers between devices, per_device(): lax.all_to_all(processed, ('seq', 'exp'), split_axis=0, concat_axis=0, ti...  51.7 us
    ppermute x8, starting transfers between devices, ring_gather(): moving[which][0] = lax.ppermute(moving[which][0], axis, right)  30.6 us
    ppermute x6, starting transfers between devices, ring_gather(): moving[which][1] = lax.ppermute(moving[which][1], axis, left)  25.2 us
    dot_general x3, matrix products, attend(): jnp.einsum('hqk,khd->qhd', probs, values, preferred_element_type=jnp.floa...  13.2 us
    unnamed x34, local copies, waits for them, and re-layouts  10.7 us
    sub x3, matrix products, attend(): weights = jnp.exp(scores - top)  10.5 us
    all_to_all x1, starting transfers between devices, per_device(): lax.all_to_all(processed, ('seq', 'exp'), split_axis=0, concat_axis=0, ti...  8.49 us
  transfers between devices with their start and end apart: 17, of which 6 were waited for; matrix products, arithmetic and copies ran while one was open for 24% of the time, Pallas kernels for 0%

profile of v4, /device:TPU:24, one launch (start us, length us, event | category | flops | bytes accessed | tf_op | source)
XLA Modules:
  0.0 285.1 jit_solution(17260585797787395479)
XLA Ops:
  6.5 4.8 %collective-permute-start.2 = (bf16[192,1024]{1,0:T(8,128)(2,1)}, bf16[192,1024]{1,0:T(8,128)(2,1)S(1)}, u32[]{:S(2)}, u32[]{:S(2)}) collective-permute-start(bf16[192,1024]{1,0:T(8,128)(2,1)} %bitcast.174), channel_id=1, source_target_pairs={{0,8},{8,16},{16,24},{24,32},{32,40},{40,48},{48,56},{56,0},{1,9},... | collective-permute-start | bytes 1179656 | tf_op jit(solution)/shard_map/ppermute | solution.py:22
  13.3 4.3 %collective-permute-start = (bf16[128,384]{1,0:T(8,128)(2,1)}, bf16[128,384]{1,0:T(8,128)(2,1)S(1)}, u32[]{:S(2)}, u32[]{:S(2)}) collective-permute-start(bf16[128,384]{1,0:T(8,128)(2,1)} %param.13), channel_id=1, source_target_pairs={{0,1},{1,2},{2,3},{3,4},{4,5},{5,6},{6,7},{7,0},{8,9},{9,10},{10,1... | collective-permute-start | bytes 294920 | tf_op jit(solution)/shard_map/ppermute | solution.py:22
  17.6 8.6 %collective-permute-start.1 = (bf16[128,384]{1,0:T(8,128)(2,1)}, bf16[128,384]{1,0:T(8,128)(2,1)S(1)}, u32[]{:S(2)}, u32[]{:S(2)}) collective-permute-start(bf16[128,384]{1,0:T(8,128)(2,1)} %param.13), channel_id=1, source_target_pairs={{0,7},{1,0},{2,1},{3,2},{4,3},{5,4},{6,5},{7,6},{8,15},{9,8},{10,9... | collective-permute-start | bytes 294920 | tf_op jit(solution)/shard_map/ppermute | solution.py:25
  33.7 5.3 %collective-permute-start.6 = (bf16[192,1024]{1,0:T(8,128)(2,1)S(1)}, bf16[192,1024]{1,0:T(8,128)(2,1)S(1)}, u32[]{:S(2)}, u32[]{:S(2)}) collective-permute-start(bf16[192,1024]{1,0:T(8,128)(2,1)S(1)} %collective-permute-done.2), channel_id=1, source_target_pairs={{0,8},{8,16},{16,24},{24,32},{32,40},{40,48},{48,56},{56,0},{1,9},... | collective-permute-start | bytes 1179656 | tf_op jit(solution)/shard_map/ppermute | solution.py:22
  42.8 5.1 %collective-permute-start.5 = (bf16[128,384]{1,0:T(8,128)(2,1)}, bf16[128,384]{1,0:T(8,128)(2,1)S(1)}, u32[]{:S(2)}, u32[]{:S(2)}) collective-permute-start(bf16[128,384]{1,0:T(8,128)(2,1)} %copy-done.6), channel_id=1, source_target_pairs={{0,7},{1,0},{2,1},{3,2},{4,3},{5,4},{6,5},{7,6},{8,15},{9,8},{10,9... | collective-permute-start | bytes 294920 | tf_op jit(solution)/shard_map/ppermute | solution.py:25
  52.3 3.4 %collective-permute-start.10 = (bf16[192,1024]{1,0:T(8,128)(2,1)S(1)}, bf16[192,1024]{1,0:T(8,128)(2,1)S(1)}, u32[]{:S(2)}, u32[]{:S(2)}) collective-permute-start(bf16[192,1024]{1,0:T(8,128)(2,1)S(1)} %collective-permute-done.6), channel_id=1, source_target_pairs={{0,8},{8,16},{16,24},{24,32},{32,40},{40,48},{48,56},{56,0},{1,9},... | collective-permute-start | bytes 1179656 | tf_op jit(solution)/shard_map/ppermute | solution.py:22
  55.6 2.5 collective-permute-start.11
  60.0 5.1 %collective-permute-start.9 = (bf16[128,384]{1,0:T(8,128)(2,1)S(1)}, bf16[128,384]{1,0:T(8,128)(2,1)S(1)}, u32[]{:S(2)}, u32[]{:S(2)}) collective-permute-start(bf16[128,384]{1,0:T(8,128)(2,1)S(1)} %collective-permute-done.5), channel_id=1, source_target_pairs={{0,7},{1,0},{2,1},{3,2},{4,3},{5,4},{6,5},{7,6},{8,15},{9,8},{10,9... | collective-permute-start | bytes 294920 | tf_op jit(solution)/shard_map/ppermute | solution.py:25
  67.4 4.9 %collective-permute-start.13 = (bf16[192,1024]{1,0:T(8,128)(2,1)S(1)}, bf16[192,1024]{1,0:T(8,128)(2,1)S(1)}, u32[]{:S(2)}, u32[]{:S(2)}) collective-permute-start(bf16[192,1024]{1,0:T(8,128)(2,1)S(1)} %collective-permute-done.10), channel_id=1, source_target_pairs={{0,8},{8,16},{16,24},{24,32},{32,40},{40,48},{48,56},{56,0},{1,9},... | collective-permute-start | bytes 1179656 | tf_op jit(solution)/shard_map/ppermute | solution.py:22
  72.3 4.1 %collective-permute-start.12 = (bf16[128,384]{1,0:T(8,128)(2,1)S(1)}, bf16[128,384]{1,0:T(8,128)(2,1)S(1)}, u32[]{:S(2)}, u32[]{:S(2)}) collective-permute-start(bf16[128,384]{1,0:T(8,128)(2,1)S(1)} %collective-permute-done.8), channel_id=1, source_target_pairs={{0,1},{1,2},{2,3},{3,4},{4,5},{5,6},{6,7},{7,0},{8,9},{9,10},{10,1... | collective-permute-start | bytes 294920 | tf_op jit(solution)/shard_map/ppermute | solution.py:22
  77.3 3.1 %collective-permute-done.12 = bf16[128,384]{1,0:T(8,128)(2,1)S(1)} collective-permute-done((bf16[128,384]{1,0:T(8,128)(2,1)S(1)}, bf16[128,384]{1,0:T(8,128)(2,1)S(1)}, u32[]{:S(2)}, u32[]{:S(2)}) %collective-permute-start.12) | collective-permute-done | bytes 98336 | tf_op jit(solution)/shard_map/ppermute | solution.py:22
  85.8 4.8 %convolution_convert_fusion = bf16[1536,384]{1,0:T(8,128)(2,1)} fusion(bf16[1536,1024]{1,0:T(8,128)(2,1)} %bitcast.178, bf16[1024,384]{1,0:T(8,128)(2,1)S(1)} %bitcast.176), kind=kOutput, calls=%fused_computation.29 | convolution fusion | flops 1208549376 | bytes 5111808 | tf_op jit(solution)/shard_map/dot_general | solution.py:56
  94.3 2.4 fusion.81
  98.1 2.3 reshape_squeeze.7
  100.4 2.3 reshape_squeeze.8
  103.5 28.5 %while.12 = (s32[]{:T(128)}, bf16[3,512,2,64]{1,3,2,0:T(8,128)(2,1)}, s32[3]{0:T(128)S(1)}, pred[12,1536]{1,0:T(8,128)(4,1)S(1)}, bf16[1536,2,64]{0,2,1:T(8,128)...) while((s32[]{:T(128)}, ...), condition=%wide.region_3.4_spmd, body=%wide.region_0.3_spmd.sunk | while | flops 618205184 | bytes 5532574 | solution.py:90
  105.1 3.5 %fusion.102 = f32[2,512]{1,0:T(2,128)S(1)} fusion(pred[512,1536]{1,0:T(8,128)(4,1)S(1)} %bitcast.169, bf16[1536,2,64]{0,2,1:T(8,128)(2,1)} %get-tuple-element.227, bf16[1536,2,64]{0,2,1:T(8,128)(2,1)} %get-tuple-element.226, s32[]{:T(128)S(6)} %select_n.230), kind=kOutput, calls=%fused_computation.138.clone.1 | convolution fusion | flops 207619584 | bytes 1314820 | tf_op jit(solution)/shard_map/while/body/eval_jaxpr/sub | solution.py:84
  108.6 4.4 %fusion.103 = bf16[3,512,2,64]{1,3,2,0:T(8,128)(2,1)} fusion(bf16[3,512,2,64]{1,3,2,0:T(8,128)(2,1)} %get-tuple-element.208, s32[]{:T(128)} %get-tuple-element.207, bf16[1536,2,64]{0,2,1:T(8,128)(2,1)} %get-tuple-element.228, f32[2,512]{1,0:T(2,128)S(1)} %fusion.102, pred[512,1536]{1,0:T(8,128)(4,1)S(1)} %bitcast.170, ...), kind=kOutput, calls=%fused_computation.14.clone.1 | convolution fusion | flops 410585600 | bytes 1839620 | tf_op jit(solution)/shard_map/while/body/eval_jaxpr/hqk,khd->qhd/dot_general | solution.py:86
  114.6 3.5 %fusion.102 = f32[2,512]{1,0:T(2,128)S(1)} fusion(pred[512,1536]{1,0:T(8,128)(4,1)S(1)} %bitcast.169, bf16[1536,2,64]{0,2,1:T(8,128)(2,1)} %get-tuple-element.227, bf16[1536,2,64]{0,2,1:T(8,128)(2,1)} %get-tuple-element.226, s32[]{:T(128)S(6)} %select_n.230), kind=kOutput, calls=%fused_computation.138.clone.1 | convolution fusion | flops 207619584 | bytes 1314820 | tf_op jit(solution)/shard_map/while/body/eval_jaxpr/sub | solution.py:84
  118.1 4.4 %fusion.103 = bf16[3,512,2,64]{1,3,2,0:T(8,128)(2,1)} fusion(bf16[3,512,2,64]{1,3,2,0:T(8,128)(2,1)} %get-tuple-element.208, s32[]{:T(128)} %get-tuple-element.207, bf16[1536,2,64]{0,2,1:T(8,128)(2,1)} %get-tuple-element.228, f32[2,512]{1,0:T(2,128)S(1)} %fusion.102, pred[512,1536]{1,0:T(8,128)(4,1)S(1)} %bitcast.170, ...), kind=kOutput, calls=%fused_computation.14.clone.1 | convolution fusion | flops 410585600 | bytes 1839620 | tf_op jit(solution)/shard_map/while/body/eval_jaxpr/hqk,khd->qhd/dot_general | solution.py:86
  124.1 3.5 %fusion.102 = f32[2,512]{1,0:T(2,128)S(1)} fusion(pred[512,1536]{1,0:T(8,128)(4,1)S(1)} %bitcast.169, bf16[1536,2,64]{0,2,1:T(8,128)(2,1)} %get-tuple-element.227, bf16[1536,2,64]{0,2,1:T(8,128)(2,1)} %get-tuple-element.226, s32[]{:T(128)S(6)} %select_n.230), kind=kOutput, calls=%fused_computation.138.clone.1 | convolution fusion | flops 207619584 | bytes 1314820 | tf_op jit(solution)/shard_map/while/body/eval_jaxpr/sub | solution.py:84
  127.6 4.4 %fusion.103 = bf16[3,512,2,64]{1,3,2,0:T(8,128)(2,1)} fusion(bf16[3,512,2,64]{1,3,2,0:T(8,128)(2,1)} %get-tuple-element.208, s32[]{:T(128)} %get-tuple-element.207, bf16[1536,2,64]{0,2,1:T(8,128)(2,1)} %get-tuple-element.228, f32[2,512]{1,0:T(2,128)S(1)} %fusion.102, pred[512,1536]{1,0:T(8,128)(4,1)S(1)} %bitcast.170, ...), kind=kOutput, calls=%fused_computation.14.clone.1 | convolution fusion | flops 410585600 | bytes 1839620 | tf_op jit(solution)/shard_map/while/body/eval_jaxpr/hqk,khd->qhd/dot_general | solution.py:86
  135.3 5.4 %all-to-all-start = ((bf16[8,192,128]{2,1,0:T(8,128)(2,1)}), bf16[8,192,128]{2,1,0:T(8,128)(2,1)S(1)}, u32[]{:S(2)}, u32[]{:S(2)}) async-start(bf16[8,192,128]{2,1,0:T(8,128)(2,1)} %reshape.316), calls=%async_computation | async-start | bytes 786432 | tf_op jit(solution)/shard_map/all_to_all | solution.py:92
  141.6 3.9 %copy.45 = bf16[8,8,128,128]{2,3,1,0:T(8,128)(2,1)} copy(bf16[8,8,128,128]{3,2,1,0:T(8,128)(2,1)} %bitcast.173) | data formatting | bytes 4194304 | tf_op jit(solution)/shard_map/reshape | solution.py:93
  145.5 3.8 %all-to-all-done = bf16[8,192,128]{2,1,0:T(8,128)(2,1)S(1)} async-done(((bf16[8,192,128]{2,1,0:T(8,128)(2,1)}), bf16[8,192,128]{2,1,0:T(8,128)(2,1)S(1)}, u32[]{:S(2)}, u32[]{:S(2)}) %all-to-all-start) | async-done | bytes 393248 | tf_op jit(solution)/shard_map/all_to_all | solution.py:92
  150.1 2.7 multiply_reduce_fusion
  154.3 53.6 %all_to_all.26 = bf16[64,12,1024]{2,1,0:T(8,128)(2,1)S(1)} all-to-all(bf16[64,12,1024]{2,1,0:T(8,128)(2,1)S(1)} %copy.51), channel_id=1, replica_groups=mesh['sub'=8,'seq'=8,'exp'=8] {'seq','exp'}, dimensions={0} | all-to-all | bytes 3145728 | tf_op jit(solution)/shard_map/all_to_all | solution.py:115
  207.9 2.2 fusion.33
  211.2 2.2 copy.53
  213.4 8.5 %all-to-all-start.2 = ((bf16[64,12,1024]{2,1,0:T(8,128)(2,1)}), bf16[64,12,1024]{2,1,0:T(8,128)(2,1)}, u32[]{:S(2)}, u32[]{:S(2)}) async-start(bf16[64,12,1024]{2,1,0:T(8,128)(2,1)} %copy.53), calls=%async_computation.2 | async-start | bytes 4194304 | tf_op jit(solution)/shard_map/all_to_all | solution.py:121
  221.9 51.7 %all-to-all-done.2 = bf16[64,12,1024]{2,1,0:T(8,128)(2,1)} async-done(((bf16[64,12,1024]{2,1,0:T(8,128)(2,1)}), bf16[64,12,1024]{2,1,0:T(8,128)(2,1)}, u32[]{:S(2)}, u32[]{:S(2)}) %all-to-all-start.2) | async-done | bytes 1572896 | tf_op jit(solution)/shard_map/all_to_all | solution.py:121
  273.5 3.8 %fusion.41 = f32[2,192,1024]{2,1,0:T(8,128)S(1)} fusion(bf16[64,12,1024]{2,1,0:T(8,128)(2,1)} %all-to-all-done.2, s32[192,2]{0,1:T(2,128)S(1)} %copy.50, s32[64,12]{0,1:T(8,128)S(1)} %multiply_add_fusion), kind=kOutput, calls=%fused_computation.42 | convolution fusion | flops 604274688 | bytes 3150336 | tf_op jit(solution)/shard_map/ecnk,ecd->knd/dot_general | solution.py:122
  (121 shorter events, 44.6 us)
Async XLA Ops:
  6.5 201.4 %copy-start = (bf16[1,1024,1024]{2,1,0:T(8,128)(2,1)S(1)}, bf16[1,1024,1024]{2,1,0:T(8,128)(2,1)}, u32[]{:S(2)}) copy-start(bf16[1,1024,1024]{2,1,0:T(8,128)(2,1)} %param.18) | copy-start | bytes 6291460
  6.5 135.1 %all-gather.3.cloned.1.call-start = ((), (), s32[]{:S(2)}) async-start(), calls=%async_computation.3 | async-start | bytes 2129920 | tf_op jit(solution)/shard_map/all_gather | solution.py:51
  6.5 26.5 %collective-permute-start.2 = (bf16[192,1024]{1,0:T(8,128)(2,1)}, bf16[192,1024]{1,0:T(8,128)(2,1)S(1)}, u32[]{:S(2)}, u32[]{:S(2)}) collective-permute-start(bf16[192,1024]{1,0:T(8,128)(2,1)} %bitcast.174), channel_id=1, source_target_pairs={{0,8},{8,16},{16,24},{24,32},{32,40},{40,48},{48,56},{56,0},{1,9},... | collective-permute-start | bytes 1179656 | tf_op jit(solution)/shard_map/ppermute | solution.py:22
  11.4 22.4 %collective-permute-start.3 = (bf16[192,1024]{1,0:T(8,128)(2,1)}, bf16[192,1024]{1,0:T(8,128)(2,1)S(1)}, u32[]{:S(2)}, u32[]{:S(2)}) collective-permute-start(bf16[192,1024]{1,0:T(8,128)(2,1)} %bitcast.175), channel_id=1, source_target_pairs={{0,56},{8,0},{16,8},{24,16},{32,24},{40,32},{48,40},{56,48},{1,57}... | collective-permute-start | bytes 1179656 | tf_op jit(solution)/shard_map/ppermute | solution.py:25
  13.3 19.7 %collective-permute-start = (bf16[128,384]{1,0:T(8,128)(2,1)}, bf16[128,384]{1,0:T(8,128)(2,1)S(1)}, u32[]{:S(2)}, u32[]{:S(2)}) collective-permute-start(bf16[128,384]{1,0:T(8,128)(2,1)} %param.13), channel_id=1, source_target_pairs={{0,1},{1,2},{2,3},{3,4},{4,5},{5,6},{6,7},{7,0},{8,9},{9,10},{10,1... | collective-permute-start | bytes 294920 | tf_op jit(solution)/shard_map/ppermute | solution.py:22
  17.6 15.5 %collective-permute-start.1 = (bf16[128,384]{1,0:T(8,128)(2,1)}, bf16[128,384]{1,0:T(8,128)(2,1)S(1)}, u32[]{:S(2)}, u32[]{:S(2)}) collective-permute-start(bf16[128,384]{1,0:T(8,128)(2,1)} %param.13), channel_id=1, source_target_pairs={{0,7},{1,0},{2,1},{3,2},{4,3},{5,4},{6,5},{7,6},{8,15},{9,8},{10,9... | collective-permute-start | bytes 294920 | tf_op jit(solution)/shard_map/ppermute | solution.py:25
  33.0 0.6 copy-start.4
  33.1 0.7 copy-start.6
  33.7 46.8 %copy-start.5 = (bf16[128,384]{1,0:T(8,128)(2,1)S(1)}, bf16[128,384]{1,0:T(8,128)(2,1)}, u32[]{:S(2)}) copy-start(bf16[128,384]{1,0:T(8,128)(2,1)} %copy-done.4) | copy-start | bytes 294916
  33.7 16.8 %collective-permute-start.6 = (bf16[192,1024]{1,0:T(8,128)(2,1)S(1)}, bf16[192,1024]{1,0:T(8,128)(2,1)S(1)}, u32[]{:S(2)}, u32[]{:S(2)}) collective-permute-start(bf16[192,1024]{1,0:T(8,128)(2,1)S(1)} %collective-permute-done.2), channel_id=1, source_target_pairs={{0,8},{8,16},{16,24},{24,32},{32,40},{40,48},{48,56},{56,0},{1,9},... | collective-permute-start | bytes 1179656 | tf_op jit(solution)/shard_map/ppermute | solution.py:22
  39.0 13.3 %collective-permute-start.7 = (bf16[192,1024]{1,0:T(8,128)(2,1)S(1)}, bf16[192,1024]{1,0:T(8,128)(2,1)S(1)}, u32[]{:S(2)}, u32[]{:S(2)}) collective-permute-start(bf16[192,1024]{1,0:T(8,128)(2,1)S(1)} %collective-permute-done.3), channel_id=1, source_target_pairs={{0,56},{8,0},{16,8},{24,16},{32,24},{40,32},{48,40},{56,48},{1,57}... | collective-permute-start | bytes 1179656 | tf_op jit(solution)/shard_map/ppermute | solution.py:25
  40.9 8.7 %collective-permute-start.4 = (bf16[128,384]{1,0:T(8,128)(2,1)}, bf16[128,384]{1,0:T(8,128)(2,1)S(1)}, u32[]{:S(2)}, u32[]{:S(2)}) collective-permute-start(bf16[128,384]{1,0:T(8,128)(2,1)} %copy-done.4), channel_id=1, source_target_pairs={{0,1},{1,2},{2,3},{3,4},{4,5},{5,6},{6,7},{7,0},{8,9},{9,10},{10,1... | collective-permute-start | bytes 294920 | tf_op jit(solution)/shard_map/ppermute | solution.py:22
  42.8 7.6 %collective-permute-start.5 = (bf16[128,384]{1,0:T(8,128)(2,1)}, bf16[128,384]{1,0:T(8,128)(2,1)S(1)}, u32[]{:S(2)}, u32[]{:S(2)}) collective-permute-start(bf16[128,384]{1,0:T(8,128)(2,1)} %copy-done.6), channel_id=1, source_target_pairs={{0,7},{1,0},{2,1},{3,2},{4,3},{5,4},{6,5},{7,6},{8,15},{9,8},{10,9... | collective-permute-start | bytes 294920 | tf_op jit(solution)/shard_map/ppermute | solution.py:25
  52.3 15.1 %collective-permute-start.10 = (bf16[192,1024]{1,0:T(8,128)(2,1)S(1)}, bf16[192,1024]{1,0:T(8,128)(2,1)S(1)}, u32[]{:S(2)}, u32[]{:S(2)}) collective-permute-start(bf16[192,1024]{1,0:T(8,128)(2,1)S(1)} %collective-permute-done.6), channel_id=1, source_target_pairs={{0,8},{8,16},{16,24},{24,32},{32,40},{40,48},{48,56},{56,0},{1,9},... | collective-permute-start | bytes 1179656 | tf_op jit(solution)/shard_map/ppermute | solution.py:22
  55.6 11.7 %collective-permute-start.11 = (bf16[192,1024]{1,0:T(8,128)(2,1)S(1)}, bf16[192,1024]{1,0:T(8,128)(2,1)S(1)}, u32[]{:S(2)}, u32[]{:S(2)}) collective-permute-start(bf16[192,1024]{1,0:T(8,128)(2,1)S(1)} %collective-permute-done.7), channel_id=1, source_target_pairs={{0,56},{8,0},{16,8},{24,16},{32,24},{40,32},{48,40},{56,48},{1,57}... | collective-permute-start | bytes 1179656 | tf_op jit(solution)/shard_map/ppermute | solution.py:25
  58.1 7.9 %collective-permute-start.8 = (bf16[128,384]{1,0:T(8,128)(2,1)S(1)}, bf16[128,384]{1,0:T(8,128)(2,1)S(1)}, u32[]{:S(2)}, u32[]{:S(2)}) collective-permute-start(bf16[128,384]{1,0:T(8,128)(2,1)S(1)} %collective-permute-done.4), channel_id=1, source_target_pairs={{0,1},{1,2},{2,3},{3,4},{4,5},{5,6},{6,7},{7,0},{8,9},{9,10},{10,1... | collective-permute-start | bytes 294920 | tf_op jit(solution)/shard_map/ppermute | solution.py:22
  60.0 7.3 %collective-permute-start.9 = (bf16[128,384]{1,0:T(8,128)(2,1)S(1)}, bf16[128,384]{1,0:T(8,128)(2,1)S(1)}, u32[]{:S(2)}, u32[]{:S(2)}) collective-permute-start(bf16[128,384]{1,0:T(8,128)(2,1)S(1)} %collective-permute-done.5), channel_id=1, source_target_pairs={{0,7},{1,0},{2,1},{3,2},{4,3},{5,4},{6,5},{7,6},{8,15},{9,8},{10,9... | collective-permute-start | bytes 294920 | tf_op jit(solution)/shard_map/ppermute | solution.py:25
  67.4 13.1 %collective-permute-start.13 = (bf16[192,1024]{1,0:T(8,128)(2,1)S(1)}, bf16[192,1024]{1,0:T(8,128)(2,1)S(1)}, u32[]{:S(2)}, u32[]{:S(2)}) collective-permute-start(bf16[192,1024]{1,0:T(8,128)(2,1)S(1)} %collective-permute-done.10), channel_id=1, source_target_pairs={{0,8},{8,16},{16,24},{24,32},{32,40},{40,48},{48,56},{56,0},{1,9},... | collective-permute-start | bytes 1179656 | tf_op jit(solution)/shard_map/ppermute | solution.py:22
  72.3 8.1 %collective-permute-start.12 = (bf16[128,384]{1,0:T(8,128)(2,1)S(1)}, bf16[128,384]{1,0:T(8,128)(2,1)S(1)}, u32[]{:S(2)}, u32[]{:S(2)}) collective-permute-start(bf16[128,384]{1,0:T(8,128)(2,1)S(1)} %collective-permute-done.8), channel_id=1, source_target_pairs={{0,1},{1,2},{2,3},{3,4},{4,5},{5,6},{6,7},{7,0},{8,9},{9,10},{10,1... | collective-permute-start | bytes 294920 | tf_op jit(solution)/shard_map/ppermute | solution.py:22
  80.6 3.2 %copy-start.2 = (bf16[8,128,384]{2,1,0:T(8,128)(2,1)}, bf16[8,128,384]{2,1,0:T(8,128)(2,1)S(1)}, u32[]{:S(2)}) copy-start(bf16[8,128,384]{2,1,0:T(8,128)(2,1)S(1)} %bitcast_dynamic-update-slice_fusion.7) | copy-start | bytes 2359300
  105.1 3.5 %copy-start.3 = (bf16[1536,2,64]{0,2,1:T(8,128)(2,1)S(1)}, bf16[1536,2,64]{0,2,1:T(8,128)(2,1)}, u32[]{:S(2)}) copy-start(bf16[1536,2,64]{0,2,1:T(8,128)(2,1)} %get-tuple-element.227) | copy-start | bytes 1179652 | tf_op jit(solution)/shard_map/while
  114.6 3.5 %copy-start.3 = (bf16[1536,2,64]{0,2,1:T(8,128)(2,1)S(1)}, bf16[1536,2,64]{0,2,1:T(8,128)(2,1)}, u32[]{:S(2)}) copy-start(bf16[1536,2,64]{0,2,1:T(8,128)(2,1)} %get-tuple-element.227) | copy-start | bytes 1179652 | tf_op jit(solution)/shard_map/while
  124.1 3.5 %copy-start.3 = (bf16[1536,2,64]{0,2,1:T(8,128)(2,1)S(1)}, bf16[1536,2,64]{0,2,1:T(8,128)(2,1)}, u32[]{:S(2)}) copy-start(bf16[1536,2,64]{0,2,1:T(8,128)(2,1)} %get-tuple-element.227) | copy-start | bytes 1179652 | tf_op jit(solution)/shard_map/while
  135.3 14.0 %all-to-all-start = ((bf16[8,192,128]{2,1,0:T(8,128)(2,1)}), bf16[8,192,128]{2,1,0:T(8,128)(2,1)S(1)}, u32[]{:S(2)}, u32[]{:S(2)}) async-start(bf16[8,192,128]{2,1,0:T(8,128)(2,1)} %reshape.316), calls=%async_computation | async-start | bytes 786432 | tf_op jit(solution)/shard_map/all_to_all | solution.py:92
  141.6 11.2 %copy-start.7 = (f32[1024]{0:T(1024)S(1)}, f32[1024]{0:T(1024)}, u32[]{:S(2)}) copy-start(f32[1024]{0:T(1024)} %param.15) | copy-start | bytes 12292
  149.3 0.7 copy-start.1
  207.9 2.2 copy-start.9
  211.1 10.7 %copy-start.8 = (f32[1,192,2]{1,2,0:T(2,128)S(1)}, f32[1,192,2]{1,2,0:T(2,128)}, u32[]{:S(2)}) copy-start(f32[1,192,2]{1,2,0:T(2,128)} %param.17) | copy-start | bytes 4612
  213.4 60.2 %all-to-all-start.2 = ((bf16[64,12,1024]{2,1,0:T(8,128)(2,1)}), bf16[64,12,1024]{2,1,0:T(8,128)(2,1)}, u32[]{:S(2)}, u32[]{:S(2)}) async-start(bf16[64,12,1024]{2,1,0:T(8,128)(2,1)} %copy.53), calls=%async_computation.2 | async-start | bytes 4194304 | tf_op jit(solution)/shard_map/all_to_all | solution.py:121
Sparse Core Ops, SparseCore 0:
  26.3 82.6 all-gather.2

commit v5 on v4

--- a/solution.py
+++ b/solution.py
@@ -1,13 +1,66 @@
+import functools
 import math
 
 import jax
 import jax.numpy as jnp
 from jax import lax
+from jax.experimental import pallas as pl
+from jax.experimental.pallas import tpu as pltpu
 from jax.sharding import PartitionSpec as P
 
 HEAD_DIM = 64
 TOP = 2
 BLOCK = 128
+TILE = 64
+
+
+def attention_kernel(me_ref, mask_ref, proj_ref, out_ref, *, chunk, chunks, heads, blocks):
+    tile = pl.program_id(0)
+    me = me_ref[0]
+    per_chunk = chunk // TILE
+    ring_chunk = (tile // per_chunk - me + chunks) % chunks
+    start = pl.multiple_of(ring_chunk * chunk + (tile % per_chunk) * TILE, TILE)
+    query_block = (tile * TILE) // BLOCK
+    nodes = chunk * chunks
+    key_tiles = nodes // TILE
+    lane_tile = lax.broadcasted_iota(jnp.int32, (1, nodes), 1) // TILE
+    allowed = jnp.zeros((1, nodes), jnp.int32)
+    for t in range(key_tiles):
+        node = ((me + t // per_chunk) % chunks) * chunk + (t % per_chunk) * TILE
+        bit = mask_ref[query_block * blocks + node // BLOCK]
+        allowed = jnp.where(lane_tile == t, bit, allowed)
+    allowed = allowed > 0
+    rows = proj_ref[pl.ds(start, TILE), :]
+    scale = 1.0 / math.sqrt(HEAD_DIM)
+    for h in range(heads):
+        base = h * 3 * HEAD_DIM
+        q = rows[:, base:base + HEAD_DIM]
+        k = proj_ref[:, base + HEAD_DIM:base + 2 * HEAD_DIM]
+        v = proj_ref[:, base + 2 * HEAD_DIM:base + 3 * HEAD_DIM]
+        scores = lax.dot_general(q, k, (((1,), (1,)), ((), ())), preferred_element_type=jnp.float32) * scale
+        scores = jnp.where(allowed, scores, -1e30)
+        top = jnp.max(scores, axis=-1, keepdims=True)
+        weights = jnp.exp(scores - top)
+        probs = (weights / jnp.sum(weights, axis=-1, keepdims=True)).astype(jnp.bfloat16)
+        out = jnp.dot(probs, v, preferred_element_type=jnp.float32)
+        out_ref[:, h * HEAD_DIM:(h + 1) * HEAD_DIM] = out.astype(out_ref.dtype)
+
+
+def attention(me, mask, projected, chunk, chunks):
+    nodes, cols = projected.shape
+    heads = cols // (3 * HEAD_DIM)
+    blocks = mask.shape[-1]
+    kernel = functools.partial(attention_kernel, chunk=chunk, chunks=chunks, heads=heads, blocks=blocks)
+    return pl.pallas_call(
+        kernel,
+        out_shape=jax.ShapeDtypeStruct((nodes, heads * HEAD_DIM), jnp.bfloat16),
+        grid_spec=pltpu.PrefetchScalarGridSpec(
+            num_scalar_prefetch=2,
+            grid=(nodes // TILE,),
+            in_specs=[pl.BlockSpec((nodes, cols), lambda t, me, mask: (0, 0))],
+            out_specs=pl.BlockSpec((TILE, heads * HEAD_DIM), lambda t, me, mask: (t, 0)),
+        ),
+    )(me.reshape(1), mask.reshape(-1), projected)
 
 
 def ring_gather(pieces, axes, counts):
@@ -56,39 +109,8 @@
     projected = jnp.dot(gathered, cols_slice, preferred_element_type=jnp.float32).astype(
         jnp.bfloat16
     )
-    nodes = projected.shape[0]
-    heads_here = head_cols // (3 * HEAD_DIM)
-    split = projected.reshape(seq_count, node_dev, heads_here, 3, HEAD_DIM)
-    me = lax.axis_index("seq")
-    to_node = (jnp.arange(seq_count, dtype=jnp.int32) - me) % seq_count
-    to_ring = (jnp.arange(seq_count, dtype=jnp.int32) + me) % seq_count
-    query = jnp.take(split[:, :, :, 0], to_node, axis=0).reshape(nodes, heads_here, HEAD_DIM)
-    keys = split[:, :, :, 1].reshape(nodes, heads_here, HEAD_DIM)
-    values = split[:, :, :, 2].reshape(nodes, heads_here, HEAD_DIM)
-    col_mask = jnp.repeat(block_mask[0], BLOCK, axis=1) > 0
-    col_mask = jnp.take(col_mask.reshape(-1, seq_count, node_dev), to_ring, axis=1)
-    col_mask = col_mask.reshape(-1, nodes)
-    span = math.gcd(nodes, 512)
-    scale = 1.0 / math.sqrt(HEAD_DIM)
-
-    def attend(index):
-        start = index * span
-        rows_query = lax.dynamic_slice_in_dim(query, start, span, 0)
-        rows_mask = lax.dynamic_slice_in_dim(col_mask, start // BLOCK, span // BLOCK, 0)
-        allowed = jnp.repeat(rows_mask, BLOCK, axis=0)
-        scores = (
-            jnp.einsum("qhd,khd->hqk", rows_query, keys, preferred_element_type=jnp.float32) * scale
-        )
-        scores = jnp.where(allowed[None], scores, -1e30)
-        top = jnp.max(scores, axis=-1, keepdims=True)
-        weights = jnp.exp(scores - top)
-        probs = (weights / jnp.sum(weights, axis=-1, keepdims=True)).astype(jnp.bfloat16)
-        return jnp.einsum("hqk,khd->qhd", probs, values, preferred_element_type=jnp.float32).astype(
-            jnp.bfloat16
-        )
-
-    blocks = lax.map(attend, jnp.arange(nodes // span, dtype=jnp.int32))
-    attended = blocks.reshape(nodes, heads_here * HEAD_DIM)
+    me = lax.axis_index("seq").astype(jnp.int32)
+    attended = attention(me, block_mask[0], projected, node_dev, seq_count)
     node_attended = lax.all_to_all(attended, "seq", split_axis=0, concat_axis=1, tiled=True)
     out_tiles = out_all.reshape(seq_count, exp_count, w_out.shape[0], w_out.shape[1])
     attn_out = jnp.einsum(

time: 287 us -> 281 us (0.979)
  the two profiles are of different devices: /device:TPU:24 before, /device:TPU:26 now
where the time goes in v5:
time: 281 us; the launch traced here: 280 us
  starting transfers between devices  69.5 us (25%)
  waiting for transfers between devices  60.6 us (22%)
  blocking collectives  53.7 us (19%)
  Pallas kernels  34.3 us (12%)
  local copies, waits for them, and re-layouts  29.7 us (11%)
  matrix products  15.1 us (5%)
  between operations  13.8 us (5%)
  other arithmetic  3.19 us (1%)
    all_to_all x1, blocking collectives, per_device(): lax.all_to_all(outgoing, ('seq', 'exp'), split_axis=0, concat_axis=0, til...  53.7 us
    all_to_all x1, waiting for transfers between devices, per_device(): lax.all_to_all(processed, ('seq', 'exp'), split_axis=0, concat_axis=0, ti...  51.2 us
    pallas_call x1, Pallas kernels, attention(): pl.pallas_call(kernel, out_shape=jax.ShapeDtypeStruct((nodes, heads * HEA...  34.3 us
    ppermute x8, starting transfers between devices, ring_gather(): moving[which][0] = lax.ppermute(moving[which][0], axis, right)  30.2 us
    ppermute x6, starting transfers between devices, ring_gather(): moving[which][1] = lax.ppermute(moving[which][1], axis, left)  25.3 us
    unnamed x37, local copies, waits for them, and re-layouts  18 us
    all_to_all x1, starting transfers between devices, per_device(): lax.all_to_all(processed, ('seq', 'exp'), split_axis=0, concat_axis=0, ti...  8.67 us
  transfers between devices with their start and end apart: 17, of which 7 were waited for; matrix products, arithmetic and copies ran while one was open for 11% of the time, Pallas kernels for 12%

profile of v5, /device:TPU:26, one launch (start us, length us, event | category | flops | bytes accessed | tf_op | source)
XLA Modules:
  0.0 279.9 jit_solution(5457843182458904127)
XLA Ops:
  6.5 4.8 %collective-permute-start.2 = (bf16[192,1024]{1,0:T(8,128)(2,1)}, bf16[192,1024]{1,0:T(8,128)(2,1)S(1)}, u32[]{:S(2)}, u32[]{:S(2)}) collective-permute-start(bf16[192,1024]{1,0:T(8,128)(2,1)} %bitcast.126), channel_id=1, source_target_pairs={{0,8},{8,16},{16,24},{24,32},{32,40},{40,48},{48,56},{56,0},{1,9},... | collective-permute-start | bytes 1179656 | tf_op jit(solution)/shard_map/ppermute | solution.py:75
  11.4 1.9 collective-permute-start.3
  13.3 4.3 %collective-permute-start = (bf16[128,384]{1,0:T(8,128)(2,1)}, bf16[128,384]{1,0:T(8,128)(2,1)S(1)}, u32[]{:S(2)}, u32[]{:S(2)}) collective-permute-start(bf16[128,384]{1,0:T(8,128)(2,1)} %param.11), channel_id=1, source_target_pairs={{0,1},{1,2},{2,3},{3,4},{4,5},{5,6},{6,7},{7,0},{8,9},{9,10},{10,1... | collective-permute-start | bytes 294920 | tf_op jit(solution)/shard_map/ppermute | solution.py:75
  17.6 8.6 %collective-permute-start.1 = (bf16[128,384]{1,0:T(8,128)(2,1)}, bf16[128,384]{1,0:T(8,128)(2,1)S(1)}, u32[]{:S(2)}, u32[]{:S(2)}) collective-permute-start(bf16[128,384]{1,0:T(8,128)(2,1)} %param.11), channel_id=1, source_target_pairs={{0,7},{1,0},{2,1},{3,2},{4,3},{5,4},{6,5},{7,6},{8,15},{9,8},{10,9... | collective-permute-start | bytes 294920 | tf_op jit(solution)/shard_map/ppermute | solution.py:78
  26.2 1.8 constant_dynamic-update-slice_fusion
  33.6 5.1 %collective-permute-start.6 = (bf16[192,1024]{1,0:T(8,128)(2,1)S(1)}, bf16[192,1024]{1,0:T(8,128)(2,1)S(1)}, u32[]{:S(2)}, u32[]{:S(2)}) collective-permute-start(bf16[192,1024]{1,0:T(8,128)(2,1)S(1)} %collective-permute-done.2), channel_id=1, source_target_pairs={{0,8},{8,16},{16,24},{24,32},{32,40},{40,48},{48,56},{56,0},{1,9},... | collective-permute-start | bytes 1179656 | tf_op jit(solution)/shard_map/ppermute | solution.py:75
  38.8 2.1 collective-permute-start.7
  40.8 1.9 collective-permute-start.4
  42.8 5.1 %collective-permute-start.5 = (bf16[128,384]{1,0:T(8,128)(2,1)}, bf16[128,384]{1,0:T(8,128)(2,1)S(1)}, u32[]{:S(2)}, u32[]{:S(2)}) collective-permute-start(bf16[128,384]{1,0:T(8,128)(2,1)} %copy-done.7), channel_id=1, source_target_pairs={{0,7},{1,0},{2,1},{3,2},{4,3},{5,4},{6,5},{7,6},{8,15},{9,8},{10,9... | collective-permute-start | bytes 294920 | tf_op jit(solution)/shard_map/ppermute | solution.py:78
  52.2 3.4 %collective-permute-start.10 = (bf16[192,1024]{1,0:T(8,128)(2,1)S(1)}, bf16[192,1024]{1,0:T(8,128)(2,1)S(1)}, u32[]{:S(2)}, u32[]{:S(2)}) collective-permute-start(bf16[192,1024]{1,0:T(8,128)(2,1)S(1)} %collective-permute-done.6), channel_id=1, source_target_pairs={{0,8},{8,16},{16,24},{24,32},{32,40},{40,48},{48,56},{56,0},{1,9},... | collective-permute-start | bytes 1179656 | tf_op jit(solution)/shard_map/ppermute | solution.py:75
  55.6 2.4 collective-permute-start.11
  58.0 1.9 collective-permute-start.8
  59.9 5.1 %collective-permute-start.9 = (bf16[128,384]{1,0:T(8,128)(2,1)S(1)}, bf16[128,384]{1,0:T(8,128)(2,1)S(1)}, u32[]{:S(2)}, u32[]{:S(2)}) collective-permute-start(bf16[128,384]{1,0:T(8,128)(2,1)S(1)} %collective-permute-done.5), channel_id=1, source_target_pairs={{0,7},{1,0},{2,1},{3,2},{4,3},{5,4},{6,5},{7,6},{8,15},{9,8},{10,9... | collective-permute-start | bytes 294920 | tf_op jit(solution)/shard_map/ppermute | solution.py:78
  67.5 4.8 %collective-permute-start.13 = (bf16[192,1024]{1,0:T(8,128)(2,1)S(1)}, bf16[192,1024]{1,0:T(8,128)(2,1)S(1)}, u32[]{:S(2)}, u32[]{:S(2)}) collective-permute-start(bf16[192,1024]{1,0:T(8,128)(2,1)S(1)} %collective-permute-done.10), channel_id=1, source_target_pairs={{0,8},{8,16},{16,24},{24,32},{32,40},{40,48},{48,56},{56,0},{1,9},... | collective-permute-start | bytes 1179656 | tf_op jit(solution)/shard_map/ppermute | solution.py:75
  72.3 4.0 %collective-permute-start.12 = (bf16[128,384]{1,0:T(8,128)(2,1)S(1)}, bf16[128,384]{1,0:T(8,128)(2,1)S(1)}, u32[]{:S(2)}, u32[]{:S(2)}) collective-permute-start(bf16[128,384]{1,0:T(8,128)(2,1)S(1)} %collective-permute-done.8), channel_id=1, source_target_pairs={{0,1},{1,2},{2,3},{3,4},{4,5},{5,6},{6,7},{7,0},{8,9},{9,10},{10,1... | collective-permute-start | bytes 294920 | tf_op jit(solution)/shard_map/ppermute | solution.py:75
  77.7 2.7 collective-permute-done.12
  83.0 1.8 gather_fusion
  84.9 1.8 bitcast_dynamic-update-slice_fusion.3
  86.7 1.8 bitcast_dynamic-update-slice_fusion.2
  88.4 1.8 bitcast_dynamic-update-slice_fusion.1
  91.1 4.8 %convolution_convert_fusion.proj_ref = bf16[1536,384]{1,0:T(8,128)(2,1)} fusion(bf16[1536,1024]{1,0:T(8,128)(2,1)} %bitcast.129, bf16[1024,384]{1,0:T(8,128)(2,1)S(1)} %bitcast.128), kind=kOutput, calls=%fused_computation.1 | convolution fusion | flops 1208549376 | bytes 5111808 | tf_op jit(solution)/shard_map/dot_general | solution.py:109
  95.9 34.3 %shard_map.91 = bf16[1536,128]{1,0:T(8,128)(2,1)} custom-call(s32[1]{0:T(128)} %bitcast.1.me_ref, s32[144]{0:T(256)} %reshape_squeeze.4.mask_ref, bf16[1536,384]{1,0:T(8,128)(2,1)} %convolution_convert_fusion.proj_ref), custom_call_target="tpu_custom_call" | custom-call | tf_op jit(solution)/shard_map/pallas_call | solution.py:54
  130.2 5.4 %all-to-all-start = ((bf16[8,192,128]{2,1,0:T(8,128)(2,1)}), bf16[8,192,128]{2,1,0:T(8,128)(2,1)S(1)}, u32[]{:S(2)}, u32[]{:S(2)}) async-start(bf16[8,192,128]{2,1,0:T(8,128)(2,1)} %bitcast.125), calls=%async_computation | async-start | bytes 786432 | tf_op jit(solution)/shard_map/all_to_all | solution.py:114
  136.5 3.9 %copy.17 = bf16[8,8,128,128]{2,3,1,0:T(8,128)(2,1)} copy(bf16[8,8,128,128]{3,2,1,0:T(8,128)(2,1)} %bitcast.124) | data formatting | bytes 4194304 | tf_op jit(solution)/shard_map/reshape | solution.py:115
  140.4 3.8 %all-to-all-done = bf16[8,192,128]{2,1,0:T(8,128)(2,1)S(1)} async-done(((bf16[8,192,128]{2,1,0:T(8,128)(2,1)}), bf16[8,192,128]{2,1,0:T(8,128)(2,1)S(1)}, u32[]{:S(2)}, u32[]{:S(2)}) %all-to-all-start) | async-done | bytes 393248 | tf_op jit(solution)/shard_map/all_to_all | solution.py:114
  145.0 2.7 multiply_reduce_fusion
  149.2 53.7 %all_to_all.26 = bf16[64,12,1024]{2,1,0:T(8,128)(2,1)S(1)} all-to-all(bf16[64,12,1024]{2,1,0:T(8,128)(2,1)S(1)} %copy.23), channel_id=1, replica_groups=mesh['sub'=8,'seq'=8,'exp'=8] {'seq','exp'}, dimensions={0} | all-to-all | bytes 3145728 | tf_op jit(solution)/shard_map/all_to_all | solution.py:137
  202.9 2.2 fusion
  206.2 2.2 copy.25
  208.4 8.7 %all-to-all-start.2 = ((bf16[64,12,1024]{2,1,0:T(8,128)(2,1)}), bf16[64,12,1024]{2,1,0:T(8,128)(2,1)}, u32[]{:S(2)}, u32[]{:S(2)}) async-start(bf16[64,12,1024]{2,1,0:T(8,128)(2,1)} %copy.25), calls=%async_computation.2 | async-start | bytes 4194304 | tf_op jit(solution)/shard_map/all_to_all | solution.py:143
  217.1 51.2 %all-to-all-done.2 = bf16[64,12,1024]{2,1,0:T(8,128)(2,1)} async-done(((bf16[64,12,1024]{2,1,0:T(8,128)(2,1)}), bf16[64,12,1024]{2,1,0:T(8,128)(2,1)}, u32[]{:S(2)}, u32[]{:S(2)}) %all-to-all-start.2) | async-done | bytes 1572896 | tf_op jit(solution)/shard_map/all_to_all | solution.py:143
  268.3 3.8 %fusion.8 = f32[2,192,1024]{2,1,0:T(8,128)S(1)} fusion(bf16[64,12,1024]{2,1,0:T(8,128)(2,1)} %all-to-all-done.2, s32[192,2]{0,1:T(2,128)S(1)} %copy.22, s32[64,12]{0,1:T(8,128)S(1)} %multiply_add_fusion), kind=kOutput, calls=%fused_computation.14 | convolution fusion | flops 604274688 | bytes 3150336 | tf_op jit(solution)/shard_map/ecnk,ecd->knd/dot_general | solution.py:144
  (75 shorter events, 22.4 us)
Async XLA Ops:
  6.5 196.4 %copy-start = (bf16[1,1024,1024]{2,1,0:T(8,128)(2,1)S(1)}, bf16[1,1024,1024]{2,1,0:T(8,128)(2,1)}, u32[]{:S(2)}) copy-start(bf16[1,1024,1024]{2,1,0:T(8,128)(2,1)} %param.16) | copy-start | bytes 6291460
  6.5 130.0 %all-gather.3.cloned.1.call-start = ((), (), s32[]{:S(2)}) async-start(), calls=%async_computation.3 | async-start | bytes 2129920 | tf_op jit(solution)/shard_map/all_gather | solution.py:104
  6.5 26.5 %collective-permute-start.2 = (bf16[192,1024]{1,0:T(8,128)(2,1)}, bf16[192,1024]{1,0:T(8,128)(2,1)S(1)}, u32[]{:S(2)}, u32[]{:S(2)}) collective-permute-start(bf16[192,1024]{1,0:T(8,128)(2,1)} %bitcast.126), channel_id=1, source_target_pairs={{0,8},{8,16},{16,24},{24,32},{32,40},{40,48},{48,56},{56,0},{1,9},... | collective-permute-start | bytes 1179656 | tf_op jit(solution)/shard_map/ppermute | solution.py:75
  11.4 21.7 %collective-permute-start.3 = (bf16[192,1024]{1,0:T(8,128)(2,1)}, bf16[192,1024]{1,0:T(8,128)(2,1)S(1)}, u32[]{:S(2)}, u32[]{:S(2)}) collective-permute-start(bf16[192,1024]{1,0:T(8,128)(2,1)} %bitcast.127), channel_id=1, source_target_pairs={{0,56},{8,0},{16,8},{24,16},{32,24},{40,32},{48,40},{56,48},{1,57}... | collective-permute-start | bytes 1179656 | tf_op jit(solution)/shard_map/ppermute | solution.py:78
  13.3 19.7 %collective-permute-start = (bf16[128,384]{1,0:T(8,128)(2,1)}, bf16[128,384]{1,0:T(8,128)(2,1)S(1)}, u32[]{:S(2)}, u32[]{:S(2)}) collective-permute-start(bf16[128,384]{1,0:T(8,128)(2,1)} %param.11), channel_id=1, source_target_pairs={{0,1},{1,2},{2,3},{3,4},{4,5},{5,6},{6,7},{7,0},{8,9},{9,10},{10,1... | collective-permute-start | bytes 294920 | tf_op jit(solution)/shard_map/ppermute | solution.py:75
  17.6 15.4 %collective-permute-start.1 = (bf16[128,384]{1,0:T(8,128)(2,1)}, bf16[128,384]{1,0:T(8,128)(2,1)S(1)}, u32[]{:S(2)}, u32[]{:S(2)}) collective-permute-start(bf16[128,384]{1,0:T(8,128)(2,1)} %param.11), channel_id=1, source_target_pairs={{0,7},{1,0},{2,1},{3,2},{4,3},{5,4},{6,5},{7,6},{8,15},{9,8},{10,9... | collective-permute-start | bytes 294920 | tf_op jit(solution)/shard_map/ppermute | solution.py:78
  33.0 0.6 copy-start.5
  33.0 0.7 copy-start.7
  33.6 16.8 %collective-permute-start.6 = (bf16[192,1024]{1,0:T(8,128)(2,1)S(1)}, bf16[192,1024]{1,0:T(8,128)(2,1)S(1)}, u32[]{:S(2)}, u32[]{:S(2)}) collective-permute-start(bf16[192,1024]{1,0:T(8,128)(2,1)S(1)} %collective-permute-done.2), channel_id=1, source_target_pairs={{0,8},{8,16},{16,24},{24,32},{32,40},{40,48},{48,56},{56,0},{1,9},... | collective-permute-start | bytes 1179656 | tf_op jit(solution)/shard_map/ppermute | solution.py:75
  38.8 43.6 %copy-start.6 = (bf16[128,384]{1,0:T(8,128)(2,1)S(1)}, bf16[128,384]{1,0:T(8,128)(2,1)}, u32[]{:S(2)}) copy-start(bf16[128,384]{1,0:T(8,128)(2,1)} %copy-done.5) | copy-start | bytes 294916
  38.8 13.4 %collective-permute-start.7 = (bf16[192,1024]{1,0:T(8,128)(2,1)S(1)}, bf16[192,1024]{1,0:T(8,128)(2,1)S(1)}, u32[]{:S(2)}, u32[]{:S(2)}) collective-permute-start(bf16[192,1024]{1,0:T(8,128)(2,1)S(1)} %collective-permute-done.3), channel_id=1, source_target_pairs={{0,56},{8,0},{16,8},{24,16},{32,24},{40,32},{48,40},{56,48},{1,57}... | collective-permute-start | bytes 1179656 | tf_op jit(solution)/shard_map/ppermute | solution.py:78
  40.8 9.4 %collective-permute-start.4 = (bf16[128,384]{1,0:T(8,128)(2,1)}, bf16[128,384]{1,0:T(8,128)(2,1)S(1)}, u32[]{:S(2)}, u32[]{:S(2)}) collective-permute-start(bf16[128,384]{1,0:T(8,128)(2,1)} %copy-done.5), channel_id=1, source_target_pairs={{0,1},{1,2},{2,3},{3,4},{4,5},{5,6},{6,7},{7,0},{8,9},{9,10},{10,1... | collective-permute-start | bytes 294920 | tf_op jit(solution)/shard_map/ppermute | solution.py:75
  42.8 7.6 %collective-permute-start.5 = (bf16[128,384]{1,0:T(8,128)(2,1)}, bf16[128,384]{1,0:T(8,128)(2,1)S(1)}, u32[]{:S(2)}, u32[]{:S(2)}) collective-permute-start(bf16[128,384]{1,0:T(8,128)(2,1)} %copy-done.7), channel_id=1, source_target_pairs={{0,7},{1,0},{2,1},{3,2},{4,3},{5,4},{6,5},{7,6},{8,15},{9,8},{10,9... | collective-permute-start | bytes 294920 | tf_op jit(solution)/shard_map/ppermute | solution.py:78
  50.4 31.9 %copy-start.2 = (bf16[192,1024]{1,0:T(8,128)(2,1)}, bf16[192,1024]{1,0:T(8,128)(2,1)S(1)}, u32[]{:S(2)}) copy-start(bf16[192,1024]{1,0:T(8,128)(2,1)S(1)} %collective-permute-done.6) | copy-start | bytes 1179652
  52.2 15.1 %collective-permute-start.10 = (bf16[192,1024]{1,0:T(8,128)(2,1)S(1)}, bf16[192,1024]{1,0:T(8,128)(2,1)S(1)}, u32[]{:S(2)}, u32[]{:S(2)}) collective-permute-start(bf16[192,1024]{1,0:T(8,128)(2,1)S(1)} %collective-permute-done.6), channel_id=1, source_target_pairs={{0,8},{8,16},{16,24},{24,32},{32,40},{40,48},{48,56},{56,0},{1,9},... | collective-permute-start | bytes 1179656 | tf_op jit(solution)/shard_map/ppermute | solution.py:75
  55.6 11.9 %collective-permute-start.11 = (bf16[192,1024]{1,0:T(8,128)(2,1)S(1)}, bf16[192,1024]{1,0:T(8,128)(2,1)S(1)}, u32[]{:S(2)}, u32[]{:S(2)}) collective-permute-start(bf16[192,1024]{1,0:T(8,128)(2,1)S(1)} %collective-permute-done.7), channel_id=1, source_target_pairs={{0,56},{8,0},{16,8},{24,16},{32,24},{40,32},{48,40},{56,48},{1,57}... | collective-permute-start | bytes 1179656 | tf_op jit(solution)/shard_map/ppermute | solution.py:78
  58.0 8.5 %collective-permute-start.8 = (bf16[128,384]{1,0:T(8,128)(2,1)S(1)}, bf16[128,384]{1,0:T(8,128)(2,1)S(1)}, u32[]{:S(2)}, u32[]{:S(2)}) collective-permute-start(bf16[128,384]{1,0:T(8,128)(2,1)S(1)} %collective-permute-done.4), channel_id=1, source_target_pairs={{0,1},{1,2},{2,3},{3,4},{4,5},{5,6},{6,7},{7,0},{8,9},{9,10},{10,1... | collective-permute-start | bytes 294920 | tf_op jit(solution)/shard_map/ppermute | solution.py:75
  59.9 7.3 %collective-permute-start.9 = (bf16[128,384]{1,0:T(8,128)(2,1)S(1)}, bf16[128,384]{1,0:T(8,128)(2,1)S(1)}, u32[]{:S(2)}, u32[]{:S(2)}) collective-permute-start(bf16[128,384]{1,0:T(8,128)(2,1)S(1)} %collective-permute-done.5), channel_id=1, source_target_pairs={{0,7},{1,0},{2,1},{3,2},{4,3},{5,4},{6,5},{7,6},{8,15},{9,8},{10,9... | collective-permute-start | bytes 294920 | tf_op jit(solution)/shard_map/ppermute | solution.py:78
  67.3 15.1 %copy-start.3 = (bf16[192,1024]{1,0:T(8,128)(2,1)}, bf16[192,1024]{1,0:T(8,128)(2,1)S(1)}, u32[]{:S(2)}) copy-start(bf16[192,1024]{1,0:T(8,128)(2,1)S(1)} %collective-permute-done.10) | copy-start | bytes 1179652
  67.5 12.9 %collective-permute-start.13 = (bf16[192,1024]{1,0:T(8,128)(2,1)S(1)}, bf16[192,1024]{1,0:T(8,128)(2,1)S(1)}, u32[]{:S(2)}, u32[]{:S(2)}) collective-permute-start(bf16[192,1024]{1,0:T(8,128)(2,1)S(1)} %collective-permute-done.10), channel_id=1, source_target_pairs={{0,8},{8,16},{16,24},{24,32},{32,40},{40,48},{48,56},{56,0},{1,9},... | collective-permute-start | bytes 1179656 | tf_op jit(solution)/shard_map/ppermute | solution.py:75
  72.3 8.1 %collective-permute-start.12 = (bf16[128,384]{1,0:T(8,128)(2,1)S(1)}, bf16[128,384]{1,0:T(8,128)(2,1)S(1)}, u32[]{:S(2)}, u32[]{:S(2)}) collective-permute-start(bf16[128,384]{1,0:T(8,128)(2,1)S(1)} %collective-permute-done.8), channel_id=1, source_target_pairs={{0,1},{1,2},{2,3},{3,4},{4,5},{5,6},{6,7},{7,0},{8,9},{9,10},{10,1... | collective-permute-start | bytes 294920 | tf_op jit(solution)/shard_map/ppermute | solution.py:75
  80.4 2.0 copy-start.4
  130.2 14.0 %all-to-all-start = ((bf16[8,192,128]{2,1,0:T(8,128)(2,1)}), bf16[8,192,128]{2,1,0:T(8,128)(2,1)S(1)}, u32[]{:S(2)}, u32[]{:S(2)}) async-start(bf16[8,192,128]{2,1,0:T(8,128)(2,1)} %bitcast.125), calls=%async_computation | async-start | bytes 786432 | tf_op jit(solution)/shard_map/all_to_all | solution.py:114
  140.4 7.2 %copy-start.8 = (f32[1024]{0:T(1024)S(1)}, f32[1024]{0:T(1024)}, u32[]{:S(2)}) copy-start(f32[1024]{0:T(1024)} %param.13) | copy-start | bytes 12292
  144.2 0.7 copy-start.1
  202.9 2.2 copy-start.10
  208.4 8.7 %copy-start.9 = (f32[1,192,2]{1,2,0:T(2,128)S(1)}, f32[1,192,2]{1,2,0:T(2,128)}, u32[]{:S(2)}) copy-start(f32[1,192,2]{1,2,0:T(2,128)} %param.15) | copy-start | bytes 4612
  208.4 59.9 %all-to-all-start.2 = ((bf16[64,12,1024]{2,1,0:T(8,128)(2,1)}), bf16[64,12,1024]{2,1,0:T(8,128)(2,1)}, u32[]{:S(2)}, u32[]{:S(2)}) async-start(bf16[64,12,1024]{2,1,0:T(8,128)(2,1)} %copy.25), calls=%async_computation.2 | async-start | bytes 4194304 | tf_op jit(solution)/shard_map/all_to_all | solution.py:143
Sparse Core Ops, SparseCore 0:
  26.3 82.6 all-gather.2

commit v6 on v5

--- a/solution.py
+++ b/solution.py
@@ -15,22 +15,24 @@
 
 
 def attention_kernel(me_ref, mask_ref, proj_ref, out_ref, *, chunk, chunks, heads, blocks):
-    tile = pl.program_id(0)
+    c = pl.program_id(0)
     me = me_ref[0]
+    start = pl.multiple_of(((c - me + chunks) % chunks) * chunk, TILE)
+    nodes = chunk * chunks
     per_chunk = chunk // TILE
-    ring_chunk = (tile // per_chunk - me + chunks) % chunks
-    start = pl.multiple_of(ring_chunk * chunk + (tile % per_chunk) * TILE, TILE)
-    query_block = (tile * TILE) // BLOCK
-    nodes = chunk * chunks
-    key_tiles = nodes // TILE
+    first = (c * chunk) // BLOCK
+    split_row = (first + 1) * BLOCK - c * chunk
     lane_tile = lax.broadcasted_iota(jnp.int32, (1, nodes), 1) // TILE
-    allowed = jnp.zeros((1, nodes), jnp.int32)
-    for t in range(key_tiles):
+    lanes_a = jnp.zeros((1, nodes), jnp.int32)
+    lanes_b = jnp.zeros((1, nodes), jnp.int32)
+    for t in range(nodes // TILE):
         node = ((me + t // per_chunk) % chunks) * chunk + (t % per_chunk) * TILE
-        bit = mask_ref[query_block * blocks + node // BLOCK]
-        allowed = jnp.where(lane_tile == t, bit, allowed)
-    allowed = allowed > 0
-    rows = proj_ref[pl.ds(start, TILE), :]
+        lanes_a = jnp.where(lane_tile == t, mask_ref[first * blocks + node // BLOCK], lanes_a)
+        second = jnp.minimum(first + 1, blocks - 1)
+        lanes_b = jnp.where(lane_tile == t, mask_ref[second * blocks + node // BLOCK], lanes_b)
+    row = lax.broadcasted_iota(jnp.int32, (chunk, 1), 0)
+    allowed = jnp.where(row < split_row, lanes_a, lanes_b) > 0
+    rows = proj_ref[pl.ds(start, chunk), :]
     scale = 1.0 / math.sqrt(HEAD_DIM)
     for h in range(heads):
         base = h * 3 * HEAD_DIM
@@ -41,7 +43,8 @@
         scores = jnp.where(allowed, scores, -1e30)
         top = jnp.max(scores, axis=-1, keepdims=True)
         weights = jnp.exp(scores - top)
-        probs = (weights / jnp.sum(weights, axis=-1, keepdims=True)).astype(jnp.bfloat16)
+        inverse = 1.0 / jnp.sum(weights, axis=-1, keepdims=True)
+        probs = (weights * inverse).astype(jnp.bfloat16)
         out = jnp.dot(probs, v, preferred_element_type=jnp.float32)
         out_ref[:, h * HEAD_DIM:(h + 1) * HEAD_DIM] = out.astype(out_ref.dtype)
 
@@ -56,9 +59,9 @@
         out_shape=jax.ShapeDtypeStruct((nodes, heads * HEAD_DIM), jnp.bfloat16),
         grid_spec=pltpu.PrefetchScalarGridSpec(
             num_scalar_prefetch=2,
-            grid=(nodes // TILE,),
-            in_specs=[pl.BlockSpec((nodes, cols), lambda t, me, mask: (0, 0))],
-            out_specs=pl.BlockSpec((TILE, heads * HEAD_DIM), lambda t, me, mask: (t, 0)),
+            grid=(chunks,),
+            in_specs=[pl.BlockSpec((nodes, cols), lambda c, me, mask: (0, 0))],
+            out_specs=pl.BlockSpec((chunk, heads * HEAD_DIM), lambda c, me, mask: (c, 0)),
         ),
     )(me.reshape(1), mask.reshape(-1), projected)
 

time: 281 us -> 265 us (0.943)
  the two profiles are of different devices: /device:TPU:26 before, /device:TPU:24 now
where the time goes in v6:
time: 265 us; the launch traced here: 264 us
  starting transfers between devices  69.2 us (26%)
  waiting for transfers between devices  61.3 us (23%)
  blocking collectives  53.8 us (20%)
  local copies, waits for them, and re-layouts  29.7 us (11%)
  Pallas kernels  18.2 us (7%)
  matrix products  15.1 us (6%)
  between operations  13.8 us (5%)
  other arithmetic  3.19 us (1%)
    all_to_all x1, blocking collectives, per_device(): lax.all_to_all(outgoing, ('seq', 'exp'), split_axis=0, concat_axis=0, til...  53.8 us
    all_to_all x1, waiting for transfers between devices, per_device(): lax.all_to_all(processed, ('seq', 'exp'), split_axis=0, concat_axis=0, ti...  51.9 us
    ppermute x8, starting transfers between devices, ring_gather(): moving[which][0] = lax.ppermute(moving[which][0], axis, right)  30.2 us
    ppermute x6, starting transfers between devices, ring_gather(): moving[which][1] = lax.ppermute(moving[which][1], axis, left)  25.3 us
    pallas_call x1, Pallas kernels, attention(): pl.pallas_call(kernel, out_shape=jax.ShapeDtypeStruct((nodes, heads * HEA...  18.2 us
    unnamed x37, local copies, waits for them, and re-layouts  18 us
    all_to_all x1, starting transfers between devices, per_device(): lax.all_to_all(processed, ('seq', 'exp'), split_axis=0, concat_axis=0, ti...  8.32 us
    all_to_all x1, starting transfers between devices, per_device(): lax.all_to_all(attended, 'seq', split_axis=0, concat_axis=1, tiled=True)  5.38 us
  transfers between devices with their start and end apart: 17, of which 7 were waited for; matrix products, arithmetic and copies ran while one was open for 12% of the time, Pallas kernels for 7%

profile of v6, /device:TPU:24, one launch (start us, length us, event | category | flops | bytes accessed | tf_op | source)
XLA Modules:
  0.0 264.1 jit_solution(1402706368635870840)
XLA Ops:
  6.5 4.8 %collective-permute-start.2 = (bf16[192,1024]{1,0:T(8,128)(2,1)}, bf16[192,1024]{1,0:T(8,128)(2,1)S(1)}, u32[]{:S(2)}, u32[]{:S(2)}) collective-permute-start(bf16[192,1024]{1,0:T(8,128)(2,1)} %bitcast.126), channel_id=1, source_target_pairs={{0,8},{8,16},{16,24},{24,32},{32,40},{40,48},{48,56},{56,0},{1,9},... | collective-permute-start | bytes 1179656 | tf_op jit(solution)/shard_map/ppermute | solution.py:78
  11.4 1.9 collective-permute-start.3
  13.3 4.3 %collective-permute-start = (bf16[128,384]{1,0:T(8,128)(2,1)}, bf16[128,384]{1,0:T(8,128)(2,1)S(1)}, u32[]{:S(2)}, u32[]{:S(2)}) collective-permute-start(bf16[128,384]{1,0:T(8,128)(2,1)} %param.11), channel_id=1, source_target_pairs={{0,1},{1,2},{2,3},{3,4},{4,5},{5,6},{6,7},{7,0},{8,9},{9,10},{10,1... | collective-permute-start | bytes 294920 | tf_op jit(solution)/shard_map/ppermute | solution.py:78
  17.6 8.6 %collective-permute-start.1 = (bf16[128,384]{1,0:T(8,128)(2,1)}, bf16[128,384]{1,0:T(8,128)(2,1)S(1)}, u32[]{:S(2)}, u32[]{:S(2)}) collective-permute-start(bf16[128,384]{1,0:T(8,128)(2,1)} %param.11), channel_id=1, source_target_pairs={{0,7},{1,0},{2,1},{3,2},{4,3},{5,4},{6,5},{7,6},{8,15},{9,8},{10,9... | collective-permute-start | bytes 294920 | tf_op jit(solution)/shard_map/ppermute | solution.py:81
  26.2 1.8 constant_dynamic-update-slice_fusion
  33.6 5.1 %collective-permute-start.6 = (bf16[192,1024]{1,0:T(8,128)(2,1)S(1)}, bf16[192,1024]{1,0:T(8,128)(2,1)S(1)}, u32[]{:S(2)}, u32[]{:S(2)}) collective-permute-start(bf16[192,1024]{1,0:T(8,128)(2,1)S(1)} %collective-permute-done.2), channel_id=1, source_target_pairs={{0,8},{8,16},{16,24},{24,32},{32,40},{40,48},{48,56},{56,0},{1,9},... | collective-permute-start | bytes 1179656 | tf_op jit(solution)/shard_map/ppermute | solution.py:78
  38.8 2.1 collective-permute-start.7
  40.8 1.9 collective-permute-start.4
  42.8 5.1 %collective-permute-start.5 = (bf16[128,384]{1,0:T(8,128)(2,1)}, bf16[128,384]{1,0:T(8,128)(2,1)S(1)}, u32[]{:S(2)}, u32[]{:S(2)}) collective-permute-start(bf16[128,384]{1,0:T(8,128)(2,1)} %copy-done.7), channel_id=1, source_target_pairs={{0,7},{1,0},{2,1},{3,2},{4,3},{5,4},{6,5},{7,6},{8,15},{9,8},{10,9... | collective-permute-start | bytes 294920 | tf_op jit(solution)/shard_map/ppermute | solution.py:81
  52.2 3.4 %collective-permute-start.10 = (bf16[192,1024]{1,0:T(8,128)(2,1)S(1)}, bf16[192,1024]{1,0:T(8,128)(2,1)S(1)}, u32[]{:S(2)}, u32[]{:S(2)}) collective-permute-start(bf16[192,1024]{1,0:T(8,128)(2,1)S(1)} %collective-permute-done.6), channel_id=1, source_target_pairs={{0,8},{8,16},{16,24},{24,32},{32,40},{40,48},{48,56},{56,0},{1,9},... | collective-permute-start | bytes 1179656 | tf_op jit(solution)/shard_map/ppermute | solution.py:78
  55.6 2.4 collective-permute-start.11
  58.0 1.9 collective-permute-start.8
  59.9 5.1 %collective-permute-start.9 = (bf16[128,384]{1,0:T(8,128)(2,1)S(1)}, bf16[128,384]{1,0:T(8,128)(2,1)S(1)}, u32[]{:S(2)}, u32[]{:S(2)}) collective-permute-start(bf16[128,384]{1,0:T(8,128)(2,1)S(1)} %collective-permute-done.5), channel_id=1, source_target_pairs={{0,7},{1,0},{2,1},{3,2},{4,3},{5,4},{6,5},{7,6},{8,15},{9,8},{10,9... | collective-permute-start | bytes 294920 | tf_op jit(solution)/shard_map/ppermute | solution.py:81
  67.5 4.8 %collective-permute-start.13 = (bf16[192,1024]{1,0:T(8,128)(2,1)S(1)}, bf16[192,1024]{1,0:T(8,128)(2,1)S(1)}, u32[]{:S(2)}, u32[]{:S(2)}) collective-permute-start(bf16[192,1024]{1,0:T(8,128)(2,1)S(1)} %collective-permute-done.10), channel_id=1, source_target_pairs={{0,8},{8,16},{16,24},{24,32},{32,40},{40,48},{48,56},{56,0},{1,9},... | collective-permute-start | bytes 1179656 | tf_op jit(solution)/shard_map/ppermute | solution.py:78
  72.3 4.0 %collective-permute-start.12 = (bf16[128,384]{1,0:T(8,128)(2,1)S(1)}, bf16[128,384]{1,0:T(8,128)(2,1)S(1)}, u32[]{:S(2)}, u32[]{:S(2)}) collective-permute-start(bf16[128,384]{1,0:T(8,128)(2,1)S(1)} %collective-permute-done.8), channel_id=1, source_target_pairs={{0,1},{1,2},{2,3},{3,4},{4,5},{5,6},{6,7},{7,0},{8,9},{9,10},{10,1... | collective-permute-start | bytes 294920 | tf_op jit(solution)/shard_map/ppermute | solution.py:78
  77.7 2.7 %collective-permute-done.12 = bf16[128,384]{1,0:T(8,128)(2,1)S(1)} collective-permute-done((bf16[128,384]{1,0:T(8,128)(2,1)S(1)}, bf16[128,384]{1,0:T(8,128)(2,1)S(1)}, u32[]{:S(2)}, u32[]{:S(2)}) %collective-permute-start.12) | collective-permute-done | bytes 98336 | tf_op jit(solution)/shard_map/ppermute | solution.py:78
  83.0 1.8 gather_fusion
  84.9 1.8 bitcast_dynamic-update-slice_fusion.3
  86.7 1.8 bitcast_dynamic-update-slice_fusion.2
  88.4 1.8 bitcast_dynamic-update-slice_fusion.1
  91.1 4.8 %convolution_convert_fusion.proj_ref = bf16[1536,384]{1,0:T(8,128)(2,1)} fusion(bf16[1536,1024]{1,0:T(8,128)(2,1)} %bitcast.129, bf16[1024,384]{1,0:T(8,128)(2,1)S(1)} %bitcast.128), kind=kOutput, calls=%fused_computation.1 | convolution fusion | flops 1208549376 | bytes 5111808 | tf_op jit(solution)/shard_map/dot_general | solution.py:112
  95.9 18.2 %shard_map.91 = bf16[1536,128]{1,0:T(8,128)(2,1)} custom-call(s32[1]{0:T(128)} %bitcast.1.me_ref, s32[144]{0:T(256)} %reshape_squeeze.4.mask_ref, bf16[1536,384]{1,0:T(8,128)(2,1)} %convolution_convert_fusion.proj_ref), custom_call_target="tpu_custom_call" | custom-call | tf_op jit(solution)/shard_map/pallas_call | solution.py:57
  114.1 5.4 %all-to-all-start = ((bf16[8,192,128]{2,1,0:T(8,128)(2,1)}), bf16[8,192,128]{2,1,0:T(8,128)(2,1)S(1)}, u32[]{:S(2)}, u32[]{:S(2)}) async-start(bf16[8,192,128]{2,1,0:T(8,128)(2,1)} %bitcast.125), calls=%async_computation | async-start | bytes 786432 | tf_op jit(solution)/shard_map/all_to_all | solution.py:117
  120.4 3.9 %copy.17 = bf16[8,8,128,128]{2,3,1,0:T(8,128)(2,1)} copy(bf16[8,8,128,128]{3,2,1,0:T(8,128)(2,1)} %bitcast.124) | data formatting | bytes 4194304 | tf_op jit(solution)/shard_map/reshape | solution.py:118
  124.3 3.8 %all-to-all-done = bf16[8,192,128]{2,1,0:T(8,128)(2,1)S(1)} async-done(((bf16[8,192,128]{2,1,0:T(8,128)(2,1)}), bf16[8,192,128]{2,1,0:T(8,128)(2,1)S(1)}, u32[]{:S(2)}, u32[]{:S(2)}) %all-to-all-start) | async-done | bytes 393248 | tf_op jit(solution)/shard_map/all_to_all | solution.py:117
  128.8 2.7 %multiply_reduce_fusion = (f32[192]{0:T(256)S(1)}, f32[192,1024]{1,0:T(8,128)S(1)}) fusion(bf16[1024,128,8]{1,0,2:T(8,128)(2,1)} %bitcast.123, bf16[8,192,128]{2,1,0:T(8,128)(2,1)} %copy-done.1, bf16[1,192,1024]{2,1,0:T(8,128)(2,1)} %param.9), kind=kOutput, calls=%fused_computation.28 | convolution fusion | flops 403439424 | bytes 3670784 | tf_op jit(solution)/shard_map/nsk,sekc->nec/dot_general | solution.py:119
  133.1 53.8 %all_to_all.26 = bf16[64,12,1024]{2,1,0:T(8,128)(2,1)S(1)} all-to-all(bf16[64,12,1024]{2,1,0:T(8,128)(2,1)S(1)} %copy.23), channel_id=1, replica_groups=mesh['sub'=8,'seq'=8,'exp'=8] {'seq','exp'}, dimensions={0} | all-to-all | bytes 3145728 | tf_op jit(solution)/shard_map/all_to_all | solution.py:140
  186.8 2.2 fusion
  190.1 2.2 copy.25
  192.3 8.3 %all-to-all-start.2 = ((bf16[64,12,1024]{2,1,0:T(8,128)(2,1)}), bf16[64,12,1024]{2,1,0:T(8,128)(2,1)}, u32[]{:S(2)}, u32[]{:S(2)}) async-start(bf16[64,12,1024]{2,1,0:T(8,128)(2,1)} %copy.25), calls=%async_computation.2 | async-start | bytes 4194304 | tf_op jit(solution)/shard_map/all_to_all | solution.py:146
  200.6 51.9 %all-to-all-done.2 = bf16[64,12,1024]{2,1,0:T(8,128)(2,1)} async-done(((bf16[64,12,1024]{2,1,0:T(8,128)(2,1)}), bf16[64,12,1024]{2,1,0:T(8,128)(2,1)}, u32[]{:S(2)}, u32[]{:S(2)}) %all-to-all-start.2) | async-done | bytes 1572896 | tf_op jit(solution)/shard_map/all_to_all | solution.py:146
  252.5 3.8 %fusion.8 = f32[2,192,1024]{2,1,0:T(8,128)S(1)} fusion(bf16[64,12,1024]{2,1,0:T(8,128)(2,1)} %all-to-all-done.2, s32[192,2]{0,1:T(2,128)S(1)} %copy.22, s32[64,12]{0,1:T(8,128)S(1)} %multiply_add_fusion), kind=kOutput, calls=%fused_computation.14 | convolution fusion | flops 604274688 | bytes 3150336 | tf_op jit(solution)/shard_map/ecnk,ecd->knd/dot_general | solution.py:147
  (75 shorter events, 22.4 us)
Async XLA Ops:
  6.5 180.3 %copy-start = (bf16[1,1024,1024]{2,1,0:T(8,128)(2,1)S(1)}, bf16[1,1024,1024]{2,1,0:T(8,128)(2,1)}, u32[]{:S(2)}) copy-start(bf16[1,1024,1024]{2,1,0:T(8,128)(2,1)} %param.16) | copy-start | bytes 6291460
  6.5 113.8 %all-gather.3.cloned.1.call-start = ((), (), s32[]{:S(2)}) async-start(), calls=%async_computation.3 | async-start | bytes 2129920 | tf_op jit(solution)/shard_map/all_gather | solution.py:107
  6.5 26.5 %collective-permute-start.2 = (bf16[192,1024]{1,0:T(8,128)(2,1)}, bf16[192,1024]{1,0:T(8,128)(2,1)S(1)}, u32[]{:S(2)}, u32[]{:S(2)}) collective-permute-start(bf16[192,1024]{1,0:T(8,128)(2,1)} %bitcast.126), channel_id=1, source_target_pairs={{0,8},{8,16},{16,24},{24,32},{32,40},{40,48},{48,56},{56,0},{1,9},... | collective-permute-start | bytes 1179656 | tf_op jit(solution)/shard_map/ppermute | solution.py:78
  11.4 21.7 %collective-permute-start.3 = (bf16[192,1024]{1,0:T(8,128)(2,1)}, bf16[192,1024]{1,0:T(8,128)(2,1)S(1)}, u32[]{:S(2)}, u32[]{:S(2)}) collective-permute-start(bf16[192,1024]{1,0:T(8,128)(2,1)} %bitcast.127), channel_id=1, source_target_pairs={{0,56},{8,0},{16,8},{24,16},{32,24},{40,32},{48,40},{56,48},{1,57}... | collective-permute-start | bytes 1179656 | tf_op jit(solution)/shard_map/ppermute | solution.py:81
  13.3 19.7 %collective-permute-start = (bf16[128,384]{1,0:T(8,128)(2,1)}, bf16[128,384]{1,0:T(8,128)(2,1)S(1)}, u32[]{:S(2)}, u32[]{:S(2)}) collective-permute-start(bf16[128,384]{1,0:T(8,128)(2,1)} %param.11), channel_id=1, source_target_pairs={{0,1},{1,2},{2,3},{3,4},{4,5},{5,6},{6,7},{7,0},{8,9},{9,10},{10,1... | collective-permute-start | bytes 294920 | tf_op jit(solution)/shard_map/ppermute | solution.py:78
  17.6 15.4 %collective-permute-start.1 = (bf16[128,384]{1,0:T(8,128)(2,1)}, bf16[128,384]{1,0:T(8,128)(2,1)S(1)}, u32[]{:S(2)}, u32[]{:S(2)}) collective-permute-start(bf16[128,384]{1,0:T(8,128)(2,1)} %param.11), channel_id=1, source_target_pairs={{0,7},{1,0},{2,1},{3,2},{4,3},{5,4},{6,5},{7,6},{8,15},{9,8},{10,9... | collective-permute-start | bytes 294920 | tf_op jit(solution)/shard_map/ppermute | solution.py:81
  33.0 0.6 copy-start.5
  33.0 0.7 copy-start.7
  33.6 16.8 %collective-permute-start.6 = (bf16[192,1024]{1,0:T(8,128)(2,1)S(1)}, bf16[192,1024]{1,0:T(8,128)(2,1)S(1)}, u32[]{:S(2)}, u32[]{:S(2)}) collective-permute-start(bf16[192,1024]{1,0:T(8,128)(2,1)S(1)} %collective-permute-done.2), channel_id=1, source_target_pairs={{0,8},{8,16},{16,24},{24,32},{32,40},{40,48},{48,56},{56,0},{1,9},... | collective-permute-start | bytes 1179656 | tf_op jit(solution)/shard_map/ppermute | solution.py:78
  38.8 43.6 %copy-start.6 = (bf16[128,384]{1,0:T(8,128)(2,1)S(1)}, bf16[128,384]{1,0:T(8,128)(2,1)}, u32[]{:S(2)}) copy-start(bf16[128,384]{1,0:T(8,128)(2,1)} %copy-done.5) | copy-start | bytes 294916
  38.8 13.4 %collective-permute-start.7 = (bf16[192,1024]{1,0:T(8,128)(2,1)S(1)}, bf16[192,1024]{1,0:T(8,128)(2,1)S(1)}, u32[]{:S(2)}, u32[]{:S(2)}) collective-permute-start(bf16[192,1024]{1,0:T(8,128)(2,1)S(1)} %collective-permute-done.3), channel_id=1, source_target_pairs={{0,56},{8,0},{16,8},{24,16},{32,24},{40,32},{48,40},{56,48},{1,57}... | collective-permute-start | bytes 1179656 | tf_op jit(solution)/shard_map/ppermute | solution.py:81
  40.8 9.4 %collective-permute-start.4 = (bf16[128,384]{1,0:T(8,128)(2,1)}, bf16[128,384]{1,0:T(8,128)(2,1)S(1)}, u32[]{:S(2)}, u32[]{:S(2)}) collective-permute-start(bf16[128,384]{1,0:T(8,128)(2,1)} %copy-done.5), channel_id=1, source_target_pairs={{0,1},{1,2},{2,3},{3,4},{4,5},{5,6},{6,7},{7,0},{8,9},{9,10},{10,1... | collective-permute-start | bytes 294920 | tf_op jit(solution)/shard_map/ppermute | solution.py:78
  42.8 7.6 %collective-permute-start.5 = (bf16[128,384]{1,0:T(8,128)(2,1)}, bf16[128,384]{1,0:T(8,128)(2,1)S(1)}, u32[]{:S(2)}, u32[]{:S(2)}) collective-permute-start(bf16[128,384]{1,0:T(8,128)(2,1)} %copy-done.7), channel_id=1, source_target_pairs={{0,7},{1,0},{2,1},{3,2},{4,3},{5,4},{6,5},{7,6},{8,15},{9,8},{10,9... | collective-permute-start | bytes 294920 | tf_op jit(solution)/shard_map/ppermute | solution.py:81
  50.4 31.9 %copy-start.2 = (bf16[192,1024]{1,0:T(8,128)(2,1)}, bf16[192,1024]{1,0:T(8,128)(2,1)S(1)}, u32[]{:S(2)}) copy-start(bf16[192,1024]{1,0:T(8,128)(2,1)S(1)} %collective-permute-done.6) | copy-start | bytes 1179652
  52.2 15.1 %collective-permute-start.10 = (bf16[192,1024]{1,0:T(8,128)(2,1)S(1)}, bf16[192,1024]{1,0:T(8,128)(2,1)S(1)}, u32[]{:S(2)}, u32[]{:S(2)}) collective-permute-start(bf16[192,1024]{1,0:T(8,128)(2,1)S(1)} %collective-permute-done.6), channel_id=1, source_target_pairs={{0,8},{8,16},{16,24},{24,32},{32,40},{40,48},{48,56},{56,0},{1,9},... | collective-permute-start | bytes 1179656 | tf_op jit(solution)/shard_map/ppermute | solution.py:78
  55.6 11.9 %collective-permute-start.11 = (bf16[192,1024]{1,0:T(8,128)(2,1)S(1)}, bf16[192,1024]{1,0:T(8,128)(2,1)S(1)}, u32[]{:S(2)}, u32[]{:S(2)}) collective-permute-start(bf16[192,1024]{1,0:T(8,128)(2,1)S(1)} %collective-permute-done.7), channel_id=1, source_target_pairs={{0,56},{8,0},{16,8},{24,16},{32,24},{40,32},{48,40},{56,48},{1,57}... | collective-permute-start | bytes 1179656 | tf_op jit(solution)/shard_map/ppermute | solution.py:81
  58.0 8.5 %collective-permute-start.8 = (bf16[128,384]{1,0:T(8,128)(2,1)S(1)}, bf16[128,384]{1,0:T(8,128)(2,1)S(1)}, u32[]{:S(2)}, u32[]{:S(2)}) collective-permute-start(bf16[128,384]{1,0:T(8,128)(2,1)S(1)} %collective-permute-done.4), channel_id=1, source_target_pairs={{0,1},{1,2},{2,3},{3,4},{4,5},{5,6},{6,7},{7,0},{8,9},{9,10},{10,1... | collective-permute-start | bytes 294920 | tf_op jit(solution)/shard_map/ppermute | solution.py:78
  59.9 7.3 %collective-permute-start.9 = (bf16[128,384]{1,0:T(8,128)(2,1)S(1)}, bf16[128,384]{1,0:T(8,128)(2,1)S(1)}, u32[]{:S(2)}, u32[]{:S(2)}) collective-permute-start(bf16[128,384]{1,0:T(8,128)(2,1)S(1)} %collective-permute-done.5), channel_id=1, source_target_pairs={{0,7},{1,0},{2,1},{3,2},{4,3},{5,4},{6,5},{7,6},{8,15},{9,8},{10,9... | collective-permute-start | bytes 294920 | tf_op jit(solution)/shard_map/ppermute | solution.py:81
  67.3 15.1 %copy-start.3 = (bf16[192,1024]{1,0:T(8,128)(2,1)}, bf16[192,1024]{1,0:T(8,128)(2,1)S(1)}, u32[]{:S(2)}) copy-start(bf16[192,1024]{1,0:T(8,128)(2,1)S(1)} %collective-permute-done.10) | copy-start | bytes 1179652
  67.5 12.9 %collective-permute-start.13 = (bf16[192,1024]{1,0:T(8,128)(2,1)S(1)}, bf16[192,1024]{1,0:T(8,128)(2,1)S(1)}, u32[]{:S(2)}, u32[]{:S(2)}) collective-permute-start(bf16[192,1024]{1,0:T(8,128)(2,1)S(1)} %collective-permute-done.10), channel_id=1, source_target_pairs={{0,8},{8,16},{16,24},{24,32},{32,40},{40,48},{48,56},{56,0},{1,9},... | collective-permute-start | bytes 1179656 | tf_op jit(solution)/shard_map/ppermute | solution.py:78
  72.3 8.1 %collective-permute-start.12 = (bf16[128,384]{1,0:T(8,128)(2,1)S(1)}, bf16[128,384]{1,0:T(8,128)(2,1)S(1)}, u32[]{:S(2)}, u32[]{:S(2)}) collective-permute-start(bf16[128,384]{1,0:T(8,128)(2,1)S(1)} %collective-permute-done.8), channel_id=1, source_target_pairs={{0,1},{1,2},{2,3},{3,4},{4,5},{5,6},{6,7},{7,0},{8,9},{9,10},{10,1... | collective-permute-start | bytes 294920 | tf_op jit(solution)/shard_map/ppermute | solution.py:78
  80.4 2.0 copy-start.4
  114.1 14.0 %all-to-all-start = ((bf16[8,192,128]{2,1,0:T(8,128)(2,1)}), bf16[8,192,128]{2,1,0:T(8,128)(2,1)S(1)}, u32[]{:S(2)}, u32[]{:S(2)}) async-start(bf16[8,192,128]{2,1,0:T(8,128)(2,1)} %bitcast.125), calls=%async_computation | async-start | bytes 786432 | tf_op jit(solution)/shard_map/all_to_all | solution.py:117
  124.3 7.2 %copy-start.8 = (f32[1024]{0:T(1024)S(1)}, f32[1024]{0:T(1024)}, u32[]{:S(2)}) copy-start(f32[1024]{0:T(1024)} %param.13) | copy-start | bytes 12292
  128.1 0.7 copy-start.1
  186.8 2.2 copy-start.10
  192.3 8.3 %copy-start.9 = (f32[1,192,2]{1,2,0:T(2,128)S(1)}, f32[1,192,2]{1,2,0:T(2,128)}, u32[]{:S(2)}) copy-start(f32[1,192,2]{1,2,0:T(2,128)} %param.15) | copy-start | bytes 4612
  192.3 60.3 %all-to-all-start.2 = ((bf16[64,12,1024]{2,1,0:T(8,128)(2,1)}), bf16[64,12,1024]{2,1,0:T(8,128)(2,1)}, u32[]{:S(2)}, u32[]{:S(2)}) async-start(bf16[64,12,1024]{2,1,0:T(8,128)(2,1)} %copy.25), calls=%async_computation.2 | async-start | bytes 4194304 | tf_op jit(solution)/shard_map/all_to_all | solution.py:146
Sparse Core Ops, SparseCore 0:
  26.3 82.6 all-gather.2

commit v7 on v6

--- a/solution.py
+++ b/solution.py
@@ -14,7 +14,7 @@
 TILE = 64
 
 
-def attention_kernel(me_ref, mask_ref, proj_ref, out_ref, *, chunk, chunks, heads, blocks):
+def attention_kernel(me_ref, mask_ref, proj_ref, out_ref, keys_t, *, chunk, chunks, heads, blocks):
     c = pl.program_id(0)
     me = me_ref[0]
     start = pl.multiple_of(((c - me + chunks) % chunks) * chunk, TILE)
@@ -34,12 +34,18 @@
     allowed = jnp.where(row < split_row, lanes_a, lanes_b) > 0
     rows = proj_ref[pl.ds(start, chunk), :]
     scale = 1.0 / math.sqrt(HEAD_DIM)
+
+    @pl.when(c == 0)
+    def _():
+        for h in range(heads):
+            base = h * 3 * HEAD_DIM
+            keys_t[h] = proj_ref[:, base + HEAD_DIM:base + 2 * HEAD_DIM].T
+
     for h in range(heads):
         base = h * 3 * HEAD_DIM
         q = rows[:, base:base + HEAD_DIM]
-        k = proj_ref[:, base + HEAD_DIM:base + 2 * HEAD_DIM]
         v = proj_ref[:, base + 2 * HEAD_DIM:base + 3 * HEAD_DIM]
-        scores = lax.dot_general(q, k, (((1,), (1,)), ((), ())), preferred_element_type=jnp.float32) * scale
+        scores = jnp.dot(q, keys_t[h], preferred_element_type=jnp.float32) * scale
         scores = jnp.where(allowed, scores, -1e30)
         top = jnp.max(scores, axis=-1, keepdims=True)
         weights = jnp.exp(scores - top)
@@ -62,6 +68,7 @@
             grid=(chunks,),
             in_specs=[pl.BlockSpec((nodes, cols), lambda c, me, mask: (0, 0))],
             out_specs=pl.BlockSpec((chunk, heads * HEAD_DIM), lambda c, me, mask: (c, 0)),
+            scratch_shapes=[pltpu.VMEM((heads, HEAD_DIM, nodes), jnp.bfloat16)],
         ),
     )(me.reshape(1), mask.reshape(-1), projected)
 

time: 265 us -> 266 us (level)
  no operation moved by 1% of the time
where the time goes in v7:
time: 266 us; the launch traced here: 265 us
  starting transfers between devices  69.4 us (26%)
  waiting for transfers between devices  60.7 us (23%)
  blocking collectives  53.8 us (20%)
  local copies, waits for them, and re-layouts  29.7 us (11%)
  Pallas kernels  19.1 us (7%)
  matrix products  15 us (6%)
  between operations  13.8 us (5%)
  other arithmetic  3.19 us (1%)
    all_to_all x1, blocking collectives, per_device(): lax.all_to_all(outgoing, ('seq', 'exp'), split_axis=0, concat_axis=0, til...  53.8 us
    all_to_all x1, waiting for transfers between devices, per_device(): lax.all_to_all(processed, ('seq', 'exp'), split_axis=0, concat_axis=0, ti...  51.3 us
    ppermute x8, starting transfers between devices, ring_gather(): moving[which][0] = lax.ppermute(moving[which][0], axis, right)  30.2 us
    ppermute x6, starting transfers between devices, ring_gather(): moving[which][1] = lax.ppermute(moving[which][1], axis, left)  25.3 us
    pallas_call x1, Pallas kernels, attention(): pl.pallas_call(kernel, out_shape=jax.ShapeDtypeStruct((nodes, heads * HEA...  19.1 us
    unnamed x37, local copies, waits for them, and re-layouts  18 us
    all_to_all x1, starting transfers between devices, per_device(): lax.all_to_all(processed, ('seq', 'exp'), split_axis=0, concat_axis=0, ti...  8.5 us
    all_to_all x1, starting transfers between devices, per_device(): lax.all_to_all(attended, 'seq', split_axis=0, concat_axis=1, tiled=True)  5.39 us
  transfers between devices with their start and end apart: 17, of which 7 were waited for; matrix products, arithmetic and copies ran while one was open for 12% of the time, Pallas kernels for 7%

profile of v7, /device:TPU:24, one launch (start us, length us, event | category | flops | bytes accessed | tf_op | source)
XLA Modules:
  0.0 264.6 jit_solution(1062024760845093809)
XLA Ops:
  6.5 4.8 %collective-permute-start.2 = (bf16[192,1024]{1,0:T(8,128)(2,1)}, bf16[192,1024]{1,0:T(8,128)(2,1)S(1)}, u32[]{:S(2)}, u32[]{:S(2)}) collective-permute-start(bf16[192,1024]{1,0:T(8,128)(2,1)} %bitcast.126), channel_id=1, source_target_pairs={{0,8},{8,16},{16,24},{24,32},{32,40},{40,48},{48,56},{56,0},{1,9},... | collective-permute-start | bytes 1179656 | tf_op jit(solution)/shard_map/ppermute | solution.py:85
  11.4 1.9 collective-permute-start.3
  13.3 4.3 %collective-permute-start = (bf16[128,384]{1,0:T(8,128)(2,1)}, bf16[128,384]{1,0:T(8,128)(2,1)S(1)}, u32[]{:S(2)}, u32[]{:S(2)}) collective-permute-start(bf16[128,384]{1,0:T(8,128)(2,1)} %param.11), channel_id=1, source_target_pairs={{0,1},{1,2},{2,3},{3,4},{4,5},{5,6},{6,7},{7,0},{8,9},{9,10},{10,1... | collective-permute-start | bytes 294920 | tf_op jit(solution)/shard_map/ppermute | solution.py:85
  17.6 8.6 %collective-permute-start.1 = (bf16[128,384]{1,0:T(8,128)(2,1)}, bf16[128,384]{1,0:T(8,128)(2,1)S(1)}, u32[]{:S(2)}, u32[]{:S(2)}) collective-permute-start(bf16[128,384]{1,0:T(8,128)(2,1)} %param.11), channel_id=1, source_target_pairs={{0,7},{1,0},{2,1},{3,2},{4,3},{5,4},{6,5},{7,6},{8,15},{9,8},{10,9... | collective-permute-start | bytes 294920 | tf_op jit(solution)/shard_map/ppermute | solution.py:88
  26.2 1.8 constant_dynamic-update-slice_fusion
  33.6 5.1 %collective-permute-start.6 = (bf16[192,1024]{1,0:T(8,128)(2,1)S(1)}, bf16[192,1024]{1,0:T(8,128)(2,1)S(1)}, u32[]{:S(2)}, u32[]{:S(2)}) collective-permute-start(bf16[192,1024]{1,0:T(8,128)(2,1)S(1)} %collective-permute-done.2), channel_id=1, source_target_pairs={{0,8},{8,16},{16,24},{24,32},{32,40},{40,48},{48,56},{56,0},{1,9},... | collective-permute-start | bytes 1179656 | tf_op jit(solution)/shard_map/ppermute | solution.py:85
  38.8 2.1 collective-permute-start.7
  40.8 1.9 collective-permute-start.4
  42.8 5.1 %collective-permute-start.5 = (bf16[128,384]{1,0:T(8,128)(2,1)}, bf16[128,384]{1,0:T(8,128)(2,1)S(1)}, u32[]{:S(2)}, u32[]{:S(2)}) collective-permute-start(bf16[128,384]{1,0:T(8,128)(2,1)} %copy-done.7), channel_id=1, source_target_pairs={{0,7},{1,0},{2,1},{3,2},{4,3},{5,4},{6,5},{7,6},{8,15},{9,8},{10,9... | collective-permute-start | bytes 294920 | tf_op jit(solution)/shard_map/ppermute | solution.py:88
  52.2 3.4 %collective-permute-start.10 = (bf16[192,1024]{1,0:T(8,128)(2,1)S(1)}, bf16[192,1024]{1,0:T(8,128)(2,1)S(1)}, u32[]{:S(2)}, u32[]{:S(2)}) collective-permute-start(bf16[192,1024]{1,0:T(8,128)(2,1)S(1)} %collective-permute-done.6), channel_id=1, source_target_pairs={{0,8},{8,16},{16,24},{24,32},{32,40},{40,48},{48,56},{56,0},{1,9},... | collective-permute-start | bytes 1179656 | tf_op jit(solution)/shard_map/ppermute | solution.py:85
  55.6 2.4 collective-permute-start.11
  58.0 1.9 collective-permute-start.8
  59.9 5.1 %collective-permute-start.9 = (bf16[128,384]{1,0:T(8,128)(2,1)S(1)}, bf16[128,384]{1,0:T(8,128)(2,1)S(1)}, u32[]{:S(2)}, u32[]{:S(2)}) collective-permute-start(bf16[128,384]{1,0:T(8,128)(2,1)S(1)} %collective-permute-done.5), channel_id=1, source_target_pairs={{0,7},{1,0},{2,1},{3,2},{4,3},{5,4},{6,5},{7,6},{8,15},{9,8},{10,9... | collective-permute-start | bytes 294920 | tf_op jit(solution)/shard_map/ppermute | solution.py:88
  67.5 4.8 %collective-permute-start.13 = (bf16[192,1024]{1,0:T(8,128)(2,1)S(1)}, bf16[192,1024]{1,0:T(8,128)(2,1)S(1)}, u32[]{:S(2)}, u32[]{:S(2)}) collective-permute-start(bf16[192,1024]{1,0:T(8,128)(2,1)S(1)} %collective-permute-done.10), channel_id=1, source_target_pairs={{0,8},{8,16},{16,24},{24,32},{32,40},{40,48},{48,56},{56,0},{1,9},... | collective-permute-start | bytes 1179656 | tf_op jit(solution)/shard_map/ppermute | solution.py:85
  72.3 4.0 %collective-permute-start.12 = (bf16[128,384]{1,0:T(8,128)(2,1)S(1)}, bf16[128,384]{1,0:T(8,128)(2,1)S(1)}, u32[]{:S(2)}, u32[]{:S(2)}) collective-permute-start(bf16[128,384]{1,0:T(8,128)(2,1)S(1)} %collective-permute-done.8), channel_id=1, source_target_pairs={{0,1},{1,2},{2,3},{3,4},{4,5},{5,6},{6,7},{7,0},{8,9},{9,10},{10,1... | collective-permute-start | bytes 294920 | tf_op jit(solution)/shard_map/ppermute | solution.py:85
  77.7 2.7 %collective-permute-done.12 = bf16[128,384]{1,0:T(8,128)(2,1)S(1)} collective-permute-done((bf16[128,384]{1,0:T(8,128)(2,1)S(1)}, bf16[128,384]{1,0:T(8,128)(2,1)S(1)}, u32[]{:S(2)}, u32[]{:S(2)}) %collective-permute-start.12) | collective-permute-done | bytes 98336 | tf_op jit(solution)/shard_map/ppermute | solution.py:85
  83.0 1.8 gather_fusion
  84.9 1.8 bitcast_dynamic-update-slice_fusion.3
  86.7 1.8 bitcast_dynamic-update-slice_fusion.2
  88.4 1.8 bitcast_dynamic-update-slice_fusion.1
  91.1 4.8 %convolution_convert_fusion.proj_ref = bf16[1536,384]{1,0:T(8,128)(2,1)} fusion(bf16[1536,1024]{1,0:T(8,128)(2,1)} %bitcast.129, bf16[1024,384]{1,0:T(8,128)(2,1)S(1)} %bitcast.128), kind=kOutput, calls=%fused_computation.1 | convolution fusion | flops 1208549376 | bytes 5111808 | tf_op jit(solution)/shard_map/dot_general | solution.py:119
  95.9 19.1 %shard_map.91 = bf16[1536,128]{1,0:T(8,128)(2,1)} custom-call(s32[1]{0:T(128)} %bitcast.1.me_ref, s32[144]{0:T(256)} %reshape_squeeze.4.mask_ref, bf16[1536,384]{1,0:T(8,128)(2,1)} %convolution_convert_fusion.proj_ref), custom_call_target="tpu_custom_call" | custom-call | tf_op jit(solution)/shard_map/pallas_call | solution.py:63
  115.0 5.4 %all-to-all-start = ((bf16[8,192,128]{2,1,0:T(8,128)(2,1)}), bf16[8,192,128]{2,1,0:T(8,128)(2,1)S(1)}, u32[]{:S(2)}, u32[]{:S(2)}) async-start(bf16[8,192,128]{2,1,0:T(8,128)(2,1)} %bitcast.125), calls=%async_computation | async-start | bytes 786432 | tf_op jit(solution)/shard_map/all_to_all | solution.py:124
  121.3 3.9 %copy.17 = bf16[8,8,128,128]{2,3,1,0:T(8,128)(2,1)} copy(bf16[8,8,128,128]{3,2,1,0:T(8,128)(2,1)} %bitcast.124) | data formatting | bytes 4194304 | tf_op jit(solution)/shard_map/reshape | solution.py:125
  125.2 3.8 %all-to-all-done = bf16[8,192,128]{2,1,0:T(8,128)(2,1)S(1)} async-done(((bf16[8,192,128]{2,1,0:T(8,128)(2,1)}), bf16[8,192,128]{2,1,0:T(8,128)(2,1)S(1)}, u32[]{:S(2)}, u32[]{:S(2)}) %all-to-all-start) | async-done | bytes 393248 | tf_op jit(solution)/shard_map/all_to_all | solution.py:124
  129.8 2.7 %multiply_reduce_fusion = (f32[192]{0:T(256)S(1)}, f32[192,1024]{1,0:T(8,128)S(1)}) fusion(bf16[1024,128,8]{1,0,2:T(8,128)(2,1)} %bitcast.123, bf16[8,192,128]{2,1,0:T(8,128)(2,1)} %copy-done.1, bf16[1,192,1024]{2,1,0:T(8,128)(2,1)} %param.9), kind=kOutput, calls=%fused_computation.28 | convolution fusion | flops 403439424 | bytes 3670784 | tf_op jit(solution)/shard_map/nsk,sekc->nec/dot_general | solution.py:126
  134.0 53.8 %all_to_all.26 = bf16[64,12,1024]{2,1,0:T(8,128)(2,1)S(1)} all-to-all(bf16[64,12,1024]{2,1,0:T(8,128)(2,1)S(1)} %copy.23), channel_id=1, replica_groups=mesh['sub'=8,'seq'=8,'exp'=8] {'seq','exp'}, dimensions={0} | all-to-all | bytes 3145728 | tf_op jit(solution)/shard_map/all_to_all | solution.py:147
  187.8 2.2 fusion
  191.0 2.2 copy.25
  193.2 8.5 %all-to-all-start.2 = ((bf16[64,12,1024]{2,1,0:T(8,128)(2,1)}), bf16[64,12,1024]{2,1,0:T(8,128)(2,1)}, u32[]{:S(2)}, u32[]{:S(2)}) async-start(bf16[64,12,1024]{2,1,0:T(8,128)(2,1)} %copy.25), calls=%async_computation.2 | async-start | bytes 4194304 | tf_op jit(solution)/shard_map/all_to_all | solution.py:153
  201.7 51.3 %all-to-all-done.2 = bf16[64,12,1024]{2,1,0:T(8,128)(2,1)} async-done(((bf16[64,12,1024]{2,1,0:T(8,128)(2,1)}), bf16[64,12,1024]{2,1,0:T(8,128)(2,1)}, u32[]{:S(2)}, u32[]{:S(2)}) %all-to-all-start.2) | async-done | bytes 1572896 | tf_op jit(solution)/shard_map/all_to_all | solution.py:153
  253.0 3.8 %fusion.8 = f32[2,192,1024]{2,1,0:T(8,128)S(1)} fusion(bf16[64,12,1024]{2,1,0:T(8,128)(2,1)} %all-to-all-done.2, s32[192,2]{0,1:T(2,128)S(1)} %copy.22, s32[64,12]{0,1:T(8,128)S(1)} %multiply_add_fusion), kind=kOutput, calls=%fused_computation.14 | convolution fusion | flops 604274688 | bytes 3150336 | tf_op jit(solution)/shard_map/ecnk,ecd->knd/dot_general | solution.py:154
  (75 shorter events, 22.4 us)
Async XLA Ops:
  6.5 181.2 %copy-start = (bf16[1,1024,1024]{2,1,0:T(8,128)(2,1)S(1)}, bf16[1,1024,1024]{2,1,0:T(8,128)(2,1)}, u32[]{:S(2)}) copy-start(bf16[1,1024,1024]{2,1,0:T(8,128)(2,1)} %param.16) | copy-start | bytes 6291460
  6.5 114.8 %all-gather.3.cloned.1.call-start = ((), (), s32[]{:S(2)}) async-start(), calls=%async_computation.3 | async-start | bytes 2129920 | tf_op jit(solution)/shard_map/all_gather | solution.py:114
  6.5 26.5 %collective-permute-start.2 = (bf16[192,1024]{1,0:T(8,128)(2,1)}, bf16[192,1024]{1,0:T(8,128)(2,1)S(1)}, u32[]{:S(2)}, u32[]{:S(2)}) collective-permute-start(bf16[192,1024]{1,0:T(8,128)(2,1)} %bitcast.126), channel_id=1, source_target_pairs={{0,8},{8,16},{16,24},{24,32},{32,40},{40,48},{48,56},{56,0},{1,9},... | collective-permute-start | bytes 1179656 | tf_op jit(solution)/shard_map/ppermute | solution.py:85
  11.4 21.7 %collective-permute-start.3 = (bf16[192,1024]{1,0:T(8,128)(2,1)}, bf16[192,1024]{1,0:T(8,128)(2,1)S(1)}, u32[]{:S(2)}, u32[]{:S(2)}) collective-permute-start(bf16[192,1024]{1,0:T(8,128)(2,1)} %bitcast.127), channel_id=1, source_target_pairs={{0,56},{8,0},{16,8},{24,16},{32,24},{40,32},{48,40},{56,48},{1,57}... | collective-permute-start | bytes 1179656 | tf_op jit(solution)/shard_map/ppermute | solution.py:88
  13.3 19.7 %collective-permute-start = (bf16[128,384]{1,0:T(8,128)(2,1)}, bf16[128,384]{1,0:T(8,128)(2,1)S(1)}, u32[]{:S(2)}, u32[]{:S(2)}) collective-permute-start(bf16[128,384]{1,0:T(8,128)(2,1)} %param.11), channel_id=1, source_target_pairs={{0,1},{1,2},{2,3},{3,4},{4,5},{5,6},{6,7},{7,0},{8,9},{9,10},{10,1... | collective-permute-start | bytes 294920 | tf_op jit(solution)/shard_map/ppermute | solution.py:85
  17.6 15.4 %collective-permute-start.1 = (bf16[128,384]{1,0:T(8,128)(2,1)}, bf16[128,384]{1,0:T(8,128)(2,1)S(1)}, u32[]{:S(2)}, u32[]{:S(2)}) collective-permute-start(bf16[128,384]{1,0:T(8,128)(2,1)} %param.11), channel_id=1, source_target_pairs={{0,7},{1,0},{2,1},{3,2},{4,3},{5,4},{6,5},{7,6},{8,15},{9,8},{10,9... | collective-permute-start | bytes 294920 | tf_op jit(solution)/shard_map/ppermute | solution.py:88
  33.0 0.6 copy-start.5
  33.0 0.7 copy-start.7
  33.6 16.8 %collective-permute-start.6 = (bf16[192,1024]{1,0:T(8,128)(2,1)S(1)}, bf16[192,1024]{1,0:T(8,128)(2,1)S(1)}, u32[]{:S(2)}, u32[]{:S(2)}) collective-permute-start(bf16[192,1024]{1,0:T(8,128)(2,1)S(1)} %collective-permute-done.2), channel_id=1, source_target_pairs={{0,8},{8,16},{16,24},{24,32},{32,40},{40,48},{48,56},{56,0},{1,9},... | collective-permute-start | bytes 1179656 | tf_op jit(solution)/shard_map/ppermute | solution.py:85
  38.8 43.6 %copy-start.6 = (bf16[128,384]{1,0:T(8,128)(2,1)S(1)}, bf16[128,384]{1,0:T(8,128)(2,1)}, u32[]{:S(2)}) copy-start(bf16[128,384]{1,0:T(8,128)(2,1)} %copy-done.5) | copy-start | bytes 294916
  38.8 13.4 %collective-permute-start.7 = (bf16[192,1024]{1,0:T(8,128)(2,1)S(1)}, bf16[192,1024]{1,0:T(8,128)(2,1)S(1)}, u32[]{:S(2)}, u32[]{:S(2)}) collective-permute-start(bf16[192,1024]{1,0:T(8,128)(2,1)S(1)} %collective-permute-done.3), channel_id=1, source_target_pairs={{0,56},{8,0},{16,8},{24,16},{32,24},{40,32},{48,40},{56,48},{1,57}... | collective-permute-start | bytes 1179656 | tf_op jit(solution)/shard_map/ppermute | solution.py:88
  40.8 9.4 %collective-permute-start.4 = (bf16[128,384]{1,0:T(8,128)(2,1)}, bf16[128,384]{1,0:T(8,128)(2,1)S(1)}, u32[]{:S(2)}, u32[]{:S(2)}) collective-permute-start(bf16[128,384]{1,0:T(8,128)(2,1)} %copy-done.5), channel_id=1, source_target_pairs={{0,1},{1,2},{2,3},{3,4},{4,5},{5,6},{6,7},{7,0},{8,9},{9,10},{10,1... | collective-permute-start | bytes 294920 | tf_op jit(solution)/shard_map/ppermute | solution.py:85
  42.8 7.6 %collective-permute-start.5 = (bf16[128,384]{1,0:T(8,128)(2,1)}, bf16[128,384]{1,0:T(8,128)(2,1)S(1)}, u32[]{:S(2)}, u32[]{:S(2)}) collective-permute-start(bf16[128,384]{1,0:T(8,128)(2,1)} %copy-done.7), channel_id=1, source_target_pairs={{0,7},{1,0},{2,1},{3,2},{4,3},{5,4},{6,5},{7,6},{8,15},{9,8},{10,9... | collective-permute-start | bytes 294920 | tf_op jit(solution)/shard_map/ppermute | solution.py:88
  50.4 31.9 %copy-start.2 = (bf16[192,1024]{1,0:T(8,128)(2,1)}, bf16[192,1024]{1,0:T(8,128)(2,1)S(1)}, u32[]{:S(2)}) copy-start(bf16[192,1024]{1,0:T(8,128)(2,1)S(1)} %collective-permute-done.6) | copy-start | bytes 1179652
  52.2 15.1 %collective-permute-start.10 = (bf16[192,1024]{1,0:T(8,128)(2,1)S(1)}, bf16[192,1024]{1,0:T(8,128)(2,1)S(1)}, u32[]{:S(2)}, u32[]{:S(2)}) collective-permute-start(bf16[192,1024]{1,0:T(8,128)(2,1)S(1)} %collective-permute-done.6), channel_id=1, source_target_pairs={{0,8},{8,16},{16,24},{24,32},{32,40},{40,48},{48,56},{56,0},{1,9},... | collective-permute-start | bytes 1179656 | tf_op jit(solution)/shard_map/ppermute | solution.py:85
  55.6 11.9 %collective-permute-start.11 = (bf16[192,1024]{1,0:T(8,128)(2,1)S(1)}, bf16[192,1024]{1,0:T(8,128)(2,1)S(1)}, u32[]{:S(2)}, u32[]{:S(2)}) collective-permute-start(bf16[192,1024]{1,0:T(8,128)(2,1)S(1)} %collective-permute-done.7), channel_id=1, source_target_pairs={{0,56},{8,0},{16,8},{24,16},{32,24},{40,32},{48,40},{56,48},{1,57}... | collective-permute-start | bytes 1179656 | tf_op jit(solution)/shard_map/ppermute | solution.py:88
  58.0 8.5 %collective-permute-start.8 = (bf16[128,384]{1,0:T(8,128)(2,1)S(1)}, bf16[128,384]{1,0:T(8,128)(2,1)S(1)}, u32[]{:S(2)}, u32[]{:S(2)}) collective-permute-start(bf16[128,384]{1,0:T(8,128)(2,1)S(1)} %collective-permute-done.4), channel_id=1, source_target_pairs={{0,1},{1,2},{2,3},{3,4},{4,5},{5,6},{6,7},{7,0},{8,9},{9,10},{10,1... | collective-permute-start | bytes 294920 | tf_op jit(solution)/shard_map/ppermute | solution.py:85
  59.9 7.3 %collective-permute-start.9 = (bf16[128,384]{1,0:T(8,128)(2,1)S(1)}, bf16[128,384]{1,0:T(8,128)(2,1)S(1)}, u32[]{:S(2)}, u32[]{:S(2)}) collective-permute-start(bf16[128,384]{1,0:T(8,128)(2,1)S(1)} %collective-permute-done.5), channel_id=1, source_target_pairs={{0,7},{1,0},{2,1},{3,2},{4,3},{5,4},{6,5},{7,6},{8,15},{9,8},{10,9... | collective-permute-start | bytes 294920 | tf_op jit(solution)/shard_map/ppermute | solution.py:88
  67.3 15.1 %copy-start.3 = (bf16[192,1024]{1,0:T(8,128)(2,1)}, bf16[192,1024]{1,0:T(8,128)(2,1)S(1)}, u32[]{:S(2)}) copy-start(bf16[192,1024]{1,0:T(8,128)(2,1)S(1)} %collective-permute-done.10) | copy-start | bytes 1179652
  67.5 12.9 %collective-permute-start.13 = (bf16[192,1024]{1,0:T(8,128)(2,1)S(1)}, bf16[192,1024]{1,0:T(8,128)(2,1)S(1)}, u32[]{:S(2)}, u32[]{:S(2)}) collective-permute-start(bf16[192,1024]{1,0:T(8,128)(2,1)S(1)} %collective-permute-done.10), channel_id=1, source_target_pairs={{0,8},{8,16},{16,24},{24,32},{32,40},{40,48},{48,56},{56,0},{1,9},... | collective-permute-start | bytes 1179656 | tf_op jit(solution)/shard_map/ppermute | solution.py:85
  72.3 8.1 %collective-permute-start.12 = (bf16[128,384]{1,0:T(8,128)(2,1)S(1)}, bf16[128,384]{1,0:T(8,128)(2,1)S(1)}, u32[]{:S(2)}, u32[]{:S(2)}) collective-permute-start(bf16[128,384]{1,0:T(8,128)(2,1)S(1)} %collective-permute-done.8), channel_id=1, source_target_pairs={{0,1},{1,2},{2,3},{3,4},{4,5},{5,6},{6,7},{7,0},{8,9},{9,10},{10,1... | collective-permute-start | bytes 294920 | tf_op jit(solution)/shard_map/ppermute | solution.py:85
  80.4 2.0 copy-start.4
  115.0 14.0 %all-to-all-start = ((bf16[8,192,128]{2,1,0:T(8,128)(2,1)}), bf16[8,192,128]{2,1,0:T(8,128)(2,1)S(1)}, u32[]{:S(2)}, u32[]{:S(2)}) async-start(bf16[8,192,128]{2,1,0:T(8,128)(2,1)} %bitcast.125), calls=%async_computation | async-start | bytes 786432 | tf_op jit(solution)/shard_map/all_to_all | solution.py:124
  125.2 7.2 %copy-start.8 = (f32[1024]{0:T(1024)S(1)}, f32[1024]{0:T(1024)}, u32[]{:S(2)}) copy-start(f32[1024]{0:T(1024)} %param.13) | copy-start | bytes 12292
  129.0 0.7 copy-start.1
  187.8 2.2 copy-start.10
  193.2 8.5 %copy-start.9 = (f32[1,192,2]{1,2,0:T(2,128)S(1)}, f32[1,192,2]{1,2,0:T(2,128)}, u32[]{:S(2)}) copy-start(f32[1,192,2]{1,2,0:T(2,128)} %param.15) | copy-start | bytes 4612
  193.2 59.8 %all-to-all-start.2 = ((bf16[64,12,1024]{2,1,0:T(8,128)(2,1)}), bf16[64,12,1024]{2,1,0:T(8,128)(2,1)}, u32[]{:S(2)}, u32[]{:S(2)}) async-start(bf16[64,12,1024]{2,1,0:T(8,128)(2,1)} %copy.25), calls=%async_computation.2 | async-start | bytes 4194304 | tf_op jit(solution)/shard_map/all_to_all | solution.py:153
Sparse Core Ops, SparseCore 0:
  26.3 82.6 all-gather.2

commit v8 on v6

--- a/solution.py
+++ b/solution.py
@@ -14,32 +14,48 @@
 TILE = 64
 
 
-def attention_kernel(me_ref, mask_ref, proj_ref, out_ref, *, chunk, chunks, heads, blocks):
+def attention_kernel(
+    me_ref, mask_ref, *refs, chunk, chunks, heads, blocks, width, pieces, piece_rows
+):
+    chunk_refs = refs[:chunks]
+    w_ref, out_ref, proj, w_rows, keys_t = refs[chunks:]
     c = pl.program_id(0)
     me = me_ref[0]
+    nodes = chunk * chunks
+
+    @pl.when(c == 0)
+    def _():
+        for b in range(pieces):
+            w_rows[b * piece_rows:(b + 1) * piece_rows, :] = w_ref[(b - me_ref[1] + pieces) % pieces]
+        for j in range(chunks):
+            proj[j * chunk:(j + 1) * chunk, :] = jnp.dot(
+                chunk_refs[j][...], w_rows[...], preferred_element_type=jnp.float32
+            ).astype(proj.dtype)
+        for h in range(heads):
+            base = h * 3 * HEAD_DIM
+            keys_t[h] = proj[:, base + HEAD_DIM:base + 2 * HEAD_DIM].T
+
     start = pl.multiple_of(((c - me + chunks) % chunks) * chunk, TILE)
-    nodes = chunk * chunks
     per_chunk = chunk // TILE
     first = (c * chunk) // BLOCK
     split_row = (first + 1) * BLOCK - c * chunk
     lane_tile = lax.broadcasted_iota(jnp.int32, (1, nodes), 1) // TILE
     lanes_a = jnp.zeros((1, nodes), jnp.int32)
     lanes_b = jnp.zeros((1, nodes), jnp.int32)
+    second = jnp.minimum(first + 1, blocks - 1)
     for t in range(nodes // TILE):
         node = ((me + t // per_chunk) % chunks) * chunk + (t % per_chunk) * TILE
         lanes_a = jnp.where(lane_tile == t, mask_ref[first * blocks + node // BLOCK], lanes_a)
-        second = jnp.minimum(first + 1, blocks - 1)
         lanes_b = jnp.where(lane_tile == t, mask_ref[second * blocks + node // BLOCK], lanes_b)
     row = lax.broadcasted_iota(jnp.int32, (chunk, 1), 0)
     allowed = jnp.where(row < split_row, lanes_a, lanes_b) > 0
-    rows = proj_ref[pl.ds(start, chunk), :]
+    rows = proj[pl.ds(start, chunk), :]
     scale = 1.0 / math.sqrt(HEAD_DIM)
     for h in range(heads):
         base = h * 3 * HEAD_DIM
         q = rows[:, base:base + HEAD_DIM]
-        k = proj_ref[:, base + HEAD_DIM:base + 2 * HEAD_DIM]
-        v = proj_ref[:, base + 2 * HEAD_DIM:base + 3 * HEAD_DIM]
-        scores = lax.dot_general(q, k, (((1,), (1,)), ((), ())), preferred_element_type=jnp.float32) * scale
+        v = proj[:, base + 2 * HEAD_DIM:base + 3 * HEAD_DIM]
+        scores = jnp.dot(q, keys_t[h], preferred_element_type=jnp.float32) * scale
         scores = jnp.where(allowed, scores, -1e30)
         top = jnp.max(scores, axis=-1, keepdims=True)
         weights = jnp.exp(scores - top)
@@ -49,21 +65,34 @@
         out_ref[:, h * HEAD_DIM:(h + 1) * HEAD_DIM] = out.astype(out_ref.dtype)
 
 
-def attention(me, mask, projected, chunk, chunks):
-    nodes, cols = projected.shape
+def attention(me, mask, chunk_list, w_stack):
+    chunks = len(chunk_list)
+    chunk, width = chunk_list[0].shape
+    pieces, piece_rows, cols = w_stack.shape
+    nodes = chunk * chunks
     heads = cols // (3 * HEAD_DIM)
     blocks = mask.shape[-1]
-    kernel = functools.partial(attention_kernel, chunk=chunk, chunks=chunks, heads=heads, blocks=blocks)
+    kernel = functools.partial(
+        attention_kernel, chunk=chunk, chunks=chunks, heads=heads, blocks=blocks, width=width,
+        pieces=pieces, piece_rows=piece_rows,
+    )
+    whole = lambda c, me, mask: (0, 0)
     return pl.pallas_call(
         kernel,
         out_shape=jax.ShapeDtypeStruct((nodes, heads * HEAD_DIM), jnp.bfloat16),
         grid_spec=pltpu.PrefetchScalarGridSpec(
             num_scalar_prefetch=2,
             grid=(chunks,),
-            in_specs=[pl.BlockSpec((nodes, cols), lambda c, me, mask: (0, 0))],
+            in_specs=[pl.BlockSpec((chunk, width), whole)] * chunks
+            + [pl.BlockSpec((pieces, piece_rows, cols), lambda c, me, mask: (0, 0, 0))],
             out_specs=pl.BlockSpec((chunk, heads * HEAD_DIM), lambda c, me, mask: (c, 0)),
+            scratch_shapes=[
+                pltpu.VMEM((nodes, cols), jnp.bfloat16),
+                pltpu.VMEM((pieces * piece_rows, cols), jnp.bfloat16),
+                pltpu.VMEM((heads, HEAD_DIM, nodes), jnp.bfloat16),
+            ],
         ),
-    )(me.reshape(1), mask.reshape(-1), projected)
+    )(me, mask.reshape(-1), *chunk_list, w_stack)
 
 
 def ring_gather(pieces, axes, counts):
@@ -89,12 +118,6 @@
     return relatives
 
 
-def in_order(relative, axis, count):
-    me = lax.axis_index(axis)
-    order = (jnp.arange(count, dtype=jnp.int32) - me) % count
-    return jnp.take(jnp.stack(relative), order, axis=0)
-
-
 def per_device(
     node_features, block_mask, w_qkv, w_out, norm_gain, routes, gates, w_gate_up, w_down
 ):
@@ -106,14 +129,8 @@
     head_cols = w_qkv.shape[1]
     out_all = lax.all_gather(w_out[None], ("seq", "exp"), axis=0, tiled=True)
     col_pieces, chunks = ring_gather((w_qkv, feats), ("exp", "seq"), (exp_count, seq_count))
-    cols_slice = in_order(col_pieces, "exp", exp_count)
-    cols_slice = cols_slice.reshape(exp_count * w_qkv.shape[0], head_cols)
-    gathered = jnp.stack(chunks).reshape(seq_count * node_dev, width)
-    projected = jnp.dot(gathered, cols_slice, preferred_element_type=jnp.float32).astype(
-        jnp.bfloat16
-    )
-    me = lax.axis_index("seq").astype(jnp.int32)
-    attended = attention(me, block_mask[0], projected, node_dev, seq_count)
+    me = jnp.stack([lax.axis_index("seq"), lax.axis_index("exp")]).astype(jnp.int32)
+    attended = attention(me, block_mask[0], chunks, jnp.stack(col_pieces))
     node_attended = lax.all_to_all(attended, "seq", split_axis=0, concat_axis=1, tiled=True)
     out_tiles = out_all.reshape(seq_count, exp_count, w_out.shape[0], w_out.shape[1])
     attn_out = jnp.einsum(

time: 265 us -> 262 us (0.989)
  the two profiles are of different devices: /device:TPU:24 before, /device:TPU:28 now
where the time goes in v8:
time: 262 us; the launch traced here: 261 us
  starting transfers between devices  72.1 us (28%)
  waiting for transfers between devices  69.5 us (27%)
  blocking collectives  53.9 us (21%)
  Pallas kernels  20.3 us (8%)
  local copies, waits for them, and re-layouts  15.6 us (6%)
  between operations  13.7 us (5%)
  matrix products  10.3 us (4%)
  other arithmetic  5.47 us (2%)
    all_to_all x1, waiting for transfers between devices, per_device(): lax.all_to_all(processed, ('seq', 'exp'), split_axis=0, concat_axis=0, ti...  54.4 us
    all_to_all x1, blocking collectives, per_device(): lax.all_to_all(outgoing, ('seq', 'exp'), split_axis=0, concat_axis=0, til...  53.9 us
    ppermute x8, starting transfers between devices, ring_gather(): moving[which][0] = lax.ppermute(moving[which][0], axis, right)  32.8 us
    ppermute x6, starting transfers between devices, ring_gather(): moving[which][1] = lax.ppermute(moving[which][1], axis, left)  24.4 us
    pallas_call x1, Pallas kernels, attention(): pl.pallas_call(kernel, out_shape=jax.ShapeDtypeStruct((nodes, heads * HEA...  20.3 us
    all_to_all x1, starting transfers between devices, per_device(): lax.all_to_all(processed, ('seq', 'exp'), split_axis=0, concat_axis=0, ti...  8.26 us
    all_to_all x1, starting transfers between devices, per_device(): lax.all_to_all(attended, 'seq', split_axis=0, concat_axis=1, tiled=True)  6.68 us
    unnamed x26, local copies, waits for them, and re-layouts  6.25 us
  transfers between devices with their start and end apart: 17, of which 8 were waited for; matrix products, arithmetic and copies ran while one was open for 6% of the time, Pallas kernels for 8%

profile of v8, /device:TPU:28, one launch (start us, length us, event | category | flops | bytes accessed | tf_op | source)
XLA Modules:
  0.0 260.9 jit_solution(18376305605450029337)
XLA Ops:
  7.3 4.7 %collective-permute-start.2 = (bf16[192,1024]{1,0:T(8,128)(2,1)}, bf16[192,1024]{1,0:T(8,128)(2,1)S(1)}, u32[]{:S(2)}, u32[]{:S(2)}) collective-permute-start(bf16[192,1024]{1,0:T(8,128)(2,1)} %bitcast.107), channel_id=1, source_target_pairs={{0,8},{8,16},{16,24},{24,32},{32,40},{40,48},{48,56},{56,0},{1,9},... | collective-permute-start | bytes 1179656 | tf_op jit(solution)/shard_map/ppermute | solution.py:107
  12.0 1.9 collective-permute-start.3
  13.9 4.3 %collective-permute-start = (bf16[128,384]{1,0:T(8,128)(2,1)}, bf16[128,384]{1,0:T(8,128)(2,1)S(1)}, u32[]{:S(2)}, u32[]{:S(2)}) collective-permute-start(bf16[128,384]{1,0:T(8,128)(2,1)} %param.11), channel_id=1, source_target_pairs={{0,1},{1,2},{2,3},{3,4},{4,5},{5,6},{6,7},{7,0},{8,9},{9,10},{10,1... | collective-permute-start | bytes 294920 | tf_op jit(solution)/shard_map/ppermute | solution.py:107
  18.2 8.6 %collective-permute-start.1 = (bf16[128,384]{1,0:T(8,128)(2,1)}, bf16[128,384]{1,0:T(8,128)(2,1)}, u32[]{:S(2)}, u32[]{:S(2)}) collective-permute-start(bf16[128,384]{1,0:T(8,128)(2,1)} %param.11), channel_id=1, source_target_pairs={{0,7},{1,0},{2,1},{3,2},{4,3},{5,4},{6,5},{7,6},{8,15},{9,8},{10,9... | collective-permute-start | bytes 294920 | tf_op jit(solution)/shard_map/ppermute | solution.py:110
  27.6 1.6 collective-permute-done.1
  29.3 5.1 %collective-permute-start.6 = (bf16[192,1024]{1,0:T(8,128)(2,1)S(1)}, bf16[192,1024]{1,0:T(8,128)(2,1)}, u32[]{:S(2)}, u32[]{:S(2)}) collective-permute-start(bf16[192,1024]{1,0:T(8,128)(2,1)S(1)} %collective-permute-done.2.refs_7_), channel_id=1, source_target_pairs={{0,8},{8,16},{16,24},{24,32},{32,40},{40,48},{48,56},{56,0},{1,9},... | collective-permute-start | bytes 1179656 | tf_op jit(solution)/shard_map/ppermute | solution.py:107
  34.4 1.9 collective-permute-start.7
  36.4 1.9 collective-permute-start.4
  38.3 6.4 %collective-permute-start.5 = (bf16[128,384]{1,0:T(8,128)(2,1)}, bf16[128,384]{1,0:T(8,128)(2,1)}, u32[]{:S(2)}, u32[]{:S(2)}) collective-permute-start(bf16[128,384]{1,0:T(8,128)(2,1)} %collective-permute-done.1), channel_id=1, source_target_pairs={{0,7},{1,0},{2,1},{3,2},{4,3},{5,4},{6,5},{7,6},{8,15},{9,8},{10,9... | collective-permute-start | bytes 294920 | tf_op jit(solution)/shard_map/ppermute | solution.py:110
  47.6 3.8 %collective-permute-start.10 = (bf16[192,1024]{1,0:T(8,128)(2,1)}, bf16[192,1024]{1,0:T(8,128)(2,1)}, u32[]{:S(2)}, u32[]{:S(2)}) collective-permute-start(bf16[192,1024]{1,0:T(8,128)(2,1)} %collective-permute-done.6.refs_6_), channel_id=1, source_target_pairs={{0,8},{8,16},{16,24},{24,32},{32,40},{40,48},{48,56},{56,0},{1,9},... | collective-permute-start | bytes 1179656 | tf_op jit(solution)/shard_map/ppermute | solution.py:107
  51.5 2.0 collective-permute-start.11
  55.7 2.1 reduce-window.6
  58.4 3.9 %collective-permute-start.8 = (bf16[128,384]{1,0:T(8,128)(2,1)}, bf16[128,384]{1,0:T(8,128)(2,1)S(1)}, u32[]{:S(2)}, u32[]{:S(2)}) collective-permute-start(bf16[128,384]{1,0:T(8,128)(2,1)} %collective-permute-done.4), channel_id=1, source_target_pairs={{0,1},{1,2},{2,3},{3,4},{4,5},{5,6},{6,7},{7,0},{8,9},{9,10},{10,1... | collective-permute-start | bytes 294920 | tf_op jit(solution)/shard_map/ppermute | solution.py:107
  62.3 3.5 %collective-permute-start.9 = (bf16[128,384]{1,0:T(8,128)(2,1)}, bf16[128,384]{1,0:T(8,128)(2,1)S(1)}, u32[]{:S(2)}, u32[]{:S(2)}) collective-permute-start(bf16[128,384]{1,0:T(8,128)(2,1)} %collective-permute-done.5), channel_id=1, source_target_pairs={{0,7},{1,0},{2,1},{3,2},{4,3},{5,4},{6,5},{7,6},{8,15},{9,8},{10,9... | collective-permute-start | bytes 294920 | tf_op jit(solution)/shard_map/ppermute | solution.py:110
  66.7 2.3 collective-permute-done.9
  69.0 5.1 %collective-permute-start.13 = (bf16[192,1024]{1,0:T(8,128)(2,1)}, bf16[192,1024]{1,0:T(8,128)(2,1)S(1)}, u32[]{:S(2)}, u32[]{:S(2)}) collective-permute-start(bf16[192,1024]{1,0:T(8,128)(2,1)} %collective-permute-done.10.refs_5_), channel_id=1, source_target_pairs={{0,8},{8,16},{16,24},{24,32},{32,40},{40,48},{48,56},{56,0},{1,9},... | collective-permute-start | bytes 1179656 | tf_op jit(solution)/shard_map/ppermute | solution.py:107
  75.0 3.9 %collective-permute-start.12 = (bf16[128,384]{1,0:T(8,128)(2,1)S(1)}, bf16[128,384]{1,0:T(8,128)(2,1)S(1)}, u32[]{:S(2)}, u32[]{:S(2)}) collective-permute-start(bf16[128,384]{1,0:T(8,128)(2,1)S(1)} %collective-permute-done.8), channel_id=1, source_target_pairs={{0,1},{1,2},{2,3},{3,4},{4,5},{5,6},{6,7},{7,0},{8,9},{9,10},{10,1... | collective-permute-start | bytes 294920 | tf_op jit(solution)/shard_map/ppermute | solution.py:107
  79.0 4.9 %collective-permute-done.12 = bf16[128,384]{1,0:T(8,128)(2,1)S(1)} collective-permute-done((bf16[128,384]{1,0:T(8,128)(2,1)S(1)}, bf16[128,384]{1,0:T(8,128)(2,1)S(1)}, u32[]{:S(2)}, u32[]{:S(2)}) %collective-permute-start.12) | collective-permute-done | bytes 98336 | tf_op jit(solution)/shard_map/ppermute | solution.py:107
  84.0 1.0 bitcast_dynamic-update-slice_fusion.1
  86.8 20.3 %shard_map.91 = bf16[1536,128]{1,0:T(8,128)(2,1)} custom-call(s32[2]{0:T(128)} %pad_add_fusion.me_ref, s32[144]{0:T(256)} %reshape_squeeze.4.mask_ref, bf16[192,1024]{1,0:T(8,128)(2,1)} %bitcast.109, bf16[192,1024]{1,0:T(8,128)(2,1)} %collective-permute-done.3.refs_1_, bf16[192,1024]{1,0:T(8,128)(2,1)} %collective-permute-done.7.refs_2_, ...), custom_call_target="tpu_custom_call" | custom-call | tf_op jit(solution)/shard_map/pallas_call | solution.py:80
  107.1 6.7 %all-to-all-start = ((bf16[8,192,128]{2,1,0:T(8,128)(2,1)}), bf16[8,192,128]{2,1,0:T(8,128)(2,1)S(1)}, u32[]{:S(2)}, u32[]{:S(2)}) async-start(bf16[8,192,128]{2,1,0:T(8,128)(2,1)} %bitcast.106), calls=%async_computation | async-start | bytes 786432 | tf_op jit(solution)/shard_map/all_to_all | solution.py:134
  114.7 3.9 %copy.17 = bf16[8,8,128,128]{2,3,1,0:T(8,128)(2,1)} copy(bf16[8,8,128,128]{3,2,1,0:T(8,128)(2,1)} %bitcast.105) | data formatting | bytes 4194304 | tf_op jit(solution)/shard_map/reshape | solution.py:135
  118.6 3.7 %all-to-all-done = bf16[8,192,128]{2,1,0:T(8,128)(2,1)S(1)} async-done(((bf16[8,192,128]{2,1,0:T(8,128)(2,1)}), bf16[8,192,128]{2,1,0:T(8,128)(2,1)S(1)}, u32[]{:S(2)}, u32[]{:S(2)}) %all-to-all-start) | async-done | bytes 393248 | tf_op jit(solution)/shard_map/all_to_all | solution.py:134
  123.0 2.7 %multiply_reduce_fusion = (f32[192]{0:T(256)S(1)}, f32[192,1024]{1,0:T(8,128)S(1)}) fusion(bf16[1024,128,8]{1,0,2:T(8,128)(2,1)} %bitcast.104, bf16[8,192,128]{2,1,0:T(8,128)(2,1)} %copy-done.1, bf16[1,192,1024]{2,1,0:T(8,128)(2,1)} %param.9), kind=kOutput, calls=%fused_computation.26 | convolution fusion | flops 403439424 | bytes 3670784 | tf_op jit(solution)/shard_map/nsk,sekc->nec/dot_general | solution.py:136
  127.3 53.9 %all_to_all.26 = bf16[64,12,1024]{2,1,0:T(8,128)(2,1)S(1)} all-to-all(bf16[64,12,1024]{2,1,0:T(8,128)(2,1)S(1)} %copy.23), channel_id=1, replica_groups=mesh['sub'=8,'seq'=8,'exp'=8] {'seq','exp'}, dimensions={0} | all-to-all | bytes 3145728 | tf_op jit(solution)/shard_map/all_to_all | solution.py:157
  181.2 2.2 fusion
  183.4 1.0 convolution_convert_fusion
  184.4 2.2 copy.25
  186.6 8.3 %all-to-all-start.2 = ((bf16[64,12,1024]{2,1,0:T(8,128)(2,1)}), bf16[64,12,1024]{2,1,0:T(8,128)(2,1)}, u32[]{:S(2)}, u32[]{:S(2)}) async-start(bf16[64,12,1024]{2,1,0:T(8,128)(2,1)} %copy.25), calls=%async_computation.2 | async-start | bytes 4194304 | tf_op jit(solution)/shard_map/all_to_all | solution.py:163
  194.9 54.4 %all-to-all-done.2 = bf16[64,12,1024]{2,1,0:T(8,128)(2,1)} async-done(((bf16[64,12,1024]{2,1,0:T(8,128)(2,1)}), bf16[64,12,1024]{2,1,0:T(8,128)(2,1)}, u32[]{:S(2)}, u32[]{:S(2)}) %all-to-all-start.2) | async-done | bytes 1572896 | tf_op jit(solution)/shard_map/all_to_all | solution.py:163
  249.3 3.8 %fusion.8 = f32[2,192,1024]{2,1,0:T(8,128)S(1)} fusion(bf16[64,12,1024]{2,1,0:T(8,128)(2,1)} %all-to-all-done.2, s32[192,2]{0,1:T(2,128)S(1)} %copy.22, s32[64,12]{0,1:T(8,128)S(1)} %multiply_add_fusion), kind=kOutput, calls=%fused_computation.12 | convolution fusion | flops 604274688 | bytes 3150336 | tf_op jit(solution)/shard_map/ecnk,ecd->knd/dot_general | solution.py:164
  253.1 1.0 fusion.27
  (58 shorter events, 14.1 us)
Async XLA Ops:
  6.5 174.7 %copy-start = (bf16[1,1024,1024]{2,1,0:T(8,128)(2,1)S(1)}, bf16[1,1024,1024]{2,1,0:T(8,128)(2,1)}, u32[]{:S(2)}) copy-start(bf16[1,1024,1024]{2,1,0:T(8,128)(2,1)} %param.16) | copy-start | bytes 6291460
  6.5 108.2 %all-gather.3.cloned.1.call-start = ((), (), s32[]{:S(2)}) async-start(), calls=%async_computation.3 | async-start | bytes 2129920 | tf_op jit(solution)/shard_map/all_gather | solution.py:130
  7.3 22.0 %collective-permute-start.2 = (bf16[192,1024]{1,0:T(8,128)(2,1)}, bf16[192,1024]{1,0:T(8,128)(2,1)S(1)}, u32[]{:S(2)}, u32[]{:S(2)}) collective-permute-start(bf16[192,1024]{1,0:T(8,128)(2,1)} %bitcast.107), channel_id=1, source_target_pairs={{0,8},{8,16},{16,24},{24,32},{32,40},{40,48},{48,56},{56,0},{1,9},... | collective-permute-start | bytes 1179656 | tf_op jit(solution)/shard_map/ppermute | solution.py:107
  12.0 17.3 %collective-permute-start.3 = (bf16[192,1024]{1,0:T(8,128)(2,1)}, bf16[192,1024]{1,0:T(8,128)(2,1)}, u32[]{:S(2)}, u32[]{:S(2)}) collective-permute-start(bf16[192,1024]{1,0:T(8,128)(2,1)} %bitcast.108), channel_id=1, source_target_pairs={{0,56},{8,0},{16,8},{24,16},{32,24},{40,32},{48,40},{56,48},{1,57}... | collective-permute-start | bytes 1179656 | tf_op jit(solution)/shard_map/ppermute | solution.py:110
  13.9 13.7 %collective-permute-start = (bf16[128,384]{1,0:T(8,128)(2,1)}, bf16[128,384]{1,0:T(8,128)(2,1)S(1)}, u32[]{:S(2)}, u32[]{:S(2)}) collective-permute-start(bf16[128,384]{1,0:T(8,128)(2,1)} %param.11), channel_id=1, source_target_pairs={{0,1},{1,2},{2,3},{3,4},{4,5},{5,6},{6,7},{7,0},{8,9},{9,10},{10,1... | collective-permute-start | bytes 294920 | tf_op jit(solution)/shard_map/ppermute | solution.py:107
  18.2 11.1 %collective-permute-start.1 = (bf16[128,384]{1,0:T(8,128)(2,1)}, bf16[128,384]{1,0:T(8,128)(2,1)}, u32[]{:S(2)}, u32[]{:S(2)}) collective-permute-start(bf16[128,384]{1,0:T(8,128)(2,1)} %param.11), channel_id=1, source_target_pairs={{0,7},{1,0},{2,1},{3,2},{4,3},{5,4},{6,5},{7,6},{8,15},{9,8},{10,9... | collective-permute-start | bytes 294920 | tf_op jit(solution)/shard_map/ppermute | solution.py:110
  27.6 27.4 %copy-start.5 = (bf16[128,384]{1,0:T(8,128)(2,1)}, bf16[128,384]{1,0:T(8,128)(2,1)S(1)}, u32[]{:S(2)}) copy-start(bf16[128,384]{1,0:T(8,128)(2,1)S(1)} %collective-permute-done) | copy-start | bytes 294916
  29.3 56.7 %copy-start.3 = (bf16[192,1024]{1,0:T(8,128)(2,1)}, bf16[192,1024]{1,0:T(8,128)(2,1)S(1)}, u32[]{:S(2)}) copy-start(bf16[192,1024]{1,0:T(8,128)(2,1)S(1)} %collective-permute-done.2.refs_7_) | copy-start | bytes 1179652
  29.3 17.9 %collective-permute-start.6 = (bf16[192,1024]{1,0:T(8,128)(2,1)S(1)}, bf16[192,1024]{1,0:T(8,128)(2,1)}, u32[]{:S(2)}, u32[]{:S(2)}) collective-permute-start(bf16[192,1024]{1,0:T(8,128)(2,1)S(1)} %collective-permute-done.2.refs_7_), channel_id=1, source_target_pairs={{0,8},{8,16},{16,24},{24,32},{32,40},{40,48},{48,56},{56,0},{1,9},... | collective-permute-start | bytes 1179656 | tf_op jit(solution)/shard_map/ppermute | solution.py:107
  34.4 13.2 %collective-permute-start.7 = (bf16[192,1024]{1,0:T(8,128)(2,1)}, bf16[192,1024]{1,0:T(8,128)(2,1)}, u32[]{:S(2)}, u32[]{:S(2)}) collective-permute-start(bf16[192,1024]{1,0:T(8,128)(2,1)} %collective-permute-done.3.refs_1_), channel_id=1, source_target_pairs={{0,56},{8,0},{16,8},{24,16},{32,24},{40,32},{48,40},{56,48},{1,57}... | collective-permute-start | bytes 1179656 | tf_op jit(solution)/shard_map/ppermute | solution.py:110
  36.4 10.2 %collective-permute-start.4 = (bf16[128,384]{1,0:T(8,128)(2,1)S(1)}, bf16[128,384]{1,0:T(8,128)(2,1)}, u32[]{:S(2)}, u32[]{:S(2)}) collective-permute-start(bf16[128,384]{1,0:T(8,128)(2,1)S(1)} %collective-permute-done), channel_id=1, source_target_pairs={{0,1},{1,2},{2,3},{3,4},{4,5},{5,6},{6,7},{7,0},{8,9},{9,10},{10,1... | collective-permute-start | bytes 294920 | tf_op jit(solution)/shard_map/ppermute | solution.py:107
  38.3 8.9 %collective-permute-start.5 = (bf16[128,384]{1,0:T(8,128)(2,1)}, bf16[128,384]{1,0:T(8,128)(2,1)}, u32[]{:S(2)}, u32[]{:S(2)}) collective-permute-start(bf16[128,384]{1,0:T(8,128)(2,1)} %collective-permute-done.1), channel_id=1, source_target_pairs={{0,7},{1,0},{2,1},{3,2},{4,3},{5,4},{6,5},{7,6},{8,15},{9,8},{10,9... | collective-permute-start | bytes 294920 | tf_op jit(solution)/shard_map/ppermute | solution.py:110
  47.6 21.4 %collective-permute-start.10 = (bf16[192,1024]{1,0:T(8,128)(2,1)}, bf16[192,1024]{1,0:T(8,128)(2,1)}, u32[]{:S(2)}, u32[]{:S(2)}) collective-permute-start(bf16[192,1024]{1,0:T(8,128)(2,1)} %collective-permute-done.6.refs_6_), channel_id=1, source_target_pairs={{0,8},{8,16},{16,24},{24,32},{32,40},{40,48},{48,56},{56,0},{1,9},... | collective-permute-start | bytes 1179656 | tf_op jit(solution)/shard_map/ppermute | solution.py:107
  51.5 17.5 %collective-permute-start.11 = (bf16[192,1024]{1,0:T(8,128)(2,1)}, bf16[192,1024]{1,0:T(8,128)(2,1)}, u32[]{:S(2)}, u32[]{:S(2)}) collective-permute-start(bf16[192,1024]{1,0:T(8,128)(2,1)} %collective-permute-done.7.refs_2_), channel_id=1, source_target_pairs={{0,56},{8,0},{16,8},{24,16},{32,24},{40,32},{48,40},{56,48},{1,57}... | collective-permute-start | bytes 1179656 | tf_op jit(solution)/shard_map/ppermute | solution.py:110
  58.4 8.3 %collective-permute-start.8 = (bf16[128,384]{1,0:T(8,128)(2,1)}, bf16[128,384]{1,0:T(8,128)(2,1)S(1)}, u32[]{:S(2)}, u32[]{:S(2)}) collective-permute-start(bf16[128,384]{1,0:T(8,128)(2,1)} %collective-permute-done.4), channel_id=1, source_target_pairs={{0,1},{1,2},{2,3},{3,4},{4,5},{5,6},{6,7},{7,0},{8,9},{9,10},{10,1... | collective-permute-start | bytes 294920 | tf_op jit(solution)/shard_map/ppermute | solution.py:107
  62.3 6.7 %collective-permute-start.9 = (bf16[128,384]{1,0:T(8,128)(2,1)}, bf16[128,384]{1,0:T(8,128)(2,1)S(1)}, u32[]{:S(2)}, u32[]{:S(2)}) collective-permute-start(bf16[128,384]{1,0:T(8,128)(2,1)} %collective-permute-done.5), channel_id=1, source_target_pairs={{0,7},{1,0},{2,1},{3,2},{4,3},{5,4},{6,5},{7,6},{8,15},{9,8},{10,9... | collective-permute-start | bytes 294920 | tf_op jit(solution)/shard_map/ppermute | solution.py:110
  69.0 14.9 %collective-permute-start.13 = (bf16[192,1024]{1,0:T(8,128)(2,1)}, bf16[192,1024]{1,0:T(8,128)(2,1)S(1)}, u32[]{:S(2)}, u32[]{:S(2)}) collective-permute-start(bf16[192,1024]{1,0:T(8,128)(2,1)} %collective-permute-done.10.refs_5_), channel_id=1, source_target_pairs={{0,8},{8,16},{16,24},{24,32},{32,40},{40,48},{48,56},{56,0},{1,9},... | collective-permute-start | bytes 1179656 | tf_op jit(solution)/shard_map/ppermute | solution.py:107
  75.0 8.9 %collective-permute-start.12 = (bf16[128,384]{1,0:T(8,128)(2,1)S(1)}, bf16[128,384]{1,0:T(8,128)(2,1)S(1)}, u32[]{:S(2)}, u32[]{:S(2)}) collective-permute-start(bf16[128,384]{1,0:T(8,128)(2,1)S(1)} %collective-permute-done.8), channel_id=1, source_target_pairs={{0,1},{1,2},{2,3},{3,4},{4,5},{5,6},{6,7},{7,0},{8,9},{9,10},{10,1... | collective-permute-start | bytes 294920 | tf_op jit(solution)/shard_map/ppermute | solution.py:107
  83.9 1.1 copy-start.4
  86.0 0.9 copy-start.2
  107.1 15.2 %all-to-all-start = ((bf16[8,192,128]{2,1,0:T(8,128)(2,1)}), bf16[8,192,128]{2,1,0:T(8,128)(2,1)S(1)}, u32[]{:S(2)}, u32[]{:S(2)}) async-start(bf16[8,192,128]{2,1,0:T(8,128)(2,1)} %bitcast.106), calls=%async_computation | async-start | bytes 786432 | tf_op jit(solution)/shard_map/all_to_all | solution.py:134
  122.3 0.7 copy-start.1
  123.0 2.7 %copy-start.6 = (f32[1024]{0:T(1024)S(1)}, f32[1024]{0:T(1024)}, u32[]{:S(2)}) copy-start(f32[1024]{0:T(1024)} %param.13) | copy-start | bytes 12292
  181.2 2.2 copy-start.8
  186.6 8.3 %copy-start.7 = (f32[1,192,2]{1,2,0:T(2,128)S(1)}, f32[1,192,2]{1,2,0:T(2,128)}, u32[]{:S(2)}) copy-start(f32[1,192,2]{1,2,0:T(2,128)} %param.15) | copy-start | bytes 4612
  186.6 62.7 %all-to-all-start.2 = ((bf16[64,12,1024]{2,1,0:T(8,128)(2,1)}), bf16[64,12,1024]{2,1,0:T(8,128)(2,1)}, u32[]{:S(2)}, u32[]{:S(2)}) async-start(bf16[64,12,1024]{2,1,0:T(8,128)(2,1)} %copy.25), calls=%async_computation.2 | async-start | bytes 4194304 | tf_op jit(solution)/shard_map/all_to_all | solution.py:163
Sparse Core Ops, SparseCore 0:
  10.4 88.3 all-gather.2

commit v9 on v8

--- a/solution.py
+++ b/solution.py
@@ -154,13 +154,17 @@
         "ecn,nd->ecd", jnp.sum(select, axis=3), normed, preferred_element_type=jnp.float32
     ).astype(jnp.bfloat16)
     hidden_units = w_down.shape[1]
-    received = lax.all_to_all(outgoing, ("seq", "exp"), split_axis=0, concat_axis=0, tiled=True)
-    both = jnp.einsum("eck,kf->ecf", received, w_gate_up[0], preferred_element_type=jnp.float32)
-    hidden = (jax.nn.silu(both[..., :hidden_units]) * both[..., hidden_units:]).astype(jnp.bfloat16)
-    processed = jnp.einsum(
-        "ecf,fd->ecd", hidden, w_down[0], preferred_element_type=jnp.float32
-    ).astype(jnp.bfloat16)
-    returned = lax.all_to_all(processed, ("seq", "exp"), split_axis=0, concat_axis=0, tiled=True)
+    lanes = 128
+    packed = (experts, capacity * width // lanes, lanes)
+    received = lax.all_to_all(
+        outgoing.reshape(packed), ("seq", "exp"), split_axis=0, concat_axis=0, tiled=True
+    ).reshape(experts * capacity, width)
+    both = jnp.dot(received, w_gate_up[0], preferred_element_type=jnp.float32)
+    hidden = (jax.nn.silu(both[:, :hidden_units]) * both[:, hidden_units:]).astype(jnp.bfloat16)
+    processed = jnp.dot(hidden, w_down[0], preferred_element_type=jnp.float32).astype(jnp.bfloat16)
+    returned = lax.all_to_all(
+        processed.reshape(packed), ("seq", "exp"), split_axis=0, concat_axis=0, tiled=True
+    ).reshape(experts, capacity, width)
     picked = jnp.einsum("ecnk,ecd->knd", select, returned, preferred_element_type=jnp.float32)
     expert_sum = picked[0] * gates[0][:, 0, None] + picked[1] * gates[0][:, 1, None]
     return (mixed + expert_sum).astype(jnp.bfloat16)[None]

time: 262 us -> 253 us (0.966)
  the two profiles are of different devices: /device:TPU:28 before, /device:TPU:26 now
where the time goes in v9:
time: 253 us; the launch traced here: 252 us
  starting transfers between devices  72.4 us (29%)
  waiting for transfers between devices  54.4 us (22%)
  blocking collectives  42.9 us (17%)
  local copies, waits for them, and re-layouts  30 us (12%)
  Pallas kernels  20.3 us (8%)
  between operations  13.7 us (5%)
  matrix products  12.5 us (5%)
  other arithmetic  5.47 us (2%)
    all_to_all x1, blocking collectives, per_device(): lax.all_to_all(outgoing.reshape(packed), ('seq', 'exp'), split_axis=0, co...  42.9 us
    all_to_all x1, waiting for transfers between devices, per_device(): lax.all_to_all(processed.reshape(packed), ('seq', 'exp'), split_axis=0, c...  39.2 us
    ppermute x8, starting transfers between devices, ring_gather(): moving[which][0] = lax.ppermute(moving[which][0], axis, right)  32.8 us
    ppermute x6, starting transfers between devices, ring_gather(): moving[which][1] = lax.ppermute(moving[which][1], axis, left)  24.3 us
    pallas_call x1, Pallas kernels, attention(): pl.pallas_call(kernel, out_shape=jax.ShapeDtypeStruct((nodes, heads * HEA...  20.3 us
    all_to_all x1, starting transfers between devices, per_device(): lax.all_to_all(processed.reshape(packed), ('seq', 'exp'), split_axis=0, c...  8.53 us
    all_to_all x1, starting transfers between devices, per_device(): lax.all_to_all(attended, 'seq', split_axis=0, concat_axis=1, tiled=True)  6.72 us
    unnamed x26, local copies, waits for them, and re-layouts  6.25 us
  transfers between devices with their start and end apart: 17, of which 8 were waited for; matrix products, arithmetic and copies ran while one was open for 6% of the time, Pallas kernels for 8%

profile of v9, /device:TPU:26, one launch (start us, length us, event | category | flops | bytes accessed | tf_op | source)
XLA Modules:
  0.0 251.7 jit_solution(15015468888027326732)
XLA Ops:
  7.3 4.7 %collective-permute-start.2 = (bf16[192,1024]{1,0:T(8,128)(2,1)}, bf16[192,1024]{1,0:T(8,128)(2,1)S(1)}, u32[]{:S(2)}, u32[]{:S(2)}) collective-permute-start(bf16[192,1024]{1,0:T(8,128)(2,1)} %bitcast.106), channel_id=1, source_target_pairs={{0,8},{8,16},{16,24},{24,32},{32,40},{40,48},{48,56},{56,0},{1,9},... | collective-permute-start | bytes 1179656 | tf_op jit(solution)/shard_map/ppermute | solution.py:107
  12.0 1.9 collective-permute-start.3
  13.9 4.3 %collective-permute-start = (bf16[128,384]{1,0:T(8,128)(2,1)}, bf16[128,384]{1,0:T(8,128)(2,1)S(1)}, u32[]{:S(2)}, u32[]{:S(2)}) collective-permute-start(bf16[128,384]{1,0:T(8,128)(2,1)} %param.11), channel_id=1, source_target_pairs={{0,1},{1,2},{2,3},{3,4},{4,5},{5,6},{6,7},{7,0},{8,9},{9,10},{10,1... | collective-permute-start | bytes 294920 | tf_op jit(solution)/shard_map/ppermute | solution.py:107
  18.2 8.6 %collective-permute-start.1 = (bf16[128,384]{1,0:T(8,128)(2,1)}, bf16[128,384]{1,0:T(8,128)(2,1)}, u32[]{:S(2)}, u32[]{:S(2)}) collective-permute-start(bf16[128,384]{1,0:T(8,128)(2,1)} %param.11), channel_id=1, source_target_pairs={{0,7},{1,0},{2,1},{3,2},{4,3},{5,4},{6,5},{7,6},{8,15},{9,8},{10,9... | collective-permute-start | bytes 294920 | tf_op jit(solution)/shard_map/ppermute | solution.py:110
  29.3 5.1 %collective-permute-start.6 = (bf16[192,1024]{1,0:T(8,128)(2,1)S(1)}, bf16[192,1024]{1,0:T(8,128)(2,1)}, u32[]{:S(2)}, u32[]{:S(2)}) collective-permute-start(bf16[192,1024]{1,0:T(8,128)(2,1)S(1)} %collective-permute-done.2.refs_7_), channel_id=1, source_target_pairs={{0,8},{8,16},{16,24},{24,32},{32,40},{40,48},{48,56},{56,0},{1,9},... | collective-permute-start | bytes 1179656 | tf_op jit(solution)/shard_map/ppermute | solution.py:107
  34.4 1.9 collective-permute-start.7
  38.3 6.4 %collective-permute-start.5 = (bf16[128,384]{1,0:T(8,128)(2,1)}, bf16[128,384]{1,0:T(8,128)(2,1)}, u32[]{:S(2)}, u32[]{:S(2)}) collective-permute-start(bf16[128,384]{1,0:T(8,128)(2,1)} %collective-permute-done.1), channel_id=1, source_target_pairs={{0,7},{1,0},{2,1},{3,2},{4,3},{5,4},{6,5},{7,6},{8,15},{9,8},{10,9... | collective-permute-start | bytes 294920 | tf_op jit(solution)/shard_map/ppermute | solution.py:110
  47.6 3.8 %collective-permute-start.10 = (bf16[192,1024]{1,0:T(8,128)(2,1)}, bf16[192,1024]{1,0:T(8,128)(2,1)}, u32[]{:S(2)}, u32[]{:S(2)}) collective-permute-start(bf16[192,1024]{1,0:T(8,128)(2,1)} %collective-permute-done.6.refs_6_), channel_id=1, source_target_pairs={{0,8},{8,16},{16,24},{24,32},{32,40},{40,48},{48,56},{56,0},{1,9},... | collective-permute-start | bytes 1179656 | tf_op jit(solution)/shard_map/ppermute | solution.py:107
  51.5 2.0 collective-permute-start.11
  55.7 2.1 reduce-window.6
  58.4 3.9 %collective-permute-start.8 = (bf16[128,384]{1,0:T(8,128)(2,1)}, bf16[128,384]{1,0:T(8,128)(2,1)S(1)}, u32[]{:S(2)}, u32[]{:S(2)}) collective-permute-start(bf16[128,384]{1,0:T(8,128)(2,1)} %collective-permute-done.4), channel_id=1, source_target_pairs={{0,1},{1,2},{2,3},{3,4},{4,5},{5,6},{6,7},{7,0},{8,9},{9,10},{10,1... | collective-permute-start | bytes 294920 | tf_op jit(solution)/shard_map/ppermute | solution.py:107
  62.3 3.5 %collective-permute-start.9 = (bf16[128,384]{1,0:T(8,128)(2,1)}, bf16[128,384]{1,0:T(8,128)(2,1)S(1)}, u32[]{:S(2)}, u32[]{:S(2)}) collective-permute-start(bf16[128,384]{1,0:T(8,128)(2,1)} %collective-permute-done.5), channel_id=1, source_target_pairs={{0,7},{1,0},{2,1},{3,2},{4,3},{5,4},{6,5},{7,6},{8,15},{9,8},{10,9... | collective-permute-start | bytes 294920 | tf_op jit(solution)/shard_map/ppermute | solution.py:110
  66.7 2.3 collective-permute-done.9
  69.0 5.1 %collective-permute-start.13 = (bf16[192,1024]{1,0:T(8,128)(2,1)}, bf16[192,1024]{1,0:T(8,128)(2,1)S(1)}, u32[]{:S(2)}, u32[]{:S(2)}) collective-permute-start(bf16[192,1024]{1,0:T(8,128)(2,1)} %collective-permute-done.10.refs_5_), channel_id=1, source_target_pairs={{0,8},{8,16},{16,24},{24,32},{32,40},{40,48},{48,56},{56,0},{1,9},... | collective-permute-start | bytes 1179656 | tf_op jit(solution)/shard_map/ppermute | solution.py:107
  75.0 3.9 %collective-permute-start.12 = (bf16[128,384]{1,0:T(8,128)(2,1)S(1)}, bf16[128,384]{1,0:T(8,128)(2,1)S(1)}, u32[]{:S(2)}, u32[]{:S(2)}) collective-permute-start(bf16[128,384]{1,0:T(8,128)(2,1)S(1)} %collective-permute-done.8), channel_id=1, source_target_pairs={{0,1},{1,2},{2,3},{3,4},{4,5},{5,6},{6,7},{7,0},{8,9},{9,10},{10,1... | collective-permute-start | bytes 294920 | tf_op jit(solution)/shard_map/ppermute | solution.py:107
  79.0 4.9 %collective-permute-done.12 = bf16[128,384]{1,0:T(8,128)(2,1)S(1)} collective-permute-done((bf16[128,384]{1,0:T(8,128)(2,1)S(1)}, bf16[128,384]{1,0:T(8,128)(2,1)S(1)}, u32[]{:S(2)}, u32[]{:S(2)}) %collective-permute-start.12) | collective-permute-done | bytes 98336 | tf_op jit(solution)/shard_map/ppermute | solution.py:107
  86.8 20.3 %shard_map.91 = bf16[1536,128]{1,0:T(8,128)(2,1)} custom-call(s32[2]{0:T(128)} %pad_add_fusion.me_ref, s32[144]{0:T(256)} %reshape_squeeze.4.mask_ref, bf16[192,1024]{1,0:T(8,128)(2,1)} %bitcast.108, bf16[192,1024]{1,0:T(8,128)(2,1)} %collective-permute-done.3.refs_1_, bf16[192,1024]{1,0:T(8,128)(2,1)} %collective-permute-done.7.refs_2_, ...), custom_call_target="tpu_custom_call" | custom-call | tf_op jit(solution)/shard_map/pallas_call | solution.py:80
  107.1 6.7 %all-to-all-start = ((bf16[8,192,128]{2,1,0:T(8,128)(2,1)}), bf16[8,192,128]{2,1,0:T(8,128)(2,1)S(1)}, u32[]{:S(2)}, u32[]{:S(2)}) async-start(bf16[8,192,128]{2,1,0:T(8,128)(2,1)} %bitcast.105), calls=%async_computation | async-start | bytes 786432 | tf_op jit(solution)/shard_map/all_to_all | solution.py:134
  114.7 3.9 %copy.11 = bf16[8,8,128,128]{2,3,1,0:T(8,128)(2,1)} copy(bf16[8,8,128,128]{3,2,1,0:T(8,128)(2,1)} %bitcast.104) | data formatting | bytes 4194304 | tf_op jit(solution)/shard_map/reshape | solution.py:135
  118.7 3.7 %all-to-all-done = bf16[8,192,128]{2,1,0:T(8,128)(2,1)S(1)} async-done(((bf16[8,192,128]{2,1,0:T(8,128)(2,1)}), bf16[8,192,128]{2,1,0:T(8,128)(2,1)S(1)}, u32[]{:S(2)}, u32[]{:S(2)}) %all-to-all-start) | async-done | bytes 393248 | tf_op jit(solution)/shard_map/all_to_all | solution.py:134
  123.1 2.7 %multiply_reduce_fusion = (f32[192]{0:T(256)S(1)}, f32[192,1024]{1,0:T(8,128)S(1)}) fusion(bf16[1024,128,8]{1,0,2:T(8,128)(2,1)} %bitcast.103, bf16[8,192,128]{2,1,0:T(8,128)(2,1)} %copy-done.1, bf16[1,192,1024]{2,1,0:T(8,128)(2,1)} %param.9), kind=kOutput, calls=%fused_computation.25 | convolution fusion | flops 403439424 | bytes 3670784 | tf_op jit(solution)/shard_map/nsk,sekc->nec/dot_general | solution.py:136
  126.4 2.2 copy.17
  128.7 4.0 %reshape.72 = bf16[64,96,128]{2,1,0:T(8,128)(2,1)} reshape(bf16[64,12,1024]{2,1,0:T(8,128)(2,1)} %copy.17) | data formatting | bytes 3145728 | tf_op jit(solution)/shard_map/reshape | solution.py:160
  132.6 42.9 %all_to_all.26 = bf16[64,96,128]{2,1,0:T(8,128)(2,1)} all-to-all(bf16[64,96,128]{2,1,0:T(8,128)(2,1)} %reshape.72), channel_id=1, replica_groups=mesh['sub'=8,'seq'=8,'exp'=8] {'seq','exp'}, dimensions={0} | all-to-all | bytes 3145728 | tf_op jit(solution)/shard_map/all_to_all | solution.py:159
  175.6 3.7 %reshape.73 = bf16[768,1024]{1,0:T(8,128)(2,1)} reshape(bf16[64,96,128]{2,1,0:T(8,128)(2,1)} %all_to_all.26) | data formatting | bytes 3145728 | tf_op jit(solution)/shard_map/reshape | solution.py:161
  179.3 3.3 %fusion = f32[768,1024]{1,0:T(8,128)S(1)} fusion(bf16[768,1024]{1,0:T(8,128)(2,1)} %reshape.73, bf16[1,1024,1024]{2,1,0:T(8,128)(2,1)S(1)} %copy-done), kind=kOutput, calls=%fused_computation | convolution fusion | flops 1610612736 | bytes 6815744 | tf_op jit(solution)/shard_map/dot_general | solution.py:162
  182.6 2.2 convolution_convert_fusion
  184.7 3.7 %reshape.74 = bf16[64,96,128]{2,1,0:T(8,128)(2,1)} reshape(bf16[768,1024]{1,0:T(8,128)(2,1)} %convolution_convert_fusion) | data formatting | bytes 3145728 | tf_op jit(solution)/shard_map/reshape | solution.py:166
  188.4 8.5 %all-to-all-start.2 = ((bf16[64,96,128]{2,1,0:T(8,128)(2,1)}), bf16[64,96,128]{2,1,0:T(8,128)(2,1)}, u32[]{:S(2)}, u32[]{:S(2)}) async-start(bf16[64,96,128]{2,1,0:T(8,128)(2,1)} %reshape.74), calls=%async_computation.2 | async-start | bytes 3145728 | tf_op jit(solution)/shard_map/all_to_all | solution.py:165
  197.0 39.2 %all-to-all-done.2 = bf16[64,96,128]{2,1,0:T(8,128)(2,1)} async-done(((bf16[64,96,128]{2,1,0:T(8,128)(2,1)}), bf16[64,96,128]{2,1,0:T(8,128)(2,1)}, u32[]{:S(2)}, u32[]{:S(2)}) %all-to-all-start.2) | async-done | bytes 1572896 | tf_op jit(solution)/shard_map/all_to_all | solution.py:165
  236.2 4.0 %reshape.75 = bf16[64,12,1024]{2,1,0:T(8,128)(2,1)} reshape(bf16[64,96,128]{2,1,0:T(8,128)(2,1)} %all-to-all-done.2) | data formatting | bytes 3145728 | tf_op jit(solution)/shard_map/reshape | solution.py:167
  240.2 3.8 %fusion.7 = f32[2,192,1024]{2,1,0:T(8,128)S(1)} fusion(bf16[64,12,1024]{2,1,0:T(8,128)(2,1)} %reshape.75, s32[192,2]{0,1:T(2,128)S(1)} %copy.16, s32[64,12]{0,1:T(8,128)S(1)} %multiply_add_fusion), kind=kOutput, calls=%fused_computation.11 | convolution fusion | flops 604274688 | bytes 3150336 | tf_op jit(solution)/shard_map/ecnk,ecd->knd/dot_general | solution.py:168
  (61 shorter events, 18.8 us)
Async XLA Ops:
  6.5 172.7 %copy-start = (bf16[1,1024,1024]{2,1,0:T(8,128)(2,1)S(1)}, bf16[1,1024,1024]{2,1,0:T(8,128)(2,1)}, u32[]{:S(2)}) copy-start(bf16[1,1024,1024]{2,1,0:T(8,128)(2,1)} %param.16) | copy-start | bytes 6291460
  6.5 108.2 %all-gather.3.cloned.1.call-start = ((), (), s32[]{:S(2)}) async-start(), calls=%async_computation.3 | async-start | bytes 2129920 | tf_op jit(solution)/shard_map/all_gather | solution.py:130
  7.3 22.0 %collective-permute-start.2 = (bf16[192,1024]{1,0:T(8,128)(2,1)}, bf16[192,1024]{1,0:T(8,128)(2,1)S(1)}, u32[]{:S(2)}, u32[]{:S(2)}) collective-permute-start(bf16[192,1024]{1,0:T(8,128)(2,1)} %bitcast.106), channel_id=1, source_target_pairs={{0,8},{8,16},{16,24},{24,32},{32,40},{40,48},{48,56},{56,0},{1,9},... | collective-permute-start | bytes 1179656 | tf_op jit(solution)/shard_map/ppermute | solution.py:107
  12.0 17.3 %collective-permute-start.3 = (bf16[192,1024]{1,0:T(8,128)(2,1)}, bf16[192,1024]{1,0:T(8,128)(2,1)}, u32[]{:S(2)}, u32[]{:S(2)}) collective-permute-start(bf16[192,1024]{1,0:T(8,128)(2,1)} %bitcast.107), channel_id=1, source_target_pairs={{0,56},{8,0},{16,8},{24,16},{32,24},{40,32},{48,40},{56,48},{1,57}... | collective-permute-start | bytes 1179656 | tf_op jit(solution)/shard_map/ppermute | solution.py:110
  13.9 13.7 %collective-permute-start = (bf16[128,384]{1,0:T(8,128)(2,1)}, bf16[128,384]{1,0:T(8,128)(2,1)S(1)}, u32[]{:S(2)}, u32[]{:S(2)}) collective-permute-start(bf16[128,384]{1,0:T(8,128)(2,1)} %param.11), channel_id=1, source_target_pairs={{0,1},{1,2},{2,3},{3,4},{4,5},{5,6},{6,7},{7,0},{8,9},{9,10},{10,1... | collective-permute-start | bytes 294920 | tf_op jit(solution)/shard_map/ppermute | solution.py:107
  18.2 11.1 %collective-permute-start.1 = (bf16[128,384]{1,0:T(8,128)(2,1)}, bf16[128,384]{1,0:T(8,128)(2,1)}, u32[]{:S(2)}, u32[]{:S(2)}) collective-permute-start(bf16[128,384]{1,0:T(8,128)(2,1)} %param.11), channel_id=1, source_target_pairs={{0,7},{1,0},{2,1},{3,2},{4,3},{5,4},{6,5},{7,6},{8,15},{9,8},{10,9... | collective-permute-start | bytes 294920 | tf_op jit(solution)/shard_map/ppermute | solution.py:110
  27.6 27.4 %copy-start.5 = (bf16[128,384]{1,0:T(8,128)(2,1)}, bf16[128,384]{1,0:T(8,128)(2,1)S(1)}, u32[]{:S(2)}) copy-start(bf16[128,384]{1,0:T(8,128)(2,1)S(1)} %collective-permute-done) | copy-start | bytes 294916
  29.3 56.6 %copy-start.3 = (bf16[192,1024]{1,0:T(8,128)(2,1)}, bf16[192,1024]{1,0:T(8,128)(2,1)S(1)}, u32[]{:S(2)}) copy-start(bf16[192,1024]{1,0:T(8,128)(2,1)S(1)} %collective-permute-done.2.refs_7_) | copy-start | bytes 1179652
  29.3 17.9 %collective-permute-start.6 = (bf16[192,1024]{1,0:T(8,128)(2,1)S(1)}, bf16[192,1024]{1,0:T(8,128)(2,1)}, u32[]{:S(2)}, u32[]{:S(2)}) collective-permute-start(bf16[192,1024]{1,0:T(8,128)(2,1)S(1)} %collective-permute-done.2.refs_7_), channel_id=1, source_target_pairs={{0,8},{8,16},{16,24},{24,32},{32,40},{40,48},{48,56},{56,0},{1,9},... | collective-permute-start | bytes 1179656 | tf_op jit(solution)/shard_map/ppermute | solution.py:107
  34.4 13.2 %collective-permute-start.7 = (bf16[192,1024]{1,0:T(8,128)(2,1)}, bf16[192,1024]{1,0:T(8,128)(2,1)}, u32[]{:S(2)}, u32[]{:S(2)}) collective-permute-start(bf16[192,1024]{1,0:T(8,128)(2,1)} %collective-permute-done.3.refs_1_), channel_id=1, source_target_pairs={{0,56},{8,0},{16,8},{24,16},{32,24},{40,32},{48,40},{56,48},{1,57}... | collective-permute-start | bytes 1179656 | tf_op jit(solution)/shard_map/ppermute | solution.py:110
  36.4 10.2 %collective-permute-start.4 = (bf16[128,384]{1,0:T(8,128)(2,1)S(1)}, bf16[128,384]{1,0:T(8,128)(2,1)}, u32[]{:S(2)}, u32[]{:S(2)}) collective-permute-start(bf16[128,384]{1,0:T(8,128)(2,1)S(1)} %collective-permute-done), channel_id=1, source_target_pairs={{0,1},{1,2},{2,3},{3,4},{4,5},{5,6},{6,7},{7,0},{8,9},{9,10},{10,1... | collective-permute-start | bytes 294920 | tf_op jit(solution)/shard_map/ppermute | solution.py:107
  38.3 8.9 %collective-permute-start.5 = (bf16[128,384]{1,0:T(8,128)(2,1)}, bf16[128,384]{1,0:T(8,128)(2,1)}, u32[]{:S(2)}, u32[]{:S(2)}) collective-permute-start(bf16[128,384]{1,0:T(8,128)(2,1)} %collective-permute-done.1), channel_id=1, source_target_pairs={{0,7},{1,0},{2,1},{3,2},{4,3},{5,4},{6,5},{7,6},{8,15},{9,8},{10,9... | collective-permute-start | bytes 294920 | tf_op jit(solution)/shard_map/ppermute | solution.py:110
  47.6 21.4 %collective-permute-start.10 = (bf16[192,1024]{1,0:T(8,128)(2,1)}, bf16[192,1024]{1,0:T(8,128)(2,1)}, u32[]{:S(2)}, u32[]{:S(2)}) collective-permute-start(bf16[192,1024]{1,0:T(8,128)(2,1)} %collective-permute-done.6.refs_6_), channel_id=1, source_target_pairs={{0,8},{8,16},{16,24},{24,32},{32,40},{40,48},{48,56},{56,0},{1,9},... | collective-permute-start | bytes 1179656 | tf_op jit(solution)/shard_map/ppermute | solution.py:107
  51.5 17.5 %collective-permute-start.11 = (bf16[192,1024]{1,0:T(8,128)(2,1)}, bf16[192,1024]{1,0:T(8,128)(2,1)}, u32[]{:S(2)}, u32[]{:S(2)}) collective-permute-start(bf16[192,1024]{1,0:T(8,128)(2,1)} %collective-permute-done.7.refs_2_), channel_id=1, source_target_pairs={{0,56},{8,0},{16,8},{24,16},{32,24},{40,32},{48,40},{56,48},{1,57}... | collective-permute-start | bytes 1179656 | tf_op jit(solution)/shard_map/ppermute | solution.py:110
  58.4 8.3 %collective-permute-start.8 = (bf16[128,384]{1,0:T(8,128)(2,1)}, bf16[128,384]{1,0:T(8,128)(2,1)S(1)}, u32[]{:S(2)}, u32[]{:S(2)}) collective-permute-start(bf16[128,384]{1,0:T(8,128)(2,1)} %collective-permute-done.4), channel_id=1, source_target_pairs={{0,1},{1,2},{2,3},{3,4},{4,5},{5,6},{6,7},{7,0},{8,9},{9,10},{10,1... | collective-permute-start | bytes 294920 | tf_op jit(solution)/shard_map/ppermute | solution.py:107
  62.3 6.7 %collective-permute-start.9 = (bf16[128,384]{1,0:T(8,128)(2,1)}, bf16[128,384]{1,0:T(8,128)(2,1)S(1)}, u32[]{:S(2)}, u32[]{:S(2)}) collective-permute-start(bf16[128,384]{1,0:T(8,128)(2,1)} %collective-permute-done.5), channel_id=1, source_target_pairs={{0,7},{1,0},{2,1},{3,2},{4,3},{5,4},{6,5},{7,6},{8,15},{9,8},{10,9... | collective-permute-start | bytes 294920 | tf_op jit(solution)/shard_map/ppermute | solution.py:110
  69.0 14.9 %collective-permute-start.13 = (bf16[192,1024]{1,0:T(8,128)(2,1)}, bf16[192,1024]{1,0:T(8,128)(2,1)S(1)}, u32[]{:S(2)}, u32[]{:S(2)}) collective-permute-start(bf16[192,1024]{1,0:T(8,128)(2,1)} %collective-permute-done.10.refs_5_), channel_id=1, source_target_pairs={{0,8},{8,16},{16,24},{24,32},{32,40},{40,48},{48,56},{56,0},{1,9},... | collective-permute-start | bytes 1179656 | tf_op jit(solution)/shard_map/ppermute | solution.py:107
  75.0 8.9 %collective-permute-start.12 = (bf16[128,384]{1,0:T(8,128)(2,1)S(1)}, bf16[128,384]{1,0:T(8,128)(2,1)S(1)}, u32[]{:S(2)}, u32[]{:S(2)}) collective-permute-start(bf16[128,384]{1,0:T(8,128)(2,1)S(1)} %collective-permute-done.8), channel_id=1, source_target_pairs={{0,1},{1,2},{2,3},{3,4},{4,5},{5,6},{6,7},{7,0},{8,9},{9,10},{10,1... | collective-permute-start | bytes 294920 | tf_op jit(solution)/shard_map/ppermute | solution.py:107
  83.9 1.1 copy-start.4
  85.9 0.9 copy-start.2
  107.1 15.2 %all-to-all-start = ((bf16[8,192,128]{2,1,0:T(8,128)(2,1)}), bf16[8,192,128]{2,1,0:T(8,128)(2,1)S(1)}, u32[]{:S(2)}, u32[]{:S(2)}) async-start(bf16[8,192,128]{2,1,0:T(8,128)(2,1)} %bitcast.105), calls=%async_computation | async-start | bytes 786432 | tf_op jit(solution)/shard_map/all_to_all | solution.py:134
  122.3 0.7 copy-start.1
  123.1 2.7 %copy-start.6 = (f32[1024]{0:T(1024)S(1)}, f32[1024]{0:T(1024)}, u32[]{:S(2)}) copy-start(f32[1024]{0:T(1024)} %param.13) | copy-start | bytes 12292
  179.3 3.3 %copy-start.8 = (bf16[1,512,1024]{2,1,0:T(8,128)(2,1)S(1)}, bf16[1,512,1024]{2,1,0:T(8,128)(2,1)}, u32[]{:S(2)}) copy-start(bf16[1,512,1024]{2,1,0:T(8,128)(2,1)} %param.17) | copy-start | bytes 3145732
  188.4 8.5 %copy-start.7 = (f32[1,192,2]{1,2,0:T(2,128)S(1)}, f32[1,192,2]{1,2,0:T(2,128)}, u32[]{:S(2)}) copy-start(f32[1,192,2]{1,2,0:T(2,128)} %param.15) | copy-start | bytes 4612
  188.4 47.8 %all-to-all-start.2 = ((bf16[64,96,128]{2,1,0:T(8,128)(2,1)}), bf16[64,96,128]{2,1,0:T(8,128)(2,1)}, u32[]{:S(2)}, u32[]{:S(2)}) async-start(bf16[64,96,128]{2,1,0:T(8,128)(2,1)} %reshape.74), calls=%async_computation.2 | async-start | bytes 3145728 | tf_op jit(solution)/shard_map/all_to_all | solution.py:165
Sparse Core Ops, SparseCore 0:
  10.4 88.4 all-gather.2

commit v10 on v9

--- a/solution.py
+++ b/solution.py
@@ -148,10 +148,10 @@
     earlier = jnp.cumsum(onehot, axis=0, dtype=jnp.int32) - onehot
     slots = jnp.sum(earlier * onehot, axis=1, dtype=jnp.int32)
     position = (pair_routes * capacity + slots).reshape(node_dev, TOP)
-    places = jnp.arange(experts * capacity, dtype=jnp.int32).reshape(experts, capacity)
-    select = (places[:, :, None, None] == position[None, None]).astype(jnp.bfloat16)
-    outgoing = jnp.einsum(
-        "ecn,nd->ecd", jnp.sum(select, axis=3), normed, preferred_element_type=jnp.float32
+    places = jnp.arange(experts * capacity, dtype=jnp.int32)
+    select = (places[:, None, None] == position[None]).astype(jnp.bfloat16)
+    outgoing = jnp.dot(
+        jnp.sum(select, axis=2), normed, preferred_element_type=jnp.float32
     ).astype(jnp.bfloat16)
     hidden_units = w_down.shape[1]
     lanes = 128
@@ -164,8 +164,8 @@
     processed = jnp.dot(hidden, w_down[0], preferred_element_type=jnp.float32).astype(jnp.bfloat16)
     returned = lax.all_to_all(
         processed.reshape(packed), ("seq", "exp"), split_axis=0, concat_axis=0, tiled=True
-    ).reshape(experts, capacity, width)
-    picked = jnp.einsum("ecnk,ecd->knd", select, returned, preferred_element_type=jnp.float32)
+    ).reshape(experts * capacity, width)
+    picked = jnp.einsum("pnk,pd->knd", select, returned, preferred_element_type=jnp.float32)
     expert_sum = picked[0] * gates[0][:, 0, None] + picked[1] * gates[0][:, 1, None]
     return (mixed + expert_sum).astype(jnp.bfloat16)[None]
 

time: 253 us -> 247 us (0.976)
  local copies, waits for them, and re-layouts: 30 us -> 26.4 us
    unnamed x26 -> x38, local copies, waits for them, and re-layouts: 6.25 us -> 6.27 us
  transfers between devices with their start and end apart: 17 -> 17, of which waited for: 8 -> 9; matrix products, arithmetic and copies ran while one was open for 6% -> 5% of each run, Pallas kernels for 8% -> 8%
where the time goes in v10:
time: 247 us; the launch traced here: 245 us
  starting transfers between devices  73.4 us (30%)
  waiting for transfers between devices  53 us (21%)
  blocking collectives  41.9 us (17%)
  local copies, waits for them, and re-layouts  26.4 us (11%)
  Pallas kernels  20.3 us (8%)
  between operations  13.7 us (6%)
  matrix products  12.2 us (5%)
  other arithmetic  4.29 us (2%)
    all_to_all x1, blocking collectives, per_device(): lax.all_to_all(outgoing.reshape(packed), ('seq', 'exp'), split_axis=0, co...  41.9 us
    all_to_all x1, waiting for transfers between devices, per_device(): lax.all_to_all(processed.reshape(packed), ('seq', 'exp'), split_axis=0, c...  38.6 us
    ppermute x8, starting transfers between devices, ring_gather(): moving[which][0] = lax.ppermute(moving[which][0], axis, right)  32.6 us
    ppermute x6, starting transfers between devices, ring_gather(): moving[which][1] = lax.ppermute(moving[which][1], axis, left)  24.3 us
    pallas_call x1, Pallas kernels, attention(): pl.pallas_call(kernel, out_shape=jax.ShapeDtypeStruct((nodes, heads * HEA...  20.3 us
    all_to_all x1, starting transfers between devices, per_device(): lax.all_to_all(processed.reshape(packed), ('seq', 'exp'), split_axis=0, c...  8.96 us
    all_to_all x1, starting transfers between devices, per_device(): lax.all_to_all(attended, 'seq', split_axis=0, concat_axis=1, tiled=True)  7.46 us
    unnamed x38, local copies, waits for them, and re-layouts  6.27 us
  transfers between devices with their start and end apart: 17, of which 9 were waited for; matrix products, arithmetic and copies ran while one was open for 5% of the time, Pallas kernels for 8%

profile of v10, /device:TPU:26, one launch (start us, length us, event | category | flops | bytes accessed | tf_op | source)
XLA Modules:
  0.0 245.1 jit_solution(1064329054070956871)
XLA Ops:
  7.3 4.7 %collective-permute-start.2 = (bf16[192,1024]{1,0:T(8,128)(2,1)}, bf16[192,1024]{1,0:T(8,128)(2,1)S(1)}, u32[]{:S(2)}, u32[]{:S(2)}) collective-permute-start(bf16[192,1024]{1,0:T(8,128)(2,1)} %bitcast.96), channel_id=1, source_target_pairs={{0,8},{8,16},{16,24},{24,32},{32,40},{40,48},{48,56},{56,0},{1,9},... | collective-permute-start | bytes 1179656 | tf_op jit(solution)/shard_map/ppermute | solution.py:107
  12.0 1.9 collective-permute-start.3
  13.9 4.3 %collective-permute-start = (bf16[128,384]{1,0:T(8,128)(2,1)}, bf16[128,384]{1,0:T(8,128)(2,1)S(1)}, u32[]{:S(2)}, u32[]{:S(2)}) collective-permute-start(bf16[128,384]{1,0:T(8,128)(2,1)} %param.11), channel_id=1, source_target_pairs={{0,1},{1,2},{2,3},{3,4},{4,5},{5,6},{6,7},{7,0},{8,9},{9,10},{10,1... | collective-permute-start | bytes 294920 | tf_op jit(solution)/shard_map/ppermute | solution.py:107
  18.2 8.6 %collective-permute-start.1 = (bf16[128,384]{1,0:T(8,128)(2,1)}, bf16[128,384]{1,0:T(8,128)(2,1)S(1)}, u32[]{:S(2)}, u32[]{:S(2)}) collective-permute-start(bf16[128,384]{1,0:T(8,128)(2,1)} %param.11), channel_id=1, source_target_pairs={{0,7},{1,0},{2,1},{3,2},{4,3},{5,4},{6,5},{7,6},{8,15},{9,8},{10,9... | collective-permute-start | bytes 294920 | tf_op jit(solution)/shard_map/ppermute | solution.py:110
  29.3 5.1 %collective-permute-start.6 = (bf16[192,1024]{1,0:T(8,128)(2,1)S(1)}, bf16[192,1024]{1,0:T(8,128)(2,1)}, u32[]{:S(2)}, u32[]{:S(2)}) collective-permute-start(bf16[192,1024]{1,0:T(8,128)(2,1)S(1)} %collective-permute-done.2.refs_7_), channel_id=1, source_target_pairs={{0,8},{8,16},{16,24},{24,32},{32,40},{40,48},{48,56},{56,0},{1,9},... | collective-permute-start | bytes 1179656 | tf_op jit(solution)/shard_map/ppermute | solution.py:107
  34.5 1.9 collective-permute-start.7
  36.4 1.9 collective-permute-start.4
  38.3 6.3 %collective-permute-start.5 = (bf16[128,384]{1,0:T(8,128)(2,1)S(1)}, bf16[128,384]{1,0:T(8,128)(2,1)S(1)}, u32[]{:S(2)}, u32[]{:S(2)}) collective-permute-start(bf16[128,384]{1,0:T(8,128)(2,1)S(1)} %collective-permute-done.1), channel_id=1, source_target_pairs={{0,7},{1,0},{2,1},{3,2},{4,3},{5,4},{6,5},{7,6},{8,15},{9,8},{10,9... | collective-permute-start | bytes 294920 | tf_op jit(solution)/shard_map/ppermute | solution.py:110
  47.3 3.8 %collective-permute-start.10 = (bf16[192,1024]{1,0:T(8,128)(2,1)}, bf16[192,1024]{1,0:T(8,128)(2,1)}, u32[]{:S(2)}, u32[]{:S(2)}) collective-permute-start(bf16[192,1024]{1,0:T(8,128)(2,1)} %collective-permute-done.6.refs_6_), channel_id=1, source_target_pairs={{0,8},{8,16},{16,24},{24,32},{32,40},{40,48},{48,56},{56,0},{1,9},... | collective-permute-start | bytes 1179656 | tf_op jit(solution)/shard_map/ppermute | solution.py:107
  51.1 2.1 collective-permute-start.11
  57.0 3.8 %collective-permute-start.8 = (bf16[128,384]{1,0:T(8,128)(2,1)}, bf16[128,384]{1,0:T(8,128)(2,1)S(1)}, u32[]{:S(2)}, u32[]{:S(2)}) collective-permute-start(bf16[128,384]{1,0:T(8,128)(2,1)} %copy-done.8), channel_id=1, source_target_pairs={{0,1},{1,2},{2,3},{3,4},{4,5},{5,6},{6,7},{7,0},{8,9},{9,10},{10,1... | collective-permute-start | bytes 294920 | tf_op jit(solution)/shard_map/ppermute | solution.py:107
  60.8 3.5 %collective-permute-start.9 = (bf16[128,384]{1,0:T(8,128)(2,1)}, bf16[128,384]{1,0:T(8,128)(2,1)S(1)}, u32[]{:S(2)}, u32[]{:S(2)}) collective-permute-start(bf16[128,384]{1,0:T(8,128)(2,1)} %copy-done.10), channel_id=1, source_target_pairs={{0,7},{1,0},{2,1},{3,2},{4,3},{5,4},{6,5},{7,6},{8,15},{9,8},{10,9... | collective-permute-start | bytes 294920 | tf_op jit(solution)/shard_map/ppermute | solution.py:110
  65.3 2.3 collective-permute-done.9
  67.5 5.1 %collective-permute-start.13 = (bf16[192,1024]{1,0:T(8,128)(2,1)}, bf16[192,1024]{1,0:T(8,128)(2,1)S(1)}, u32[]{:S(2)}, u32[]{:S(2)}) collective-permute-start(bf16[192,1024]{1,0:T(8,128)(2,1)} %collective-permute-done.10.refs_5_), channel_id=1, source_target_pairs={{0,8},{8,16},{16,24},{24,32},{32,40},{40,48},{48,56},{56,0},{1,9},... | collective-permute-start | bytes 1179656 | tf_op jit(solution)/shard_map/ppermute | solution.py:107
  73.6 3.9 %collective-permute-start.12 = (bf16[128,384]{1,0:T(8,128)(2,1)S(1)}, bf16[128,384]{1,0:T(8,128)(2,1)S(1)}, u32[]{:S(2)}, u32[]{:S(2)}) collective-permute-start(bf16[128,384]{1,0:T(8,128)(2,1)S(1)} %collective-permute-done.8), channel_id=1, source_target_pairs={{0,1},{1,2},{2,3},{3,4},{4,5},{5,6},{6,7},{7,0},{8,9},{9,10},{10,1... | collective-permute-start | bytes 294920 | tf_op jit(solution)/shard_map/ppermute | solution.py:107
  77.5 4.3 %collective-permute-done.12 = bf16[128,384]{1,0:T(8,128)(2,1)S(1)} collective-permute-done((bf16[128,384]{1,0:T(8,128)(2,1)S(1)}, bf16[128,384]{1,0:T(8,128)(2,1)S(1)}, u32[]{:S(2)}, u32[]{:S(2)}) %collective-permute-start.12) | collective-permute-done | bytes 98336 | tf_op jit(solution)/shard_map/ppermute | solution.py:107
  83.8 20.3 %shard_map.91 = bf16[1536,128]{1,0:T(8,128)(2,1)} custom-call(s32[2]{0:T(128)} %pad_add_fusion.me_ref, s32[144]{0:T(256)} %reshape_squeeze.4.mask_ref, bf16[192,1024]{1,0:T(8,128)(2,1)} %bitcast.98, bf16[192,1024]{1,0:T(8,128)(2,1)} %copy-done.6, bf16[192,1024]{1,0:T(8,128)(2,1)} %collective-permute-done.7.refs_2_, ...), custom_call_target="tpu_custom_call" | custom-call | tf_op jit(solution)/shard_map/pallas_call | solution.py:80
  104.1 7.5 %all-to-all-start = ((bf16[8,192,128]{2,1,0:T(8,128)(2,1)}), bf16[8,192,128]{2,1,0:T(8,128)(2,1)S(1)}, u32[]{:S(2)}, u32[]{:S(2)}) async-start(bf16[8,192,128]{2,1,0:T(8,128)(2,1)} %bitcast.95), calls=%async_computation | async-start | bytes 786432 | tf_op jit(solution)/shard_map/all_to_all | solution.py:134
  114.2 4.0 %copy.25 = bf16[8,8,128,128]{2,3,1,0:T(8,128)(2,1)} copy(bf16[8,8,128,128]{3,2,1,0:T(8,128)(2,1)} %bitcast.94) | data formatting | bytes 4194304 | tf_op jit(solution)/shard_map/reshape | solution.py:135
  118.1 1.9 all-to-all-done
  120.8 2.7 %multiply_reduce_fusion = (f32[192]{0:T(256)S(1)}, f32[192,1024]{1,0:T(8,128)S(1)}) fusion(bf16[1024,128,8]{1,0,2:T(8,128)(2,1)} %bitcast.93, bf16[8,192,128]{2,1,0:T(8,128)(2,1)} %copy-done.2, bf16[1,192,1024]{2,1,0:T(8,128)(2,1)S(1)} %copy-done.1), kind=kOutput, calls=%fused_computation.21 | convolution fusion | flops 403439424 | bytes 3670784 | tf_op jit(solution)/shard_map/nsk,sekc->nec/dot_general | solution.py:136
  123.5 1.8 convolution_convert_fusion.1
  125.3 3.7 %reshape.51 = bf16[64,96,128]{2,1,0:T(8,128)(2,1)} reshape(bf16[768,1024]{1,0:T(8,128)(2,1)} %convolution_convert_fusion.1) | data formatting | bytes 3145728 | tf_op jit(solution)/shard_map/reshape | solution.py:160
  129.0 41.9 %all_to_all.26 = bf16[64,96,128]{2,1,0:T(8,128)(2,1)} all-to-all(bf16[64,96,128]{2,1,0:T(8,128)(2,1)} %reshape.51), channel_id=1, replica_groups=mesh['sub'=8,'seq'=8,'exp'=8] {'seq','exp'}, dimensions={0} | all-to-all | bytes 3145728 | tf_op jit(solution)/shard_map/all_to_all | solution.py:159
  170.9 3.7 %reshape.52 = bf16[768,1024]{1,0:T(8,128)(2,1)} reshape(bf16[64,96,128]{2,1,0:T(8,128)(2,1)} %all_to_all.26) | data formatting | bytes 3145728 | tf_op jit(solution)/shard_map/reshape | solution.py:161
  174.7 3.3 %fusion = f32[768,1024]{1,0:T(8,128)S(1)} fusion(bf16[768,1024]{1,0:T(8,128)(2,1)} %reshape.52, bf16[1,1024,1024]{2,1,0:T(8,128)(2,1)S(1)} %copy-done), kind=kOutput, calls=%fused_computation | convolution fusion | flops 1610612736 | bytes 6815744 | tf_op jit(solution)/shard_map/dot_general | solution.py:162
  177.9 2.2 convolution_convert_fusion
  180.1 3.7 %reshape.53 = bf16[64,96,128]{2,1,0:T(8,128)(2,1)} reshape(bf16[768,1024]{1,0:T(8,128)(2,1)} %convolution_convert_fusion) | data formatting | bytes 3145728 | tf_op jit(solution)/shard_map/reshape | solution.py:166
  183.8 9.0 %all-to-all-start.2 = ((bf16[64,96,128]{2,1,0:T(8,128)(2,1)}), bf16[64,96,128]{2,1,0:T(8,128)(2,1)}, u32[]{:S(2)}, u32[]{:S(2)}) async-start(bf16[64,96,128]{2,1,0:T(8,128)(2,1)} %reshape.53), calls=%async_computation.2 | async-start | bytes 3145728 | tf_op jit(solution)/shard_map/all_to_all | solution.py:165
  192.8 38.6 %all-to-all-done.2 = bf16[64,96,128]{2,1,0:T(8,128)(2,1)} async-done(((bf16[64,96,128]{2,1,0:T(8,128)(2,1)}), bf16[64,96,128]{2,1,0:T(8,128)(2,1)}, u32[]{:S(2)}, u32[]{:S(2)}) %all-to-all-start.2) | async-done | bytes 1572896 | tf_op jit(solution)/shard_map/all_to_all | solution.py:165
  231.4 3.7 %reshape.58 = bf16[768,1024,1]{1,0,2:T(8,128)(2,1)} reshape(bf16[64,96,128]{2,1,0:T(8,128)(2,1)} %all-to-all-done.2) | data formatting | bytes 3145728 | tf_op jit(solution)/shard_map/reshape | solution.py:167
  235.1 2.2 convolution_bitcast_fusion
  (71 shorter events, 17.9 us)
Async XLA Ops:
  6.5 168.1 %copy-start = (bf16[1,1024,1024]{2,1,0:T(8,128)(2,1)S(1)}, bf16[1,1024,1024]{2,1,0:T(8,128)(2,1)}, u32[]{:S(2)}) copy-start(bf16[1,1024,1024]{2,1,0:T(8,128)(2,1)} %param.16) | copy-start | bytes 6291460
  6.5 107.6 %all-gather.3.cloned.1.call-start = ((), (), s32[]{:S(2)}) async-start(), calls=%async_computation.3 | async-start | bytes 2129920 | tf_op jit(solution)/shard_map/all_gather | solution.py:130
  7.3 22.0 %collective-permute-start.2 = (bf16[192,1024]{1,0:T(8,128)(2,1)}, bf16[192,1024]{1,0:T(8,128)(2,1)S(1)}, u32[]{:S(2)}, u32[]{:S(2)}) collective-permute-start(bf16[192,1024]{1,0:T(8,128)(2,1)} %bitcast.96), channel_id=1, source_target_pairs={{0,8},{8,16},{16,24},{24,32},{32,40},{40,48},{48,56},{56,0},{1,9},... | collective-permute-start | bytes 1179656 | tf_op jit(solution)/shard_map/ppermute | solution.py:107
  12.0 17.3 %collective-permute-start.3 = (bf16[192,1024]{1,0:T(8,128)(2,1)}, bf16[192,1024]{1,0:T(8,128)(2,1)S(1)}, u32[]{:S(2)}, u32[]{:S(2)}) collective-permute-start(bf16[192,1024]{1,0:T(8,128)(2,1)} %bitcast.97), channel_id=1, source_target_pairs={{0,56},{8,0},{16,8},{24,16},{32,24},{40,32},{48,40},{56,48},{1,57}... | collective-permute-start | bytes 1179656 | tf_op jit(solution)/shard_map/ppermute | solution.py:110
  13.9 13.7 %collective-permute-start = (bf16[128,384]{1,0:T(8,128)(2,1)}, bf16[128,384]{1,0:T(8,128)(2,1)S(1)}, u32[]{:S(2)}, u32[]{:S(2)}) collective-permute-start(bf16[128,384]{1,0:T(8,128)(2,1)} %param.11), channel_id=1, source_target_pairs={{0,1},{1,2},{2,3},{3,4},{4,5},{5,6},{6,7},{7,0},{8,9},{9,10},{10,1... | collective-permute-start | bytes 294920 | tf_op jit(solution)/shard_map/ppermute | solution.py:107
  18.2 11.1 %collective-permute-start.1 = (bf16[128,384]{1,0:T(8,128)(2,1)}, bf16[128,384]{1,0:T(8,128)(2,1)S(1)}, u32[]{:S(2)}, u32[]{:S(2)}) collective-permute-start(bf16[128,384]{1,0:T(8,128)(2,1)} %param.11), channel_id=1, source_target_pairs={{0,7},{1,0},{2,1},{3,2},{4,3},{5,4},{6,5},{7,6},{8,15},{9,8},{10,9... | collective-permute-start | bytes 294920 | tf_op jit(solution)/shard_map/ppermute | solution.py:110
  29.3 21.8 %copy-start.9 = (bf16[128,384]{1,0:T(8,128)(2,1)}, bf16[128,384]{1,0:T(8,128)(2,1)S(1)}, u32[]{:S(2)}) copy-start(bf16[128,384]{1,0:T(8,128)(2,1)S(1)} %collective-permute-done.1) | copy-start | bytes 294916
  29.3 53.7 %copy-start.5 = (bf16[192,1024]{1,0:T(8,128)(2,1)}, bf16[192,1024]{1,0:T(8,128)(2,1)S(1)}, u32[]{:S(2)}) copy-start(bf16[192,1024]{1,0:T(8,128)(2,1)S(1)} %collective-permute-done.2.refs_7_) | copy-start | bytes 1179652
  29.3 21.8 %copy-start.6 = (bf16[192,1024]{1,0:T(8,128)(2,1)}, bf16[192,1024]{1,0:T(8,128)(2,1)S(1)}, u32[]{:S(2)}) copy-start(bf16[192,1024]{1,0:T(8,128)(2,1)S(1)} %collective-permute-done.3.refs_1_) | copy-start | bytes 1179652
  29.3 17.5 %collective-permute-start.6 = (bf16[192,1024]{1,0:T(8,128)(2,1)S(1)}, bf16[192,1024]{1,0:T(8,128)(2,1)}, u32[]{:S(2)}, u32[]{:S(2)}) collective-permute-start(bf16[192,1024]{1,0:T(8,128)(2,1)S(1)} %collective-permute-done.2.refs_7_), channel_id=1, source_target_pairs={{0,8},{8,16},{16,24},{24,32},{32,40},{40,48},{48,56},{56,0},{1,9},... | collective-permute-start | bytes 1179656 | tf_op jit(solution)/shard_map/ppermute | solution.py:107
  34.5 12.9 %collective-permute-start.7 = (bf16[192,1024]{1,0:T(8,128)(2,1)S(1)}, bf16[192,1024]{1,0:T(8,128)(2,1)}, u32[]{:S(2)}, u32[]{:S(2)}) collective-permute-start(bf16[192,1024]{1,0:T(8,128)(2,1)S(1)} %collective-permute-done.3.refs_1_), channel_id=1, source_target_pairs={{0,56},{8,0},{16,8},{24,16},{32,24},{40,32},{48,40},{56,48},{1,57}... | collective-permute-start | bytes 1179656 | tf_op jit(solution)/shard_map/ppermute | solution.py:110
  36.4 8.9 %collective-permute-start.4 = (bf16[128,384]{1,0:T(8,128)(2,1)S(1)}, bf16[128,384]{1,0:T(8,128)(2,1)S(1)}, u32[]{:S(2)}, u32[]{:S(2)}) collective-permute-start(bf16[128,384]{1,0:T(8,128)(2,1)S(1)} %collective-permute-done), channel_id=1, source_target_pairs={{0,1},{1,2},{2,3},{3,4},{4,5},{5,6},{6,7},{7,0},{8,9},{9,10},{10,1... | collective-permute-start | bytes 294920 | tf_op jit(solution)/shard_map/ppermute | solution.py:107
  38.3 8.5 %collective-permute-start.5 = (bf16[128,384]{1,0:T(8,128)(2,1)S(1)}, bf16[128,384]{1,0:T(8,128)(2,1)S(1)}, u32[]{:S(2)}, u32[]{:S(2)}) collective-permute-start(bf16[128,384]{1,0:T(8,128)(2,1)S(1)} %collective-permute-done.1), channel_id=1, source_target_pairs={{0,7},{1,0},{2,1},{3,2},{4,3},{5,4},{6,5},{7,6},{8,15},{9,8},{10,9... | collective-permute-start | bytes 294920 | tf_op jit(solution)/shard_map/ppermute | solution.py:110
  45.3 5.8 %copy-start.8 = (bf16[128,384]{1,0:T(8,128)(2,1)}, bf16[128,384]{1,0:T(8,128)(2,1)S(1)}, u32[]{:S(2)}) copy-start(bf16[128,384]{1,0:T(8,128)(2,1)S(1)} %collective-permute-done.4) | copy-start | bytes 294916
  46.8 4.3 %copy-start.10 = (bf16[128,384]{1,0:T(8,128)(2,1)}, bf16[128,384]{1,0:T(8,128)(2,1)S(1)}, u32[]{:S(2)}) copy-start(bf16[128,384]{1,0:T(8,128)(2,1)S(1)} %collective-permute-done.5) | copy-start | bytes 294916
  47.3 20.2 %collective-permute-start.10 = (bf16[192,1024]{1,0:T(8,128)(2,1)}, bf16[192,1024]{1,0:T(8,128)(2,1)}, u32[]{:S(2)}, u32[]{:S(2)}) collective-permute-start(bf16[192,1024]{1,0:T(8,128)(2,1)} %collective-permute-done.6.refs_6_), channel_id=1, source_target_pairs={{0,8},{8,16},{16,24},{24,32},{32,40},{40,48},{48,56},{56,0},{1,9},... | collective-permute-start | bytes 1179656 | tf_op jit(solution)/shard_map/ppermute | solution.py:107
  51.1 16.4 %collective-permute-start.11 = (bf16[192,1024]{1,0:T(8,128)(2,1)}, bf16[192,1024]{1,0:T(8,128)(2,1)}, u32[]{:S(2)}, u32[]{:S(2)}) collective-permute-start(bf16[192,1024]{1,0:T(8,128)(2,1)} %collective-permute-done.7.refs_2_), channel_id=1, source_target_pairs={{0,56},{8,0},{16,8},{24,16},{32,24},{40,32},{48,40},{56,48},{1,57}... | collective-permute-start | bytes 1179656 | tf_op jit(solution)/shard_map/ppermute | solution.py:110
  57.0 8.3 %collective-permute-start.8 = (bf16[128,384]{1,0:T(8,128)(2,1)}, bf16[128,384]{1,0:T(8,128)(2,1)S(1)}, u32[]{:S(2)}, u32[]{:S(2)}) collective-permute-start(bf16[128,384]{1,0:T(8,128)(2,1)} %copy-done.8), channel_id=1, source_target_pairs={{0,1},{1,2},{2,3},{3,4},{4,5},{5,6},{6,7},{7,0},{8,9},{9,10},{10,1... | collective-permute-start | bytes 294920 | tf_op jit(solution)/shard_map/ppermute | solution.py:107
  60.8 6.7 %collective-permute-start.9 = (bf16[128,384]{1,0:T(8,128)(2,1)}, bf16[128,384]{1,0:T(8,128)(2,1)S(1)}, u32[]{:S(2)}, u32[]{:S(2)}) collective-permute-start(bf16[128,384]{1,0:T(8,128)(2,1)} %copy-done.10), channel_id=1, source_target_pairs={{0,7},{1,0},{2,1},{3,2},{4,3},{5,4},{6,5},{7,6},{8,15},{9,8},{10,9... | collective-permute-start | bytes 294920 | tf_op jit(solution)/shard_map/ppermute | solution.py:110
  67.5 14.3 %collective-permute-start.13 = (bf16[192,1024]{1,0:T(8,128)(2,1)}, bf16[192,1024]{1,0:T(8,128)(2,1)S(1)}, u32[]{:S(2)}, u32[]{:S(2)}) collective-permute-start(bf16[192,1024]{1,0:T(8,128)(2,1)} %collective-permute-done.10.refs_5_), channel_id=1, source_target_pairs={{0,8},{8,16},{16,24},{24,32},{32,40},{40,48},{48,56},{56,0},{1,9},... | collective-permute-start | bytes 1179656 | tf_op jit(solution)/shard_map/ppermute | solution.py:107
  73.6 8.2 %collective-permute-start.12 = (bf16[128,384]{1,0:T(8,128)(2,1)S(1)}, bf16[128,384]{1,0:T(8,128)(2,1)S(1)}, u32[]{:S(2)}, u32[]{:S(2)}) collective-permute-start(bf16[128,384]{1,0:T(8,128)(2,1)S(1)} %collective-permute-done.8), channel_id=1, source_target_pairs={{0,1},{1,2},{2,3},{3,4},{4,5},{5,6},{6,7},{7,0},{8,9},{9,10},{10,1... | collective-permute-start | bytes 294920 | tf_op jit(solution)/shard_map/ppermute | solution.py:107
  81.8 1.1 copy-start.7
  83.0 0.9 copy-start.4
  104.1 9.1 %copy-start.11 = (s32[1,192,2]{1,2,0:T(2,128)S(1)}, s32[1,192,2]{1,2,0:T(2,128)}, u32[]{:S(2)}) copy-start(s32[1,192,2]{1,2,0:T(2,128)} %param.14) | copy-start | bytes 4612
  104.1 15.9 %all-to-all-start = ((bf16[8,192,128]{2,1,0:T(8,128)(2,1)}), bf16[8,192,128]{2,1,0:T(8,128)(2,1)S(1)}, u32[]{:S(2)}, u32[]{:S(2)}) async-start(bf16[8,192,128]{2,1,0:T(8,128)(2,1)} %bitcast.95), calls=%async_computation | async-start | bytes 786432 | tf_op jit(solution)/shard_map/all_to_all | solution.py:134
  114.2 6.6 %copy-start.1 = (bf16[1,192,1024]{2,1,0:T(8,128)(2,1)S(1)}, bf16[1,192,1024]{2,1,0:T(8,128)(2,1)}, u32[]{:S(2)}) copy-start(bf16[1,192,1024]{2,1,0:T(8,128)(2,1)} %param.9) | copy-start | bytes 1179652
  120.0 0.7 copy-start.2
  120.8 2.7 %copy-start.3 = (bf16[768,192]{0,1:T(8,128)(2,1)S(1)}, bf16[768,192]{0,1:T(8,128)(2,1)}, u32[]{:S(2)}) copy-start(bf16[768,192]{0,1:T(8,128)(2,1)} %fusion.13) | copy-start | bytes 884740
  120.8 2.7 %copy-start.12 = (f32[1024]{0:T(1024)S(1)}, f32[1024]{0:T(1024)}, u32[]{:S(2)}) copy-start(f32[1024]{0:T(1024)} %param.13) | copy-start | bytes 12292
  174.6 3.3 %copy-start.14 = (bf16[1,512,1024]{2,1,0:T(8,128)(2,1)S(1)}, bf16[1,512,1024]{2,1,0:T(8,128)(2,1)}, u32[]{:S(2)}) copy-start(bf16[1,512,1024]{2,1,0:T(8,128)(2,1)} %param.17) | copy-start | bytes 3145732
  183.8 9.0 %copy-start.13 = (f32[1,192,2]{1,2,0:T(2,128)S(1)}, f32[1,192,2]{1,2,0:T(2,128)}, u32[]{:S(2)}) copy-start(f32[1,192,2]{1,2,0:T(2,128)} %param.15) | copy-start | bytes 4612
  183.8 47.6 %all-to-all-start.2 = ((bf16[64,96,128]{2,1,0:T(8,128)(2,1)}), bf16[64,96,128]{2,1,0:T(8,128)(2,1)}, u32[]{:S(2)}, u32[]{:S(2)}) async-start(bf16[64,96,128]{2,1,0:T(8,128)(2,1)} %reshape.53), calls=%async_computation.2 | async-start | bytes 3145728 | tf_op jit(solution)/shard_map/all_to_all | solution.py:165
Sparse Core Ops, SparseCore 0:
  10.4 88.0 all-gather.2

commit v11 on v10

--- a/solution.py
+++ b/solution.py
@@ -150,14 +150,17 @@
     position = (pair_routes * capacity + slots).reshape(node_dev, TOP)
     places = jnp.arange(experts * capacity, dtype=jnp.int32)
     select = (places[:, None, None] == position[None]).astype(jnp.bfloat16)
-    outgoing = jnp.dot(
-        jnp.sum(select, axis=2), normed, preferred_element_type=jnp.float32
-    ).astype(jnp.bfloat16)
-    hidden_units = w_down.shape[1]
     lanes = 128
     packed = (experts, capacity * width // lanes, lanes)
+    outgoing = jnp.einsum(
+        "pn,njl->pjl",
+        jnp.sum(select, axis=2),
+        normed.reshape(node_dev, width // lanes, lanes),
+        preferred_element_type=jnp.float32,
+    ).reshape(packed).astype(jnp.bfloat16)
+    hidden_units = w_down.shape[1]
     received = lax.all_to_all(
-        outgoing.reshape(packed), ("seq", "exp"), split_axis=0, concat_axis=0, tiled=True
+        outgoing, ("seq", "exp"), split_axis=0, concat_axis=0, tiled=True
     ).reshape(experts * capacity, width)
     both = jnp.dot(received, w_gate_up[0], preferred_element_type=jnp.float32)
     hidden = (jax.nn.silu(both[:, :hidden_units]) * both[:, hidden_units:]).astype(jnp.bfloat16)

time: 247 us -> 242 us (0.980)
  the two profiles are of different devices: /device:TPU:26 before, /device:TPU:22 now
where the time goes in v11:
time: 242 us; the launch traced here: 241 us
  starting transfers between devices  74.6 us (31%)
  waiting for transfers between devices  51.4 us (21%)
  blocking collectives  41.5 us (17%)
  local copies, waits for them, and re-layouts  23.7 us (10%)
  Pallas kernels  20.3 us (8%)
  between operations  13.8 us (6%)
  matrix products  11 us (5%)
  other arithmetic  4.29 us (2%)
    all_to_all x1, blocking collectives, per_device(): lax.all_to_all(outgoing, ('seq', 'exp'), split_axis=0, concat_axis=0, til...  41.5 us
    all_to_all x1, waiting for transfers between devices, per_device(): lax.all_to_all(processed.reshape(packed), ('seq', 'exp'), split_axis=0, c...  37.8 us
    ppermute x8, starting transfers between devices, ring_gather(): moving[which][0] = lax.ppermute(moving[which][0], axis, right)  29.6 us
    ppermute x6, starting transfers between devices, ring_gather(): moving[which][1] = lax.ppermute(moving[which][1], axis, left)  26.8 us
    pallas_call x1, Pallas kernels, attention(): pl.pallas_call(kernel, out_shape=jax.ShapeDtypeStruct((nodes, heads * HEA...  20.3 us
    all_to_all x1, starting transfers between devices, per_device(): lax.all_to_all(attended, 'seq', split_axis=0, concat_axis=1, tiled=True)  9.39 us
    all_to_all x1, starting transfers between devices, per_device(): lax.all_to_all(processed.reshape(packed), ('seq', 'exp'), split_axis=0, c...  8.73 us
    unnamed x38, local copies, waits for them, and re-layouts  6.27 us
  transfers between devices with their start and end apart: 17, of which 8 were waited for; matrix products, arithmetic and copies ran while one was open for 6% of the time, Pallas kernels for 8%

profile of v11, /device:TPU:22, one launch (start us, length us, event | category | flops | bytes accessed | tf_op | source)
XLA Modules:
  0.0 240.5 jit_solution(1079335305021347933)
XLA Ops:
  7.3 3.5 %collective-permute-start.2 = (bf16[192,1024]{1,0:T(8,128)(2,1)}, bf16[192,1024]{1,0:T(8,128)(2,1)S(1)}, u32[]{:S(2)}, u32[]{:S(2)}) collective-permute-start(bf16[192,1024]{1,0:T(8,128)(2,1)} %bitcast.107), channel_id=1, source_target_pairs={{0,8},{8,16},{16,24},{24,32},{32,40},{40,48},{48,56},{56,0},{1,9},... | collective-permute-start | bytes 1179656 | tf_op jit(solution)/shard_map/ppermute | solution.py:107
  10.8 2.4 collective-permute-start.3
  13.1 4.3 %collective-permute-start = (bf16[128,384]{1,0:T(8,128)(2,1)}, bf16[128,384]{1,0:T(8,128)(2,1)S(1)}, u32[]{:S(2)}, u32[]{:S(2)}) collective-permute-start(bf16[128,384]{1,0:T(8,128)(2,1)} %param.11), channel_id=1, source_target_pairs={{0,1},{1,2},{2,3},{3,4},{4,5},{5,6},{6,7},{7,0},{8,9},{9,10},{10,1... | collective-permute-start | bytes 294920 | tf_op jit(solution)/shard_map/ppermute | solution.py:107
  17.4 8.6 %collective-permute-start.1 = (bf16[128,384]{1,0:T(8,128)(2,1)}, bf16[128,384]{1,0:T(8,128)(2,1)S(1)}, u32[]{:S(2)}, u32[]{:S(2)}) collective-permute-start(bf16[128,384]{1,0:T(8,128)(2,1)} %param.11), channel_id=1, source_target_pairs={{0,7},{1,0},{2,1},{3,2},{4,3},{5,4},{6,5},{7,6},{8,15},{9,8},{10,9... | collective-permute-start | bytes 294920 | tf_op jit(solution)/shard_map/ppermute | solution.py:110
  26.9 1.6 collective-permute-done.1
  28.5 4.3 %collective-permute-start.6 = (bf16[192,1024]{1,0:T(8,128)(2,1)S(1)}, bf16[192,1024]{1,0:T(8,128)(2,1)}, u32[]{:S(2)}, u32[]{:S(2)}) collective-permute-start(bf16[192,1024]{1,0:T(8,128)(2,1)S(1)} %collective-permute-done.2.refs_7_), channel_id=1, source_target_pairs={{0,8},{8,16},{16,24},{24,32},{32,40},{40,48},{48,56},{56,0},{1,9},... | collective-permute-start | bytes 1179656 | tf_op jit(solution)/shard_map/ppermute | solution.py:107
  32.8 1.9 collective-permute-start.7
  34.7 1.9 collective-permute-start.4
  36.7 7.5 %collective-permute-start.5 = (bf16[128,384]{1,0:T(8,128)(2,1)S(1)}, bf16[128,384]{1,0:T(8,128)(2,1)S(1)}, u32[]{:S(2)}, u32[]{:S(2)}) collective-permute-start(bf16[128,384]{1,0:T(8,128)(2,1)S(1)} %collective-permute-done.1), channel_id=1, source_target_pairs={{0,7},{1,0},{2,1},{3,2},{4,3},{5,4},{6,5},{7,6},{8,15},{9,8},{10,9... | collective-permute-start | bytes 294920 | tf_op jit(solution)/shard_map/ppermute | solution.py:110
  44.9 1.4 collective-permute-done.5
  46.4 4.5 %collective-permute-start.10 = (bf16[192,1024]{1,0:T(8,128)(2,1)}, bf16[192,1024]{1,0:T(8,128)(2,1)}, u32[]{:S(2)}, u32[]{:S(2)}) collective-permute-start(bf16[192,1024]{1,0:T(8,128)(2,1)} %collective-permute-done.6.refs_6_), channel_id=1, source_target_pairs={{0,8},{8,16},{16,24},{24,32},{32,40},{40,48},{48,56},{56,0},{1,9},... | collective-permute-start | bytes 1179656 | tf_op jit(solution)/shard_map/ppermute | solution.py:107
  50.9 1.9 collective-permute-start.11
  56.6 2.7 %collective-permute-start.8 = (bf16[128,384]{1,0:T(8,128)(2,1)}, bf16[128,384]{1,0:T(8,128)(2,1)S(1)}, u32[]{:S(2)}, u32[]{:S(2)}) collective-permute-start(bf16[128,384]{1,0:T(8,128)(2,1)} %copy-done.8), channel_id=1, source_target_pairs={{0,1},{1,2},{2,3},{3,4},{4,5},{5,6},{6,7},{7,0},{8,9},{9,10},{10,1... | collective-permute-start | bytes 294920 | tf_op jit(solution)/shard_map/ppermute | solution.py:107
  59.3 4.6 %collective-permute-start.9 = (bf16[128,384]{1,0:T(8,128)(2,1)}, bf16[128,384]{1,0:T(8,128)(2,1)S(1)}, u32[]{:S(2)}, u32[]{:S(2)}) collective-permute-start(bf16[128,384]{1,0:T(8,128)(2,1)} %copy-done.10), channel_id=1, source_target_pairs={{0,7},{1,0},{2,1},{3,2},{4,3},{5,4},{6,5},{7,6},{8,15},{9,8},{10,9... | collective-permute-start | bytes 294920 | tf_op jit(solution)/shard_map/ppermute | solution.py:110
  64.8 1.6 collective-permute-done.9
  66.4 4.6 %collective-permute-start.13 = (bf16[192,1024]{1,0:T(8,128)(2,1)}, bf16[192,1024]{1,0:T(8,128)(2,1)S(1)}, u32[]{:S(2)}, u32[]{:S(2)}) collective-permute-start(bf16[192,1024]{1,0:T(8,128)(2,1)} %collective-permute-done.10.refs_5_), channel_id=1, source_target_pairs={{0,8},{8,16},{16,24},{24,32},{32,40},{40,48},{48,56},{56,0},{1,9},... | collective-permute-start | bytes 1179656 | tf_op jit(solution)/shard_map/ppermute | solution.py:107
  71.9 3.9 %collective-permute-start.12 = (bf16[128,384]{1,0:T(8,128)(2,1)S(1)}, bf16[128,384]{1,0:T(8,128)(2,1)S(1)}, u32[]{:S(2)}, u32[]{:S(2)}) collective-permute-start(bf16[128,384]{1,0:T(8,128)(2,1)S(1)} %collective-permute-done.8), channel_id=1, source_target_pairs={{0,1},{1,2},{2,3},{3,4},{4,5},{5,6},{6,7},{7,0},{8,9},{9,10},{10,1... | collective-permute-start | bytes 294920 | tf_op jit(solution)/shard_map/ppermute | solution.py:107
  75.9 4.1 %collective-permute-done.12 = bf16[128,384]{1,0:T(8,128)(2,1)S(1)} collective-permute-done((bf16[128,384]{1,0:T(8,128)(2,1)S(1)}, bf16[128,384]{1,0:T(8,128)(2,1)S(1)}, u32[]{:S(2)}, u32[]{:S(2)}) %collective-permute-start.12) | collective-permute-done | bytes 98336 | tf_op jit(solution)/shard_map/ppermute | solution.py:107
  82.0 20.3 %shard_map.91 = bf16[1536,128]{1,0:T(8,128)(2,1)} custom-call(s32[2]{0:T(128)} %pad_add_fusion.me_ref, s32[144]{0:T(256)} %reshape_squeeze.4.mask_ref, bf16[192,1024]{1,0:T(8,128)(2,1)} %bitcast.109, bf16[192,1024]{1,0:T(8,128)(2,1)} %copy-done.6, bf16[192,1024]{1,0:T(8,128)(2,1)} %collective-permute-done.7.refs_2_, ...), custom_call_target="tpu_custom_call" | custom-call | tf_op jit(solution)/shard_map/pallas_call | solution.py:80
  102.3 9.4 %all-to-all-start = ((bf16[8,192,128]{2,1,0:T(8,128)(2,1)}), bf16[8,192,128]{2,1,0:T(8,128)(2,1)S(1)}, u32[]{:S(2)}, u32[]{:S(2)}) async-start(bf16[8,192,128]{2,1,0:T(8,128)(2,1)} %bitcast.106), calls=%async_computation | async-start | bytes 786432 | tf_op jit(solution)/shard_map/all_to_all | solution.py:134
  114.3 4.0 %copy.21 = bf16[8,8,128,128]{2,3,1,0:T(8,128)(2,1)} copy(bf16[8,8,128,128]{3,2,1,0:T(8,128)(2,1)} %bitcast.105) | data formatting | bytes 4194304 | tf_op jit(solution)/shard_map/reshape | solution.py:135
  118.3 2.5 %all-to-all-done = bf16[8,192,128]{2,1,0:T(8,128)(2,1)S(1)} async-done(((bf16[8,192,128]{2,1,0:T(8,128)(2,1)}), bf16[8,192,128]{2,1,0:T(8,128)(2,1)S(1)}, u32[]{:S(2)}, u32[]{:S(2)}) %all-to-all-start) | async-done | bytes 393248 | tf_op jit(solution)/shard_map/all_to_all | solution.py:134
  121.5 2.7 %multiply_reduce_fusion = (f32[192]{0:T(256)S(1)}, f32[192,1024]{1,0:T(8,128)S(1)}) fusion(bf16[1024,128,8]{1,0,2:T(8,128)(2,1)} %bitcast.103, bf16[8,192,128]{2,1,0:T(8,128)(2,1)} %copy-done.2, bf16[1,192,1024]{2,1,0:T(8,128)(2,1)S(1)} %copy-done.1), kind=kOutput, calls=%fused_computation.21 | convolution fusion | flops 403439424 | bytes 3670784 | tf_op jit(solution)/shard_map/nsk,sekc->nec/dot_general | solution.py:136
  125.9 41.5 %all_to_all.26 = bf16[64,96,128]{2,1,0:T(8,128)(2,1)} all-to-all(bf16[64,96,128]{2,1,0:T(8,128)(2,1)S(1)} %bitcast.104), channel_id=1, replica_groups=mesh['sub'=8,'seq'=8,'exp'=8] {'seq','exp'}, dimensions={0} | all-to-all | bytes 3145728 | tf_op jit(solution)/shard_map/all_to_all | solution.py:162
  167.4 3.7 %reshape.54 = bf16[768,1024]{1,0:T(8,128)(2,1)} reshape(bf16[64,96,128]{2,1,0:T(8,128)(2,1)} %all_to_all.26) | data formatting | bytes 3145728 | tf_op jit(solution)/shard_map/reshape | solution.py:164
  171.1 3.3 %fusion = f32[768,1024]{1,0:T(8,128)S(1)} fusion(bf16[768,1024]{1,0:T(8,128)(2,1)} %reshape.54, bf16[1,1024,1024]{2,1,0:T(8,128)(2,1)S(1)} %copy-done), kind=kOutput, calls=%fused_computation | convolution fusion | flops 1610612736 | bytes 6815744 | tf_op jit(solution)/shard_map/dot_general | solution.py:165
  174.4 2.2 convolution_convert_fusion
  176.6 3.7 %reshape.55 = bf16[64,96,128]{2,1,0:T(8,128)(2,1)} reshape(bf16[768,1024]{1,0:T(8,128)(2,1)} %convolution_convert_fusion) | data formatting | bytes 3145728 | tf_op jit(solution)/shard_map/reshape | solution.py:169
  180.3 8.7 %all-to-all-start.2 = ((bf16[64,96,128]{2,1,0:T(8,128)(2,1)}), bf16[64,96,128]{2,1,0:T(8,128)(2,1)}, u32[]{:S(2)}, u32[]{:S(2)}) async-start(bf16[64,96,128]{2,1,0:T(8,128)(2,1)} %reshape.55), calls=%async_computation.2 | async-start | bytes 3145728 | tf_op jit(solution)/shard_map/all_to_all | solution.py:168
  189.0 37.8 %all-to-all-done.2 = bf16[64,96,128]{2,1,0:T(8,128)(2,1)} async-done(((bf16[64,96,128]{2,1,0:T(8,128)(2,1)}), bf16[64,96,128]{2,1,0:T(8,128)(2,1)}, u32[]{:S(2)}, u32[]{:S(2)}) %all-to-all-start.2) | async-done | bytes 1572896 | tf_op jit(solution)/shard_map/all_to_all | solution.py:168
  226.8 3.7 %reshape.61 = bf16[768,1024,1]{1,0,2:T(8,128)(2,1)} reshape(bf16[64,96,128]{2,1,0:T(8,128)(2,1)} %all-to-all-done.2) | data formatting | bytes 3145728 | tf_op jit(solution)/shard_map/reshape | solution.py:170
  230.5 2.2 convolution_bitcast_fusion
  (71 shorter events, 15.9 us)
Async XLA Ops:
  6.5 164.6 %copy-start = (bf16[1,1024,1024]{2,1,0:T(8,128)(2,1)S(1)}, bf16[1,1024,1024]{2,1,0:T(8,128)(2,1)}, u32[]{:S(2)}) copy-start(bf16[1,1024,1024]{2,1,0:T(8,128)(2,1)} %param.16) | copy-start | bytes 6291460
  6.5 107.8 %all-gather.3.cloned.1.call-start = ((), (), s32[]{:S(2)}) async-start(), calls=%async_computation.3 | async-start | bytes 2129920 | tf_op jit(solution)/shard_map/all_gather | solution.py:130
  7.3 21.3 %collective-permute-start.2 = (bf16[192,1024]{1,0:T(8,128)(2,1)}, bf16[192,1024]{1,0:T(8,128)(2,1)S(1)}, u32[]{:S(2)}, u32[]{:S(2)}) collective-permute-start(bf16[192,1024]{1,0:T(8,128)(2,1)} %bitcast.107), channel_id=1, source_target_pairs={{0,8},{8,16},{16,24},{24,32},{32,40},{40,48},{48,56},{56,0},{1,9},... | collective-permute-start | bytes 1179656 | tf_op jit(solution)/shard_map/ppermute | solution.py:107
  10.8 17.8 %collective-permute-start.3 = (bf16[192,1024]{1,0:T(8,128)(2,1)}, bf16[192,1024]{1,0:T(8,128)(2,1)S(1)}, u32[]{:S(2)}, u32[]{:S(2)}) collective-permute-start(bf16[192,1024]{1,0:T(8,128)(2,1)} %bitcast.108), channel_id=1, source_target_pairs={{0,56},{8,0},{16,8},{24,16},{32,24},{40,32},{48,40},{56,48},{1,57}... | collective-permute-start | bytes 1179656 | tf_op jit(solution)/shard_map/ppermute | solution.py:110
  13.1 13.7 %collective-permute-start = (bf16[128,384]{1,0:T(8,128)(2,1)}, bf16[128,384]{1,0:T(8,128)(2,1)S(1)}, u32[]{:S(2)}, u32[]{:S(2)}) collective-permute-start(bf16[128,384]{1,0:T(8,128)(2,1)} %param.11), channel_id=1, source_target_pairs={{0,1},{1,2},{2,3},{3,4},{4,5},{5,6},{6,7},{7,0},{8,9},{9,10},{10,1... | collective-permute-start | bytes 294920 | tf_op jit(solution)/shard_map/ppermute | solution.py:107
  17.4 11.1 %collective-permute-start.1 = (bf16[128,384]{1,0:T(8,128)(2,1)}, bf16[128,384]{1,0:T(8,128)(2,1)S(1)}, u32[]{:S(2)}, u32[]{:S(2)}) collective-permute-start(bf16[128,384]{1,0:T(8,128)(2,1)} %param.11), channel_id=1, source_target_pairs={{0,7},{1,0},{2,1},{3,2},{4,3},{5,4},{6,5},{7,6},{8,15},{9,8},{10,9... | collective-permute-start | bytes 294920 | tf_op jit(solution)/shard_map/ppermute | solution.py:110
  28.5 22.3 %copy-start.9 = (bf16[128,384]{1,0:T(8,128)(2,1)}, bf16[128,384]{1,0:T(8,128)(2,1)S(1)}, u32[]{:S(2)}) copy-start(bf16[128,384]{1,0:T(8,128)(2,1)S(1)} %collective-permute-done.1) | copy-start | bytes 294916
  28.5 52.6 %copy-start.5 = (bf16[192,1024]{1,0:T(8,128)(2,1)}, bf16[192,1024]{1,0:T(8,128)(2,1)S(1)}, u32[]{:S(2)}) copy-start(bf16[192,1024]{1,0:T(8,128)(2,1)S(1)} %collective-permute-done.2.refs_7_) | copy-start | bytes 1179652
  28.5 22.3 %copy-start.6 = (bf16[192,1024]{1,0:T(8,128)(2,1)}, bf16[192,1024]{1,0:T(8,128)(2,1)S(1)}, u32[]{:S(2)}) copy-start(bf16[192,1024]{1,0:T(8,128)(2,1)S(1)} %collective-permute-done.3.refs_1_) | copy-start | bytes 1179652
  28.5 17.8 %collective-permute-start.6 = (bf16[192,1024]{1,0:T(8,128)(2,1)S(1)}, bf16[192,1024]{1,0:T(8,128)(2,1)}, u32[]{:S(2)}, u32[]{:S(2)}) collective-permute-start(bf16[192,1024]{1,0:T(8,128)(2,1)S(1)} %collective-permute-done.2.refs_7_), channel_id=1, source_target_pairs={{0,8},{8,16},{16,24},{24,32},{32,40},{40,48},{48,56},{56,0},{1,9},... | collective-permute-start | bytes 1179656 | tf_op jit(solution)/shard_map/ppermute | solution.py:107
  32.8 13.5 %collective-permute-start.7 = (bf16[192,1024]{1,0:T(8,128)(2,1)S(1)}, bf16[192,1024]{1,0:T(8,128)(2,1)}, u32[]{:S(2)}, u32[]{:S(2)}) collective-permute-start(bf16[192,1024]{1,0:T(8,128)(2,1)S(1)} %collective-permute-done.3.refs_1_), channel_id=1, source_target_pairs={{0,56},{8,0},{16,8},{24,16},{32,24},{40,32},{48,40},{56,48},{1,57}... | collective-permute-start | bytes 1179656 | tf_op jit(solution)/shard_map/ppermute | solution.py:110
  34.7 10.2 %collective-permute-start.4 = (bf16[128,384]{1,0:T(8,128)(2,1)S(1)}, bf16[128,384]{1,0:T(8,128)(2,1)S(1)}, u32[]{:S(2)}, u32[]{:S(2)}) collective-permute-start(bf16[128,384]{1,0:T(8,128)(2,1)S(1)} %collective-permute-done), channel_id=1, source_target_pairs={{0,1},{1,2},{2,3},{3,4},{4,5},{5,6},{6,7},{7,0},{8,9},{9,10},{10,1... | collective-permute-start | bytes 294920 | tf_op jit(solution)/shard_map/ppermute | solution.py:107
  36.7 9.7 %collective-permute-start.5 = (bf16[128,384]{1,0:T(8,128)(2,1)S(1)}, bf16[128,384]{1,0:T(8,128)(2,1)S(1)}, u32[]{:S(2)}, u32[]{:S(2)}) collective-permute-start(bf16[128,384]{1,0:T(8,128)(2,1)S(1)} %collective-permute-done.1), channel_id=1, source_target_pairs={{0,7},{1,0},{2,1},{3,2},{4,3},{5,4},{6,5},{7,6},{8,15},{9,8},{10,9... | collective-permute-start | bytes 294920 | tf_op jit(solution)/shard_map/ppermute | solution.py:110
  44.9 6.0 %copy-start.8 = (bf16[128,384]{1,0:T(8,128)(2,1)}, bf16[128,384]{1,0:T(8,128)(2,1)S(1)}, u32[]{:S(2)}) copy-start(bf16[128,384]{1,0:T(8,128)(2,1)S(1)} %collective-permute-done.4) | copy-start | bytes 294916
  46.3 4.5 %copy-start.10 = (bf16[128,384]{1,0:T(8,128)(2,1)}, bf16[128,384]{1,0:T(8,128)(2,1)S(1)}, u32[]{:S(2)}) copy-start(bf16[128,384]{1,0:T(8,128)(2,1)S(1)} %collective-permute-done.5) | copy-start | bytes 294916
  46.4 20.0 %collective-permute-start.10 = (bf16[192,1024]{1,0:T(8,128)(2,1)}, bf16[192,1024]{1,0:T(8,128)(2,1)}, u32[]{:S(2)}, u32[]{:S(2)}) collective-permute-start(bf16[192,1024]{1,0:T(8,128)(2,1)} %collective-permute-done.6.refs_6_), channel_id=1, source_target_pairs={{0,8},{8,16},{16,24},{24,32},{32,40},{40,48},{48,56},{56,0},{1,9},... | collective-permute-start | bytes 1179656 | tf_op jit(solution)/shard_map/ppermute | solution.py:107
  50.9 15.5 %collective-permute-start.11 = (bf16[192,1024]{1,0:T(8,128)(2,1)}, bf16[192,1024]{1,0:T(8,128)(2,1)}, u32[]{:S(2)}, u32[]{:S(2)}) collective-permute-start(bf16[192,1024]{1,0:T(8,128)(2,1)} %collective-permute-done.7.refs_2_), channel_id=1, source_target_pairs={{0,56},{8,0},{16,8},{24,16},{32,24},{40,32},{48,40},{56,48},{1,57}... | collective-permute-start | bytes 1179656 | tf_op jit(solution)/shard_map/ppermute | solution.py:110
  56.6 8.2 %collective-permute-start.8 = (bf16[128,384]{1,0:T(8,128)(2,1)}, bf16[128,384]{1,0:T(8,128)(2,1)S(1)}, u32[]{:S(2)}, u32[]{:S(2)}) collective-permute-start(bf16[128,384]{1,0:T(8,128)(2,1)} %copy-done.8), channel_id=1, source_target_pairs={{0,1},{1,2},{2,3},{3,4},{4,5},{5,6},{6,7},{7,0},{8,9},{9,10},{10,1... | collective-permute-start | bytes 294920 | tf_op jit(solution)/shard_map/ppermute | solution.py:107
  59.3 7.1 %collective-permute-start.9 = (bf16[128,384]{1,0:T(8,128)(2,1)}, bf16[128,384]{1,0:T(8,128)(2,1)S(1)}, u32[]{:S(2)}, u32[]{:S(2)}) collective-permute-start(bf16[128,384]{1,0:T(8,128)(2,1)} %copy-done.10), channel_id=1, source_target_pairs={{0,7},{1,0},{2,1},{3,2},{4,3},{5,4},{6,5},{7,6},{8,15},{9,8},{10,9... | collective-permute-start | bytes 294920 | tf_op jit(solution)/shard_map/ppermute | solution.py:110
  66.4 13.6 %collective-permute-start.13 = (bf16[192,1024]{1,0:T(8,128)(2,1)}, bf16[192,1024]{1,0:T(8,128)(2,1)S(1)}, u32[]{:S(2)}, u32[]{:S(2)}) collective-permute-start(bf16[192,1024]{1,0:T(8,128)(2,1)} %collective-permute-done.10.refs_5_), channel_id=1, source_target_pairs={{0,8},{8,16},{16,24},{24,32},{32,40},{40,48},{48,56},{56,0},{1,9},... | collective-permute-start | bytes 1179656 | tf_op jit(solution)/shard_map/ppermute | solution.py:107
  71.9 8.1 %collective-permute-start.12 = (bf16[128,384]{1,0:T(8,128)(2,1)S(1)}, bf16[128,384]{1,0:T(8,128)(2,1)S(1)}, u32[]{:S(2)}, u32[]{:S(2)}) collective-permute-start(bf16[128,384]{1,0:T(8,128)(2,1)S(1)} %collective-permute-done.8), channel_id=1, source_target_pairs={{0,1},{1,2},{2,3},{3,4},{4,5},{5,6},{6,7},{7,0},{8,9},{9,10},{10,1... | collective-permute-start | bytes 294920 | tf_op jit(solution)/shard_map/ppermute | solution.py:107
  80.0 1.1 copy-start.7
  81.1 0.9 copy-start.4
  102.3 11.1 %copy-start.11 = (s32[1,192,2]{1,2,0:T(2,128)S(1)}, s32[1,192,2]{1,2,0:T(2,128)}, u32[]{:S(2)}) copy-start(s32[1,192,2]{1,2,0:T(2,128)} %param.14) | copy-start | bytes 4612
  102.3 18.4 %all-to-all-start = ((bf16[8,192,128]{2,1,0:T(8,128)(2,1)}), bf16[8,192,128]{2,1,0:T(8,128)(2,1)S(1)}, u32[]{:S(2)}, u32[]{:S(2)}) async-start(bf16[8,192,128]{2,1,0:T(8,128)(2,1)} %bitcast.106), calls=%async_computation | async-start | bytes 786432 | tf_op jit(solution)/shard_map/all_to_all | solution.py:134
  114.3 7.2 %copy-start.1 = (bf16[1,192,1024]{2,1,0:T(8,128)(2,1)S(1)}, bf16[1,192,1024]{2,1,0:T(8,128)(2,1)}, u32[]{:S(2)}) copy-start(bf16[1,192,1024]{2,1,0:T(8,128)(2,1)} %param.9) | copy-start | bytes 1179652
  120.8 0.7 copy-start.2
  121.5 2.7 %copy-start.3 = (bf16[768,192]{0,1:T(8,128)(2,1)S(1)}, bf16[768,192]{0,1:T(8,128)(2,1)}, u32[]{:S(2)}) copy-start(bf16[768,192]{0,1:T(8,128)(2,1)} %fusion.13) | copy-start | bytes 884740
  121.5 2.7 %copy-start.12 = (f32[1024]{0:T(1024)S(1)}, f32[1024]{0:T(1024)}, u32[]{:S(2)}) copy-start(f32[1024]{0:T(1024)} %param.13) | copy-start | bytes 12292
  171.1 3.3 %copy-start.14 = (bf16[1,512,1024]{2,1,0:T(8,128)(2,1)S(1)}, bf16[1,512,1024]{2,1,0:T(8,128)(2,1)}, u32[]{:S(2)}) copy-start(bf16[1,512,1024]{2,1,0:T(8,128)(2,1)} %param.17) | copy-start | bytes 3145732
  180.3 8.7 %copy-start.13 = (f32[1,192,2]{1,2,0:T(2,128)S(1)}, f32[1,192,2]{1,2,0:T(2,128)}, u32[]{:S(2)}) copy-start(f32[1,192,2]{1,2,0:T(2,128)} %param.15) | copy-start | bytes 4612
  180.3 46.5 %all-to-all-start.2 = ((bf16[64,96,128]{2,1,0:T(8,128)(2,1)}), bf16[64,96,128]{2,1,0:T(8,128)(2,1)}, u32[]{:S(2)}, u32[]{:S(2)}) async-start(bf16[64,96,128]{2,1,0:T(8,128)(2,1)} %reshape.55), calls=%async_computation.2 | async-start | bytes 3145728 | tf_op jit(solution)/shard_map/all_to_all | solution.py:168
Sparse Core Ops, SparseCore 0:
  10.4 88.4 all-gather.2

commit v12 on v11

--- a/solution.py
+++ b/solution.py
@@ -161,14 +161,26 @@
     hidden_units = w_down.shape[1]
     received = lax.all_to_all(
         outgoing, ("seq", "exp"), split_axis=0, concat_axis=0, tiled=True
-    ).reshape(experts * capacity, width)
-    both = jnp.dot(received, w_gate_up[0], preferred_element_type=jnp.float32)
+    ).reshape(experts * capacity, width // lanes, lanes)
+    both = jnp.einsum(
+        "pjl,jlf->pf",
+        received,
+        w_gate_up[0].reshape(width // lanes, lanes, -1),
+        preferred_element_type=jnp.float32,
+    )
     hidden = (jax.nn.silu(both[:, :hidden_units]) * both[:, hidden_units:]).astype(jnp.bfloat16)
-    processed = jnp.dot(hidden, w_down[0], preferred_element_type=jnp.float32).astype(jnp.bfloat16)
+    processed = jnp.einsum(
+        "pf,fjl->pjl",
+        hidden,
+        w_down[0].reshape(hidden_units, width // lanes, lanes),
+        preferred_element_type=jnp.float32,
+    ).astype(jnp.bfloat16)
     returned = lax.all_to_all(
         processed.reshape(packed), ("seq", "exp"), split_axis=0, concat_axis=0, tiled=True
-    ).reshape(experts * capacity, width)
-    picked = jnp.einsum("pnk,pd->knd", select, returned, preferred_element_type=jnp.float32)
+    ).reshape(experts * capacity, width // lanes, lanes)
+    picked = jnp.einsum(
+        "pnk,pjl->knjl", select, returned, preferred_element_type=jnp.float32
+    ).reshape(TOP, node_dev, width)
     expert_sum = picked[0] * gates[0][:, 0, None] + picked[1] * gates[0][:, 1, None]
     return (mixed + expert_sum).astype(jnp.bfloat16)[None]
 

time: 242 us -> 234 us (0.967)
  blocking collectives: 41.5 us -> 0 us
  waiting for transfers between devices: 51.4 us -> 81.5 us
  starting transfers between devices: 74.6 us -> 83.7 us
  local copies, waits for them, and re-layouts: 23.7 us -> 19.5 us
    all_to_all x1 -> x0, blocking collectives: 41.5 us -> none  [per_device(): lax.all_to_all(outgoing, ('seq', 'exp'), split_axis=0, concat_axis=0, til...]
    all_to_all x0 -> x1, waiting for transfers between devices: none -> 30 us  [per_device(): lax.all_to_all(outgoing, ('seq', 'exp'), split_axis=0, concat_axis=0, til...]
    reshape x3 -> x0, local copies, waits for them, and re-layouts: 11.1 us -> none  [the longest x1 3.69 us: per_device(): received = lax.all_to_all(outgoing, ('seq', 'exp'), split_axis=0, concat_...]
    all_to_all x0 -> x1, starting transfers between devices: none -> 9.13 us  [per_device(): lax.all_to_all(outgoing, ('seq', 'exp'), split_axis=0, concat_axis=0, til...]
    unnamed x38 -> x39, local copies, waits for them, and re-layouts: 6.27 us -> 8.77 us
  transfers between devices with their start and end apart: 17 -> 18, of which waited for: 8 -> 9; matrix products, arithmetic and copies ran while one was open for 6% -> 7% of each run, Pallas kernels for 8% -> 9%
where the time goes in v12:
time: 234 us; the launch traced here: 233 us
  starting transfers between devices  83.7 us (36%)
  waiting for transfers between devices  81.5 us (35%)
  Pallas kernels  20.3 us (9%)
  local copies, waits for them, and re-layouts  19.5 us (8%)
  between operations  13.8 us (6%)
  matrix products  9.91 us (4%)
  other arithmetic  4.41 us (2%)
    all_to_all x1, waiting for transfers between devices, per_device(): lax.all_to_all(processed.reshape(packed), ('seq', 'exp'), split_axis=0, c...  37.9 us
    all_to_all x1, waiting for transfers between devices, per_device(): lax.all_to_all(outgoing, ('seq', 'exp'), split_axis=0, concat_axis=0, til...  30 us
    ppermute x8, starting transfers between devices, ring_gather(): moving[which][0] = lax.ppermute(moving[which][0], axis, right)  29.6 us
    ppermute x6, starting transfers between devices, ring_gather(): moving[which][1] = lax.ppermute(moving[which][1], axis, left)  26.8 us
    pallas_call x1, Pallas kernels, attention(): pl.pallas_call(kernel, out_shape=jax.ShapeDtypeStruct((nodes, heads * HEA...  20.3 us
    all_to_all x1, starting transfers between devices, per_device(): lax.all_to_all(attended, 'seq', split_axis=0, concat_axis=1, tiled=True)  9.4 us
    all_to_all x1, starting transfers between devices, per_device(): lax.all_to_all(outgoing, ('seq', 'exp'), split_axis=0, concat_axis=0, til...  9.13 us
    unnamed x39, local copies, waits for them, and re-layouts  8.77 us
  transfers between devices with their start and end apart: 18, of which 9 were waited for; matrix products, arithmetic and copies ran while one was open for 7% of the time, Pallas kernels for 9%

profile of v12, /device:TPU:22, one launch (start us, length us, event | category | flops | bytes accessed | tf_op | source)
XLA Modules:
  0.0 233.2 jit_solution(3875231749400983111)
XLA Ops:
  7.3 3.5 %collective-permute-start.2 = (bf16[192,1024]{1,0:T(8,128)(2,1)}, bf16[192,1024]{1,0:T(8,128)(2,1)S(1)}, u32[]{:S(2)}, u32[]{:S(2)}) collective-permute-start(bf16[192,1024]{1,0:T(8,128)(2,1)} %bitcast.121), channel_id=1, source_target_pairs={{0,8},{8,16},{16,24},{24,32},{32,40},{40,48},{48,56},{56,0},{1,9},... | collective-permute-start | bytes 1179656 | tf_op jit(solution)/shard_map/ppermute | solution.py:107
  10.8 2.4 %collective-permute-start.3 = (bf16[192,1024]{1,0:T(8,128)(2,1)}, bf16[192,1024]{1,0:T(8,128)(2,1)S(1)}, u32[]{:S(2)}, u32[]{:S(2)}) collective-permute-start(bf16[192,1024]{1,0:T(8,128)(2,1)} %bitcast.122), channel_id=1, source_target_pairs={{0,56},{8,0},{16,8},{24,16},{32,24},{40,32},{48,40},{56,48},{1,57}... | collective-permute-start | bytes 1179656 | tf_op jit(solution)/shard_map/ppermute | solution.py:110
  13.1 4.3 %collective-permute-start = (bf16[128,384]{1,0:T(8,128)(2,1)}, bf16[128,384]{1,0:T(8,128)(2,1)S(1)}, u32[]{:S(2)}, u32[]{:S(2)}) collective-permute-start(bf16[128,384]{1,0:T(8,128)(2,1)} %param.11), channel_id=1, source_target_pairs={{0,1},{1,2},{2,3},{3,4},{4,5},{5,6},{6,7},{7,0},{8,9},{9,10},{10,1... | collective-permute-start | bytes 294920 | tf_op jit(solution)/shard_map/ppermute | solution.py:107
  17.4 8.6 %collective-permute-start.1 = (bf16[128,384]{1,0:T(8,128)(2,1)}, bf16[128,384]{1,0:T(8,128)(2,1)S(1)}, u32[]{:S(2)}, u32[]{:S(2)}) collective-permute-start(bf16[128,384]{1,0:T(8,128)(2,1)} %param.11), channel_id=1, source_target_pairs={{0,7},{1,0},{2,1},{3,2},{4,3},{5,4},{6,5},{7,6},{8,15},{9,8},{10,9... | collective-permute-start | bytes 294920 | tf_op jit(solution)/shard_map/ppermute | solution.py:110
  26.9 1.6 collective-permute-done.1
  28.5 4.3 %collective-permute-start.6 = (bf16[192,1024]{1,0:T(8,128)(2,1)S(1)}, bf16[192,1024]{1,0:T(8,128)(2,1)}, u32[]{:S(2)}, u32[]{:S(2)}) collective-permute-start(bf16[192,1024]{1,0:T(8,128)(2,1)S(1)} %collective-permute-done.2.refs_7_), channel_id=1, source_target_pairs={{0,8},{8,16},{16,24},{24,32},{32,40},{40,48},{48,56},{56,0},{1,9},... | collective-permute-start | bytes 1179656 | tf_op jit(solution)/shard_map/ppermute | solution.py:107
  32.8 1.9 collective-permute-start.7
  34.7 1.9 collective-permute-start.4
  36.7 7.5 %collective-permute-start.5 = (bf16[128,384]{1,0:T(8,128)(2,1)S(1)}, bf16[128,384]{1,0:T(8,128)(2,1)S(1)}, u32[]{:S(2)}, u32[]{:S(2)}) collective-permute-start(bf16[128,384]{1,0:T(8,128)(2,1)S(1)} %collective-permute-done.1), channel_id=1, source_target_pairs={{0,7},{1,0},{2,1},{3,2},{4,3},{5,4},{6,5},{7,6},{8,15},{9,8},{10,9... | collective-permute-start | bytes 294920 | tf_op jit(solution)/shard_map/ppermute | solution.py:110
  44.9 1.4 collective-permute-done.5
  46.4 4.5 %collective-permute-start.10 = (bf16[192,1024]{1,0:T(8,128)(2,1)}, bf16[192,1024]{1,0:T(8,128)(2,1)}, u32[]{:S(2)}, u32[]{:S(2)}) collective-permute-start(bf16[192,1024]{1,0:T(8,128)(2,1)} %collective-permute-done.6.refs_6_), channel_id=1, source_target_pairs={{0,8},{8,16},{16,24},{24,32},{32,40},{40,48},{48,56},{56,0},{1,9},... | collective-permute-start | bytes 1179656 | tf_op jit(solution)/shard_map/ppermute | solution.py:107
  50.9 1.9 collective-permute-start.11
  56.6 2.7 %collective-permute-start.8 = (bf16[128,384]{1,0:T(8,128)(2,1)}, bf16[128,384]{1,0:T(8,128)(2,1)S(1)}, u32[]{:S(2)}, u32[]{:S(2)}) collective-permute-start(bf16[128,384]{1,0:T(8,128)(2,1)} %copy-done.9), channel_id=1, source_target_pairs={{0,1},{1,2},{2,3},{3,4},{4,5},{5,6},{6,7},{7,0},{8,9},{9,10},{10,1... | collective-permute-start | bytes 294920 | tf_op jit(solution)/shard_map/ppermute | solution.py:107
  59.3 4.6 %collective-permute-start.9 = (bf16[128,384]{1,0:T(8,128)(2,1)}, bf16[128,384]{1,0:T(8,128)(2,1)S(1)}, u32[]{:S(2)}, u32[]{:S(2)}) collective-permute-start(bf16[128,384]{1,0:T(8,128)(2,1)} %copy-done.11), channel_id=1, source_target_pairs={{0,7},{1,0},{2,1},{3,2},{4,3},{5,4},{6,5},{7,6},{8,15},{9,8},{10,9... | collective-permute-start | bytes 294920 | tf_op jit(solution)/shard_map/ppermute | solution.py:110
  64.8 1.6 collective-permute-done.9
  66.4 4.6 %collective-permute-start.13 = (bf16[192,1024]{1,0:T(8,128)(2,1)}, bf16[192,1024]{1,0:T(8,128)(2,1)S(1)}, u32[]{:S(2)}, u32[]{:S(2)}) collective-permute-start(bf16[192,1024]{1,0:T(8,128)(2,1)} %collective-permute-done.10.refs_5_), channel_id=1, source_target_pairs={{0,8},{8,16},{16,24},{24,32},{32,40},{40,48},{48,56},{56,0},{1,9},... | collective-permute-start | bytes 1179656 | tf_op jit(solution)/shard_map/ppermute | solution.py:107
  72.0 3.9 %collective-permute-start.12 = (bf16[128,384]{1,0:T(8,128)(2,1)S(1)}, bf16[128,384]{1,0:T(8,128)(2,1)S(1)}, u32[]{:S(2)}, u32[]{:S(2)}) collective-permute-start(bf16[128,384]{1,0:T(8,128)(2,1)S(1)} %collective-permute-done.8), channel_id=1, source_target_pairs={{0,1},{1,2},{2,3},{3,4},{4,5},{5,6},{6,7},{7,0},{8,9},{9,10},{10,1... | collective-permute-start | bytes 294920 | tf_op jit(solution)/shard_map/ppermute | solution.py:107
  75.9 4.1 %collective-permute-done.12 = bf16[128,384]{1,0:T(8,128)(2,1)S(1)} collective-permute-done((bf16[128,384]{1,0:T(8,128)(2,1)S(1)}, bf16[128,384]{1,0:T(8,128)(2,1)S(1)}, u32[]{:S(2)}, u32[]{:S(2)}) %collective-permute-start.12) | collective-permute-done | bytes 98336 | tf_op jit(solution)/shard_map/ppermute | solution.py:107
  82.0 20.3 %shard_map.91 = bf16[1536,128]{1,0:T(8,128)(2,1)} custom-call(s32[2]{0:T(128)} %pad_add_fusion.me_ref, s32[144]{0:T(256)} %reshape_squeeze.10.mask_ref, bf16[192,1024]{1,0:T(8,128)(2,1)} %bitcast.123, bf16[192,1024]{1,0:T(8,128)(2,1)} %copy-done.7, bf16[192,1024]{1,0:T(8,128)(2,1)} %collective-permute-done.7.refs_2_, ...), custom_call_target="tpu_custom_call" | custom-call | tf_op jit(solution)/shard_map/pallas_call | solution.py:80
  102.4 9.4 %all-to-all-start = ((bf16[8,192,128]{2,1,0:T(8,128)(2,1)}), bf16[8,192,128]{2,1,0:T(8,128)(2,1)S(1)}, u32[]{:S(2)}, u32[]{:S(2)}) async-start(bf16[8,192,128]{2,1,0:T(8,128)(2,1)} %bitcast.120), calls=%async_computation | async-start | bytes 786432 | tf_op jit(solution)/shard_map/all_to_all | solution.py:134
  114.4 4.0 %copy.30 = bf16[8,8,128,128]{2,3,1,0:T(8,128)(2,1)} copy(bf16[8,8,128,128]{3,2,1,0:T(8,128)(2,1)} %bitcast.119) | data formatting | bytes 4194304 | tf_op jit(solution)/shard_map/reshape | solution.py:135
  118.3 2.5 %all-to-all-done = bf16[8,192,128]{2,1,0:T(8,128)(2,1)S(1)} async-done(((bf16[8,192,128]{2,1,0:T(8,128)(2,1)}), bf16[8,192,128]{2,1,0:T(8,128)(2,1)S(1)}, u32[]{:S(2)}, u32[]{:S(2)}) %all-to-all-start) | async-done | bytes 393248 | tf_op jit(solution)/shard_map/all_to_all | solution.py:134
  121.6 2.7 %multiply_reduce_fusion = (f32[192]{0:T(256)S(1)}, f32[192,1024]{1,0:T(8,128)S(1)}) fusion(bf16[1024,128,8]{1,0,2:T(8,128)(2,1)} %bitcast.114, bf16[8,192,128]{2,1,0:T(8,128)(2,1)} %copy-done.2, bf16[1,192,1024]{2,1,0:T(8,128)(2,1)S(1)} %copy-done.1), kind=kOutput, calls=%fused_computation.22 | convolution fusion | flops 403439424 | bytes 3670784 | tf_op jit(solution)/shard_map/nsk,sekc->nec/dot_general | solution.py:136
  125.0 2.2 copy.36
  127.1 9.1 %all-to-all-start.1 = ((bf16[64,96,128]{2,1,0:T(8,128)(2,1)}), bf16[64,96,128]{2,1,0:T(8,128)(2,1)}, u32[]{:S(2)}, u32[]{:S(2)}) async-start(bf16[64,96,128]{2,1,0:T(8,128)(2,1)} %bitcast.116), calls=%async_computation.1 | async-start | bytes 3145728 | tf_op jit(solution)/shard_map/all_to_all | solution.py:162
  136.2 2.5 %copy.48 = bf16[64,8,8,128]{3,2,1,0:T(8,128)(2,1)} copy(bf16[64,8,8,128]{3,1,2,0:T(8,128)(2,1)} %bitcast.124) | data formatting | bytes 2097152
  138.7 30.0 %all-to-all-done.1 = bf16[64,96,128]{2,1,0:T(8,128)(2,1)} async-done(((bf16[64,96,128]{2,1,0:T(8,128)(2,1)}), bf16[64,96,128]{2,1,0:T(8,128)(2,1)}, u32[]{:S(2)}, u32[]{:S(2)}) %all-to-all-start.1) | async-done | bytes 1572896 | tf_op jit(solution)/shard_map/all_to_all | solution.py:162
  168.8 3.3 %convolution_bitcast_fusion = f32[768,1024]{1,0:T(8,128)S(1)} fusion(bf16[8,128,1024]{2,1,0:T(8,128)(2,1)S(1)} %bitcast.113, bf16[768,8,128]{2,1,0:T(8,128)(2,1)} %bitcast.21), kind=kOutput, calls=%fused_computation | convolution fusion | flops 1610612736 | bytes 6815744 | tf_op jit(solution)/shard_map/pjl,jlf->pf/dot_general | solution.py:165
  173.1 2.2 copy.39
  175.3 8.7 %all-to-all-start.2 = ((bf16[64,96,128]{2,1,0:T(8,128)(2,1)}), bf16[64,96,128]{2,1,0:T(8,128)(2,1)}, u32[]{:S(2)}, u32[]{:S(2)}) async-start(bf16[64,96,128]{2,1,0:T(8,128)(2,1)} %bitcast.115), calls=%async_computation.2 | async-start | bytes 3145728 | tf_op jit(solution)/shard_map/all_to_all | solution.py:178
  184.0 37.9 %all-to-all-done.2 = bf16[64,96,128]{2,1,0:T(8,128)(2,1)} async-done(((bf16[64,96,128]{2,1,0:T(8,128)(2,1)}), bf16[64,96,128]{2,1,0:T(8,128)(2,1)}, u32[]{:S(2)}, u32[]{:S(2)}) %all-to-all-start.2) | async-done | bytes 1572896 | tf_op jit(solution)/shard_map/all_to_all | solution.py:178
  221.9 2.2 fusion.4
  (74 shorter events, 17.2 us)
Async XLA Ops:
  6.5 162.2 %copy-start = (bf16[1,1024,1024]{2,1,0:T(8,128)(2,1)S(1)}, bf16[1,1024,1024]{2,1,0:T(8,128)(2,1)}, u32[]{:S(2)}) copy-start(bf16[1,1024,1024]{2,1,0:T(8,128)(2,1)} %param.16) | copy-start | bytes 6291460
  6.5 107.8 %all-gather.3.cloned.1.call-start = ((), (), s32[]{:S(2)}) async-start(), calls=%async_computation.3 | async-start | bytes 2129920 | tf_op jit(solution)/shard_map/all_gather | solution.py:130
  7.3 21.3 %collective-permute-start.2 = (bf16[192,1024]{1,0:T(8,128)(2,1)}, bf16[192,1024]{1,0:T(8,128)(2,1)S(1)}, u32[]{:S(2)}, u32[]{:S(2)}) collective-permute-start(bf16[192,1024]{1,0:T(8,128)(2,1)} %bitcast.121), channel_id=1, source_target_pairs={{0,8},{8,16},{16,24},{24,32},{32,40},{40,48},{48,56},{56,0},{1,9},... | collective-permute-start | bytes 1179656 | tf_op jit(solution)/shard_map/ppermute | solution.py:107
  10.8 17.8 %collective-permute-start.3 = (bf16[192,1024]{1,0:T(8,128)(2,1)}, bf16[192,1024]{1,0:T(8,128)(2,1)S(1)}, u32[]{:S(2)}, u32[]{:S(2)}) collective-permute-start(bf16[192,1024]{1,0:T(8,128)(2,1)} %bitcast.122), channel_id=1, source_target_pairs={{0,56},{8,0},{16,8},{24,16},{32,24},{40,32},{48,40},{56,48},{1,57}... | collective-permute-start | bytes 1179656 | tf_op jit(solution)/shard_map/ppermute | solution.py:110
  13.1 13.7 %collective-permute-start = (bf16[128,384]{1,0:T(8,128)(2,1)}, bf16[128,384]{1,0:T(8,128)(2,1)S(1)}, u32[]{:S(2)}, u32[]{:S(2)}) collective-permute-start(bf16[128,384]{1,0:T(8,128)(2,1)} %param.11), channel_id=1, source_target_pairs={{0,1},{1,2},{2,3},{3,4},{4,5},{5,6},{6,7},{7,0},{8,9},{9,10},{10,1... | collective-permute-start | bytes 294920 | tf_op jit(solution)/shard_map/ppermute | solution.py:107
  17.4 11.1 %collective-permute-start.1 = (bf16[128,384]{1,0:T(8,128)(2,1)}, bf16[128,384]{1,0:T(8,128)(2,1)S(1)}, u32[]{:S(2)}, u32[]{:S(2)}) collective-permute-start(bf16[128,384]{1,0:T(8,128)(2,1)} %param.11), channel_id=1, source_target_pairs={{0,7},{1,0},{2,1},{3,2},{4,3},{5,4},{6,5},{7,6},{8,15},{9,8},{10,9... | collective-permute-start | bytes 294920 | tf_op jit(solution)/shard_map/ppermute | solution.py:110
  28.5 22.3 %copy-start.10 = (bf16[128,384]{1,0:T(8,128)(2,1)}, bf16[128,384]{1,0:T(8,128)(2,1)S(1)}, u32[]{:S(2)}) copy-start(bf16[128,384]{1,0:T(8,128)(2,1)S(1)} %collective-permute-done.1) | copy-start | bytes 294916
  28.5 52.6 %copy-start.6 = (bf16[192,1024]{1,0:T(8,128)(2,1)}, bf16[192,1024]{1,0:T(8,128)(2,1)S(1)}, u32[]{:S(2)}) copy-start(bf16[192,1024]{1,0:T(8,128)(2,1)S(1)} %collective-permute-done.2.refs_7_) | copy-start | bytes 1179652
  28.5 22.3 %copy-start.7 = (bf16[192,1024]{1,0:T(8,128)(2,1)}, bf16[192,1024]{1,0:T(8,128)(2,1)S(1)}, u32[]{:S(2)}) copy-start(bf16[192,1024]{1,0:T(8,128)(2,1)S(1)} %collective-permute-done.3.refs_1_) | copy-start | bytes 1179652
  28.5 17.8 %collective-permute-start.6 = (bf16[192,1024]{1,0:T(8,128)(2,1)S(1)}, bf16[192,1024]{1,0:T(8,128)(2,1)}, u32[]{:S(2)}, u32[]{:S(2)}) collective-permute-start(bf16[192,1024]{1,0:T(8,128)(2,1)S(1)} %collective-permute-done.2.refs_7_), channel_id=1, source_target_pairs={{0,8},{8,16},{16,24},{24,32},{32,40},{40,48},{48,56},{56,0},{1,9},... | collective-permute-start | bytes 1179656 | tf_op jit(solution)/shard_map/ppermute | solution.py:107
  32.8 13.5 %collective-permute-start.7 = (bf16[192,1024]{1,0:T(8,128)(2,1)S(1)}, bf16[192,1024]{1,0:T(8,128)(2,1)}, u32[]{:S(2)}, u32[]{:S(2)}) collective-permute-start(bf16[192,1024]{1,0:T(8,128)(2,1)S(1)} %collective-permute-done.3.refs_1_), channel_id=1, source_target_pairs={{0,56},{8,0},{16,8},{24,16},{32,24},{40,32},{48,40},{56,48},{1,57}... | collective-permute-start | bytes 1179656 | tf_op jit(solution)/shard_map/ppermute | solution.py:110
  34.7 10.2 %collective-permute-start.4 = (bf16[128,384]{1,0:T(8,128)(2,1)S(1)}, bf16[128,384]{1,0:T(8,128)(2,1)S(1)}, u32[]{:S(2)}, u32[]{:S(2)}) collective-permute-start(bf16[128,384]{1,0:T(8,128)(2,1)S(1)} %collective-permute-done), channel_id=1, source_target_pairs={{0,1},{1,2},{2,3},{3,4},{4,5},{5,6},{6,7},{7,0},{8,9},{9,10},{10,1... | collective-permute-start | bytes 294920 | tf_op jit(solution)/shard_map/ppermute | solution.py:107
  36.7 9.7 %collective-permute-start.5 = (bf16[128,384]{1,0:T(8,128)(2,1)S(1)}, bf16[128,384]{1,0:T(8,128)(2,1)S(1)}, u32[]{:S(2)}, u32[]{:S(2)}) collective-permute-start(bf16[128,384]{1,0:T(8,128)(2,1)S(1)} %collective-permute-done.1), channel_id=1, source_target_pairs={{0,7},{1,0},{2,1},{3,2},{4,3},{5,4},{6,5},{7,6},{8,15},{9,8},{10,9... | collective-permute-start | bytes 294920 | tf_op jit(solution)/shard_map/ppermute | solution.py:110
  44.9 6.0 %copy-start.9 = (bf16[128,384]{1,0:T(8,128)(2,1)}, bf16[128,384]{1,0:T(8,128)(2,1)S(1)}, u32[]{:S(2)}) copy-start(bf16[128,384]{1,0:T(8,128)(2,1)S(1)} %collective-permute-done.4) | copy-start | bytes 294916
  46.3 4.5 %copy-start.11 = (bf16[128,384]{1,0:T(8,128)(2,1)}, bf16[128,384]{1,0:T(8,128)(2,1)S(1)}, u32[]{:S(2)}) copy-start(bf16[128,384]{1,0:T(8,128)(2,1)S(1)} %collective-permute-done.5) | copy-start | bytes 294916
  46.4 20.0 %collective-permute-start.10 = (bf16[192,1024]{1,0:T(8,128)(2,1)}, bf16[192,1024]{1,0:T(8,128)(2,1)}, u32[]{:S(2)}, u32[]{:S(2)}) collective-permute-start(bf16[192,1024]{1,0:T(8,128)(2,1)} %collective-permute-done.6.refs_6_), channel_id=1, source_target_pairs={{0,8},{8,16},{16,24},{24,32},{32,40},{40,48},{48,56},{56,0},{1,9},... | collective-permute-start | bytes 1179656 | tf_op jit(solution)/shard_map/ppermute | solution.py:107
  50.9 15.5 %collective-permute-start.11 = (bf16[192,1024]{1,0:T(8,128)(2,1)}, bf16[192,1024]{1,0:T(8,128)(2,1)}, u32[]{:S(2)}, u32[]{:S(2)}) collective-permute-start(bf16[192,1024]{1,0:T(8,128)(2,1)} %collective-permute-done.7.refs_2_), channel_id=1, source_target_pairs={{0,56},{8,0},{16,8},{24,16},{32,24},{40,32},{48,40},{56,48},{1,57}... | collective-permute-start | bytes 1179656 | tf_op jit(solution)/shard_map/ppermute | solution.py:110
  56.6 8.2 %collective-permute-start.8 = (bf16[128,384]{1,0:T(8,128)(2,1)}, bf16[128,384]{1,0:T(8,128)(2,1)S(1)}, u32[]{:S(2)}, u32[]{:S(2)}) collective-permute-start(bf16[128,384]{1,0:T(8,128)(2,1)} %copy-done.9), channel_id=1, source_target_pairs={{0,1},{1,2},{2,3},{3,4},{4,5},{5,6},{6,7},{7,0},{8,9},{9,10},{10,1... | collective-permute-start | bytes 294920 | tf_op jit(solution)/shard_map/ppermute | solution.py:107
  59.3 7.1 %collective-permute-start.9 = (bf16[128,384]{1,0:T(8,128)(2,1)}, bf16[128,384]{1,0:T(8,128)(2,1)S(1)}, u32[]{:S(2)}, u32[]{:S(2)}) collective-permute-start(bf16[128,384]{1,0:T(8,128)(2,1)} %copy-done.11), channel_id=1, source_target_pairs={{0,7},{1,0},{2,1},{3,2},{4,3},{5,4},{6,5},{7,6},{8,15},{9,8},{10,9... | collective-permute-start | bytes 294920 | tf_op jit(solution)/shard_map/ppermute | solution.py:110
  66.4 13.6 %collective-permute-start.13 = (bf16[192,1024]{1,0:T(8,128)(2,1)}, bf16[192,1024]{1,0:T(8,128)(2,1)S(1)}, u32[]{:S(2)}, u32[]{:S(2)}) collective-permute-start(bf16[192,1024]{1,0:T(8,128)(2,1)} %collective-permute-done.10.refs_5_), channel_id=1, source_target_pairs={{0,8},{8,16},{16,24},{24,32},{32,40},{40,48},{48,56},{56,0},{1,9},... | collective-permute-start | bytes 1179656 | tf_op jit(solution)/shard_map/ppermute | solution.py:107
  72.0 8.1 %collective-permute-start.12 = (bf16[128,384]{1,0:T(8,128)(2,1)S(1)}, bf16[128,384]{1,0:T(8,128)(2,1)S(1)}, u32[]{:S(2)}, u32[]{:S(2)}) collective-permute-start(bf16[128,384]{1,0:T(8,128)(2,1)S(1)} %collective-permute-done.8), channel_id=1, source_target_pairs={{0,1},{1,2},{2,3},{3,4},{4,5},{5,6},{6,7},{7,0},{8,9},{9,10},{10,1... | collective-permute-start | bytes 294920 | tf_op jit(solution)/shard_map/ppermute | solution.py:107
  80.0 1.1 copy-start.8
  81.1 0.9 copy-start.5
  102.4 11.1 %copy-start.12 = (s32[1,192,2]{1,2,0:T(2,128)S(1)}, s32[1,192,2]{1,2,0:T(2,128)}, u32[]{:S(2)}) copy-start(s32[1,192,2]{1,2,0:T(2,128)} %param.14) | copy-start | bytes 4612
  102.4 18.5 %all-to-all-start = ((bf16[8,192,128]{2,1,0:T(8,128)(2,1)}), bf16[8,192,128]{2,1,0:T(8,128)(2,1)S(1)}, u32[]{:S(2)}, u32[]{:S(2)}) async-start(bf16[8,192,128]{2,1,0:T(8,128)(2,1)} %bitcast.120), calls=%async_computation | async-start | bytes 786432 | tf_op jit(solution)/shard_map/all_to_all | solution.py:134
  114.4 7.2 %copy-start.1 = (bf16[1,192,1024]{2,1,0:T(8,128)(2,1)S(1)}, bf16[1,192,1024]{2,1,0:T(8,128)(2,1)}, u32[]{:S(2)}) copy-start(bf16[1,192,1024]{2,1,0:T(8,128)(2,1)} %param.9) | copy-start | bytes 1179652
  121.6 2.7 %copy-start.3 = (bf16[768,192]{0,1:T(8,128)(2,1)S(1)}, bf16[768,192]{0,1:T(8,128)(2,1)}, u32[]{:S(2)}) copy-start(bf16[768,192]{0,1:T(8,128)(2,1)} %fusion.17) | copy-start | bytes 884740
  121.6 2.7 %copy-start.13 = (f32[1024]{0:T(1024)S(1)}, f32[1024]{0:T(1024)}, u32[]{:S(2)}) copy-start(f32[1024]{0:T(1024)} %param.13) | copy-start | bytes 12292
  127.1 41.6 %all-to-all-start.1 = ((bf16[64,96,128]{2,1,0:T(8,128)(2,1)}), bf16[64,96,128]{2,1,0:T(8,128)(2,1)}, u32[]{:S(2)}, u32[]{:S(2)}) async-start(bf16[64,96,128]{2,1,0:T(8,128)(2,1)} %bitcast.116), calls=%async_computation.1 | async-start | bytes 3145728 | tf_op jit(solution)/shard_map/all_to_all | solution.py:162
  168.8 3.3 %copy-start.4 = (bf16[64,8,8,128]{3,2,1,0:T(8,128)(2,1)S(1)}, bf16[64,8,8,128]{3,2,1,0:T(8,128)(2,1)}, u32[]{:S(2)}) copy-start(bf16[64,8,8,128]{3,2,1,0:T(8,128)(2,1)} %copy.48) | copy-start | bytes 3145732
  175.3 8.7 %copy-start.14 = (f32[1,192,2]{1,2,0:T(2,128)S(1)}, f32[1,192,2]{1,2,0:T(2,128)}, u32[]{:S(2)}) copy-start(f32[1,192,2]{1,2,0:T(2,128)} %param.15) | copy-start | bytes 4612
  175.3 46.6 %all-to-all-start.2 = ((bf16[64,96,128]{2,1,0:T(8,128)(2,1)}), bf16[64,96,128]{2,1,0:T(8,128)(2,1)}, u32[]{:S(2)}, u32[]{:S(2)}) async-start(bf16[64,96,128]{2,1,0:T(8,128)(2,1)} %bitcast.115), calls=%async_computation.2 | async-start | bytes 3145728 | tf_op jit(solution)/shard_map/all_to_all | solution.py:178
  (1 other events, 0.7 us)
Sparse Core Ops, SparseCore 0:
  10.4 88.4 all-gather.2

commit v13 on v12

--- a/solution.py
+++ b/solution.py
@@ -178,9 +178,12 @@
     returned = lax.all_to_all(
         processed.reshape(packed), ("seq", "exp"), split_axis=0, concat_axis=0, tiled=True
     ).reshape(experts * capacity, width // lanes, lanes)
-    picked = jnp.einsum(
-        "pnk,pjl->knjl", select, returned, preferred_element_type=jnp.float32
-    ).reshape(TOP, node_dev, width)
+    picked = [
+        jnp.einsum(
+            "pn,pjl->njl", select[:, :, k], returned, preferred_element_type=jnp.float32
+        ).reshape(node_dev, width)
+        for k in range(TOP)
+    ]
     expert_sum = picked[0] * gates[0][:, 0, None] + picked[1] * gates[0][:, 1, None]
     return (mixed + expert_sum).astype(jnp.bfloat16)[None]
 

time: 234 us -> 235 us (level)
  the two profiles are of different devices: /device:TPU:22 before, /device:TPU:20 now
where the time goes in v13:
time: 235 us; the launch traced here: 233 us
  starting transfers between devices  83.7 us (36%)
  waiting for transfers between devices  81.3 us (35%)
  Pallas kernels  20.3 us (9%)
  local copies, waits for them, and re-layouts  18.4 us (8%)
  between operations  13.8 us (6%)
  matrix products  12.4 us (5%)
  other arithmetic  3.55 us (2%)
    all_to_all x1, waiting for transfers between devices, per_device(): lax.all_to_all(processed.reshape(packed), ('seq', 'exp'), split_axis=0, c...  37.7 us
    all_to_all x1, waiting for transfers between devices, per_device(): lax.all_to_all(outgoing, ('seq', 'exp'), split_axis=0, concat_axis=0, til...  30 us
    ppermute x8, starting transfers between devices, ring_gather(): moving[which][0] = lax.ppermute(moving[which][0], axis, right)  29.6 us
    ppermute x6, starting transfers between devices, ring_gather(): moving[which][1] = lax.ppermute(moving[which][1], axis, left)  26.8 us
    pallas_call x1, Pallas kernels, attention(): pl.pallas_call(kernel, out_shape=jax.ShapeDtypeStruct((nodes, heads * HEA...  20.3 us
    all_to_all x1, starting transfers between devices, per_device(): lax.all_to_all(attended, 'seq', split_axis=0, concat_axis=1, tiled=True)  9.41 us
    all_to_all x1, starting transfers between devices, per_device(): lax.all_to_all(outgoing, ('seq', 'exp'), split_axis=0, concat_axis=0, til...  9.13 us
    unnamed x39, local copies, waits for them, and re-layouts  8.77 us
  transfers between devices with their start and end apart: 18, of which 9 were waited for; matrix products, arithmetic and copies ran while one was open for 7% of the time, Pallas kernels for 9%

profile of v13, /device:TPU:20, one launch (start us, length us, event | category | flops | bytes accessed | tf_op | source)
XLA Modules:
  0.0 233.5 jit_solution(15057210615293821277)
XLA Ops:
  7.3 3.5 %collective-permute-start.2 = (bf16[192,1024]{1,0:T(8,128)(2,1)}, bf16[192,1024]{1,0:T(8,128)(2,1)S(1)}, u32[]{:S(2)}, u32[]{:S(2)}) collective-permute-start(bf16[192,1024]{1,0:T(8,128)(2,1)} %bitcast.120), channel_id=1, source_target_pairs={{0,8},{8,16},{16,24},{24,32},{32,40},{40,48},{48,56},{56,0},{1,9},... | collective-permute-start | bytes 1179656 | tf_op jit(solution)/shard_map/ppermute | solution.py:107
  10.8 2.4 %collective-permute-start.3 = (bf16[192,1024]{1,0:T(8,128)(2,1)}, bf16[192,1024]{1,0:T(8,128)(2,1)S(1)}, u32[]{:S(2)}, u32[]{:S(2)}) collective-permute-start(bf16[192,1024]{1,0:T(8,128)(2,1)} %bitcast.121), channel_id=1, source_target_pairs={{0,56},{8,0},{16,8},{24,16},{32,24},{40,32},{48,40},{56,48},{1,57}... | collective-permute-start | bytes 1179656 | tf_op jit(solution)/shard_map/ppermute | solution.py:110
  13.1 4.3 %collective-permute-start = (bf16[128,384]{1,0:T(8,128)(2,1)}, bf16[128,384]{1,0:T(8,128)(2,1)S(1)}, u32[]{:S(2)}, u32[]{:S(2)}) collective-permute-start(bf16[128,384]{1,0:T(8,128)(2,1)} %param.11), channel_id=1, source_target_pairs={{0,1},{1,2},{2,3},{3,4},{4,5},{5,6},{6,7},{7,0},{8,9},{9,10},{10,1... | collective-permute-start | bytes 294920 | tf_op jit(solution)/shard_map/ppermute | solution.py:107
  17.4 8.6 %collective-permute-start.1 = (bf16[128,384]{1,0:T(8,128)(2,1)}, bf16[128,384]{1,0:T(8,128)(2,1)S(1)}, u32[]{:S(2)}, u32[]{:S(2)}) collective-permute-start(bf16[128,384]{1,0:T(8,128)(2,1)} %param.11), channel_id=1, source_target_pairs={{0,7},{1,0},{2,1},{3,2},{4,3},{5,4},{6,5},{7,6},{8,15},{9,8},{10,9... | collective-permute-start | bytes 294920 | tf_op jit(solution)/shard_map/ppermute | solution.py:110
  26.9 1.6 collective-permute-done.1
  28.5 4.3 %collective-permute-start.6 = (bf16[192,1024]{1,0:T(8,128)(2,1)S(1)}, bf16[192,1024]{1,0:T(8,128)(2,1)}, u32[]{:S(2)}, u32[]{:S(2)}) collective-permute-start(bf16[192,1024]{1,0:T(8,128)(2,1)S(1)} %collective-permute-done.2.refs_7_), channel_id=1, source_target_pairs={{0,8},{8,16},{16,24},{24,32},{32,40},{40,48},{48,56},{56,0},{1,9},... | collective-permute-start | bytes 1179656 | tf_op jit(solution)/shard_map/ppermute | solution.py:107
  32.8 1.9 collective-permute-start.7
  34.7 1.9 collective-permute-start.4
  36.7 7.5 %collective-permute-start.5 = (bf16[128,384]{1,0:T(8,128)(2,1)S(1)}, bf16[128,384]{1,0:T(8,128)(2,1)S(1)}, u32[]{:S(2)}, u32[]{:S(2)}) collective-permute-start(bf16[128,384]{1,0:T(8,128)(2,1)S(1)} %collective-permute-done.1), channel_id=1, source_target_pairs={{0,7},{1,0},{2,1},{3,2},{4,3},{5,4},{6,5},{7,6},{8,15},{9,8},{10,9... | collective-permute-start | bytes 294920 | tf_op jit(solution)/shard_map/ppermute | solution.py:110
  46.4 4.4 %collective-permute-start.10 = (bf16[192,1024]{1,0:T(8,128)(2,1)}, bf16[192,1024]{1,0:T(8,128)(2,1)}, u32[]{:S(2)}, u32[]{:S(2)}) collective-permute-start(bf16[192,1024]{1,0:T(8,128)(2,1)} %collective-permute-done.6.refs_6_), channel_id=1, source_target_pairs={{0,8},{8,16},{16,24},{24,32},{32,40},{40,48},{48,56},{56,0},{1,9},... | collective-permute-start | bytes 1179656 | tf_op jit(solution)/shard_map/ppermute | solution.py:107
  50.8 1.9 collective-permute-start.11
  56.6 2.7 %collective-permute-start.8 = (bf16[128,384]{1,0:T(8,128)(2,1)}, bf16[128,384]{1,0:T(8,128)(2,1)S(1)}, u32[]{:S(2)}, u32[]{:S(2)}) collective-permute-start(bf16[128,384]{1,0:T(8,128)(2,1)} %copy-done.9), channel_id=1, source_target_pairs={{0,1},{1,2},{2,3},{3,4},{4,5},{5,6},{6,7},{7,0},{8,9},{9,10},{10,1... | collective-permute-start | bytes 294920 | tf_op jit(solution)/shard_map/ppermute | solution.py:107
  59.3 4.6 %collective-permute-start.9 = (bf16[128,384]{1,0:T(8,128)(2,1)}, bf16[128,384]{1,0:T(8,128)(2,1)S(1)}, u32[]{:S(2)}, u32[]{:S(2)}) collective-permute-start(bf16[128,384]{1,0:T(8,128)(2,1)} %copy-done.11), channel_id=1, source_target_pairs={{0,7},{1,0},{2,1},{3,2},{4,3},{5,4},{6,5},{7,6},{8,15},{9,8},{10,9... | collective-permute-start | bytes 294920 | tf_op jit(solution)/shard_map/ppermute | solution.py:110
  64.8 1.6 collective-permute-done.9
  66.4 4.6 %collective-permute-start.13 = (bf16[192,1024]{1,0:T(8,128)(2,1)}, bf16[192,1024]{1,0:T(8,128)(2,1)S(1)}, u32[]{:S(2)}, u32[]{:S(2)}) collective-permute-start(bf16[192,1024]{1,0:T(8,128)(2,1)} %collective-permute-done.10.refs_5_), channel_id=1, source_target_pairs={{0,8},{8,16},{16,24},{24,32},{32,40},{40,48},{48,56},{56,0},{1,9},... | collective-permute-start | bytes 1179656 | tf_op jit(solution)/shard_map/ppermute | solution.py:107
  72.0 3.9 %collective-permute-start.12 = (bf16[128,384]{1,0:T(8,128)(2,1)S(1)}, bf16[128,384]{1,0:T(8,128)(2,1)S(1)}, u32[]{:S(2)}, u32[]{:S(2)}) collective-permute-start(bf16[128,384]{1,0:T(8,128)(2,1)S(1)} %collective-permute-done.8), channel_id=1, source_target_pairs={{0,1},{1,2},{2,3},{3,4},{4,5},{5,6},{6,7},{7,0},{8,9},{9,10},{10,1... | collective-permute-start | bytes 294920 | tf_op jit(solution)/shard_map/ppermute | solution.py:107
  75.9 4.1 %collective-permute-done.12 = bf16[128,384]{1,0:T(8,128)(2,1)S(1)} collective-permute-done((bf16[128,384]{1,0:T(8,128)(2,1)S(1)}, bf16[128,384]{1,0:T(8,128)(2,1)S(1)}, u32[]{:S(2)}, u32[]{:S(2)}) %collective-permute-start.12) | collective-permute-done | bytes 98336 | tf_op jit(solution)/shard_map/ppermute | solution.py:107
  82.1 20.3 %shard_map.91 = bf16[1536,128]{1,0:T(8,128)(2,1)} custom-call(s32[2]{0:T(128)} %pad_add_fusion.me_ref, s32[144]{0:T(256)} %reshape_squeeze.10.mask_ref, bf16[192,1024]{1,0:T(8,128)(2,1)} %bitcast.122, bf16[192,1024]{1,0:T(8,128)(2,1)} %copy-done.7, bf16[192,1024]{1,0:T(8,128)(2,1)} %collective-permute-done.7.refs_2_, ...), custom_call_target="tpu_custom_call" | custom-call | tf_op jit(solution)/shard_map/pallas_call | solution.py:80
  102.4 9.4 %all-to-all-start = ((bf16[8,192,128]{2,1,0:T(8,128)(2,1)}), bf16[8,192,128]{2,1,0:T(8,128)(2,1)S(1)}, u32[]{:S(2)}, u32[]{:S(2)}) async-start(bf16[8,192,128]{2,1,0:T(8,128)(2,1)} %bitcast.119), calls=%async_computation | async-start | bytes 786432 | tf_op jit(solution)/shard_map/all_to_all | solution.py:134
  114.4 4.0 %copy.26 = bf16[8,8,128,128]{2,3,1,0:T(8,128)(2,1)} copy(bf16[8,8,128,128]{3,2,1,0:T(8,128)(2,1)} %bitcast.118) | data formatting | bytes 4194304 | tf_op jit(solution)/shard_map/reshape | solution.py:135
  118.4 2.5 %all-to-all-done = bf16[8,192,128]{2,1,0:T(8,128)(2,1)S(1)} async-done(((bf16[8,192,128]{2,1,0:T(8,128)(2,1)}), bf16[8,192,128]{2,1,0:T(8,128)(2,1)S(1)}, u32[]{:S(2)}, u32[]{:S(2)}) %all-to-all-start) | async-done | bytes 393248 | tf_op jit(solution)/shard_map/all_to_all | solution.py:134
  121.6 2.7 %multiply_reduce_fusion = (f32[192]{0:T(256)S(1)}, f32[192,1024]{1,0:T(8,128)S(1)}) fusion(bf16[1024,128,8]{1,0,2:T(8,128)(2,1)} %bitcast.115, bf16[8,192,128]{2,1,0:T(8,128)(2,1)} %copy-done.2, bf16[1,192,1024]{2,1,0:T(8,128)(2,1)S(1)} %copy-done.1), kind=kOutput, calls=%fused_computation.24 | convolution fusion | flops 403439424 | bytes 3670784 | tf_op jit(solution)/shard_map/nsk,sekc->nec/dot_general | solution.py:136
  125.0 2.1 copy.32
  127.1 9.1 %all-to-all-start.1 = ((bf16[64,96,128]{2,1,0:T(8,128)(2,1)}), bf16[64,96,128]{2,1,0:T(8,128)(2,1)}, u32[]{:S(2)}, u32[]{:S(2)}) async-start(bf16[64,96,128]{2,1,0:T(8,128)(2,1)} %bitcast.117), calls=%async_computation.1 | async-start | bytes 3145728 | tf_op jit(solution)/shard_map/all_to_all | solution.py:162
  136.3 2.5 %copy.38 = bf16[64,8,8,128]{3,2,1,0:T(8,128)(2,1)} copy(bf16[64,8,8,128]{3,1,2,0:T(8,128)(2,1)} %bitcast.123) | data formatting | bytes 2097152
  138.8 30.0 %all-to-all-done.1 = bf16[64,96,128]{2,1,0:T(8,128)(2,1)} async-done(((bf16[64,96,128]{2,1,0:T(8,128)(2,1)}), bf16[64,96,128]{2,1,0:T(8,128)(2,1)}, u32[]{:S(2)}, u32[]{:S(2)}) %all-to-all-start.1) | async-done | bytes 1572896 | tf_op jit(solution)/shard_map/all_to_all | solution.py:162
  168.8 3.3 %convolution_bitcast_fusion = f32[768,1024]{1,0:T(8,128)S(1)} fusion(bf16[8,128,1024]{2,1,0:T(8,128)(2,1)S(1)} %bitcast.114, bf16[768,8,128]{2,1,0:T(8,128)(2,1)} %bitcast.22), kind=kOutput, calls=%fused_computation | convolution fusion | flops 1610612736 | bytes 6815744 | tf_op jit(solution)/shard_map/pjl,jlf->pf/dot_general | solution.py:165
  173.2 2.1 copy.35
  175.3 8.7 %all-to-all-start.2 = ((bf16[64,96,128]{2,1,0:T(8,128)(2,1)}), bf16[64,96,128]{2,1,0:T(8,128)(2,1)}, u32[]{:S(2)}, u32[]{:S(2)}) async-start(bf16[64,96,128]{2,1,0:T(8,128)(2,1)} %bitcast.116), calls=%async_computation.2 | async-start | bytes 3145728 | tf_op jit(solution)/shard_map/all_to_all | solution.py:178
  184.3 37.7 %all-to-all-done.2 = bf16[64,96,128]{2,1,0:T(8,128)(2,1)} async-done(((bf16[64,96,128]{2,1,0:T(8,128)(2,1)}), bf16[64,96,128]{2,1,0:T(8,128)(2,1)}, u32[]{:S(2)}, u32[]{:S(2)}) %all-to-all-start.2) | async-done | bytes 1572896 | tf_op jit(solution)/shard_map/all_to_all | solution.py:178
  222.0 1.9 fusion.17
  223.9 2.7 %fusion.24 = bf16[1,192,1024]{2,1,0:T(8,128)(2,1)} fusion(f32[192,1024]{1,0:T(8,128)S(1)} %get-tuple-element.36, f32[192,1024]{1,0:T(8,128)S(1)} %fusion.17, bf16[96,8,8,128]{3,2,1,0:T(8,128)(2,1)} %bitcast.44, pred[768,192,2]{0,1,2:T(32,128)(4,1)S(1)} %iota_compare_fusion, f32[192]{0:T(256)S(1)} %bitcast.126), kind=kOutput, calls=%fused_computation.19 | convolution fusion | flops 302776320 | bytes 3687424 | tf_op jit(solution)/shard_map/pn,pjl->njl/dot_general | solution.py:182
  (72 shorter events, 16.7 us)
Async XLA Ops:
  6.5 162.3 %copy-start = (bf16[1,1024,1024]{2,1,0:T(8,128)(2,1)S(1)}, bf16[1,1024,1024]{2,1,0:T(8,128)(2,1)}, u32[]{:S(2)}) copy-start(bf16[1,1024,1024]{2,1,0:T(8,128)(2,1)} %param.16) | copy-start | bytes 6291460
  6.5 107.9 %all-gather.3.cloned.1.call-start = ((), (), s32[]{:S(2)}) async-start(), calls=%async_computation.3 | async-start | bytes 2129920 | tf_op jit(solution)/shard_map/all_gather | solution.py:130
  7.3 21.3 %collective-permute-start.2 = (bf16[192,1024]{1,0:T(8,128)(2,1)}, bf16[192,1024]{1,0:T(8,128)(2,1)S(1)}, u32[]{:S(2)}, u32[]{:S(2)}) collective-permute-start(bf16[192,1024]{1,0:T(8,128)(2,1)} %bitcast.120), channel_id=1, source_target_pairs={{0,8},{8,16},{16,24},{24,32},{32,40},{40,48},{48,56},{56,0},{1,9},... | collective-permute-start | bytes 1179656 | tf_op jit(solution)/shard_map/ppermute | solution.py:107
  10.8 17.8 %collective-permute-start.3 = (bf16[192,1024]{1,0:T(8,128)(2,1)}, bf16[192,1024]{1,0:T(8,128)(2,1)S(1)}, u32[]{:S(2)}, u32[]{:S(2)}) collective-permute-start(bf16[192,1024]{1,0:T(8,128)(2,1)} %bitcast.121), channel_id=1, source_target_pairs={{0,56},{8,0},{16,8},{24,16},{32,24},{40,32},{48,40},{56,48},{1,57}... | collective-permute-start | bytes 1179656 | tf_op jit(solution)/shard_map/ppermute | solution.py:110
  13.1 13.7 %collective-permute-start = (bf16[128,384]{1,0:T(8,128)(2,1)}, bf16[128,384]{1,0:T(8,128)(2,1)S(1)}, u32[]{:S(2)}, u32[]{:S(2)}) collective-permute-start(bf16[128,384]{1,0:T(8,128)(2,1)} %param.11), channel_id=1, source_target_pairs={{0,1},{1,2},{2,3},{3,4},{4,5},{5,6},{6,7},{7,0},{8,9},{9,10},{10,1... | collective-permute-start | bytes 294920 | tf_op jit(solution)/shard_map/ppermute | solution.py:107
  17.4 11.1 %collective-permute-start.1 = (bf16[128,384]{1,0:T(8,128)(2,1)}, bf16[128,384]{1,0:T(8,128)(2,1)S(1)}, u32[]{:S(2)}, u32[]{:S(2)}) collective-permute-start(bf16[128,384]{1,0:T(8,128)(2,1)} %param.11), channel_id=1, source_target_pairs={{0,7},{1,0},{2,1},{3,2},{4,3},{5,4},{6,5},{7,6},{8,15},{9,8},{10,9... | collective-permute-start | bytes 294920 | tf_op jit(solution)/shard_map/ppermute | solution.py:110
  28.5 22.3 %copy-start.10 = (bf16[128,384]{1,0:T(8,128)(2,1)}, bf16[128,384]{1,0:T(8,128)(2,1)S(1)}, u32[]{:S(2)}) copy-start(bf16[128,384]{1,0:T(8,128)(2,1)S(1)} %collective-permute-done.1) | copy-start | bytes 294916
  28.5 52.6 %copy-start.6 = (bf16[192,1024]{1,0:T(8,128)(2,1)}, bf16[192,1024]{1,0:T(8,128)(2,1)S(1)}, u32[]{:S(2)}) copy-start(bf16[192,1024]{1,0:T(8,128)(2,1)S(1)} %collective-permute-done.2.refs_7_) | copy-start | bytes 1179652
  28.5 22.3 %copy-start.7 = (bf16[192,1024]{1,0:T(8,128)(2,1)}, bf16[192,1024]{1,0:T(8,128)(2,1)S(1)}, u32[]{:S(2)}) copy-start(bf16[192,1024]{1,0:T(8,128)(2,1)S(1)} %collective-permute-done.3.refs_1_) | copy-start | bytes 1179652
  28.5 17.8 %collective-permute-start.6 = (bf16[192,1024]{1,0:T(8,128)(2,1)S(1)}, bf16[192,1024]{1,0:T(8,128)(2,1)}, u32[]{:S(2)}, u32[]{:S(2)}) collective-permute-start(bf16[192,1024]{1,0:T(8,128)(2,1)S(1)} %collective-permute-done.2.refs_7_), channel_id=1, source_target_pairs={{0,8},{8,16},{16,24},{24,32},{32,40},{40,48},{48,56},{56,0},{1,9},... | collective-permute-start | bytes 1179656 | tf_op jit(solution)/shard_map/ppermute | solution.py:107
  32.8 13.5 %collective-permute-start.7 = (bf16[192,1024]{1,0:T(8,128)(2,1)S(1)}, bf16[192,1024]{1,0:T(8,128)(2,1)}, u32[]{:S(2)}, u32[]{:S(2)}) collective-permute-start(bf16[192,1024]{1,0:T(8,128)(2,1)S(1)} %collective-permute-done.3.refs_1_), channel_id=1, source_target_pairs={{0,56},{8,0},{16,8},{24,16},{32,24},{40,32},{48,40},{56,48},{1,57}... | collective-permute-start | bytes 1179656 | tf_op jit(solution)/shard_map/ppermute | solution.py:110
  34.7 10.2 %collective-permute-start.4 = (bf16[128,384]{1,0:T(8,128)(2,1)S(1)}, bf16[128,384]{1,0:T(8,128)(2,1)S(1)}, u32[]{:S(2)}, u32[]{:S(2)}) collective-permute-start(bf16[128,384]{1,0:T(8,128)(2,1)S(1)} %collective-permute-done), channel_id=1, source_target_pairs={{0,1},{1,2},{2,3},{3,4},{4,5},{5,6},{6,7},{7,0},{8,9},{9,10},{10,1... | collective-permute-start | bytes 294920 | tf_op jit(solution)/shard_map/ppermute | solution.py:107
  36.7 9.7 %collective-permute-start.5 = (bf16[128,384]{1,0:T(8,128)(2,1)S(1)}, bf16[128,384]{1,0:T(8,128)(2,1)S(1)}, u32[]{:S(2)}, u32[]{:S(2)}) collective-permute-start(bf16[128,384]{1,0:T(8,128)(2,1)S(1)} %collective-permute-done.1), channel_id=1, source_target_pairs={{0,7},{1,0},{2,1},{3,2},{4,3},{5,4},{6,5},{7,6},{8,15},{9,8},{10,9... | collective-permute-start | bytes 294920 | tf_op jit(solution)/shard_map/ppermute | solution.py:110
  44.9 5.9 %copy-start.9 = (bf16[128,384]{1,0:T(8,128)(2,1)}, bf16[128,384]{1,0:T(8,128)(2,1)S(1)}, u32[]{:S(2)}) copy-start(bf16[128,384]{1,0:T(8,128)(2,1)S(1)} %collective-permute-done.4) | copy-start | bytes 294916
  46.3 4.5 %copy-start.11 = (bf16[128,384]{1,0:T(8,128)(2,1)}, bf16[128,384]{1,0:T(8,128)(2,1)S(1)}, u32[]{:S(2)}) copy-start(bf16[128,384]{1,0:T(8,128)(2,1)S(1)} %collective-permute-done.5) | copy-start | bytes 294916
  46.4 20.1 %collective-permute-start.10 = (bf16[192,1024]{1,0:T(8,128)(2,1)}, bf16[192,1024]{1,0:T(8,128)(2,1)}, u32[]{:S(2)}, u32[]{:S(2)}) collective-permute-start(bf16[192,1024]{1,0:T(8,128)(2,1)} %collective-permute-done.6.refs_6_), channel_id=1, source_target_pairs={{0,8},{8,16},{16,24},{24,32},{32,40},{40,48},{48,56},{56,0},{1,9},... | collective-permute-start | bytes 1179656 | tf_op jit(solution)/shard_map/ppermute | solution.py:107
  50.8 15.6 %collective-permute-start.11 = (bf16[192,1024]{1,0:T(8,128)(2,1)}, bf16[192,1024]{1,0:T(8,128)(2,1)}, u32[]{:S(2)}, u32[]{:S(2)}) collective-permute-start(bf16[192,1024]{1,0:T(8,128)(2,1)} %collective-permute-done.7.refs_2_), channel_id=1, source_target_pairs={{0,56},{8,0},{16,8},{24,16},{32,24},{40,32},{48,40},{56,48},{1,57}... | collective-permute-start | bytes 1179656 | tf_op jit(solution)/shard_map/ppermute | solution.py:110
  56.6 8.2 %collective-permute-start.8 = (bf16[128,384]{1,0:T(8,128)(2,1)}, bf16[128,384]{1,0:T(8,128)(2,1)S(1)}, u32[]{:S(2)}, u32[]{:S(2)}) collective-permute-start(bf16[128,384]{1,0:T(8,128)(2,1)} %copy-done.9), channel_id=1, source_target_pairs={{0,1},{1,2},{2,3},{3,4},{4,5},{5,6},{6,7},{7,0},{8,9},{9,10},{10,1... | collective-permute-start | bytes 294920 | tf_op jit(solution)/shard_map/ppermute | solution.py:107
  59.3 7.1 %collective-permute-start.9 = (bf16[128,384]{1,0:T(8,128)(2,1)}, bf16[128,384]{1,0:T(8,128)(2,1)S(1)}, u32[]{:S(2)}, u32[]{:S(2)}) collective-permute-start(bf16[128,384]{1,0:T(8,128)(2,1)} %copy-done.11), channel_id=1, source_target_pairs={{0,7},{1,0},{2,1},{3,2},{4,3},{5,4},{6,5},{7,6},{8,15},{9,8},{10,9... | collective-permute-start | bytes 294920 | tf_op jit(solution)/shard_map/ppermute | solution.py:110
  66.4 13.6 %collective-permute-start.13 = (bf16[192,1024]{1,0:T(8,128)(2,1)}, bf16[192,1024]{1,0:T(8,128)(2,1)S(1)}, u32[]{:S(2)}, u32[]{:S(2)}) collective-permute-start(bf16[192,1024]{1,0:T(8,128)(2,1)} %collective-permute-done.10.refs_5_), channel_id=1, source_target_pairs={{0,8},{8,16},{16,24},{24,32},{32,40},{40,48},{48,56},{56,0},{1,9},... | collective-permute-start | bytes 1179656 | tf_op jit(solution)/shard_map/ppermute | solution.py:107
  72.0 8.1 %collective-permute-start.12 = (bf16[128,384]{1,0:T(8,128)(2,1)S(1)}, bf16[128,384]{1,0:T(8,128)(2,1)S(1)}, u32[]{:S(2)}, u32[]{:S(2)}) collective-permute-start(bf16[128,384]{1,0:T(8,128)(2,1)S(1)} %collective-permute-done.8), channel_id=1, source_target_pairs={{0,1},{1,2},{2,3},{3,4},{4,5},{5,6},{6,7},{7,0},{8,9},{9,10},{10,1... | collective-permute-start | bytes 294920 | tf_op jit(solution)/shard_map/ppermute | solution.py:107
  80.0 1.1 copy-start.8
  81.2 0.9 copy-start.5
  102.4 11.1 %copy-start.12 = (s32[1,192,2]{1,2,0:T(2,128)S(1)}, s32[1,192,2]{1,2,0:T(2,128)}, u32[]{:S(2)}) copy-start(s32[1,192,2]{1,2,0:T(2,128)} %param.14) | copy-start | bytes 4612
  102.4 18.5 %all-to-all-start = ((bf16[8,192,128]{2,1,0:T(8,128)(2,1)}), bf16[8,192,128]{2,1,0:T(8,128)(2,1)S(1)}, u32[]{:S(2)}, u32[]{:S(2)}) async-start(bf16[8,192,128]{2,1,0:T(8,128)(2,1)} %bitcast.119), calls=%async_computation | async-start | bytes 786432 | tf_op jit(solution)/shard_map/all_to_all | solution.py:134
  114.4 7.2 %copy-start.1 = (bf16[1,192,1024]{2,1,0:T(8,128)(2,1)S(1)}, bf16[1,192,1024]{2,1,0:T(8,128)(2,1)}, u32[]{:S(2)}) copy-start(bf16[1,192,1024]{2,1,0:T(8,128)(2,1)} %param.9) | copy-start | bytes 1179652
  121.6 2.7 %copy-start.3 = (bf16[768,192]{0,1:T(8,128)(2,1)S(1)}, bf16[768,192]{0,1:T(8,128)(2,1)}, u32[]{:S(2)}) copy-start(bf16[768,192]{0,1:T(8,128)(2,1)} %convert_reduce_fusion) | copy-start | bytes 884740
  121.6 2.7 %copy-start.13 = (f32[1024]{0:T(1024)S(1)}, f32[1024]{0:T(1024)}, u32[]{:S(2)}) copy-start(f32[1024]{0:T(1024)} %param.13) | copy-start | bytes 12292
  127.1 41.6 %all-to-all-start.1 = ((bf16[64,96,128]{2,1,0:T(8,128)(2,1)}), bf16[64,96,128]{2,1,0:T(8,128)(2,1)}, u32[]{:S(2)}, u32[]{:S(2)}) async-start(bf16[64,96,128]{2,1,0:T(8,128)(2,1)} %bitcast.117), calls=%async_computation.1 | async-start | bytes 3145728 | tf_op jit(solution)/shard_map/all_to_all | solution.py:162
  168.8 3.3 %copy-start.4 = (bf16[64,8,8,128]{3,2,1,0:T(8,128)(2,1)S(1)}, bf16[64,8,8,128]{3,2,1,0:T(8,128)(2,1)}, u32[]{:S(2)}) copy-start(bf16[64,8,8,128]{3,2,1,0:T(8,128)(2,1)} %copy.38) | copy-start | bytes 3145732
  175.3 8.7 %copy-start.14 = (f32[1,192,2]{1,2,0:T(2,128)S(1)}, f32[1,192,2]{1,2,0:T(2,128)}, u32[]{:S(2)}) copy-start(f32[1,192,2]{1,2,0:T(2,128)} %param.15) | copy-start | bytes 4612
  175.3 46.7 %all-to-all-start.2 = ((bf16[64,96,128]{2,1,0:T(8,128)(2,1)}), bf16[64,96,128]{2,1,0:T(8,128)(2,1)}, u32[]{:S(2)}, u32[]{:S(2)}) async-start(bf16[64,96,128]{2,1,0:T(8,128)(2,1)} %bitcast.116), calls=%async_computation.2 | async-start | bytes 3145728 | tf_op jit(solution)/shard_map/all_to_all | solution.py:178
  (1 other events, 0.7 us)
Sparse Core Ops, SparseCore 0:
  10.4 88.4 all-gather.2
